TPU v7x, 128 devices: a whole 4x4x4 slice. The times are simulated.
128 devices in a mesh: dp: 4 (over z_hi, core), ctx: 32 (over x, y, z_lo).
Axes of the slice: x: 4, y: 4, z: 4 (z_hi: 2, z_lo: 2; z = z_hi * 2 + z_lo), core: 2. Of those that a mesh axis runs over, the one named last changes fastest.
Arguments:
- hidden: bfloat16 [4, 8192, 8192], P('dp', 'ctx')
- norm_gain: bfloat16 [8192], replicated, may hold values from 0.5 to 2
- queries: bfloat16 [4, 8192, 4096], P('dp', 'ctx')
- key_weight: bfloat16 [8192, 512], P('dp'), may hold values from -0.0625 to 0.0625
- value_weight: bfloat16 [8192, 512], P('dp'), may hold values from -0.0625 to 0.0625
- block_lists: int32 [4, 32, 64, 12], P('dp', 'ctx'), may hold values from 0 to 63, as said below
- block_counts: int32 [4, 32, 64], P('dp', 'ctx'), may hold values from 1 to 12, as said below
Outputs:
- attended: bfloat16 [4, 8192, 4096], P('dp', 'ctx')
Inputs may be any that keep to these rules, and one draw needn't show every extreme that they name: `block_lists`: for each spreadsheet, head and query block i, the first block_counts entries are distinct key blocks: the first is i, each later one is smaller than the one before (the blocks of i's ancestors in that head's header tree, nearest first); entries past the count equal i and are to be ignored. `block_counts`: every spreadsheet has a query block with 12 listed blocks; the counts differ much from head to head.
All inputs are finite; a program needn't handle non-finite values.
Results may differ from a plain program's by a relative error of at most 0.0078.
Values may be sent and summed in bfloat16 or wider, within the bound.
No kernel may reach another device: no remote copies, remote signals or barrier semaphores. Data moves between devices by JAX's collectives and lax.ppermute only.
A program may use at most 128 MiB of HBM per device.

v0:
```python
import math

import jax
import jax.numpy as jnp
from jax import lax
from jax.sharding import PartitionSpec as P

KVH = 4
HD = 128
BLK = 128
MAXB = 12


def on_device(hidden, norm_gain, queries, key_weight, value_weight, block_lists, block_counts):
    upcast = hidden[0].astype(jnp.float32)
    mean_square = jnp.mean(upcast * upcast, axis=-1, keepdims=True)
    normed = (upcast * lax.rsqrt(mean_square + 1e-05) * norm_gain.astype(jnp.float32)).astype(
        jnp.bfloat16
    )
    local_rows = normed.shape[0]
    key_part = jnp.einsum(
        "df,td->ft",
        lax.all_gather(key_weight, "dp", axis=0, tiled=True),
        normed,
        preferred_element_type=jnp.float32,
    )
    value_part = jnp.einsum(
        "df,td->ft",
        lax.all_gather(value_weight, "dp", axis=0, tiled=True),
        normed,
        preferred_element_type=jnp.float32,
    )
    paired = jnp.stack([key_part, value_part]).astype(jnp.bfloat16)
    ctx_size = lax.axis_size("ctx")
    copies_per_head = ctx_size // KVH
    widened = jnp.broadcast_to(
        paired.reshape(2, KVH, 1, HD, local_rows), (2, KVH, copies_per_head, HD, local_rows)
    )
    widened = widened.reshape(2, ctx_size * HD, local_rows)
    head_pair = lax.all_to_all(widened, "ctx", split_axis=1, concat_axis=2, tiled=True)
    head_queries = lax.all_to_all(queries[0], "ctx", split_axis=1, concat_axis=0, tiled=True)
    sequence_rows = head_queries.shape[0]
    heads_here = head_queries.shape[1] // HD
    block_total = sequence_rows // BLK
    query_blocks = head_queries.reshape(block_total, BLK, heads_here, HD)
    key_blocks = head_pair[0].reshape(HD, block_total, BLK)
    value_blocks = head_pair[1].reshape(HD, block_total, BLK)
    lists_here = block_lists[0]
    counts_here = block_counts[0]
    score_scale = HD ** (-0.5)
    within_rows = jnp.arange(BLK)[None, :, None, None]
    within_cols = jnp.arange(BLK)[None, None, None, :]
    block_ids = jnp.arange(block_total, dtype=jnp.int32)
    group_blocks = math.gcd(block_total, 4)

    def one_group(group_index):
        first_block = group_index * group_blocks
        query_group = lax.dynamic_slice_in_dim(query_blocks, first_block, group_blocks, 0)
        lists_group = lax.dynamic_slice_in_dim(lists_here, first_block, group_blocks, 1)
        counts_group = lax.dynamic_slice_in_dim(counts_here, first_block, group_blocks, 1)

        def slot_scores(slot_index):
            chosen = lax.dynamic_index_in_dim(lists_group, slot_index, axis=2, keepdims=False)
            selector = (chosen[..., None] == block_ids).astype(jnp.bfloat16)
            picked = jnp.einsum(
                "hnb,dbk->dhnk", selector, key_blocks, preferred_element_type=jnp.float32
            ).astype(jnp.bfloat16)
            scores = (
                jnp.einsum(
                    "nthd,dhnk->nthk", query_group, picked, preferred_element_type=jnp.float32
                )
                * score_scale
            )
            live_slots = (slot_index < counts_group).T[:, None, :, None]
            allowed = live_slots & ((slot_index > 0) | (within_cols <= within_rows))
            return jnp.where(allowed, scores, -jnp.inf)

        masked = jnp.stack([slot_scores(slot_index) for slot_index in range(MAXB)])
        row_peak = jnp.max(masked, axis=(0, 4))
        exponent = jnp.exp(masked - row_peak[None, ..., None])
        denominator = jnp.sum(exponent, axis=(0, 4))
        value_selector = (lists_group[..., None] == block_ids).astype(jnp.bfloat16)
        picked_values = jnp.einsum(
            "hnsb,dbk->dhnsk", value_selector, value_blocks, preferred_element_type=jnp.float32
        ).astype(jnp.bfloat16)
        weighted = jnp.einsum(
            "snthk,dhnsk->nthd",
            exponent.astype(jnp.bfloat16),
            picked_values,
            preferred_element_type=jnp.float32,
        )
        return (weighted / denominator[..., None]).astype(jnp.bfloat16)

    grouped = lax.map(one_group, jnp.arange(block_total // group_blocks))
    attended_heads = grouped.reshape(sequence_rows, heads_here * HD)
    restored = lax.all_to_all(attended_heads, "ctx", split_axis=0, concat_axis=1, tiled=True)
    return restored[None]


def solution(mesh):
    return jax.shard_map(
        on_device,
        mesh=mesh,
        in_specs=(
            P("dp", "ctx", None),
            P(),
            P("dp", "ctx", None),
            P("dp", None),
            P("dp", None),
            P("dp", "ctx", None, None),
            P("dp", "ctx", None),
        ),
        out_specs=P("dp", "ctx", None),
        check_vma=False,
    )
```

profile of v0, /device:TPU:0, one launch (start us, length us, event | category | flops | bytes accessed | tf_op | source)
XLA Modules:
  0.0 765.8 jit_solution(2363139343889659978)
XLA Ops:
  8.0 3.1 fusion.144
  11.1 62.8 %all-gather.3.cloned.1.call-done = bf16[8192,512]{1,0:T(8,128)(2,1)} async-done(((bf16[2048,512]{1,0:T(8,128)(2,1)}), bf16[8192,512]{1,0:T(8,128)(2,1)}) %all-gather.3.cloned.1.call-update) | async-done | bytes 8388624 | tf_op jit(solution)/shard_map/all_gather | solution.py:23
  74.0 7.0 fusion.149
  81.1 56.2 %all-gather.5.cloned.1.call-done = bf16[8192,512]{1,0:T(8,128)(2,1)} async-done(((bf16[2048,512]{1,0:T(8,128)(2,1)}), bf16[8192,512]{1,0:T(8,128)(2,1)}) %all-gather.5.cloned.1.call-update) | async-done | bytes 8388624 | tf_op jit(solution)/shard_map/all_gather | solution.py:29
  137.3 7.0 fusion.152
  145.6 5.8 broadcast_in_dim.27
  151.4 7.4 all-to-all-start
  159.3 2.2 copy.88
  161.5 60.2 %all-to-all-done = bf16[2,4096,256]{2,0,1:T(2,128)(2,1)} async-done(((bf16[2,4096,256]{2,0,1:T(2,128)(2,1)}), bf16[2,4096,256]{2,0,1:T(2,128)(2,1)}, u32[]{:S(2)}, u32[]{:S(2)}) %all-to-all-start) | async-done | bytes 4194336 | tf_op jit(solution)/shard_map/all_to_all | solution.py:40
  221.7 6.5 all-to-all-start.1
  228.1 2.7 copy.85
  230.9 2.2 fusion.155
  233.1 3.2 copy.86
  236.3 2.9 copy.90
  239.2 4.1 copy.87
  243.3 3.3 copy.91
  246.6 9.7 %all-to-all-done.1 = bf16[256,32,128]{2,0,1:T(8,128)(2,1)} async-done(((bf16[256,32,128]{2,0,1:T(8,128)(2,1)}), bf16[256,32,128]{2,0,1:T(8,128)(2,1)}, u32[]{:S(2)}, u32[]{:S(2)}) %all-to-all-start.1) | async-done | bytes 2097184 | tf_op jit(solution)/shard_map/all_to_all | solution.py:41
  256.3 464.4 %while.12 = (s32[]{:T(128)}, bf16[16,4,128,1,128]{4,2,1,0,3:T(8,128)(2,1)}, s32[16]{0:T(128)S(1)}, s32[1,64,12]{1,0,2:T(1,128)S(1)}, bf16[128,64,128]{2,1,0:T(8,...) while((s32[]{:T(128)}, ...), condition=%wide.region_15.16_spmd.clone.clone, body=%wide.region_1.15_spmd.clone.clone.sunk | while | flops 611275840 | bytes 96700944 | solution.py:94
  264.8 1.1 bitcast_dynamic-update-slice_fusion.56
  268.0 1.1 bitcast_dynamic-update-slice_fusion.60
  269.6 1.1 bitcast_dynamic-update-slice_fusion.62
  274.4 1.1 bitcast_dynamic-update-slice_fusion.68
  281.1 2.5 convert_bitcast_fusion.2
  293.8 1.1 bitcast_dynamic-update-slice_fusion.56
  310.2 2.5 convert_bitcast_fusion.2
  327.6 1.1 bitcast_dynamic-update-slice_fusion.62
  332.4 1.1 bitcast_dynamic-update-slice_fusion.68
  339.2 2.5 convert_bitcast_fusion.2
  351.8 1.1 bitcast_dynamic-update-slice_fusion.56
  355.0 1.1 bitcast_dynamic-update-slice_fusion.60
  356.6 1.1 bitcast_dynamic-update-slice_fusion.62
  368.2 2.5 convert_bitcast_fusion.2
  397.2 2.5 convert_bitcast_fusion.2
  426.3 2.5 convert_bitcast_fusion.2
  455.3 2.5 convert_bitcast_fusion.2
  484.3 2.5 convert_bitcast_fusion.2
  513.3 2.5 convert_bitcast_fusion.2
  542.3 2.5 convert_bitcast_fusion.2
  571.4 2.5 convert_bitcast_fusion.2
  600.4 2.5 convert_bitcast_fusion.2
  629.4 2.5 convert_bitcast_fusion.2
  658.4 2.5 convert_bitcast_fusion.2
  675.9 1.1 bitcast_dynamic-update-slice_fusion.62
  687.5 2.5 convert_bitcast_fusion.2
  716.5 2.5 convert_bitcast_fusion.2
  720.8 31.3 %all_to_all.47 = bf16[32,256,128]{2,1,0:T(8,128)(2,1)S(1)} all-to-all(bf16[32,256,128]{2,1,0:T(8,128)(2,1)} %bitcast.662), channel_id=1, replica_groups=mesh['dp'=4,'ctx'=32] {'ctx'}, dimensions={0} | all-to-all | bytes 4194304 | tf_op jit(solution)/shard_map/all_to_all | solution.py:96
  752.1 2.9 copy.93
  754.9 4.1 copy.94
  (1370 shorter events, 396.8 us)
Async XLA Ops:
  6.5 67.4 %all-gather.3.cloned.1.call-start = ((), (), s32[]{:S(2)}) async-start(), calls=%async_computation.3 | async-start | bytes 10485760 | tf_op jit(solution)/shard_map/all_gather | solution.py:23
  7.3 130.1 %all-gather.5.cloned.1.call-start = ((), (), s32[]{:S(2)}) async-start(), calls=%async_computation.4 | async-start | bytes 10485760 | tf_op jit(solution)/shard_map/all_gather | solution.py:29
  151.4 7.5 copy-start.13
  151.4 70.3 %all-to-all-start = ((bf16[2,4096,256]{2,0,1:T(2,128)(2,1)}), bf16[2,4096,256]{2,0,1:T(2,128)(2,1)}, u32[]{:S(2)}, u32[]{:S(2)}) async-start(bf16[2,4096,256]{2,0,1:T(2,128)(2,1)} %bitcast.654), calls=%async_computation | async-start | bytes 8388608 | tf_op jit(solution)/shard_map/all_to_all | solution.py:40
  221.7 34.7 %all-to-all-start.1 = ((bf16[256,32,128]{2,0,1:T(8,128)(2,1)}), bf16[256,32,128]{2,0,1:T(8,128)(2,1)}, u32[]{:S(2)}, u32[]{:S(2)}) async-start(bf16[256,32,128]{2,0,1:T(8,128)(2,1)} %copy.88), calls=%async_computation.1 | async-start | bytes 4194304 | tf_op jit(solution)/shard_map/all_to_all | solution.py:41
  243.3 13.1 %copy-start.14 = (s32[1,1,64,12]{2,1,3,0:T(1,128)S(1)}, s32[1,1,64,12]{2,1,3,0:T(1,128)}, u32[]{:S(2)}) copy-start(s32[1,1,64,12]{2,1,3,0:T(1,128)} %param.14) | copy-start | bytes 9220
  243.3 13.1 %copy-start.18 = (s32[1,1,64]{2,1,0:T(1,128)S(1)}, s32[1,1,64]{2,1,0:T(1,128)}, u32[]{:S(2)}) copy-start(s32[1,1,64]{2,1,0:T(1,128)} %param.15) | copy-start | bytes 772
  267.5 9.9 %copy-start = (f32[4,1,128,128]{3,2,0,1:T(8,128)}, f32[4,1,128,128]{3,2,0,1:T(8,128)S(1)}, u32[]{:S(2)}) copy-start(f32[4,1,128,128]{3,2,0,1:T(8,128)S(1)} %get-tuple-element.388) | copy-start | bytes 786436 | tf_op jit(solution)/shard_map/while
  269.1 8.2 %copy-start.1 = (f32[4,1,128,128]{3,2,0,1:T(8,128)}, f32[4,1,128,128]{3,2,0,1:T(8,128)S(1)}, u32[]{:S(2)}) copy-start(f32[4,1,128,128]{3,2,0,1:T(8,128)S(1)} %get-tuple-element.392) | copy-start | bytes 786436 | tf_op jit(solution)/shard_map/while
  270.7 6.6 copy-start.3
  296.5 9.9 %copy-start = (f32[4,1,128,128]{3,2,0,1:T(8,128)}, f32[4,1,128,128]{3,2,0,1:T(8,128)S(1)}, u32[]{:S(2)}) copy-start(f32[4,1,128,128]{3,2,0,1:T(8,128)S(1)} %get-tuple-element.388) | copy-start | bytes 786436 | tf_op jit(solution)/shard_map/while
  298.1 8.2 %copy-start.1 = (f32[4,1,128,128]{3,2,0,1:T(8,128)}, f32[4,1,128,128]{3,2,0,1:T(8,128)S(1)}, u32[]{:S(2)}) copy-start(f32[4,1,128,128]{3,2,0,1:T(8,128)S(1)} %get-tuple-element.392) | copy-start | bytes 786436 | tf_op jit(solution)/shard_map/while
  325.6 9.9 %copy-start = (f32[4,1,128,128]{3,2,0,1:T(8,128)}, f32[4,1,128,128]{3,2,0,1:T(8,128)S(1)}, u32[]{:S(2)}) copy-start(f32[4,1,128,128]{3,2,0,1:T(8,128)S(1)} %get-tuple-element.388) | copy-start | bytes 786436 | tf_op jit(solution)/shard_map/while
  327.2 8.2 %copy-start.1 = (f32[4,1,128,128]{3,2,0,1:T(8,128)}, f32[4,1,128,128]{3,2,0,1:T(8,128)S(1)}, u32[]{:S(2)}) copy-start(f32[4,1,128,128]{3,2,0,1:T(8,128)S(1)} %get-tuple-element.392) | copy-start | bytes 786436 | tf_op jit(solution)/shard_map/while
  328.8 6.6 copy-start.3
  354.6 9.9 %copy-start = (f32[4,1,128,128]{3,2,0,1:T(8,128)}, f32[4,1,128,128]{3,2,0,1:T(8,128)S(1)}, u32[]{:S(2)}) copy-start(f32[4,1,128,128]{3,2,0,1:T(8,128)S(1)} %get-tuple-element.388) | copy-start | bytes 786436 | tf_op jit(solution)/shard_map/while
  356.2 8.2 %copy-start.1 = (f32[4,1,128,128]{3,2,0,1:T(8,128)}, f32[4,1,128,128]{3,2,0,1:T(8,128)S(1)}, u32[]{:S(2)}) copy-start(f32[4,1,128,128]{3,2,0,1:T(8,128)S(1)} %get-tuple-element.392) | copy-start | bytes 786436 | tf_op jit(solution)/shard_map/while
  357.8 6.6 copy-start.3
  383.6 9.9 %copy-start = (f32[4,1,128,128]{3,2,0,1:T(8,128)}, f32[4,1,128,128]{3,2,0,1:T(8,128)S(1)}, u32[]{:S(2)}) copy-start(f32[4,1,128,128]{3,2,0,1:T(8,128)S(1)} %get-tuple-element.388) | copy-start | bytes 786436 | tf_op jit(solution)/shard_map/while
  385.2 8.2 %copy-start.1 = (f32[4,1,128,128]{3,2,0,1:T(8,128)}, f32[4,1,128,128]{3,2,0,1:T(8,128)S(1)}, u32[]{:S(2)}) copy-start(f32[4,1,128,128]{3,2,0,1:T(8,128)S(1)} %get-tuple-element.392) | copy-start | bytes 786436 | tf_op jit(solution)/shard_map/while
  412.6 9.9 %copy-start = (f32[4,1,128,128]{3,2,0,1:T(8,128)}, f32[4,1,128,128]{3,2,0,1:T(8,128)S(1)}, u32[]{:S(2)}) copy-start(f32[4,1,128,128]{3,2,0,1:T(8,128)S(1)} %get-tuple-element.388) | copy-start | bytes 786436 | tf_op jit(solution)/shard_map/while
  414.2 8.2 %copy-start.1 = (f32[4,1,128,128]{3,2,0,1:T(8,128)}, f32[4,1,128,128]{3,2,0,1:T(8,128)S(1)}, u32[]{:S(2)}) copy-start(f32[4,1,128,128]{3,2,0,1:T(8,128)S(1)} %get-tuple-element.392) | copy-start | bytes 786436 | tf_op jit(solution)/shard_map/while
  415.9 6.6 copy-start.3
  441.7 9.9 %copy-start = (f32[4,1,128,128]{3,2,0,1:T(8,128)}, f32[4,1,128,128]{3,2,0,1:T(8,128)S(1)}, u32[]{:S(2)}) copy-start(f32[4,1,128,128]{3,2,0,1:T(8,128)S(1)} %get-tuple-element.388) | copy-start | bytes 786436 | tf_op jit(solution)/shard_map/while
  443.3 8.2 %copy-start.1 = (f32[4,1,128,128]{3,2,0,1:T(8,128)}, f32[4,1,128,128]{3,2,0,1:T(8,128)S(1)}, u32[]{:S(2)}) copy-start(f32[4,1,128,128]{3,2,0,1:T(8,128)S(1)} %get-tuple-element.392) | copy-start | bytes 786436 | tf_op jit(solution)/shard_map/while
  444.9 6.6 copy-start.3
  470.7 9.9 %copy-start = (f32[4,1,128,128]{3,2,0,1:T(8,128)}, f32[4,1,128,128]{3,2,0,1:T(8,128)S(1)}, u32[]{:S(2)}) copy-start(f32[4,1,128,128]{3,2,0,1:T(8,128)S(1)} %get-tuple-element.388) | copy-start | bytes 786436 | tf_op jit(solution)/shard_map/while
  472.3 8.2 %copy-start.1 = (f32[4,1,128,128]{3,2,0,1:T(8,128)}, f32[4,1,128,128]{3,2,0,1:T(8,128)S(1)}, u32[]{:S(2)}) copy-start(f32[4,1,128,128]{3,2,0,1:T(8,128)S(1)} %get-tuple-element.392) | copy-start | bytes 786436 | tf_op jit(solution)/shard_map/while
  499.7 9.9 %copy-start = (f32[4,1,128,128]{3,2,0,1:T(8,128)}, f32[4,1,128,128]{3,2,0,1:T(8,128)S(1)}, u32[]{:S(2)}) copy-start(f32[4,1,128,128]{3,2,0,1:T(8,128)S(1)} %get-tuple-element.388) | copy-start | bytes 786436 | tf_op jit(solution)/shard_map/while
  501.3 8.2 %copy-start.1 = (f32[4,1,128,128]{3,2,0,1:T(8,128)}, f32[4,1,128,128]{3,2,0,1:T(8,128)S(1)}, u32[]{:S(2)}) copy-start(f32[4,1,128,128]{3,2,0,1:T(8,128)S(1)} %get-tuple-element.392) | copy-start | bytes 786436 | tf_op jit(solution)/shard_map/while
  502.9 6.6 copy-start.3
  528.7 9.9 %copy-start = (f32[4,1,128,128]{3,2,0,1:T(8,128)}, f32[4,1,128,128]{3,2,0,1:T(8,128)S(1)}, u32[]{:S(2)}) copy-start(f32[4,1,128,128]{3,2,0,1:T(8,128)S(1)} %get-tuple-element.388) | copy-start | bytes 786436 | tf_op jit(solution)/shard_map/while
  530.3 8.2 %copy-start.1 = (f32[4,1,128,128]{3,2,0,1:T(8,128)}, f32[4,1,128,128]{3,2,0,1:T(8,128)S(1)}, u32[]{:S(2)}) copy-start(f32[4,1,128,128]{3,2,0,1:T(8,128)S(1)} %get-tuple-element.392) | copy-start | bytes 786436 | tf_op jit(solution)/shard_map/while
  532.0 6.6 copy-start.3
  557.8 9.9 %copy-start = (f32[4,1,128,128]{3,2,0,1:T(8,128)}, f32[4,1,128,128]{3,2,0,1:T(8,128)S(1)}, u32[]{:S(2)}) copy-start(f32[4,1,128,128]{3,2,0,1:T(8,128)S(1)} %get-tuple-element.388) | copy-start | bytes 786436 | tf_op jit(solution)/shard_map/while
  559.4 8.2 %copy-start.1 = (f32[4,1,128,128]{3,2,0,1:T(8,128)}, f32[4,1,128,128]{3,2,0,1:T(8,128)S(1)}, u32[]{:S(2)}) copy-start(f32[4,1,128,128]{3,2,0,1:T(8,128)S(1)} %get-tuple-element.392) | copy-start | bytes 786436 | tf_op jit(solution)/shard_map/while
  586.8 9.9 %copy-start = (f32[4,1,128,128]{3,2,0,1:T(8,128)}, f32[4,1,128,128]{3,2,0,1:T(8,128)S(1)}, u32[]{:S(2)}) copy-start(f32[4,1,128,128]{3,2,0,1:T(8,128)S(1)} %get-tuple-element.388) | copy-start | bytes 786436 | tf_op jit(solution)/shard_map/while
  588.4 8.2 %copy-start.1 = (f32[4,1,128,128]{3,2,0,1:T(8,128)}, f32[4,1,128,128]{3,2,0,1:T(8,128)S(1)}, u32[]{:S(2)}) copy-start(f32[4,1,128,128]{3,2,0,1:T(8,128)S(1)} %get-tuple-element.392) | copy-start | bytes 786436 | tf_op jit(solution)/shard_map/while
  590.0 6.6 copy-start.3
  615.8 9.9 %copy-start = (f32[4,1,128,128]{3,2,0,1:T(8,128)}, f32[4,1,128,128]{3,2,0,1:T(8,128)S(1)}, u32[]{:S(2)}) copy-start(f32[4,1,128,128]{3,2,0,1:T(8,128)S(1)} %get-tuple-element.388) | copy-start | bytes 786436 | tf_op jit(solution)/shard_map/while
  617.4 8.2 %copy-start.1 = (f32[4,1,128,128]{3,2,0,1:T(8,128)}, f32[4,1,128,128]{3,2,0,1:T(8,128)S(1)}, u32[]{:S(2)}) copy-start(f32[4,1,128,128]{3,2,0,1:T(8,128)S(1)} %get-tuple-element.392) | copy-start | bytes 786436 | tf_op jit(solution)/shard_map/while
  644.8 9.9 %copy-start = (f32[4,1,128,128]{3,2,0,1:T(8,128)}, f32[4,1,128,128]{3,2,0,1:T(8,128)S(1)}, u32[]{:S(2)}) copy-start(f32[4,1,128,128]{3,2,0,1:T(8,128)S(1)} %get-tuple-element.388) | copy-start | bytes 786436 | tf_op jit(solution)/shard_map/while
  646.4 8.2 %copy-start.1 = (f32[4,1,128,128]{3,2,0,1:T(8,128)}, f32[4,1,128,128]{3,2,0,1:T(8,128)S(1)}, u32[]{:S(2)}) copy-start(f32[4,1,128,128]{3,2,0,1:T(8,128)S(1)} %get-tuple-element.392) | copy-start | bytes 786436 | tf_op jit(solution)/shard_map/while
  673.9 9.9 %copy-start = (f32[4,1,128,128]{3,2,0,1:T(8,128)}, f32[4,1,128,128]{3,2,0,1:T(8,128)S(1)}, u32[]{:S(2)}) copy-start(f32[4,1,128,128]{3,2,0,1:T(8,128)S(1)} %get-tuple-element.388) | copy-start | bytes 786436 | tf_op jit(solution)/shard_map/while
  675.5 8.2 %copy-start.1 = (f32[4,1,128,128]{3,2,0,1:T(8,128)}, f32[4,1,128,128]{3,2,0,1:T(8,128)S(1)}, u32[]{:S(2)}) copy-start(f32[4,1,128,128]{3,2,0,1:T(8,128)S(1)} %get-tuple-element.392) | copy-start | bytes 786436 | tf_op jit(solution)/shard_map/while
  677.1 6.6 copy-start.3
  702.9 9.9 %copy-start = (f32[4,1,128,128]{3,2,0,1:T(8,128)}, f32[4,1,128,128]{3,2,0,1:T(8,128)S(1)}, u32[]{:S(2)}) copy-start(f32[4,1,128,128]{3,2,0,1:T(8,128)S(1)} %get-tuple-element.388) | copy-start | bytes 786436 | tf_op jit(solution)/shard_map/while
  704.5 8.2 %copy-start.1 = (f32[4,1,128,128]{3,2,0,1:T(8,128)}, f32[4,1,128,128]{3,2,0,1:T(8,128)S(1)}, u32[]{:S(2)}) copy-start(f32[4,1,128,128]{3,2,0,1:T(8,128)S(1)} %get-tuple-element.392) | copy-start | bytes 786436 | tf_op jit(solution)/shard_map/while
  (200 other events, 419.6 us)
Sparse Core Ops, SparseCore 0:
  9.0 64.9 all-gather.2
  75.6 61.6 all-gather.4
where the time goes:
time: 771 us; the launch traced here: 766 us
  matrix products  374 us (49%)
  waiting for transfers between devices  190 us (25%)
  local copies, waits for them, and re-layouts  107 us (14%)
  blocking collectives  31.3 us (4%)
  loops' own time  18.3 us (2%)
  other arithmetic  17 us (2%)
  starting transfers between devices  13.9 us (2%)
  between operations  13.5 us (2%)
    dot_general x192, matrix products, slot_scores(): jnp.einsum('nthd,dhnk->nthk', query_group, picked, preferred_element_type...  220 us
    dot_general x192, matrix products, slot_scores(): jnp.einsum('hnb,dbk->dhnk', selector, key_blocks, preferred_element_type=...  84.8 us
    all_gather x1, waiting for transfers between devices, on_device(): lax.all_gather(key_weight, 'dp', axis=0, tiled=True)  62.8 us
    all_to_all x1, waiting for transfers between devices, on_device(): lax.all_to_all(widened, 'ctx', split_axis=1, concat_axis=2, tiled=True)  60.2 us
    all_gather x1, waiting for transfers between devices, on_device(): lax.all_gather(value_weight, 'dp', axis=0, tiled=True)  56.2 us
    while x656, local copies, waits for them, and re-layouts  44.8 us
    dot_general x16, matrix products, one_group(): jnp.einsum('hnsb,dbk->dhnsk', value_selector, value_blocks, preferred_ele...  39.9 us
    all_to_all x1, blocking collectives, on_device(): lax.all_to_all(attended_heads, 'ctx', split_axis=0, concat_axis=1, tiled=...  31.3 us
  transfers between devices with their start and end apart: 4, of which 4 were waited for; matrix products, arithmetic and copies ran while one was open for 4% of the time, Pallas kernels for 0%

commit v1 on v0

v1 whole, which is shorter than its diff:
```python
import jax
import jax.numpy as jnp
from jax import lax
from jax.experimental import pallas as pl
from jax.experimental.pallas import tpu as pltpu
from jax.sharding import PartitionSpec as P

KVH = 4
HD = 128
BLK = 128
MAXB = 12


def attend_kernel(lists_ref, counts_ref, q_ref, k_ref, v_ref, o_ref):
    block = pl.program_id(0)
    query = q_ref[...]
    count = counts_ref[block]
    score_scale = HD ** (-0.5)
    rows = lax.broadcasted_iota(jnp.int32, (BLK, BLK), 0)
    cols = lax.broadcasted_iota(jnp.int32, (BLK, BLK), 1)
    masked = []
    for slot in range(MAXB):
        start = pl.multiple_of(lists_ref[block * MAXB + slot] * BLK, BLK)
        key_tile = k_ref[pl.ds(start, BLK), :]
        scores = (
            lax.dot_general(
                query, key_tile, (((1,), (1,)), ((), ())), preferred_element_type=jnp.float32
            )
            * score_scale
        )
        allowed = slot < count
        if slot == 0:
            allowed = jnp.logical_and(allowed, cols <= rows)
        masked.append(jnp.where(allowed, scores, -jnp.inf))
    peak = masked[0]
    for scores in masked[1:]:
        peak = jnp.maximum(peak, scores)
    row_peak = jnp.max(peak, axis=1, keepdims=True)
    denominator = jnp.zeros((BLK, 1), jnp.float32)
    weighted = jnp.zeros((BLK, HD), jnp.float32)
    for slot in range(MAXB):
        start = pl.multiple_of(lists_ref[block * MAXB + slot] * BLK, BLK)
        value_tile = v_ref[pl.ds(start, BLK), :]
        exponent = jnp.exp(masked[slot] - row_peak)
        denominator = denominator + jnp.sum(exponent, axis=1, keepdims=True)
        weighted = weighted + jnp.dot(
            exponent.astype(jnp.bfloat16), value_tile, preferred_element_type=jnp.float32
        )
    o_ref[...] = (weighted / denominator).astype(o_ref.dtype)


def attend(lists_flat, counts, head_queries, kv_rows):
    sequence_rows = head_queries.shape[0]
    block_total = sequence_rows // BLK
    return pl.pallas_call(
        attend_kernel,
        out_shape=jax.ShapeDtypeStruct((sequence_rows, HD), jnp.bfloat16),
        grid_spec=pltpu.PrefetchScalarGridSpec(
            num_scalar_prefetch=2,
            grid=(block_total,),
            in_specs=[
                pl.BlockSpec((BLK, HD), lambda i, lists, counts: (i, 0)),
                pl.BlockSpec((sequence_rows, HD), lambda i, lists, counts: (0, 0)),
                pl.BlockSpec((sequence_rows, HD), lambda i, lists, counts: (0, 1)),
            ],
            out_specs=pl.BlockSpec((BLK, HD), lambda i, lists, counts: (i, 0)),
        ),
        compiler_params=pltpu.CompilerParams(dimension_semantics=("arbitrary",)),
    )(lists_flat, counts, head_queries, kv_rows, kv_rows)


def on_device(hidden, norm_gain, queries, key_weight, value_weight, block_lists, block_counts):
    upcast = hidden[0].astype(jnp.float32)
    mean_square = jnp.mean(upcast * upcast, axis=-1, keepdims=True)
    normed = (upcast * lax.rsqrt(mean_square + 1e-05) * norm_gain.astype(jnp.float32)).astype(
        jnp.bfloat16
    )
    local_rows = normed.shape[0]
    key_part = jnp.dot(
        normed,
        lax.all_gather(key_weight, "dp", axis=0, tiled=True),
        preferred_element_type=jnp.float32,
    )
    value_part = jnp.dot(
        normed,
        lax.all_gather(value_weight, "dp", axis=0, tiled=True),
        preferred_element_type=jnp.float32,
    )
    paired = jnp.stack([key_part, value_part], axis=1).astype(jnp.bfloat16)
    ctx_size = lax.axis_size("ctx")
    copies_per_head = ctx_size // KVH
    widened = jnp.broadcast_to(
        paired.reshape(local_rows, 2, KVH, 1, HD), (local_rows, 2, KVH, copies_per_head, HD)
    )
    widened = widened.reshape(local_rows, 2, ctx_size, HD)
    head_pair = lax.all_to_all(widened, "ctx", split_axis=2, concat_axis=0, tiled=True)
    head_queries = lax.all_to_all(queries[0], "ctx", split_axis=1, concat_axis=0, tiled=True)
    sequence_rows = head_queries.shape[0]
    kv_rows = head_pair.reshape(sequence_rows, 2 * HD)
    lists_flat = block_lists[0, 0].reshape(-1)
    counts = block_counts[0, 0]
    attended_head = attend(lists_flat, counts, head_queries, kv_rows)
    restored = lax.all_to_all(attended_head, "ctx", split_axis=0, concat_axis=1, tiled=True)
    return restored[None]


def solution(mesh):
    return jax.shard_map(
        on_device,
        mesh=mesh,
        in_specs=(
            P("dp", "ctx", None),
            P(),
            P("dp", "ctx", None),
            P("dp", None),
            P("dp", None),
            P("dp", "ctx", None, None),
            P("dp", "ctx", None),
        ),
        out_specs=P("dp", "ctx", None),
        check_vma=False,
    )
```

time: 771 us -> 375 us (0.49)
  matrix products: 374 us -> 9.53 us
  local copies, waits for them, and re-layouts: 107 us -> 44.1 us
  Pallas kernels: 0 us -> 59.5 us
  loops' own time: 18.3 us -> 0 us
  other arithmetic: 17 us -> 3.17 us
  waiting for transfers between devices: 190 us -> 199 us
    dot_general x418 -> x2, matrix products: 374 us -> 9.53 us  [the longest x1 7.16 us: on_device(): jnp.dot(normed, lax.all_gather(key_weight, 'dp', axis=0, tiled=True), pre...]
    pallas_call x0 -> x1, Pallas kernels: none -> 59.5 us  [attend(): pl.pallas_call(attend_kernel, out_shape=jax.ShapeDtypeStruct((sequence_ro...]
    while x656 -> x0, local copies, waits for them, and re-layouts: 44.8 us -> none
    dot_general x0 -> x2, local copies, waits for them, and re-layouts: none -> 23.7 us  [the longest x1 11.9 us: on_device(): jnp.dot(normed, lax.all_gather(key_weight, 'dp', axis=0, tiled=True), pre...]
    another operation x1 -> x0, loops' own time: 18.3 us -> none  [on_device(): grouped = lax.map(one_group, jnp.arange(block_total // group_blocks))]
    dynamic_slice x48 -> x0, local copies, waits for them, and re-layouts: 13.1 us -> none  [the longest x16 10.4 us: on_device(): grouped = lax.map(one_group, jnp.arange(block_total // group_blocks))]
    all_to_all x1, waiting for transfers between devices: 9.75 us -> 22.7 us  [on_device(): lax.all_to_all(queries[0], 'ctx', split_axis=1, concat_axis=0, tiled=True)]
    dynamic_update_slice x32 -> x0, local copies, waits for them, and re-layouts: 12.9 us -> none  [on_device(): grouped = lax.map(one_group, jnp.arange(block_total // group_blocks))]
  transfers between devices with their start and end apart: 4 -> 4, of which waited for: 4 -> 4; matrix products, arithmetic and copies ran while one was open for 4% -> 6% of each run, Pallas kernels for 0% -> 0%
where the time goes in v1:
time: 375 us; the launch traced here: 374 us
  waiting for transfers between devices  199 us (53%)
  Pallas kernels  59.5 us (16%)
  local copies, waits for them, and re-layouts  44.1 us (12%)
  blocking collectives  31.3 us (8%)
  starting transfers between devices  13.8 us (4%)
  between operations  13.5 us (4%)
  matrix products  9.53 us (3%)
    all_gather x1, waiting for transfers between devices, on_device(): lax.all_gather(key_weight, 'dp', axis=0, tiled=True)  62.8 us
    all_to_all x1, waiting for transfers between devices, on_device(): lax.all_to_all(widened, 'ctx', split_axis=2, concat_axis=0, tiled=True)  60.2 us
    pallas_call x1, Pallas kernels, attend(): pl.pallas_call(attend_kernel, out_shape=jax.ShapeDtypeStruct((sequence_ro...  59.5 us
    all_gather x1, waiting for transfers between devices, on_device(): lax.all_gather(value_weight, 'dp', axis=0, tiled=True)  51.5 us
    all_to_all x1, blocking collectives, on_device(): lax.all_to_all(attended_head, 'ctx', split_axis=0, concat_axis=1, tiled=T...  31.3 us
    all_to_all x1, waiting for transfers between devices, on_device(): lax.all_to_all(queries[0], 'ctx', split_axis=1, concat_axis=0, tiled=True)  22.7 us
    dot_general x1, local copies, waits for them, and re-layouts, on_device(): jnp.dot(normed, lax.all_gather(key_weight, 'dp', axis=0, tiled=True), pre...  11.9 us
    dot_general x1, local copies, waits for them, and re-layouts, on_device(): jnp.dot(normed, lax.all_gather(value_weight, 'dp', axis=0, tiled=True), p...  11.8 us
  transfers between devices with their start and end apart: 4, of which 4 were waited for; matrix products, arithmetic and copies ran while one was open for 6% of the time, Pallas kernels for 0%

profile of v1, /device:TPU:0, one launch (start us, length us, event | category | flops | bytes accessed | tf_op | source)
XLA Modules:
  0.0 373.6 jit_solution(1729047263587859031)
XLA Ops:
  6.5 0.0 copy-start.4
  6.5 0.0 all-gather.3.cloned.1.call-start
  6.5 0.7 all-gather.3.cloned.1.call-update
  7.3 0.0 all-gather.5.cloned.1.call-start
  7.3 0.7 all-gather.5.cloned.1.call-update
  8.0 0.0 copy-done.4
  8.0 3.1 fusion
  11.1 62.8 %all-gather.3.cloned.1.call-done = bf16[8192,512]{1,0:T(8,128)(2,1)} async-done(((bf16[2048,512]{1,0:T(8,128)(2,1)}), bf16[8192,512]{1,0:T(8,128)(2,1)}) %all-gather.3.cloned.1.call-update) | async-done | bytes 8388624 | tf_op jit(solution)/shard_map/all_gather | solution.py:81
  74.0 11.9 %copy.15 = bf16[512,8192]{1,0:T(8,128)(2,1)} copy(bf16[512,8192]{0,1:T(8,128)(2,1)} %bitcast.43) | data formatting | bytes 16777216 | tf_op jit(solution)/shard_map/dot_general | solution.py:79
  85.8 51.5 %all-gather.5.cloned.1.call-done = bf16[8192,512]{1,0:T(8,128)(2,1)} async-done(((bf16[2048,512]{1,0:T(8,128)(2,1)}), bf16[8192,512]{1,0:T(8,128)(2,1)}) %all-gather.5.cloned.1.call-update) | async-done | bytes 8388624 | tf_op jit(solution)/shard_map/all_gather | solution.py:86
  137.3 11.8 %copy.16 = bf16[512,8192]{1,0:T(8,128)(2,1)} copy(bf16[512,8192]{0,1:T(8,128)(2,1)} %bitcast.44) | data formatting | bytes 16777216 | tf_op jit(solution)/shard_map/dot_general | solution.py:84
  149.2 0.0 copy-start
  149.2 0.0 copy-start.2
  149.2 7.2 %fusion.6 = bf16[256,1,4,128]{3,0,2,1:T(8,128)(2,1)S(1)} fusion(bf16[4,128,8192]{2,1,0:T(8,128)(2,1)} %bitcast.45, bf16[1,256,8192]{2,1,0:T(8,128)(2,1)} %param.7, f32[8192]{0:T(1024)S(1)} %convert_element_type.22, f32[256]{0:T(256)S(1)} %add_rsqrt_fusion), kind=kOutput, calls=%fused_computation.9 | convolution fusion | flops 2156003328 | bytes 12878848 | tf_op jit(solution)/shard_map/dot_general | solution.py:79
  156.3 0.0 copy-done
  156.3 1.0 copy-done.2
  157.4 2.4 fusion.9
  159.8 0.1 pad_maximum_fusion
  159.8 0.5 copy.17
  160.4 5.8 %broadcast_in_dim.4 = bf16[256,2,4,8,128]{4,1,0,3,2:T(2,128)(2,1)} broadcast(bf16[256,2,4,128]{3,1,0,2:T(2,128)(2,1)S(1)} %copy.17), dimensions={0,1,2,4} | broadcast | bytes 4718592 | tf_op jit(solution)/shard_map/broadcast_in_dim | solution.py:92
  166.1 0.0 copy-start.3
  166.1 7.4 %all-to-all-start.1 = ((bf16[256,2,32,128]{3,1,0,2:T(2,128)(2,1)}), bf16[256,2,32,128]{3,1,0,2:T(2,128)(2,1)}, u32[]{:S(2)}, u32[]{:S(2)}) async-start(bf16[256,2,32,128]{3,1,0,2:T(2,128)(2,1)} %bitcast.42), calls=%async_computation.1 | async-start | bytes 8388608 | tf_op jit(solution)/shard_map/all_to_all | solution.py:96
  173.6 0.0 copy-done.3
  173.6 0.5 copy.19
  174.1 0.0 copy-start.5
  174.1 2.1 copy.14
  176.2 60.2 %all-to-all-done.1 = bf16[256,2,32,128]{3,1,0,2:T(2,128)(2,1)} async-done(((bf16[256,2,32,128]{3,1,0,2:T(2,128)(2,1)}), bf16[256,2,32,128]{3,1,0,2:T(2,128)(2,1)}, u32[]{:S(2)}, u32[]{:S(2)}) %all-to-all-start.1) | async-done | bytes 4194336 | tf_op jit(solution)/shard_map/all_to_all | solution.py:96
  236.4 6.3 %all-to-all-start = ((bf16[256,32,128]{2,0,1:T(8,128)(2,1)}), bf16[256,32,128]{2,0,1:T(8,128)(2,1)S(1)}, u32[]{:S(2)}, u32[]{:S(2)}) async-start(bf16[256,32,128]{2,0,1:T(8,128)(2,1)} %copy.14), calls=%async_computation | async-start | bytes 4194304 | tf_op jit(solution)/shard_map/all_to_all | solution.py:97
  242.8 0.0 copy-done.5
  242.8 0.1 copy.13
  242.9 0.7 reshape_squeeze.3.lists_ref
  243.6 4.7 %copy.22 = bf16[1024,8,2,128]{3,1,2,0:T(8,128)(2,1)} copy(bf16[1024,8,2,128]{3,2,1,0:T(2,128)(2,1)} %bitcast.24) | data formatting | bytes 8388608
  248.3 22.7 %all-to-all-done = bf16[256,32,128]{2,0,1:T(8,128)(2,1)S(1)} async-done(((bf16[256,32,128]{2,0,1:T(8,128)(2,1)}), bf16[256,32,128]{2,0,1:T(8,128)(2,1)S(1)}, u32[]{:S(2)}, u32[]{:S(2)}) %all-to-all-start) | async-done | bytes 2097184 | tf_op jit(solution)/shard_map/all_to_all | solution.py:97
  271.0 0.0 copy-start.1
  271.0 1.3 copy-done.1
  272.3 59.5 %shard_map.73 = bf16[8192,128]{1,0:T(8,128)(2,1)} custom-call(s32[768]{0:T(1024)} %reshape_squeeze.3.lists_ref, s32[64]{0:T(128)} %bitcast.52, bf16[8192,128]{1,0:T(8,128)(2,1)} %bitcast.49, bf16[8192,256]{1,0:T(8,128)(2,1)} %bitcast.40, bf16[8192,256]{1,0:T(8,128)(2,1)} %bitcast.41), custom_call_target="tpu_custom_call" | custom-call | tf_op jit(solution)/shard_map/pallas_call | solution.py:55
  331.8 31.3 %all_to_all.50 = bf16[32,256,128]{2,1,0:T(8,128)(2,1)S(1)} all-to-all(bf16[32,256,128]{2,1,0:T(8,128)(2,1)} %bitcast.50), channel_id=1, replica_groups=mesh['dp'=4,'ctx'=32] {'ctx'}, dimensions={0} | all-to-all | bytes 4194304 | tf_op jit(solution)/shard_map/all_to_all | solution.py:103
  363.1 1.4 copy.18
  364.5 2.3 broadcast_in_dim.5
  (2 shorter events, 0.0 us)
Async XLA Ops:
  6.5 1.5 copy-start.4
  6.5 67.4 %all-gather.3.cloned.1.call-start = ((), (), s32[]{:S(2)}) async-start(), calls=%async_computation.3 | async-start | bytes 10485760 | tf_op jit(solution)/shard_map/all_gather | solution.py:81
  7.3 130.1 %all-gather.5.cloned.1.call-start = ((), (), s32[]{:S(2)}) async-start(), calls=%async_computation.4 | async-start | bytes 10485760 | tf_op jit(solution)/shard_map/all_gather | solution.py:86
  149.2 7.2 %copy-start = (bf16[512,8192]{1,0:T(8,128)(2,1)S(1)}, bf16[512,8192]{1,0:T(8,128)(2,1)}, u32[]{:S(2)}) copy-start(bf16[512,8192]{1,0:T(8,128)(2,1)} %copy.16) | copy-start | bytes 25165828
  149.2 8.2 %copy-start.2 = (bf16[1,256,8192]{2,1,0:T(8,128)(2,1)S(1)}, bf16[1,256,8192]{2,1,0:T(8,128)(2,1)}, u32[]{:S(2)}) copy-start(bf16[1,256,8192]{2,1,0:T(8,128)(2,1)} %param.7) | copy-start | bytes 12582916
  166.1 7.5 %copy-start.3 = (bf16[1,256,4096]{2,1,0:T(8,128)(2,1)S(1)}, bf16[1,256,4096]{2,1,0:T(8,128)(2,1)}, u32[]{:S(2)}) copy-start(bf16[1,256,4096]{2,1,0:T(8,128)(2,1)} %param.9) | copy-start | bytes 6291460
  166.1 70.3 %all-to-all-start.1 = ((bf16[256,2,32,128]{3,1,0,2:T(2,128)(2,1)}), bf16[256,2,32,128]{3,1,0,2:T(2,128)(2,1)}, u32[]{:S(2)}, u32[]{:S(2)}) async-start(bf16[256,2,32,128]{3,1,0,2:T(2,128)(2,1)} %bitcast.42), calls=%async_computation.1 | async-start | bytes 8388608 | tf_op jit(solution)/shard_map/all_to_all | solution.py:96
  174.1 68.7 %copy-start.5 = (s32[1,1,64,12]{2,1,3,0:T(1,128)S(1)}, s32[1,1,64,12]{2,1,3,0:T(1,128)}, u32[]{:S(2)}) copy-start(s32[1,1,64,12]{2,1,3,0:T(1,128)} %param.12) | copy-start | bytes 9220
  236.4 34.6 %all-to-all-start = ((bf16[256,32,128]{2,0,1:T(8,128)(2,1)}), bf16[256,32,128]{2,0,1:T(8,128)(2,1)S(1)}, u32[]{:S(2)}, u32[]{:S(2)}) async-start(bf16[256,32,128]{2,0,1:T(8,128)(2,1)} %copy.14), calls=%async_computation | async-start | bytes 4194304 | tf_op jit(solution)/shard_map/all_to_all | solution.py:97
  271.0 1.3 copy-start.1
Sparse Core Ops, SparseCore 0:
  9.0 64.9 all-gather.2
  75.6 61.6 all-gather.4

commit v2 on v1

--- a/solution.py
+++ b/solution.py
@@ -70,31 +70,30 @@
 
 
 def on_device(hidden, norm_gain, queries, key_weight, value_weight, block_lists, block_counts):
+    head_queries = lax.all_to_all(queries[0], "ctx", split_axis=1, concat_axis=0, tiled=True)
     upcast = hidden[0].astype(jnp.float32)
     mean_square = jnp.mean(upcast * upcast, axis=-1, keepdims=True)
     normed = (upcast * lax.rsqrt(mean_square + 1e-05) * norm_gain.astype(jnp.float32)).astype(
         jnp.bfloat16
     )
-    local_rows = normed.shape[0]
-    key_part = jnp.dot(
-        normed,
-        lax.all_gather(key_weight, "dp", axis=0, tiled=True),
+    local_rows, features = normed.shape
+    dp_size = lax.axis_size("dp")
+    feature_rows = features // dp_size
+    feature_split = normed.reshape(local_rows, dp_size, feature_rows).transpose(1, 0, 2)
+    gathered = lax.all_to_all(feature_split, "dp", split_axis=0, concat_axis=0, tiled=True)
+    local_weight = jnp.concatenate([key_weight, value_weight], axis=1)
+    partial = jnp.dot(
+        gathered.reshape(dp_size * local_rows, feature_rows),
+        local_weight,
         preferred_element_type=jnp.float32,
-    )
-    value_part = jnp.dot(
-        normed,
-        lax.all_gather(value_weight, "dp", axis=0, tiled=True),
-        preferred_element_type=jnp.float32,
-    )
-    paired = jnp.stack([key_part, value_part], axis=1).astype(jnp.bfloat16)
+    ).reshape(dp_size, local_rows, 2 * KVH * HD)
+    summed = lax.psum_scatter(partial, "dp", scatter_dimension=0, tiled=True)
+    paired = summed.reshape(local_rows, 2, KVH, 1, HD).astype(jnp.bfloat16)
     ctx_size = lax.axis_size("ctx")
     copies_per_head = ctx_size // KVH
-    widened = jnp.broadcast_to(
-        paired.reshape(local_rows, 2, KVH, 1, HD), (local_rows, 2, KVH, copies_per_head, HD)
-    )
+    widened = jnp.broadcast_to(paired, (local_rows, 2, KVH, copies_per_head, HD))
     widened = widened.reshape(local_rows, 2, ctx_size, HD)
     head_pair = lax.all_to_all(widened, "ctx", split_axis=2, concat_axis=0, tiled=True)
-    head_queries = lax.all_to_all(queries[0], "ctx", split_axis=1, concat_axis=0, tiled=True)
     sequence_rows = head_queries.shape[0]
     kv_rows = head_pair.reshape(sequence_rows, 2 * HD)
     lists_flat = block_lists[0, 0].reshape(-1)

time: 375 us -> 352 us (0.939)
  waiting for transfers between devices: 199 us -> 130 us
  blocking collectives: 31.3 us -> 87.1 us
  local copies, waits for them, and re-layouts: 44.1 us -> 33 us
  other arithmetic: 3.17 us -> 9.33 us
    all_gather x2 -> x0, waiting for transfers between devices: 114 us -> none  [the longest x1 62.8 us: on_device(): lax.all_gather(key_weight, 'dp', axis=0, tiled=True)]
    all_to_all x0 -> x1, blocking collectives: none -> 55 us  [on_device(): lax.all_to_all(feature_split, 'dp', split_axis=0, concat_axis=0, tiled=True)]
    reduce_scatter x0 -> x1, waiting for transfers between devices: none -> 51.1 us  [on_device(): summed = lax.psum_scatter(partial, 'dp', scatter_dimension=0, tiled=True)]
    dot_general x2 -> x0, local copies, waits for them, and re-layouts: 23.7 us -> none  [the longest x1 11.9 us: on_device(): jnp.dot(normed, lax.all_gather(key_weight, 'dp', axis=0, tiled=True), pre...]
    convert_element_type x0 -> x3, local copies, waits for them, and re-layouts: none -> 7.77 us  [the longest x1 7 us: on_device(): upcast = hidden[0].astype(jnp.float32)]
    unnamed x15 -> x16, local copies, waits for them, and re-layouts: 7.65 us -> 13 us
    transpose x0 -> x1, other arithmetic: none -> 4.74 us  [on_device(): normed.reshape(local_rows, dp_size, feature_rows).transpose(1, 0, 2)]
    dot_general x2 -> x1, matrix products: 9.53 us -> 6.19 us  [on_device(): jnp.dot(gathered.reshape(dp_size * local_rows, feature_rows), local_weigh...]
  transfers between devices with their start and end apart: 4 -> 3, of which waited for: 4 -> 3; matrix products, arithmetic and copies ran while one was open for 6% -> 2% of each run, Pallas kernels for 0% -> 0%
where the time goes in v2:
time: 352 us; the launch traced here: 351 us
  waiting for transfers between devices  130 us (37%)
  blocking collectives  87.1 us (25%)
  Pallas kernels  59.5 us (17%)
  local copies, waits for them, and re-layouts  33 us (9%)
  between operations  13.5 us (4%)
  starting transfers between devices  11.8 us (3%)
  other arithmetic  9.33 us (3%)
  matrix products  6.19 us (2%)
    pallas_call x1, Pallas kernels, attend(): pl.pallas_call(attend_kernel, out_shape=jax.ShapeDtypeStruct((sequence_ro...  59.5 us
    all_to_all x1, waiting for transfers between devices, on_device(): lax.all_to_all(widened, 'ctx', split_axis=2, concat_axis=0, tiled=True)  56.7 us
    all_to_all x1, blocking collectives, on_device(): lax.all_to_all(feature_split, 'dp', split_axis=0, concat_axis=0, tiled=True)  55 us
    reduce_scatter x1, waiting for transfers between devices, on_device(): summed = lax.psum_scatter(partial, 'dp', scatter_dimension=0, tiled=True)  51.1 us
    all_to_all x1, blocking collectives, on_device(): lax.all_to_all(attended_head, 'ctx', split_axis=0, concat_axis=1, tiled=T...  32.1 us
    all_to_all x1, waiting for transfers between devices, on_device(): lax.all_to_all(queries[0], 'ctx', split_axis=1, concat_axis=0, tiled=True)  22.5 us
    unnamed x16, local copies, waits for them, and re-layouts  13 us
    all_to_all x1, starting transfers between devices, on_device(): lax.all_to_all(widened, 'ctx', split_axis=2, concat_axis=0, tiled=True)  7.45 us
  transfers between devices with their start and end apart: 3, of which 3 were waited for; matrix products, arithmetic and copies ran while one was open for 2% of the time, Pallas kernels for 0%

profile of v2, /device:TPU:0, one launch (start us, length us, event | category | flops | bytes accessed | tf_op | source)
XLA Modules:
  0.0 350.7 jit_solution(18125969959881328367)
XLA Ops:
  6.5 0.0 reduce-scatter.2.cloned.1.call-start
  6.5 6.4 %copy.13 = bf16[1,256,8192]{1,2,0:T(8,128)(2,1)} copy(bf16[1,256,8192]{2,1,0:T(8,128)(2,1)} %param.7) | data formatting | bytes 8388608 | tf_op args[0]
  12.9 3.3 multiply_reduce_fusion
  16.2 0.0 copy-start.2
  16.2 7.0 %copy.14 = f32[256,4,2048]{2,0,1:T(8,128)} copy(bf16[256,4,2048]{0,2,1:T(8,128)(2,1)} %bitcast.31) | data formatting | bytes 12582912 | tf_op jit(solution)/shard_map/convert_element_type | solution.py:74
  23.2 0.0 copy-done.2
  23.2 4.7 %fusion = bf16[4,256,2048]{2,1,0:T(8,128)(2,1)S(1)} fusion(f32[256,4,2048]{2,0,1:T(8,128)} %copy.14, f32[4,2048]{1,0:T(4,128)S(1)} %reshape.57, f32[256]{0:T(256)S(1)} %add_rsqrt_fusion), kind=kLoop, calls=%fused_computation.2 | loop fusion | flops 6291456 | bytes 12616704 | tf_op jit(solution)/shard_map/transpose | solution.py:82
  28.0 0.0 copy-start.4
  28.0 0.0 copy-start.5
  28.0 55.0 %all_to_all.55 = bf16[4,256,2048]{2,1,0:T(8,128)(2,1)S(1)} all-to-all(bf16[4,256,2048]{2,1,0:T(8,128)(2,1)S(1)} %fusion), channel_id=1, replica_groups=mesh['dp'=4,'ctx'=32] {'dp'}, dimensions={0} | all-to-all | bytes 8388608 | tf_op jit(solution)/shard_map/all_to_all | solution.py:83
  83.0 0.0 copy-done.4
  83.0 0.0 copy-done.5
  83.0 6.2 %fusion.1 = f32[4,256,1024]{2,1,0:T(8,128)} fusion(bf16[4,256,2048]{2,1,0:T(8,128)(2,1)S(1)} %all_to_all.55, bf16[2048,512]{1,0:T(8,128)(2,1)S(1)} %copy-done.4, bf16[2048,512]{1,0:T(8,128)(2,1)S(1)} %copy-done.5), kind=kOutput, calls=%fused_computation.5 | convolution fusion | flops 4303355904 | bytes 12582912 | tf_op jit(solution)/shard_map/dot_general | solution.py:85
  89.2 0.0 reduce-scatter.2.cloned.1.call-update
  89.2 51.1 %reduce-scatter.2.cloned.1.call-done = f32[1,256,1024]{2,1,0:T(8,128)} async-done(((f32[4,256,1024]{2,1,0:T(8,128)}), f32[1,256,1024]{2,1,0:T(8,128)}) %reduce-scatter.2.cloned.1.call-update) | async-done | bytes 1048592 | tf_op jit(solution)/shard_map/reduce_scatter | solution.py:90
  140.3 1.3 convert_element_type.30
  141.6 0.4 convert_element_type.31
  142.0 0.4 copy.15
  142.4 5.8 %broadcast_in_dim.4 = bf16[256,2,4,8,128]{4,1,0,3,2:T(2,128)(2,1)} broadcast(bf16[256,2,4,128]{3,1,0,2:T(2,128)(2,1)S(1)} %copy.15), dimensions={0,1,2,4} | broadcast | bytes 4718592 | tf_op jit(solution)/shard_map/broadcast_in_dim | solution.py:94
  148.2 0.0 copy-start.1
  148.2 7.4 %all-to-all-start.2 = ((bf16[256,2,32,128]{3,1,0,2:T(2,128)(2,1)}), bf16[256,2,32,128]{3,1,0,2:T(2,128)(2,1)}, u32[]{:S(2)}, u32[]{:S(2)}) async-start(bf16[256,2,32,128]{3,1,0,2:T(2,128)(2,1)} %bitcast.32), calls=%async_computation.3 | async-start | bytes 8388608 | tf_op jit(solution)/shard_map/all_to_all | solution.py:96
  155.6 0.0 copy-done.1
  155.6 0.5 copy.17
  156.1 0.0 copy-start.3
  156.1 2.1 copy.12
  158.3 56.7 %all-to-all-done.2 = bf16[256,2,32,128]{3,1,0,2:T(2,128)(2,1)} async-done(((bf16[256,2,32,128]{3,1,0,2:T(2,128)(2,1)}), bf16[256,2,32,128]{3,1,0,2:T(2,128)(2,1)}, u32[]{:S(2)}, u32[]{:S(2)}) %all-to-all-start.2) | async-done | bytes 4194336 | tf_op jit(solution)/shard_map/all_to_all | solution.py:96
  214.9 4.3 %all-to-all-start = ((bf16[256,32,128]{2,0,1:T(8,128)(2,1)}), bf16[256,32,128]{2,0,1:T(8,128)(2,1)S(1)}, u32[]{:S(2)}, u32[]{:S(2)}) async-start(bf16[256,32,128]{2,0,1:T(8,128)(2,1)} %copy.12), calls=%async_computation | async-start | bytes 4194304 | tf_op jit(solution)/shard_map/all_to_all | solution.py:73
  219.3 0.0 copy-done.3
  219.3 0.1 copy.11
  219.4 0.7 reshape_squeeze.3.lists_ref
  220.1 4.7 %copy.20 = bf16[1024,8,2,128]{3,1,2,0:T(8,128)(2,1)} copy(bf16[1024,8,2,128]{3,2,1,0:T(2,128)(2,1)} %bitcast.19) | data formatting | bytes 8388608
  224.8 22.5 %all-to-all-done = bf16[256,32,128]{2,0,1:T(8,128)(2,1)S(1)} async-done(((bf16[256,32,128]{2,0,1:T(8,128)(2,1)}), bf16[256,32,128]{2,0,1:T(8,128)(2,1)S(1)}, u32[]{:S(2)}, u32[]{:S(2)}) %all-to-all-start) | async-done | bytes 2097184 | tf_op jit(solution)/shard_map/all_to_all | solution.py:73
  247.3 0.0 copy-start
  247.3 1.3 copy-done
  248.6 59.5 %shard_map.73 = bf16[8192,128]{1,0:T(8,128)(2,1)} custom-call(s32[768]{0:T(1024)} %reshape_squeeze.3.lists_ref, s32[64]{0:T(128)} %bitcast.38, bf16[8192,128]{1,0:T(8,128)(2,1)} %bitcast.35, bf16[8192,256]{1,0:T(8,128)(2,1)} %bitcast.29, bf16[8192,256]{1,0:T(8,128)(2,1)} %bitcast.30), custom_call_target="tpu_custom_call" | custom-call | tf_op jit(solution)/shard_map/pallas_call | solution.py:55
  308.1 32.1 %all_to_all.56 = bf16[32,256,128]{2,1,0:T(8,128)(2,1)S(1)} all-to-all(bf16[32,256,128]{2,1,0:T(8,128)(2,1)} %bitcast.36), channel_id=1, replica_groups=mesh['dp'=4,'ctx'=32] {'ctx'}, dimensions={0} | all-to-all | bytes 4194304 | tf_op jit(solution)/shard_map/all_to_all | solution.py:102
  340.2 1.4 copy.16
  341.5 2.3 broadcast_in_dim.5
  (2 shorter events, 0.0 us)
Async XLA Ops:
  6.5 133.8 %reduce-scatter.2.cloned.1.call-start = ((), (), s32[]{:S(2)}) async-start(), calls=%async_computation.5 | async-start | bytes 5242880 | tf_op jit(solution)/shard_map/reduce_scatter | solution.py:90
  16.2 7.0 %copy-start.2 = (bf16[8192]{0:T(1024)(128)(2,1)S(1)}, bf16[8192]{0:T(1024)(128)(2,1)}, u32[]{:S(2)}) copy-start(bf16[8192]{0:T(1024)(128)(2,1)} %param.8) | copy-start | bytes 49156
  28.0 55.0 %copy-start.4 = (bf16[2048,512]{1,0:T(8,128)(2,1)S(1)}, bf16[2048,512]{1,0:T(8,128)(2,1)}, u32[]{:S(2)}) copy-start(bf16[2048,512]{1,0:T(8,128)(2,1)} %param.11) | copy-start | bytes 6291460
  28.0 55.0 %copy-start.5 = (bf16[2048,512]{1,0:T(8,128)(2,1)S(1)}, bf16[2048,512]{1,0:T(8,128)(2,1)}, u32[]{:S(2)}) copy-start(bf16[2048,512]{1,0:T(8,128)(2,1)} %param.10) | copy-start | bytes 6291460
  148.2 7.5 %copy-start.1 = (bf16[1,256,4096]{2,1,0:T(8,128)(2,1)S(1)}, bf16[1,256,4096]{2,1,0:T(8,128)(2,1)}, u32[]{:S(2)}) copy-start(bf16[1,256,4096]{2,1,0:T(8,128)(2,1)} %param.9) | copy-start | bytes 6291460
  148.2 66.8 %all-to-all-start.2 = ((bf16[256,2,32,128]{3,1,0,2:T(2,128)(2,1)}), bf16[256,2,32,128]{3,1,0,2:T(2,128)(2,1)}, u32[]{:S(2)}, u32[]{:S(2)}) async-start(bf16[256,2,32,128]{3,1,0,2:T(2,128)(2,1)} %bitcast.32), calls=%async_computation.3 | async-start | bytes 8388608 | tf_op jit(solution)/shard_map/all_to_all | solution.py:96
  156.1 63.1 %copy-start.3 = (s32[1,1,64,12]{2,1,3,0:T(1,128)S(1)}, s32[1,1,64,12]{2,1,3,0:T(1,128)}, u32[]{:S(2)}) copy-start(s32[1,1,64,12]{2,1,3,0:T(1,128)} %param.12) | copy-start | bytes 9220
  214.9 32.3 %all-to-all-start = ((bf16[256,32,128]{2,0,1:T(8,128)(2,1)}), bf16[256,32,128]{2,0,1:T(8,128)(2,1)S(1)}, u32[]{:S(2)}, u32[]{:S(2)}) async-start(bf16[256,32,128]{2,0,1:T(8,128)(2,1)} %copy.12), calls=%async_computation | async-start | bytes 4194304 | tf_op jit(solution)/shard_map/all_to_all | solution.py:73
  247.3 1.3 copy-start
Sparse Core Ops, SparseCore 0:
  89.3 50.9 reduce-scatter.1

commit v3 on v1

--- a/solution.py
+++ b/solution.py
@@ -69,54 +69,90 @@
     )(lists_flat, counts, head_queries, kv_rows, kv_rows)
 
 
+ALL_AXES = ("zh", "core", "x", "y", "zl")
+CTX_AXES = ("x", "y", "zl")
+DP_AXES = ("zh", "core")
+
+
+def linear_index(zh, core, x, y, zl):
+    return (((zh * 2 + core) * 4 + x) * 4 + y) * 2 + zl
+
+
+def cross_half_pairs(flip_core):
+    pairs = []
+    for zh in range(2):
+        for core in range(2):
+            for x in range(4):
+                for y in range(4):
+                    for zl in range(2):
+                        target_core = 1 - core if flip_core else core
+                        pairs.append(
+                            (linear_index(zh, core, x, y, zl), linear_index(1 - zh, target_core, x, y, 1 - zl))
+                        )
+    return pairs
+
+
 def on_device(hidden, norm_gain, queries, key_weight, value_weight, block_lists, block_counts):
+    head_queries = lax.all_to_all(queries[0], CTX_AXES, split_axis=1, concat_axis=0, tiled=True)
     upcast = hidden[0].astype(jnp.float32)
     mean_square = jnp.mean(upcast * upcast, axis=-1, keepdims=True)
     normed = (upcast * lax.rsqrt(mean_square + 1e-05) * norm_gain.astype(jnp.float32)).astype(
         jnp.bfloat16
     )
     local_rows = normed.shape[0]
-    key_part = jnp.dot(
-        normed,
-        lax.all_gather(key_weight, "dp", axis=0, tiled=True),
-        preferred_element_type=jnp.float32,
+    local_weight = jnp.concatenate([key_weight, value_weight], axis=1)
+    weight_rows = local_weight.shape[0]
+    ctx_size = 32
+    piece_rows = weight_rows // ctx_size
+    ctx_index = lax.axis_index(CTX_AXES)
+    piece = lax.dynamic_slice_in_dim(local_weight, (ctx_index ^ 1) * piece_rows, piece_rows, axis=0)
+    same_core = lax.ppermute(piece, ALL_AXES, cross_half_pairs(False))
+    cross_core = lax.ppermute(piece, ALL_AXES, cross_half_pairs(True))
+    other_half = lax.all_gather(
+        jnp.stack([same_core, cross_core]), CTX_AXES, axis=1, tiled=True
     )
-    value_part = jnp.dot(
-        normed,
-        lax.all_gather(value_weight, "dp", axis=0, tiled=True),
-        preferred_element_type=jnp.float32,
+    sibling = lax.ppermute(local_weight, "core", [(0, 1), (1, 0)])
+    zh = lax.axis_index("zh")
+    core = lax.axis_index("core")
+    blocks = (
+        (zh * 2 + core, local_weight),
+        (zh * 2 + 1 - core, sibling),
+        ((1 - zh) * 2 + core, other_half[0]),
+        ((1 - zh) * 2 + 1 - core, other_half[1]),
     )
-    paired = jnp.stack([key_part, value_part], axis=1).astype(jnp.bfloat16)
-    ctx_size = lax.axis_size("ctx")
-    copies_per_head = ctx_size // KVH
-    widened = jnp.broadcast_to(
-        paired.reshape(local_rows, 2, KVH, 1, HD), (local_rows, 2, KVH, copies_per_head, HD)
-    )
-    widened = widened.reshape(local_rows, 2, ctx_size, HD)
-    head_pair = lax.all_to_all(widened, "ctx", split_axis=2, concat_axis=0, tiled=True)
-    head_queries = lax.all_to_all(queries[0], "ctx", split_axis=1, concat_axis=0, tiled=True)
+    summed = None
+    for block_index, weight in blocks:
+        features = lax.dynamic_slice_in_dim(normed, block_index * weight_rows, weight_rows, axis=1)
+        term = jnp.dot(features, weight, preferred_element_type=jnp.float32)
+        summed = term if summed is None else summed + term
+    paired = summed.astype(jnp.bfloat16).reshape(local_rows, 2, KVH, HD).transpose(2, 0, 1, 3)
+    by_group = lax.all_to_all(paired, "x", split_axis=0, concat_axis=0, tiled=True)
+    plane = lax.all_gather(by_group, ("y", "zl"), axis=0, tiled=True)
     sequence_rows = head_queries.shape[0]
-    kv_rows = head_pair.reshape(sequence_rows, 2 * HD)
-    lists_flat = block_lists[0, 0].reshape(-1)
+    kv_rows = plane.reshape(sequence_rows, 2 * HD)
+    lists = block_lists[0, 0]
+    source = lists // 2
+    remapped = (((source % 8) * 4 + source // 8) * 2 + lists % 2).reshape(-1)
     counts = block_counts[0, 0]
-    attended_head = attend(lists_flat, counts, head_queries, kv_rows)
-    restored = lax.all_to_all(attended_head, "ctx", split_axis=0, concat_axis=1, tiled=True)
+    attended_head = attend(remapped, counts, head_queries, kv_rows)
+    restored = lax.all_to_all(attended_head, CTX_AXES, split_axis=0, concat_axis=1, tiled=True)
     return restored[None]
 
 
 def solution(mesh):
+    fine = jax.sharding.Mesh(mesh.devices.reshape(2, 2, 4, 4, 2), ALL_AXES)
     return jax.shard_map(
         on_device,
-        mesh=mesh,
+        mesh=fine,
         in_specs=(
-            P("dp", "ctx", None),
+            P(DP_AXES, CTX_AXES, None),
             P(),
-            P("dp", "ctx", None),
-            P("dp", None),
-            P("dp", None),
-            P("dp", "ctx", None, None),
-            P("dp", "ctx", None),
+            P(DP_AXES, CTX_AXES, None),
+            P(DP_AXES, None),
+            P(DP_AXES, None),
+            P(DP_AXES, CTX_AXES, None, None),
+            P(DP_AXES, CTX_AXES, None),
         ),
-        out_specs=P("dp", "ctx", None),
+        out_specs=P(DP_AXES, CTX_AXES, None),
         check_vma=False,
     )

time: 375 us -> 461 us (1.23)
  waiting for transfers between devices: 199 us -> 285 us
  local copies, waits for them, and re-layouts: 44.1 us -> 25.3 us
  blocking collectives: 31.3 us -> 47.8 us
    all_gather x2, waiting for transfers between devices: 114 us -> 278 us  [the longest x1 178 us: on_device(): lax.all_gather(jnp.stack([same_core, cross_core]), CTX_AXES, axis=1, tile...]
    all_to_all x2 -> x1, waiting for transfers between devices: 82.9 us -> 0.01 us  [on_device(): lax.all_to_all(queries[0], CTX_AXES, split_axis=1, concat_axis=0, tiled=T...]
    dot_general x2 -> x0, local copies, waits for them, and re-layouts: 23.7 us -> none  [the longest x1 11.9 us: on_device(): jnp.dot(normed, lax.all_gather(key_weight, 'dp', axis=0, tiled=True), pre...]
    all_to_all x1 -> x2, blocking collectives: 31.3 us -> 47.8 us  [the longest x1 36.6 us: on_device(): lax.all_to_all(attended_head, CTX_AXES, split_axis=0, concat_axis=1, tile...]
    all_to_all x2 -> x1, starting transfers between devices: 13.8 us -> 5.61 us  [on_device(): lax.all_to_all(queries[0], CTX_AXES, split_axis=1, concat_axis=0, tiled=T...]
    ppermute x0 -> x3, waiting for transfers between devices: none -> 7.27 us  [the longest x1 3.88 us: on_device(): same_core = lax.ppermute(piece, ALL_AXES, cross_half_pairs(False))]
    all_gather x0 -> x1, local copies, waits for them, and re-layouts: none -> 6.54 us  [on_device(): plane = lax.all_gather(by_group, ('y', 'zl'), axis=0, tiled=True)]
    broadcast_in_dim x1 -> x0, local copies, waits for them, and re-layouts: 5.75 us -> none  [on_device(): jnp.broadcast_to(paired.reshape(local_rows, 2, KVH, 1, HD), (local_rows,...]
  transfers between devices with their start and end apart: 4 -> 6, of which waited for: 4 -> 5; matrix products, arithmetic and copies ran while one was open for 6% -> 5% of each run, Pallas kernels for 0% -> 0%
where the time goes in v3:
time: 461 us; the launch traced here: 460 us
  waiting for transfers between devices  285 us (62%)
  Pallas kernels  59.5 us (13%)
  blocking collectives  47.8 us (10%)
  local copies, waits for them, and re-layouts  25.3 us (5%)
  between operations  13.6 us (3%)
  matrix products  12.7 us (3%)
  starting transfers between devices  9.97 us (2%)
  other arithmetic  5.79 us (1%)
    all_gather x1, waiting for transfers between devices, on_device(): lax.all_gather(jnp.stack([same_core, cross_core]), CTX_AXES, axis=1, tile...  178 us
    all_gather x1, waiting for transfers between devices, on_device(): plane = lax.all_gather(by_group, ('y', 'zl'), axis=0, tiled=True)  99.6 us
    pallas_call x1, Pallas kernels, attend(): pl.pallas_call(attend_kernel, out_shape=jax.ShapeDtypeStruct((sequence_ro...  59.5 us
    all_to_all x1, blocking collectives, on_device(): lax.all_to_all(attended_head, CTX_AXES, split_axis=0, concat_axis=1, tile...  36.6 us
    dot_general x4, matrix products, on_device(): term = jnp.dot(features, weight, preferred_element_type=jnp.float32)  12.7 us
    all_to_all x1, blocking collectives, on_device(): lax.all_to_all(paired, 'x', split_axis=0, concat_axis=0, tiled=True)  11.2 us
    unnamed x22, local copies, waits for them, and re-layouts  10.1 us
  transfers between devices with their start and end apart: 6, of which 5 were waited for; matrix products, arithmetic and copies ran while one was open for 5% of the time, Pallas kernels for 0%

profile of v3, /device:TPU:0, one launch (start us, length us, event | category | flops | bytes accessed | tf_op | source)
XLA Modules:
  0.0 459.9 jit_solution(17834990866824463836)
XLA Ops:
  6.5 0.0 all-gather.3.cloned.1.call-start
  6.5 3.3 constant_dynamic-update-slice_fusion.1
  9.8 0.0 copy-done.3
  9.8 1.5 constant_dynamic-update-slice_fusion
  11.3 0.9 constant_dynamic-slice_fusion
  12.3 4.2 collective-permute-start.1
  16.5 0.0 collective-permute-start.2
  16.5 3.9 collective-permute-done.1
  20.4 2.9 collective-permute-done.2
  23.2 0.7 pad_maximum_fusion
  23.9 0.0 all-gather.3.cloned.1.call-update
  24.0 0.0 all-gather.5.cloned.1.call-start
  24.0 0.1 collective-permute-start
  24.1 0.0 copy-done.6
  24.1 0.0 copy-start
  24.2 3.3 fusion
  27.4 0.2 copy-done
  27.6 1.2 fusion.2
  28.8 1.0 copy-done.5
  29.8 1.3 fusion.11
  31.1 0.5 collective-permute-done
  31.6 0.2 copy-done.2
  31.8 4.5 convolution_add_fusion
  36.3 178.3 %all-gather.3.cloned.1.call-done = bf16[2,2048,1024]{2,1,0:T(8,128)(2,1)} async-done(((bf16[2,64,1024]{2,1,0:T(8,128)(2,1)}), bf16[2,2048,1024]{2,1,0:T(8,128)(2,1)}) %all-gather.3.cloned.1.call-update) | async-done | bytes 8388624 | tf_op jit(solution)/shard_map/all_gather | solution.py:111
  214.6 3.9 fusion.3
  218.5 1.0 copy-done.8
  219.6 3.0 fusion.7
  222.6 0.4 reshape.27
  223.0 0.1 copy.25
  223.1 11.2 %all_to_all.40 = bf16[4,256,2,128]{3,1,2,0:T(8,128)(2,1)} all-to-all(bf16[4,256,2,128]{3,1,2,0:T(8,128)(2,1)S(1)} %bitcast.47), channel_id=1, replica_groups=mesh['zh'=2,'core'=2,'x'=4,'y'=4,'zl'=2] {'x'}, dimensions={0} | all-to-all | bytes 1048576 | tf_op jit(solution)/shard_map/all_to_all | solution.py:129
  234.2 0.0 all-gather.5.cloned.1.call-update
  234.3 0.5 copy.20
  234.8 0.0 copy-start.7
  234.8 2.1 copy.16
  236.9 5.6 %all-to-all-start = ((bf16[256,32,128]{2,0,1:T(8,128)(2,1)}), bf16[256,32,128]{2,0,1:T(8,128)(2,1)S(1)}, u32[]{:S(2)}, u32[]{:S(2)}) async-start(bf16[256,32,128]{2,0,1:T(8,128)(2,1)} %copy.16), calls=%async_computation | async-start | bytes 4194304 | tf_op jit(solution)/shard_map/all_to_all | solution.py:96
  242.5 0.0 copy-done.7
  242.5 0.1 copy.15
  242.6 0.1 squeeze.14
  242.7 0.6 fusion.16.lists_ref
  243.3 99.6 %all-gather.5.cloned.1.call-done = bf16[32,256,2,128]{3,1,2,0:T(8,128)(2,1)} async-done(((bf16[4,256,2,128]{3,1,2,0:T(8,128)(2,1)}), bf16[32,256,2,128]{3,1,2,0:T(8,128)(2,1)}) %all-gather.5.cloned.1.call-update) | async-done | bytes 4194320 | tf_op jit(solution)/shard_map/all_gather | solution.py:130
  343.0 6.5 %copy.18 = bf16[32,256,2,128]{3,2,1,0:T(2,128)(2,1)S(1)} copy(bf16[32,256,2,128]{3,1,2,0:T(8,128)(2,1)} %all-gather.5.cloned.1.call-done) | data formatting | bytes 8388608 | tf_op jit(solution)/shard_map/all_gather | solution.py:130
  349.5 2.5 copy.24
  352.0 0.0 all-to-all-done
  352.0 1.3 copy-done.1
  353.3 59.5 %shard_map.73 = bf16[8192,128]{1,0:T(8,128)(2,1)} custom-call(s32[768]{0:T(1024)} %fusion.16.lists_ref, s32[64]{0:T(128)} %bitcast.50, bf16[8192,128]{1,0:T(8,128)(2,1)} %bitcast.44, bf16[8192,256]{1,0:T(8,128)(2,1)} %bitcast.39, bf16[8192,256]{1,0:T(8,128)(2,1)} %bitcast.40), custom_call_target="tpu_custom_call" | custom-call | tf_op jit(solution)/shard_map/pallas_call | solution.py:55
  412.8 36.6 %all_to_all.41 = bf16[32,256,128]{2,1,0:T(8,128)(2,1)S(1)} all-to-all(bf16[32,256,128]{2,1,0:T(8,128)(2,1)} %bitcast.45), channel_id=1, replica_groups=mesh['zh'=2,'core'=2,'x'=4,'y'=4,'zl'=2] {'x','y','zl'}, dimensions={0} | all-to-all | bytes 4194304 | tf_op jit(solution)/shard_map/all_to_all | solution.py:138
  449.4 1.4 copy.19
  450.8 2.3 broadcast_in_dim.2
  (10 shorter events, 0.0 us)
Async XLA Ops:
  6.5 3.3 copy-start.3
  6.5 208.1 %all-gather.3.cloned.1.call-start = ((), (), s32[]{:S(2)}) async-start(), calls=%async_computation.3 | async-start | bytes 8650752 | tf_op jit(solution)/shard_map/all_gather | solution.py:111
  6.5 17.6 %copy-start.6 = (bf16[8192]{0:T(1024)(128)(2,1)S(1)}, bf16[8192]{0:T(1024)(128)(2,1)}, u32[]{:S(2)}) copy-start(bf16[8192]{0:T(1024)(128)(2,1)} %param.8) | copy-start | bytes 49156
  12.3 8.1 %collective-permute-start.1 = (bf16[64,1024]{1,0:T(8,128)(2,1)S(1)}, bf16[64,1024]{1,0:T(8,128)(2,1)S(1)}, u32[]{:S(2)}, u32[]{:S(2)}) collective-permute-start(bf16[64,1024]{1,0:T(8,128)(2,1)S(1)} %constant_dynamic-slice_fusion), channel_id=1, source_target_pairs={{0,65},{1,64},{2,67},{3,66},{4,69},{5,68},{6,71},{7,70},{8,73},{9,... | collective-permute-start | bytes 393224 | tf_op jit(solution)/shard_map/ppermute | solution.py:109
  16.5 6.7 %collective-permute-start.2 = (bf16[64,1024]{1,0:T(8,128)(2,1)S(1)}, bf16[64,1024]{1,0:T(8,128)(2,1)S(1)}, u32[]{:S(2)}, u32[]{:S(2)}) collective-permute-start(bf16[64,1024]{1,0:T(8,128)(2,1)S(1)} %constant_dynamic-slice_fusion), channel_id=1, source_target_pairs={{0,97},{1,96},{2,99},{3,98},{4,101},{5,100},{6,103},{7,102},{8,105... | collective-permute-start | bytes 393224 | tf_op jit(solution)/shard_map/ppermute | solution.py:110
  24.0 319.0 %all-gather.5.cloned.1.call-start = ((), (), s32[]{:S(2)}) async-start(), calls=%async_computation.4 | async-start | bytes 4718592 | tf_op jit(solution)/shard_map/all_gather | solution.py:130
  24.0 7.6 %collective-permute-start = (bf16[2048,1024]{1,0:T(8,128)(2,1)}, bf16[2048,1024]{1,0:T(8,128)(2,1)}, u32[]{:S(2)}, u32[]{:S(2)}) collective-permute-start(bf16[2048,1024]{1,0:T(8,128)(2,1)} %constant_dynamic-update-slice_fusion), channel_id=1, source_target_pairs={{0,32},{32,0},{1,33},{33,1},{2,34},{34,2},{3,35},{35,3},{4,36},{36... | collective-permute-start | bytes 12582920 | tf_op jit(solution)/shard_map/ppermute | solution.py:114
  24.1 3.5 copy-start
  27.6 2.2 copy-start.5
  29.8 2.0 copy-start.2
  214.6 4.9 %copy-start.8 = (bf16[2,2048,1024]{2,1,0:T(8,128)(2,1)S(1)}, bf16[2,2048,1024]{2,1,0:T(8,128)(2,1)}, u32[]{:S(2)}) copy-start(bf16[2,2048,1024]{2,1,0:T(8,128)(2,1)} %all-gather.3.cloned.1.call-done) | copy-start | bytes 25165828
  219.6 14.7 %copy-start.4 = (bf16[1,256,4096]{2,1,0:T(8,128)(2,1)S(1)}, bf16[1,256,4096]{2,1,0:T(8,128)(2,1)}, u32[]{:S(2)}) copy-start(bf16[1,256,4096]{2,1,0:T(8,128)(2,1)} %param.9) | copy-start | bytes 6291460
  234.8 7.8 %copy-start.7 = (s32[1,1,64,12]{2,1,3,0:T(1,128)S(1)}, s32[1,1,64,12]{2,1,3,0:T(1,128)}, u32[]{:S(2)}) copy-start(s32[1,1,64,12]{2,1,3,0:T(1,128)} %param.12) | copy-start | bytes 9220
  236.9 115.1 %all-to-all-start = ((bf16[256,32,128]{2,0,1:T(8,128)(2,1)}), bf16[256,32,128]{2,0,1:T(8,128)(2,1)S(1)}, u32[]{:S(2)}, u32[]{:S(2)}) async-start(bf16[256,32,128]{2,0,1:T(8,128)(2,1)} %copy.16), calls=%async_computation | async-start | bytes 4194304 | tf_op jit(solution)/shard_map/all_to_all | solution.py:96
  352.0 1.3 copy-start.1
Sparse Core Ops, SparseCore 0:
  24.1 190.4 all-gather.2
  234.4 108.5 all-gather.4

commit v4 on v3

--- a/solution.py
+++ b/solution.py
@@ -99,42 +99,38 @@
     normed = (upcast * lax.rsqrt(mean_square + 1e-05) * norm_gain.astype(jnp.float32)).astype(
         jnp.bfloat16
     )
-    local_rows = normed.shape[0]
+    local_rows, features = normed.shape
     local_weight = jnp.concatenate([key_weight, value_weight], axis=1)
     weight_rows = local_weight.shape[0]
-    ctx_size = 32
-    piece_rows = weight_rows // ctx_size
-    ctx_index = lax.axis_index(CTX_AXES)
-    piece = lax.dynamic_slice_in_dim(local_weight, (ctx_index ^ 1) * piece_rows, piece_rows, axis=0)
-    same_core = lax.ppermute(piece, ALL_AXES, cross_half_pairs(False))
-    cross_core = lax.ppermute(piece, ALL_AXES, cross_half_pairs(True))
-    other_half = lax.all_gather(
-        jnp.stack([same_core, cross_core]), CTX_AXES, axis=1, tiled=True
-    )
-    sibling = lax.ppermute(local_weight, "core", [(0, 1), (1, 0)])
+    half_features = 2 * weight_rows
     zh = lax.axis_index("zh")
     core = lax.axis_index("core")
-    blocks = (
-        (zh * 2 + core, local_weight),
-        (zh * 2 + 1 - core, sibling),
-        ((1 - zh) * 2 + core, other_half[0]),
-        ((1 - zh) * 2 + 1 - core, other_half[1]),
-    )
-    summed = None
-    for block_index, weight in blocks:
-        features = lax.dynamic_slice_in_dim(normed, block_index * weight_rows, weight_rows, axis=1)
-        term = jnp.dot(features, weight, preferred_element_type=jnp.float32)
-        summed = term if summed is None else summed + term
-    paired = summed.astype(jnp.bfloat16).reshape(local_rows, 2, KVH, HD).transpose(2, 0, 1, 3)
-    by_group = lax.all_to_all(paired, "x", split_axis=0, concat_axis=0, tiled=True)
-    plane = lax.all_gather(by_group, ("y", "zl"), axis=0, tiled=True)
+    partner_pairs = cross_half_pairs(False)
+    far_features = lax.dynamic_slice_in_dim(normed, (1 - zh) * half_features, half_features, axis=1)
+    partner_rows = lax.ppermute(far_features, ALL_AXES, partner_pairs)
+    sibling = lax.ppermute(local_weight, "core", [(0, 1), (1, 0)])
+
+    def half_sum(rows, offset):
+        own = lax.dynamic_slice_in_dim(rows, offset + core * weight_rows, weight_rows, axis=1)
+        other = lax.dynamic_slice_in_dim(rows, offset + (1 - core) * weight_rows, weight_rows, axis=1)
+        return jnp.dot(own, local_weight, preferred_element_type=jnp.float32) + jnp.dot(
+            other, sibling, preferred_element_type=jnp.float32
+        )
+
+    for_partner = half_sum(partner_rows, 0)
+    from_partner = lax.ppermute(for_partner, ALL_AXES, partner_pairs)
+    summed = half_sum(normed, zh * half_features) + from_partner
+    paired = summed.reshape(local_rows, 2, KVH, 1, HD).astype(jnp.bfloat16)
+    ctx_size = lax.axis_size(CTX_AXES)
+    copies_per_head = ctx_size // KVH
+    widened = jnp.broadcast_to(paired, (local_rows, 2, KVH, copies_per_head, HD))
+    widened = widened.reshape(local_rows, 2, ctx_size, HD)
+    head_pair = lax.all_to_all(widened, CTX_AXES, split_axis=2, concat_axis=0, tiled=True)
     sequence_rows = head_queries.shape[0]
-    kv_rows = plane.reshape(sequence_rows, 2 * HD)
-    lists = block_lists[0, 0]
-    source = lists // 2
-    remapped = (((source % 8) * 4 + source // 8) * 2 + lists % 2).reshape(-1)
+    kv_rows = head_pair.reshape(sequence_rows, 2 * HD)
+    lists_flat = block_lists[0, 0].reshape(-1)
     counts = block_counts[0, 0]
-    attended_head = attend(remapped, counts, head_queries, kv_rows)
+    attended_head = attend(lists_flat, counts, head_queries, kv_rows)
     restored = lax.all_to_all(attended_head, CTX_AXES, split_axis=0, concat_axis=1, tiled=True)
     return restored[None]
 

time: 461 us -> 302 us (0.66)
  waiting for transfers between devices: 285 us -> 140 us
  blocking collectives: 47.8 us -> 32.2 us
  between operations: 13.6 us -> 0.13 us
  starting transfers between devices: 9.97 us -> 20.9 us
    all_gather x2 -> x0, waiting for transfers between devices: 278 us -> none  [the longest x1 178 us: on_device(): lax.all_gather(jnp.stack([same_core, cross_core]), CTX_AXES, axis=1, tile...]
    ppermute x2, waiting for transfers between devices: 6.74 us -> 65.9 us  [the longest x1 46.4 us: on_device(): partner_rows = lax.ppermute(far_features, ALL_AXES, partner_pairs)]
    all_to_all x0 -> x1, waiting for transfers between devices: none -> 53.7 us  [on_device(): lax.all_to_all(widened, CTX_AXES, split_axis=2, concat_axis=0, tiled=True)]
    all_to_all x1, waiting for transfers between devices: 0.01 us -> 20.8 us  [on_device(): lax.all_to_all(queries[0], CTX_AXES, split_axis=1, concat_axis=0, tiled=T...]
    all_to_all x1 -> x0, blocking collectives: 11.2 us -> none  [on_device(): lax.all_to_all(paired, 'x', split_axis=0, concat_axis=0, tiled=True)]
    all_to_all x0 -> x1, starting transfers between devices: none -> 7.58 us  [on_device(): lax.all_to_all(widened, CTX_AXES, split_axis=2, concat_axis=0, tiled=True)]
    all_gather x1 -> x0, local copies, waits for them, and re-layouts: 6.54 us -> none  [on_device(): plane = lax.all_gather(by_group, ('y', 'zl'), axis=0, tiled=True)]
    broadcast_in_dim x0 -> x1, local copies, waits for them, and re-layouts: none -> 5.75 us  [on_device(): jnp.broadcast_to(paired, (local_rows, 2, KVH, copies_per_head, HD))]
  transfers between devices with their start and end apart: 6 -> 5, of which waited for: 5 -> 4; matrix products, arithmetic and copies ran while one was open for 5% -> 6% of each run, Pallas kernels for 0% -> 0%
where the time goes in v4:
time: 302 us; the launch traced here: 301 us
  waiting for transfers between devices  140 us (46%)
  Pallas kernels  59.5 us (20%)
  blocking collectives  32.2 us (11%)
  local copies, waits for them, and re-layouts  26.4 us (9%)
  starting transfers between devices  20.9 us (7%)
  matrix products  15.1 us (5%)
  other arithmetic  6.73 us (2%)
    pallas_call x1, Pallas kernels, attend(): pl.pallas_call(attend_kernel, out_shape=jax.ShapeDtypeStruct((sequence_ro...  59.5 us
    all_to_all x1, waiting for transfers between devices, on_device(): lax.all_to_all(widened, CTX_AXES, split_axis=2, concat_axis=0, tiled=True)  53.7 us
    ppermute x1, waiting for transfers between devices, on_device(): partner_rows = lax.ppermute(far_features, ALL_AXES, partner_pairs)  46.4 us
    all_to_all x1, blocking collectives, on_device(): lax.all_to_all(attended_head, CTX_AXES, split_axis=0, concat_axis=1, tile...  32.2 us
    all_to_all x1, waiting for transfers between devices, on_device(): lax.all_to_all(queries[0], CTX_AXES, split_axis=1, concat_axis=0, tiled=T...  20.8 us
    ppermute x1, waiting for transfers between devices, on_device(): from_partner = lax.ppermute(for_partner, ALL_AXES, partner_pairs)  19.5 us
    unnamed x16, local copies, waits for them, and re-layouts  11.8 us
    all_to_all x1, starting transfers between devices, on_device(): lax.all_to_all(widened, CTX_AXES, split_axis=2, concat_axis=0, tiled=True)  7.58 us
  transfers between devices with their start and end apart: 5, of which 4 were waited for; matrix products, arithmetic and copies ran while one was open for 6% of the time, Pallas kernels for 0%

profile of v4, /device:TPU:0, one launch (start us, length us, event | category | flops | bytes accessed | tf_op | source)
XLA Modules:
  0.0 301.4 jit_solution(1731872133542463755)
XLA Ops:
  0.0 0.0 copy-start.2
  0.0 0.0 copy-start.4
  0.0 3.2 %constant_dynamic-update-slice_fusion.1 = bf16[2048,1024]{1,0:T(8,128)(2,1)} fusion(bf16[2048,512]{1,0:T(8,128)(2,1)} %param.10), kind=kLoop, calls=%fused_computation.17 | loop fusion | bytes 4194304
  3.2 0.0 copy-done.2
  3.2 1.5 constant_dynamic-update-slice_fusion
  4.7 0.0 collective-permute-start
  4.7 0.0 copy-done.4
  4.8 3.1 %fusion = f32[256]{0:T(256)S(1)} fusion(bf16[1,256,8192]{2,1,0:T(8,128)(2,1)} %param.7), kind=kLoop, calls=%fused_computation.2 | loop fusion | flops 6291200 | bytes 4195328 | tf_op jit(solution)/shard_map/reduce_sum | solution.py:98
  7.9 3.6 %fusion.2 = bf16[256,8192]{1,0:T(8,128)(2,1)S(1)} fusion(bf16[1,256,8192]{2,1,0:T(8,128)(2,1)} %param.7, f32[8192]{0:T(1024)S(1)} %convert_element_type.25, f32[256]{0:T(256)S(1)} %add_rsqrt_fusion), kind=kLoop, calls=%fused_computation.4 | loop fusion | flops 8388608 | bytes 8422400 | tf_op jit(solution)/shard_map/convert_element_type | solution.py:99
  11.5 0.0 copy-start
  11.5 2.0 copy-done
  13.5 0.1 constant_dynamic-slice_fusion
  13.6 4.2 %collective-permute-start.1 = (bf16[256,4096]{1,0:T(8,128)(2,1)S(1)}, bf16[256,4096]{1,0:T(8,128)(2,1)}, u32[]{:S(2)}, u32[]{:S(2)}) collective-permute-start(bf16[256,4096]{1,0:T(8,128)(2,1)S(1)} %constant_dynamic-slice_fusion), channel_id=1, source_target_pairs={{0,65},{1,64},{2,67},{3,66},{4,69},{5,68},{6,71},{7,70},{8,73},{9,... | collective-permute-start | bytes 6291464 | tf_op jit(solution)/shard_map/ppermute | solution.py:110
  17.8 46.4 %collective-permute-done.1 = bf16[256,4096]{1,0:T(8,128)(2,1)} collective-permute-done((bf16[256,4096]{1,0:T(8,128)(2,1)S(1)}, bf16[256,4096]{1,0:T(8,128)(2,1)}, u32[]{:S(2)}, u32[]{:S(2)}) %collective-permute-start.1) | collective-permute-done | bytes 2097184 | tf_op jit(solution)/shard_map/ppermute | solution.py:110
  64.2 0.0 collective-permute-done
  64.2 3.8 %fusion.5 = f32[256,1024]{1,0:T(8,128)S(1)} fusion(bf16[2048,1024]{1,0:T(8,128)(2,1)} %collective-permute-done, bf16[256,4096]{1,0:T(8,128)(2,1)} %collective-permute-done.1, s32[]{:T(128)S(6)} %select_n.19), kind=kOutput, calls=%fused_computation.10 | convolution fusion | flops 1073741824 | bytes 6291460 | tf_op jit(solution)/shard_map/dot_general | solution.py:116
  68.0 3.8 %convolution_add_fusion = f32[256,1024]{1,0:T(8,128)S(1)} fusion(f32[256,1024]{1,0:T(8,128)S(1)} %fusion.5, bf16[2048,1024]{1,0:T(8,128)(2,1)} %constant_dynamic-update-slice_fusion, bf16[256,4096]{1,0:T(8,128)(2,1)} %collective-permute-done.1, s32[]{:T(128)S(6)} %select_n.18), kind=kOutput, calls=%fused_computation.6 | convolution fusion | flops 1074003968 | bytes 7340036 | tf_op jit(solution)/shard_map/dot_general | solution.py:116
  71.8 3.0 %collective-permute-start.2 = (f32[256,1024]{1,0:T(8,128)S(1)}, f32[256,1024]{1,0:T(8,128)S(1)}, u32[]{:S(2)}, u32[]{:S(2)}) collective-permute-start(f32[256,1024]{1,0:T(8,128)S(1)} %convolution_add_fusion), channel_id=1, source_target_pairs={{0,65},{1,64},{2,67},{3,66},{4,69},{5,68},{6,71},{7,70},{8,73},{9,... | collective-permute-start | bytes 3145736 | tf_op jit(solution)/shard_map/ppermute | solution.py:121
  74.8 3.8 %fusion.9 = f32[256,1024]{1,0:T(8,128)S(1)} fusion(bf16[2048,1024]{1,0:T(8,128)(2,1)} %constant_dynamic-update-slice_fusion, bf16[256,8192]{1,0:T(8,128)(2,1)} %copy-done, s32[]{:T(128)S(6)} %select_n.15), kind=kOutput, calls=%fused_computation.14 | convolution fusion | flops 1073741824 | bytes 6291460 | tf_op jit(solution)/shard_map/dot_general | solution.py:116
  78.6 19.5 %collective-permute-done.2 = f32[256,1024]{1,0:T(8,128)S(1)} collective-permute-done((f32[256,1024]{1,0:T(8,128)S(1)}, f32[256,1024]{1,0:T(8,128)S(1)}, u32[]{:S(2)}, u32[]{:S(2)}) %collective-permute-start.2) | collective-permute-done | bytes 1048608 | tf_op jit(solution)/shard_map/ppermute | solution.py:121
  98.1 3.8 %fusion.4 = bf16[256,1024]{1,0:T(8,128)(2,1)S(1)} fusion(f32[256,1024]{1,0:T(8,128)S(1)} %collective-permute-done.2, f32[256,1024]{1,0:T(8,128)S(1)} %fusion.9, bf16[2048,1024]{1,0:T(8,128)(2,1)} %collective-permute-done, bf16[256,8192]{1,0:T(8,128)(2,1)} %copy-done, s32[]{:T(128)S(6)} %select_n.16), kind=kOutput, calls=%fused_computation.9 | convolution fusion | flops 1074528256 | bytes 7864324 | tf_op jit(solution)/shard_map/dot_general | solution.py:116
  101.9 0.4 convert_element_type.28
  102.3 0.4 copy.13
  102.7 5.7 %broadcast_in_dim.4 = bf16[256,2,4,8,128]{4,1,0,3,2:T(2,128)(2,1)} broadcast(bf16[256,2,4,128]{3,1,0,2:T(2,128)(2,1)S(1)} %copy.13), dimensions={0,1,2,4} | broadcast | bytes 4718592 | tf_op jit(solution)/shard_map/broadcast_in_dim | solution.py:126
  108.4 0.0 copy-start.3
  108.4 7.6 %all-to-all-start.1 = ((bf16[256,2,32,128]{3,1,0,2:T(2,128)(2,1)}), bf16[256,2,32,128]{3,1,0,2:T(2,128)(2,1)}, u32[]{:S(2)}, u32[]{:S(2)}) async-start(bf16[256,2,32,128]{3,1,0,2:T(2,128)(2,1)} %bitcast.31), calls=%async_computation.1 | async-start | bytes 8388608 | tf_op jit(solution)/shard_map/all_to_all | solution.py:128
  116.0 0.0 copy-done.3
  116.0 0.5 copy.15
  116.5 0.0 copy-start.5
  116.5 2.1 copy.12
  118.7 53.7 %all-to-all-done.1 = bf16[256,2,32,128]{3,1,0,2:T(2,128)(2,1)} async-done(((bf16[256,2,32,128]{3,1,0,2:T(2,128)(2,1)}), bf16[256,2,32,128]{3,1,0,2:T(2,128)(2,1)}, u32[]{:S(2)}, u32[]{:S(2)}) %all-to-all-start.1) | async-done | bytes 4194336 | tf_op jit(solution)/shard_map/all_to_all | solution.py:128
  172.3 6.0 %all-to-all-start = ((bf16[256,32,128]{2,0,1:T(8,128)(2,1)}), bf16[256,32,128]{2,0,1:T(8,128)(2,1)S(1)}, u32[]{:S(2)}, u32[]{:S(2)}) async-start(bf16[256,32,128]{2,0,1:T(8,128)(2,1)} %copy.12), calls=%async_computation | async-start | bytes 4194304 | tf_op jit(solution)/shard_map/all_to_all | solution.py:96
  178.4 0.0 copy-done.5
  178.4 0.1 copy.11
  178.5 0.7 reshape_squeeze.3.lists_ref
  179.2 4.7 %copy.18 = bf16[1024,8,2,128]{3,1,2,0:T(8,128)(2,1)} copy(bf16[1024,8,2,128]{3,2,1,0:T(2,128)(2,1)} %bitcast.18) | data formatting | bytes 8388608
  183.9 20.8 %all-to-all-done = bf16[256,32,128]{2,0,1:T(8,128)(2,1)S(1)} async-done(((bf16[256,32,128]{2,0,1:T(8,128)(2,1)}), bf16[256,32,128]{2,0,1:T(8,128)(2,1)S(1)}, u32[]{:S(2)}, u32[]{:S(2)}) %all-to-all-start) | async-done | bytes 2097184 | tf_op jit(solution)/shard_map/all_to_all | solution.py:96
  204.7 0.0 copy-start.1
  204.7 1.3 copy-done.1
  206.0 59.5 %shard_map.73 = bf16[8192,128]{1,0:T(8,128)(2,1)} custom-call(s32[768]{0:T(1024)} %reshape_squeeze.3.lists_ref, s32[64]{0:T(128)} %bitcast.37, bf16[8192,128]{1,0:T(8,128)(2,1)} %bitcast.34, bf16[8192,256]{1,0:T(8,128)(2,1)} %bitcast.29, bf16[8192,256]{1,0:T(8,128)(2,1)} %bitcast.30), custom_call_target="tpu_custom_call" | custom-call | tf_op jit(solution)/shard_map/pallas_call | solution.py:55
  265.5 32.2 %all_to_all.50 = bf16[32,256,128]{2,1,0:T(8,128)(2,1)S(1)} all-to-all(bf16[32,256,128]{2,1,0:T(8,128)(2,1)} %bitcast.35), channel_id=1, replica_groups=mesh['zh'=2,'core'=2,'x'=4,'y'=4,'zl'=2] {'x','y','zl'}, dimensions={0} | all-to-all | bytes 4194304 | tf_op jit(solution)/shard_map/all_to_all | solution.py:134
  297.7 1.4 copy.14
  299.1 2.3 broadcast_in_dim.5
  (2 shorter events, 0.0 us)
Async XLA Ops:
  0.0 3.2 %copy-start.2 = (bf16[2048,512]{1,0:T(8,128)(2,1)S(1)}, bf16[2048,512]{1,0:T(8,128)(2,1)}, u32[]{:S(2)}) copy-start(bf16[2048,512]{1,0:T(8,128)(2,1)} %param.11) | copy-start | bytes 6291460
  0.0 4.7 %copy-start.4 = (bf16[8192]{0:T(1024)(128)(2,1)S(1)}, bf16[8192]{0:T(1024)(128)(2,1)}, u32[]{:S(2)}) copy-start(bf16[8192]{0:T(1024)(128)(2,1)} %param.8) | copy-start | bytes 49156
  4.7 59.5 %collective-permute-start = (bf16[2048,1024]{1,0:T(8,128)(2,1)}, bf16[2048,1024]{1,0:T(8,128)(2,1)}, u32[]{:S(2)}, u32[]{:S(2)}) collective-permute-start(bf16[2048,1024]{1,0:T(8,128)(2,1)} %constant_dynamic-update-slice_fusion), channel_id=1, source_target_pairs={{0,32},{32,0},{1,33},{33,1},{2,34},{34,2},{3,35},{35,3},{4,36},{36... | collective-permute-start | bytes 12582920 | tf_op jit(solution)/shard_map/ppermute | solution.py:111
  11.5 2.0 copy-start
  13.6 50.6 %collective-permute-start.1 = (bf16[256,4096]{1,0:T(8,128)(2,1)S(1)}, bf16[256,4096]{1,0:T(8,128)(2,1)}, u32[]{:S(2)}, u32[]{:S(2)}) collective-permute-start(bf16[256,4096]{1,0:T(8,128)(2,1)S(1)} %constant_dynamic-slice_fusion), channel_id=1, source_target_pairs={{0,65},{1,64},{2,67},{3,66},{4,69},{5,68},{6,71},{7,70},{8,73},{9,... | collective-permute-start | bytes 6291464 | tf_op jit(solution)/shard_map/ppermute | solution.py:110
  71.8 26.3 %collective-permute-start.2 = (f32[256,1024]{1,0:T(8,128)S(1)}, f32[256,1024]{1,0:T(8,128)S(1)}, u32[]{:S(2)}, u32[]{:S(2)}) collective-permute-start(f32[256,1024]{1,0:T(8,128)S(1)} %convolution_add_fusion), channel_id=1, source_target_pairs={{0,65},{1,64},{2,67},{3,66},{4,69},{5,68},{6,71},{7,70},{8,73},{9,... | collective-permute-start | bytes 3145736 | tf_op jit(solution)/shard_map/ppermute | solution.py:121
  108.4 7.6 %copy-start.3 = (bf16[1,256,4096]{2,1,0:T(8,128)(2,1)S(1)}, bf16[1,256,4096]{2,1,0:T(8,128)(2,1)}, u32[]{:S(2)}) copy-start(bf16[1,256,4096]{2,1,0:T(8,128)(2,1)} %param.9) | copy-start | bytes 6291460
  108.4 63.9 %all-to-all-start.1 = ((bf16[256,2,32,128]{3,1,0,2:T(2,128)(2,1)}), bf16[256,2,32,128]{3,1,0,2:T(2,128)(2,1)}, u32[]{:S(2)}, u32[]{:S(2)}) async-start(bf16[256,2,32,128]{3,1,0,2:T(2,128)(2,1)} %bitcast.31), calls=%async_computation.1 | async-start | bytes 8388608 | tf_op jit(solution)/shard_map/all_to_all | solution.py:128
  116.5 61.8 %copy-start.5 = (s32[1,1,64,12]{2,1,3,0:T(1,128)S(1)}, s32[1,1,64,12]{2,1,3,0:T(1,128)}, u32[]{:S(2)}) copy-start(s32[1,1,64,12]{2,1,3,0:T(1,128)} %param.12) | copy-start | bytes 9220
  172.3 32.4 %all-to-all-start = ((bf16[256,32,128]{2,0,1:T(8,128)(2,1)}), bf16[256,32,128]{2,0,1:T(8,128)(2,1)S(1)}, u32[]{:S(2)}, u32[]{:S(2)}) async-start(bf16[256,32,128]{2,0,1:T(8,128)(2,1)} %copy.12), calls=%async_computation | async-start | bytes 4194304 | tf_op jit(solution)/shard_map/all_to_all | solution.py:96
  204.7 1.3 copy-start.1

commit v5 on v4

--- a/solution.py
+++ b/solution.py
@@ -11,62 +11,68 @@
 MAXB = 12
 
 
-def attend_kernel(lists_ref, counts_ref, q_ref, k_ref, v_ref, o_ref):
-    block = pl.program_id(0)
-    query = q_ref[...]
-    count = counts_ref[block]
+SUB_BLOCKS = 8
+
+
+def attend_kernel(lists_ref, counts_ref, q_ref, kt_ref, v_ref, o_ref):
+    step = pl.program_id(0)
     score_scale = HD ** (-0.5)
     rows = lax.broadcasted_iota(jnp.int32, (BLK, BLK), 0)
     cols = lax.broadcasted_iota(jnp.int32, (BLK, BLK), 1)
-    masked = []
-    for slot in range(MAXB):
-        start = pl.multiple_of(lists_ref[block * MAXB + slot] * BLK, BLK)
-        key_tile = k_ref[pl.ds(start, BLK), :]
-        scores = (
-            lax.dot_general(
-                query, key_tile, (((1,), (1,)), ((), ())), preferred_element_type=jnp.float32
+
+    def one_block(sub, carry):
+        block = step * SUB_BLOCKS + sub
+        first_row = pl.multiple_of(sub * BLK, BLK)
+        query = q_ref[pl.ds(first_row, BLK), :]
+        count = counts_ref[block]
+        masked = []
+        for slot in range(MAXB):
+            start = pl.multiple_of(lists_ref[block * MAXB + slot] * BLK, BLK)
+            key_tile = kt_ref[:, pl.ds(start, BLK)]
+            scores = jnp.dot(query, key_tile, preferred_element_type=jnp.float32) * score_scale
+            allowed = slot < count
+            if slot == 0:
+                allowed = jnp.logical_and(allowed, cols <= rows)
+            masked.append(jnp.where(allowed, scores, -jnp.inf))
+        peak = masked[0]
+        for scores in masked[1:]:
+            peak = jnp.maximum(peak, scores)
+        row_peak = jnp.max(peak, axis=1, keepdims=True)
+        denominator = jnp.zeros((BLK, 1), jnp.float32)
+        weighted = jnp.zeros((BLK, HD), jnp.float32)
+        for slot in range(MAXB):
+            start = pl.multiple_of(lists_ref[block * MAXB + slot] * BLK, BLK)
+            value_tile = v_ref[pl.ds(start, BLK), :]
+            exponent = jnp.exp(masked[slot] - row_peak)
+            denominator = denominator + jnp.sum(exponent, axis=1, keepdims=True)
+            weighted = weighted + jnp.dot(
+                exponent.astype(jnp.bfloat16), value_tile, preferred_element_type=jnp.float32
             )
-            * score_scale
-        )
-        allowed = slot < count
-        if slot == 0:
-            allowed = jnp.logical_and(allowed, cols <= rows)
-        masked.append(jnp.where(allowed, scores, -jnp.inf))
-    peak = masked[0]
-    for scores in masked[1:]:
-        peak = jnp.maximum(peak, scores)
-    row_peak = jnp.max(peak, axis=1, keepdims=True)
-    denominator = jnp.zeros((BLK, 1), jnp.float32)
-    weighted = jnp.zeros((BLK, HD), jnp.float32)
-    for slot in range(MAXB):
-        start = pl.multiple_of(lists_ref[block * MAXB + slot] * BLK, BLK)
-        value_tile = v_ref[pl.ds(start, BLK), :]
-        exponent = jnp.exp(masked[slot] - row_peak)
-        denominator = denominator + jnp.sum(exponent, axis=1, keepdims=True)
-        weighted = weighted + jnp.dot(
-            exponent.astype(jnp.bfloat16), value_tile, preferred_element_type=jnp.float32
-        )
-    o_ref[...] = (weighted / denominator).astype(o_ref.dtype)
+        o_ref[pl.ds(first_row, BLK), :] = (weighted / denominator).astype(o_ref.dtype)
+        return carry
+
+    lax.fori_loop(0, SUB_BLOCKS, one_block, 0)
 
 
-def attend(lists_flat, counts, head_queries, kv_rows):
+def attend(lists_flat, counts, head_queries, key_t, values):
     sequence_rows = head_queries.shape[0]
     block_total = sequence_rows // BLK
+    step_rows = SUB_BLOCKS * BLK
     return pl.pallas_call(
         attend_kernel,
         out_shape=jax.ShapeDtypeStruct((sequence_rows, HD), jnp.bfloat16),
         grid_spec=pltpu.PrefetchScalarGridSpec(
             num_scalar_prefetch=2,
-            grid=(block_total,),
+            grid=(block_total // SUB_BLOCKS,),
             in_specs=[
-                pl.BlockSpec((BLK, HD), lambda i, lists, counts: (i, 0)),
+                pl.BlockSpec((step_rows, HD), lambda i, lists, counts: (i, 0)),
+                pl.BlockSpec((HD, sequence_rows), lambda i, lists, counts: (0, 0)),
                 pl.BlockSpec((sequence_rows, HD), lambda i, lists, counts: (0, 0)),
-                pl.BlockSpec((sequence_rows, HD), lambda i, lists, counts: (0, 1)),
             ],
-            out_specs=pl.BlockSpec((BLK, HD), lambda i, lists, counts: (i, 0)),
+            out_specs=pl.BlockSpec((step_rows, HD), lambda i, lists, counts: (i, 0)),
         ),
         compiler_params=pltpu.CompilerParams(dimension_semantics=("arbitrary",)),
-    )(lists_flat, counts, head_queries, kv_rows, kv_rows)
+    )(lists_flat, counts, head_queries, key_t, values)
 
 
 ALL_AXES = ("zh", "core", "x", "y", "zl")
@@ -108,6 +114,7 @@
     partner_pairs = cross_half_pairs(False)
     far_features = lax.dynamic_slice_in_dim(normed, (1 - zh) * half_features, half_features, axis=1)
     partner_rows = lax.ppermute(far_features, ALL_AXES, partner_pairs)
+    head_queries, partner_rows = lax.optimization_barrier((head_queries, partner_rows))
     sibling = lax.ppermute(local_weight, "core", [(0, 1), (1, 0)])
 
     def half_sum(rows, offset):
@@ -128,9 +135,11 @@
     head_pair = lax.all_to_all(widened, CTX_AXES, split_axis=2, concat_axis=0, tiled=True)
     sequence_rows = head_queries.shape[0]
     kv_rows = head_pair.reshape(sequence_rows, 2 * HD)
+    key_t = kv_rows[:, :HD].T
+    values = kv_rows[:, HD:]
     lists_flat = block_lists[0, 0].reshape(-1)
     counts = block_counts[0, 0]
-    attended_head = attend(lists_flat, counts, head_queries, kv_rows)
+    attended_head = attend(lists_flat, counts, head_queries, key_t, values)
     restored = lax.all_to_all(attended_head, CTX_AXES, split_axis=0, concat_axis=1, tiled=True)
     return restored[None]
 

time: 302 us -> 268 us (0.89)
  waiting for transfers between devices: 140 us -> 112 us
  Pallas kernels: 59.5 us -> 51.2 us
    ppermute x1, waiting for transfers between devices: 46.4 us -> 7.89 us  [on_device(): partner_rows = lax.ppermute(far_features, ALL_AXES, partner_pairs)]
    pallas_call x1, Pallas kernels: 59.5 us -> 51.2 us  [attend(): pl.pallas_call(attend_kernel, out_shape=jax.ShapeDtypeStruct((sequence_ro...]
    all_to_all x1, waiting for transfers between devices: 20.8 us -> 28.8 us  [on_device(): lax.all_to_all(queries[0], CTX_AXES, split_axis=1, concat_axis=0, tiled=T...]
    unnamed x16, local copies, waits for them, and re-layouts: 11.8 us -> 6.55 us
where the time goes in v5:
time: 268 us; the launch traced here: 267 us
  waiting for transfers between devices  112 us (42%)
  Pallas kernels  51.2 us (19%)
  blocking collectives  32.5 us (12%)
  local copies, waits for them, and re-layouts  27.1 us (10%)
  starting transfers between devices  22.3 us (8%)
  matrix products  15.4 us (6%)
  other arithmetic  6.73 us (3%)
    all_to_all x1, waiting for transfers between devices, on_device(): lax.all_to_all(widened, CTX_AXES, split_axis=2, concat_axis=0, tiled=True)  55.5 us
    pallas_call x1, Pallas kernels, attend(): pl.pallas_call(attend_kernel, out_shape=jax.ShapeDtypeStruct((sequence_ro...  51.2 us
    all_to_all x1, blocking collectives, on_device(): lax.all_to_all(attended_head, CTX_AXES, split_axis=0, concat_axis=1, tile...  32.5 us
    all_to_all x1, waiting for transfers between devices, on_device(): lax.all_to_all(queries[0], CTX_AXES, split_axis=1, concat_axis=0, tiled=T...  28.8 us
    ppermute x1, waiting for transfers between devices, on_device(): from_partner = lax.ppermute(for_partner, ALL_AXES, partner_pairs)  19.6 us
    ppermute x1, waiting for transfers between devices, on_device(): partner_rows = lax.ppermute(far_features, ALL_AXES, partner_pairs)  7.89 us
    dot_general x2, matrix products, half_sum(): jnp.dot(other, sibling, preferred_element_type=jnp.float32)  7.81 us
    all_to_all x1, starting transfers between devices, on_device(): lax.all_to_all(widened, CTX_AXES, split_axis=2, concat_axis=0, tiled=True)  7.76 us
  transfers between devices with their start and end apart: 5, of which 4 were waited for; matrix products, arithmetic and copies ran while one was open for 6% of the time, Pallas kernels for 0%

profile of v5, /device:TPU:0, one launch (start us, length us, event | category | flops | bytes accessed | tf_op | source)
XLA Modules:
  0.0 267.1 jit_solution(10761196518666574279)
XLA Ops:
  0.0 0.0 copy-start.2
  0.0 0.0 copy-start.4
  0.0 3.2 %constant_dynamic-update-slice_fusion.1 = bf16[2048,1024]{1,0:T(8,128)(2,1)} fusion(bf16[2048,512]{1,0:T(8,128)(2,1)} %param.10), kind=kLoop, calls=%fused_computation.18 | loop fusion | bytes 4194304
  3.2 0.0 copy-done.2
  3.2 1.5 constant_dynamic-update-slice_fusion
  4.7 0.0 collective-permute-start.1
  4.7 0.0 copy-done.4
  4.7 3.1 %fusion = f32[256]{0:T(256)S(1)} fusion(bf16[1,256,8192]{2,1,0:T(8,128)(2,1)} %param.7), kind=kLoop, calls=%fused_computation.2 | loop fusion | flops 6291200 | bytes 4195328 | tf_op jit(solution)/shard_map/reduce_sum | solution.py:104
  7.9 3.6 %fusion.2 = bf16[256,8192]{1,0:T(8,128)(2,1)S(1)} fusion(bf16[1,256,8192]{2,1,0:T(8,128)(2,1)} %param.7, f32[8192]{0:T(1024)S(1)} %convert_element_type.25, f32[256]{0:T(256)S(1)} %add_rsqrt_fusion), kind=kLoop, calls=%fused_computation.4 | loop fusion | flops 8388608 | bytes 8422400 | tf_op jit(solution)/shard_map/convert_element_type | solution.py:105
  11.5 0.0 copy-start
  11.5 0.0 copy-start.3
  11.5 1.6 constant_dynamic-slice_fusion
  13.1 4.1 %collective-permute-start = (bf16[256,4096]{1,0:T(8,128)(2,1)}, bf16[256,4096]{1,0:T(8,128)(2,1)}, u32[]{:S(2)}, u32[]{:S(2)}) collective-permute-start(bf16[256,4096]{1,0:T(8,128)(2,1)} %constant_dynamic-slice_fusion), channel_id=1, source_target_pairs={{0,65},{1,64},{2,67},{3,66},{4,69},{5,68},{6,71},{7,70},{8,73},{9,... | collective-permute-start | bytes 6291464 | tf_op jit(solution)/shard_map/ppermute | solution.py:116
  17.2 0.0 copy-done.3
  17.2 0.5 copy.17
  17.7 0.0 copy-done
  17.7 2.1 copy.13
  19.8 7.3 %all-to-all-start = ((bf16[256,32,128]{2,0,1:T(8,128)(2,1)}), bf16[256,32,128]{2,0,1:T(8,128)(2,1)S(1)}, u32[]{:S(2)}, u32[]{:S(2)}) async-start(bf16[256,32,128]{2,0,1:T(8,128)(2,1)} %copy.13), calls=%async_computation | async-start | bytes 4194304 | tf_op jit(solution)/shard_map/all_to_all | solution.py:102
  27.2 28.8 %all-to-all-done = bf16[256,32,128]{2,0,1:T(8,128)(2,1)S(1)} async-done(((bf16[256,32,128]{2,0,1:T(8,128)(2,1)}), bf16[256,32,128]{2,0,1:T(8,128)(2,1)S(1)}, u32[]{:S(2)}, u32[]{:S(2)}) %all-to-all-start) | async-done | bytes 2097184 | tf_op jit(solution)/shard_map/all_to_all | solution.py:102
  55.9 0.0 copy-start.1
  55.9 7.9 %collective-permute-done = bf16[256,4096]{1,0:T(8,128)(2,1)} collective-permute-done((bf16[256,4096]{1,0:T(8,128)(2,1)}, bf16[256,4096]{1,0:T(8,128)(2,1)}, u32[]{:S(2)}, u32[]{:S(2)}) %collective-permute-start) | collective-permute-done | bytes 2097184 | tf_op jit(solution)/shard_map/ppermute | solution.py:116
  63.8 0.0 collective-permute-done.1
  63.8 3.8 %fusion.5 = f32[256,1024]{1,0:T(8,128)S(1)} fusion(bf16[2048,1024]{1,0:T(8,128)(2,1)} %collective-permute-done.1, bf16[256,4096]{1,0:T(8,128)(2,1)} %collective-permute-done, s32[]{:T(128)S(6)} %select_n.19), kind=kOutput, calls=%fused_computation.11 | convolution fusion | flops 1073741824 | bytes 6291460 | tf_op jit(solution)/shard_map/dot_general | solution.py:123
  67.6 3.8 %convolution_add_fusion = f32[256,1024]{1,0:T(8,128)S(1)} fusion(f32[256,1024]{1,0:T(8,128)S(1)} %fusion.5, bf16[2048,1024]{1,0:T(8,128)(2,1)} %constant_dynamic-update-slice_fusion, bf16[256,4096]{1,0:T(8,128)(2,1)} %collective-permute-done, s32[]{:T(128)S(6)} %select_n.18), kind=kOutput, calls=%fused_computation.7 | convolution fusion | flops 1074003968 | bytes 7340036 | tf_op jit(solution)/shard_map/dot_general | solution.py:123
  71.4 0.0 copy-done.1
  71.4 3.0 %collective-permute-start.2 = (f32[256,1024]{1,0:T(8,128)S(1)}, f32[256,1024]{1,0:T(8,128)}, u32[]{:S(2)}, u32[]{:S(2)}) collective-permute-start(f32[256,1024]{1,0:T(8,128)S(1)} %convolution_add_fusion), channel_id=1, source_target_pairs={{0,65},{1,64},{2,67},{3,66},{4,69},{5,68},{6,71},{7,70},{8,73},{9,... | collective-permute-start | bytes 3145736 | tf_op jit(solution)/shard_map/ppermute | solution.py:128
  74.4 3.8 %fusion.9 = f32[256,1024]{1,0:T(8,128)S(1)} fusion(bf16[2048,1024]{1,0:T(8,128)(2,1)} %constant_dynamic-update-slice_fusion, bf16[256,8192]{1,0:T(8,128)(2,1)} %copy-done, s32[]{:T(128)S(6)} %select_n.16), kind=kOutput, calls=%fused_computation.15 | convolution fusion | flops 1073741824 | bytes 6291460 | tf_op jit(solution)/shard_map/dot_general | solution.py:123
  78.2 19.6 %collective-permute-done.2 = f32[256,1024]{1,0:T(8,128)} collective-permute-done((f32[256,1024]{1,0:T(8,128)S(1)}, f32[256,1024]{1,0:T(8,128)}, u32[]{:S(2)}, u32[]{:S(2)}) %collective-permute-start.2) | collective-permute-done | bytes 1048608 | tf_op jit(solution)/shard_map/ppermute | solution.py:128
  97.8 4.1 %fusion.4 = bf16[256,1024]{1,0:T(8,128)(2,1)S(1)} fusion(f32[256,1024]{1,0:T(8,128)} %collective-permute-done.2, f32[256,1024]{1,0:T(8,128)S(1)} %fusion.9, bf16[2048,1024]{1,0:T(8,128)(2,1)} %collective-permute-done.1, bf16[256,8192]{1,0:T(8,128)(2,1)} %copy-done, s32[]{:T(128)S(6)} %select_n.17), kind=kOutput, calls=%fused_computation.10 | convolution fusion | flops 1074528256 | bytes 7864324 | tf_op jit(solution)/shard_map/dot_general | solution.py:123
  101.8 0.4 convert_element_type.28
  102.2 0.4 copy.14
  102.6 5.7 %broadcast_in_dim.4 = bf16[256,2,4,8,128]{4,1,0,3,2:T(2,128)(2,1)} broadcast(bf16[256,2,4,128]{3,1,0,2:T(2,128)(2,1)S(1)} %copy.14), dimensions={0,1,2,4} | broadcast | bytes 4718592 | tf_op jit(solution)/shard_map/broadcast_in_dim | solution.py:133
  108.4 0.0 copy-start.5
  108.4 7.8 %all-to-all-start.1 = ((bf16[256,2,32,128]{3,1,0,2:T(2,128)(2,1)}), bf16[256,2,32,128]{3,1,0,2:T(2,128)(2,1)}, u32[]{:S(2)}, u32[]{:S(2)}) async-start(bf16[256,2,32,128]{3,1,0,2:T(2,128)(2,1)} %bitcast.31), calls=%async_computation.1 | async-start | bytes 8388608 | tf_op jit(solution)/shard_map/all_to_all | solution.py:135
  116.1 0.0 copy-done.5
  116.1 0.1 copy.12
  116.2 0.7 reshape_squeeze.3.lists_ref
  116.9 55.5 %all-to-all-done.1 = bf16[256,2,32,128]{3,1,0,2:T(2,128)(2,1)} async-done(((bf16[256,2,32,128]{3,1,0,2:T(2,128)(2,1)}), bf16[256,2,32,128]{3,1,0,2:T(2,128)(2,1)}, u32[]{:S(2)}, u32[]{:S(2)}) %all-to-all-start.1) | async-done | bytes 4194336 | tf_op jit(solution)/shard_map/all_to_all | solution.py:135
  172.4 2.7 %copy.20 = bf16[1024,8,2,128]{3,1,2,0:T(8,128)(2,1)S(1)} copy(bf16[1024,8,2,128]{3,2,1,0:T(2,128)(2,1)} %bitcast.19) | data formatting | bytes 8388608
  175.2 1.6 fusion.15
  176.8 2.9 %copy.15.kt_ref = bf16[128,8192]{1,0:T(8,128)(2,1)} copy(bf16[128,8192]{0,1:T(8,128)(2,1)S(1)} %get-tuple-element.10) | data formatting | bytes 4194304 | tf_op jit(solution)/shard_map/transpose | solution.py:138
  179.7 51.2 %shard_map.73 = bf16[8192,128]{1,0:T(8,128)(2,1)} custom-call(s32[768]{0:T(1024)} %reshape_squeeze.3.lists_ref, s32[64]{0:T(128)} %bitcast.38, bf16[8192,128]{1,0:T(8,128)(2,1)} %bitcast.35, bf16[128,8192]{1,0:T(8,128)(2,1)} %copy.15.kt_ref, bf16[8192,128]{1,0:T(8,128)(2,1)} %get-tuple-element.9.v_ref), custom_call_target="tpu_custom_call" | custom-call | tf_op jit(solution)/shard_map/pallas_call | solution.py:61
  230.9 32.5 %all_to_all.50 = bf16[32,256,128]{2,1,0:T(8,128)(2,1)S(1)} all-to-all(bf16[32,256,128]{2,1,0:T(8,128)(2,1)} %bitcast.36), channel_id=1, replica_groups=mesh['zh'=2,'core'=2,'x'=4,'y'=4,'zl'=2] {'x','y','zl'}, dimensions={0} | all-to-all | bytes 4194304 | tf_op jit(solution)/shard_map/all_to_all | solution.py:143
  263.4 1.4 copy.16
  264.8 2.3 broadcast_in_dim.5
  (2 shorter events, 0.0 us)
Async XLA Ops:
  0.0 3.2 %copy-start.2 = (bf16[2048,512]{1,0:T(8,128)(2,1)S(1)}, bf16[2048,512]{1,0:T(8,128)(2,1)}, u32[]{:S(2)}) copy-start(bf16[2048,512]{1,0:T(8,128)(2,1)} %param.11) | copy-start | bytes 6291460
  0.0 4.7 %copy-start.4 = (bf16[8192]{0:T(1024)(128)(2,1)S(1)}, bf16[8192]{0:T(1024)(128)(2,1)}, u32[]{:S(2)}) copy-start(bf16[8192]{0:T(1024)(128)(2,1)} %param.8) | copy-start | bytes 49156
  4.7 59.1 %collective-permute-start.1 = (bf16[2048,1024]{1,0:T(8,128)(2,1)}, bf16[2048,1024]{1,0:T(8,128)(2,1)}, u32[]{:S(2)}, u32[]{:S(2)}) collective-permute-start(bf16[2048,1024]{1,0:T(8,128)(2,1)} %constant_dynamic-update-slice_fusion), channel_id=1, source_target_pairs={{0,32},{32,0},{1,33},{33,1},{2,34},{34,2},{3,35},{35,3},{4,36},{36... | collective-permute-start | bytes 12582920 | tf_op jit(solution)/shard_map/ppermute | solution.py:118
  11.5 6.2 %copy-start = (bf16[256,8192]{1,0:T(8,128)(2,1)}, bf16[256,8192]{1,0:T(8,128)(2,1)S(1)}, u32[]{:S(2)}) copy-start(bf16[256,8192]{1,0:T(8,128)(2,1)S(1)} %fusion.2) | copy-start | bytes 12582916
  11.5 5.7 %copy-start.3 = (bf16[1,256,4096]{2,1,0:T(8,128)(2,1)S(1)}, bf16[1,256,4096]{2,1,0:T(8,128)(2,1)}, u32[]{:S(2)}) copy-start(bf16[1,256,4096]{2,1,0:T(8,128)(2,1)} %param.9) | copy-start | bytes 6291460
  13.1 50.8 %collective-permute-start = (bf16[256,4096]{1,0:T(8,128)(2,1)}, bf16[256,4096]{1,0:T(8,128)(2,1)}, u32[]{:S(2)}, u32[]{:S(2)}) collective-permute-start(bf16[256,4096]{1,0:T(8,128)(2,1)} %constant_dynamic-slice_fusion), channel_id=1, source_target_pairs={{0,65},{1,64},{2,67},{3,66},{4,69},{5,68},{6,71},{7,70},{8,73},{9,... | collective-permute-start | bytes 6291464 | tf_op jit(solution)/shard_map/ppermute | solution.py:116
  19.8 36.1 %all-to-all-start = ((bf16[256,32,128]{2,0,1:T(8,128)(2,1)}), bf16[256,32,128]{2,0,1:T(8,128)(2,1)S(1)}, u32[]{:S(2)}, u32[]{:S(2)}) async-start(bf16[256,32,128]{2,0,1:T(8,128)(2,1)} %copy.13), calls=%async_computation | async-start | bytes 4194304 | tf_op jit(solution)/shard_map/all_to_all | solution.py:102
  55.9 15.5 %copy-start.1 = (bf16[256,32,128]{2,0,1:T(8,128)(2,1)}, bf16[256,32,128]{2,0,1:T(8,128)(2,1)S(1)}, u32[]{:S(2)}) copy-start(bf16[256,32,128]{2,0,1:T(8,128)(2,1)S(1)} %all-to-all-done) | copy-start | bytes 6291460
  71.4 26.4 %collective-permute-start.2 = (f32[256,1024]{1,0:T(8,128)S(1)}, f32[256,1024]{1,0:T(8,128)}, u32[]{:S(2)}, u32[]{:S(2)}) collective-permute-start(f32[256,1024]{1,0:T(8,128)S(1)} %convolution_add_fusion), channel_id=1, source_target_pairs={{0,65},{1,64},{2,67},{3,66},{4,69},{5,68},{6,71},{7,70},{8,73},{9,... | collective-permute-start | bytes 3145736 | tf_op jit(solution)/shard_map/ppermute | solution.py:128
  108.4 7.8 %copy-start.5 = (s32[1,1,64,12]{2,1,3,0:T(1,128)S(1)}, s32[1,1,64,12]{2,1,3,0:T(1,128)}, u32[]{:S(2)}) copy-start(s32[1,1,64,12]{2,1,3,0:T(1,128)} %param.12) | copy-start | bytes 9220
  108.4 64.1 %all-to-all-start.1 = ((bf16[256,2,32,128]{3,1,0,2:T(2,128)(2,1)}), bf16[256,2,32,128]{3,1,0,2:T(2,128)(2,1)}, u32[]{:S(2)}, u32[]{:S(2)}) async-start(bf16[256,2,32,128]{3,1,0,2:T(2,128)(2,1)} %bitcast.31), calls=%async_computation.1 | async-start | bytes 8388608 | tf_op jit(solution)/shard_map/all_to_all | solution.py:135

commit v6 on v5

--- a/solution.py
+++ b/solution.py
@@ -1,3 +1,5 @@
+import functools
+
 import jax
 import jax.numpy as jnp
 from jax import lax
@@ -14,16 +16,18 @@
 SUB_BLOCKS = 8
 
 
-def attend_kernel(lists_ref, counts_ref, q_ref, kt_ref, v_ref, o_ref):
+SUB_BLOCKS = 8
+
+
+def attend_kernel(parity, lists_ref, counts_ref, q_ref, kt_ref, v_ref, o_ref):
     step = pl.program_id(0)
     score_scale = HD ** (-0.5)
     rows = lax.broadcasted_iota(jnp.int32, (BLK, BLK), 0)
     cols = lax.broadcasted_iota(jnp.int32, (BLK, BLK), 1)
 
     def one_block(sub, carry):
-        block = step * SUB_BLOCKS + sub
-        first_row = pl.multiple_of(sub * BLK, BLK)
-        query = q_ref[pl.ds(first_row, BLK), :]
+        block = (step * SUB_BLOCKS + sub) * 2 + parity
+        query = q_ref[sub]
         count = counts_ref[block]
         masked = []
         for slot in range(MAXB):
@@ -48,31 +52,31 @@
             weighted = weighted + jnp.dot(
                 exponent.astype(jnp.bfloat16), value_tile, preferred_element_type=jnp.float32
             )
-        o_ref[pl.ds(first_row, BLK), :] = (weighted / denominator).astype(o_ref.dtype)
+        o_ref[sub] = (weighted / denominator).astype(o_ref.dtype)
         return carry
 
     lax.fori_loop(0, SUB_BLOCKS, one_block, 0)
 
 
-def attend(lists_flat, counts, head_queries, key_t, values):
-    sequence_rows = head_queries.shape[0]
-    block_total = sequence_rows // BLK
-    step_rows = SUB_BLOCKS * BLK
+def attend(parity, lists_flat, counts, query_pairs, key_t, values):
+    pair_total = query_pairs.shape[0]
     return pl.pallas_call(
-        attend_kernel,
-        out_shape=jax.ShapeDtypeStruct((sequence_rows, HD), jnp.bfloat16),
+        functools.partial(attend_kernel, parity),
+        out_shape=jax.ShapeDtypeStruct((pair_total, BLK, HD), jnp.bfloat16),
         grid_spec=pltpu.PrefetchScalarGridSpec(
             num_scalar_prefetch=2,
-            grid=(block_total // SUB_BLOCKS,),
+            grid=(pair_total // SUB_BLOCKS,),
             in_specs=[
-                pl.BlockSpec((step_rows, HD), lambda i, lists, counts: (i, 0)),
-                pl.BlockSpec((HD, sequence_rows), lambda i, lists, counts: (0, 0)),
-                pl.BlockSpec((sequence_rows, HD), lambda i, lists, counts: (0, 0)),
+                pl.BlockSpec(
+                    (SUB_BLOCKS, None, BLK, HD), lambda i, lists, counts: (i, parity, 0, 0)
+                ),
+                pl.BlockSpec(key_t.shape, lambda i, lists, counts: (0, 0)),
+                pl.BlockSpec(values.shape, lambda i, lists, counts: (0, 0)),
             ],
-            out_specs=pl.BlockSpec((step_rows, HD), lambda i, lists, counts: (i, 0)),
+            out_specs=pl.BlockSpec((SUB_BLOCKS, BLK, HD), lambda i, lists, counts: (i, 0, 0)),
         ),
         compiler_params=pltpu.CompilerParams(dimension_semantics=("arbitrary",)),
-    )(lists_flat, counts, head_queries, key_t, values)
+    )(lists_flat, counts, query_pairs, key_t, values)
 
 
 ALL_AXES = ("zh", "core", "x", "y", "zl")
@@ -139,8 +143,16 @@
     values = kv_rows[:, HD:]
     lists_flat = block_lists[0, 0].reshape(-1)
     counts = block_counts[0, 0]
-    attended_head = attend(lists_flat, counts, head_queries, key_t, values)
-    restored = lax.all_to_all(attended_head, CTX_AXES, split_axis=0, concat_axis=1, tiled=True)
+    query_pairs = head_queries.reshape(sequence_rows // (2 * BLK), 2, BLK, HD)
+    halves = []
+    for parity in range(2):
+        attended_half = attend(parity, lists_flat, counts, query_pairs, key_t, values)
+        halves.append(
+            lax.all_to_all(
+                attended_half.reshape(sequence_rows // 2, HD), CTX_AXES, split_axis=0, concat_axis=1, tiled=True
+            )
+        )
+    restored = jnp.stack(halves).reshape(2 * BLK, -1)
     return restored[None]
 
 

time: 268 us -> 272 us (1.015)
  blocking collectives: 32.5 us -> 0 us
  starting transfers between devices: 22.3 us -> 36.4 us
  waiting for transfers between devices: 112 us -> 122 us
  local copies, waits for them, and re-layouts: 27.1 us -> 33.7 us
  Pallas kernels: 51.2 us -> 55 us
    all_to_all x1 -> x0, blocking collectives: 32.5 us -> none  [on_device(): lax.all_to_all(attended_head, CTX_AXES, split_axis=0, concat_axis=1, tile...]
    all_to_all x0 -> x2, waiting for transfers between devices: none -> 14.2 us  [on_device(): lax.all_to_all(attended_half.reshape(sequence_rows // 2, HD), CTX_AXES, s...]
    all_to_all x0 -> x2, starting transfers between devices: none -> 14.1 us  [on_device(): lax.all_to_all(attended_half.reshape(sequence_rows // 2, HD), CTX_AXES, s...]
    unnamed x16 -> x14, local copies, waits for them, and re-layouts: 6.55 us -> 11.3 us
    pallas_call x1 -> x2, Pallas kernels: 51.2 us -> 55 us  [attend(): pl.pallas_call(functools.partial(attend_kernel, parity), out_shape=jax.Sh...]
    ppermute x1, waiting for transfers between devices: 7.89 us -> 4.39 us  [on_device(): partner_rows = lax.ppermute(far_features, ALL_AXES, partner_pairs)]
    another operation x0 -> x1, local copies, waits for them, and re-layouts: none -> 2.72 us  [on_device(): restored = jnp.stack(halves).reshape(2 * BLK, -1)]
  transfers between devices with their start and end apart: 5 -> 7, of which waited for: 4 -> 5; matrix products, arithmetic and copies ran while one was open for 6% -> 7% of each run, Pallas kernels for 0% -> 10%
where the time goes in v6:
time: 272 us; the launch traced here: 271 us
  waiting for transfers between devices  122 us (45%)
  Pallas kernels  55 us (20%)
  starting transfers between devices  36.4 us (13%)
  local copies, waits for them, and re-layouts  33.7 us (12%)
  matrix products  15.4 us (6%)
  other arithmetic  8.15 us (3%)
    all_to_all x1, waiting for transfers between devices, on_device(): lax.all_to_all(widened, CTX_AXES, split_axis=2, concat_axis=0, tiled=True)  55.3 us
    pallas_call x2, Pallas kernels, attend(): pl.pallas_call(functools.partial(attend_kernel, parity), out_shape=jax.Sh...  55 us
    all_to_all x1, waiting for transfers between devices, on_device(): lax.all_to_all(queries[0], CTX_AXES, split_axis=1, concat_axis=0, tiled=T...  28.8 us
    ppermute x1, waiting for transfers between devices, on_device(): from_partner = lax.ppermute(for_partner, ALL_AXES, partner_pairs)  19.6 us
    all_to_all x2, waiting for transfers between devices, on_device(): lax.all_to_all(attended_half.reshape(sequence_rows // 2, HD), CTX_AXES, s...  14.2 us
    all_to_all x2, starting transfers between devices, on_device(): lax.all_to_all(attended_half.reshape(sequence_rows // 2, HD), CTX_AXES, s...  14.1 us
    unnamed x14, local copies, waits for them, and re-layouts  11.3 us
    dot_general x2, matrix products, half_sum(): jnp.dot(other, sibling, preferred_element_type=jnp.float32)  7.81 us
  transfers between devices with their start and end apart: 7, of which 5 were waited for; matrix products, arithmetic and copies ran while one was open for 7% of the time, Pallas kernels for 10%

profile of v6, /device:TPU:0, one launch (start us, length us, event | category | flops | bytes accessed | tf_op | source)
XLA Modules:
  0.0 270.9 jit_solution(11522977142803119352)
XLA Ops:
  0.0 0.0 copy-start.2
  0.0 0.0 copy-start.3
  0.0 3.2 %constant_dynamic-update-slice_fusion.1 = bf16[2048,1024]{1,0:T(8,128)(2,1)} fusion(bf16[2048,512]{1,0:T(8,128)(2,1)} %param.10), kind=kLoop, calls=%fused_computation.19 | loop fusion | bytes 4194304
  3.2 0.0 copy-done.2
  3.2 1.5 constant_dynamic-update-slice_fusion
  4.7 0.0 collective-permute-start.1
  4.7 0.0 copy-done.3
  4.7 3.1 %fusion = f32[256]{0:T(256)S(1)} fusion(bf16[1,256,8192]{2,1,0:T(8,128)(2,1)} %param.7), kind=kLoop, calls=%fused_computation.2 | loop fusion | flops 6291200 | bytes 4195328 | tf_op jit(solution)/shard_map/reduce_sum | solution.py:108
  7.8 3.6 %fusion.2 = bf16[256,8192]{1,0:T(8,128)(2,1)S(1)} fusion(bf16[1,256,8192]{2,1,0:T(8,128)(2,1)} %param.7, f32[8192]{0:T(1024)S(1)} %convert_element_type.25, f32[256]{0:T(256)S(1)} %add_rsqrt_fusion), kind=kLoop, calls=%fused_computation.4 | loop fusion | flops 8388608 | bytes 8422400 | tf_op jit(solution)/shard_map/convert_element_type | solution.py:109
  11.5 0.0 copy-start.1
  11.5 2.0 copy-done.1
  13.4 1.5 constant_dynamic-slice_fusion
  15.0 4.1 %collective-permute-start = (bf16[256,4096]{1,0:T(8,128)(2,1)}, bf16[256,4096]{1,0:T(8,128)(2,1)}, u32[]{:S(2)}, u32[]{:S(2)}) collective-permute-start(bf16[256,4096]{1,0:T(8,128)(2,1)} %constant_dynamic-slice_fusion), channel_id=1, source_target_pairs={{0,65},{1,64},{2,67},{3,66},{4,69},{5,68},{6,71},{7,70},{8,73},{9,... | collective-permute-start | bytes 6291464 | tf_op jit(solution)/shard_map/ppermute | solution.py:120
  19.1 3.3 %copy.35 = bf16[1,256,4096]{1,2,0:T(8,128)(2,1)S(1)} copy(bf16[1,256,4096]{2,1,0:T(8,128)(2,1)} %param.9) | data formatting | bytes 4194304 | tf_op args[2]
  22.4 2.9 %copy.36 = bf16[256,32,128]{2,0,1:T(8,128)(2,1)} copy(bf16[256,32,128]{0,2,1:T(8,128)(2,1)S(1)} %bitcast.37) | data formatting | bytes 4194304 | tf_op jit(solution)/shard_map/all_to_all | solution.py:106
  25.3 7.3 %all-to-all-start = ((bf16[256,32,128]{2,0,1:T(8,128)(2,1)}), bf16[256,32,128]{2,0,1:T(8,128)(2,1)S(1)}, u32[]{:S(2)}, u32[]{:S(2)}) async-start(bf16[256,32,128]{2,0,1:T(8,128)(2,1)} %copy.36), calls=%async_computation | async-start | bytes 4194304 | tf_op jit(solution)/shard_map/all_to_all | solution.py:106
  32.6 28.8 %all-to-all-done = bf16[256,32,128]{2,0,1:T(8,128)(2,1)S(1)} async-done(((bf16[256,32,128]{2,0,1:T(8,128)(2,1)}), bf16[256,32,128]{2,0,1:T(8,128)(2,1)S(1)}, u32[]{:S(2)}, u32[]{:S(2)}) %all-to-all-start) | async-done | bytes 2097184 | tf_op jit(solution)/shard_map/all_to_all | solution.py:106
  61.4 0.0 copy-start
  61.4 4.4 %collective-permute-done = bf16[256,4096]{1,0:T(8,128)(2,1)} collective-permute-done((bf16[256,4096]{1,0:T(8,128)(2,1)}, bf16[256,4096]{1,0:T(8,128)(2,1)}, u32[]{:S(2)}, u32[]{:S(2)}) %collective-permute-start) | collective-permute-done | bytes 2097184 | tf_op jit(solution)/shard_map/ppermute | solution.py:120
  65.7 0.0 collective-permute-done.1
  65.7 3.8 %fusion.5 = f32[256,1024]{1,0:T(8,128)S(1)} fusion(bf16[2048,1024]{1,0:T(8,128)(2,1)} %collective-permute-done.1, bf16[256,4096]{1,0:T(8,128)(2,1)} %collective-permute-done, s32[]{:T(128)S(6)} %select_n.19), kind=kOutput, calls=%fused_computation.12 | convolution fusion | flops 1073741824 | bytes 6291460 | tf_op jit(solution)/shard_map/dot_general | solution.py:127
  69.5 3.8 %convolution_add_fusion = f32[256,1024]{1,0:T(8,128)S(1)} fusion(f32[256,1024]{1,0:T(8,128)S(1)} %fusion.5, bf16[2048,1024]{1,0:T(8,128)(2,1)} %constant_dynamic-update-slice_fusion, bf16[256,4096]{1,0:T(8,128)(2,1)} %collective-permute-done, s32[]{:T(128)S(6)} %select_n.18), kind=kOutput, calls=%fused_computation.8 | convolution fusion | flops 1074003968 | bytes 7340036 | tf_op jit(solution)/shard_map/dot_general | solution.py:127
  73.3 0.0 copy-done
  73.3 3.0 %collective-permute-start.2 = (f32[256,1024]{1,0:T(8,128)S(1)}, f32[256,1024]{1,0:T(8,128)}, u32[]{:S(2)}, u32[]{:S(2)}) collective-permute-start(f32[256,1024]{1,0:T(8,128)S(1)} %convolution_add_fusion), channel_id=1, source_target_pairs={{0,65},{1,64},{2,67},{3,66},{4,69},{5,68},{6,71},{7,70},{8,73},{9,... | collective-permute-start | bytes 3145736 | tf_op jit(solution)/shard_map/ppermute | solution.py:132
  76.3 3.8 %fusion.9 = f32[256,1024]{1,0:T(8,128)S(1)} fusion(bf16[2048,1024]{1,0:T(8,128)(2,1)} %constant_dynamic-update-slice_fusion, bf16[256,8192]{1,0:T(8,128)(2,1)} %copy-done.1, s32[]{:T(128)S(6)} %select_n.16), kind=kOutput, calls=%fused_computation.16 | convolution fusion | flops 1073741824 | bytes 6291460 | tf_op jit(solution)/shard_map/dot_general | solution.py:127
  80.1 19.6 %collective-permute-done.2 = f32[256,1024]{1,0:T(8,128)} collective-permute-done((f32[256,1024]{1,0:T(8,128)S(1)}, f32[256,1024]{1,0:T(8,128)}, u32[]{:S(2)}, u32[]{:S(2)}) %collective-permute-start.2) | collective-permute-done | bytes 1048608 | tf_op jit(solution)/shard_map/ppermute | solution.py:132
  99.7 4.1 %fusion.4 = bf16[256,1024]{1,0:T(8,128)(2,1)S(1)} fusion(f32[256,1024]{1,0:T(8,128)} %collective-permute-done.2, f32[256,1024]{1,0:T(8,128)S(1)} %fusion.9, bf16[2048,1024]{1,0:T(8,128)(2,1)} %collective-permute-done.1, bf16[256,8192]{1,0:T(8,128)(2,1)} %copy-done.1, s32[]{:T(128)S(6)} %select_n.17), kind=kOutput, calls=%fused_computation.11 | convolution fusion | flops 1074528256 | bytes 7864324 | tf_op jit(solution)/shard_map/dot_general | solution.py:127
  103.8 0.4 convert_element_type.28
  104.1 0.4 copy.37
  104.5 5.7 %broadcast_in_dim.2 = bf16[256,2,4,8,128]{4,1,0,3,2:T(2,128)(2,1)} broadcast(bf16[256,2,4,128]{3,1,0,2:T(2,128)(2,1)S(1)} %copy.37), dimensions={0,1,2,4} | broadcast | bytes 4718592 | tf_op jit(solution)/shard_map/broadcast_in_dim | solution.py:137
  110.3 7.8 %all-to-all-start.1 = ((bf16[256,2,32,128]{3,1,0,2:T(2,128)(2,1)}), bf16[256,2,32,128]{3,1,0,2:T(2,128)(2,1)}, u32[]{:S(2)}, u32[]{:S(2)}) async-start(bf16[256,2,32,128]{3,1,0,2:T(2,128)(2,1)} %bitcast.35), calls=%async_computation.1 | async-start | bytes 8388608 | tf_op jit(solution)/shard_map/all_to_all | solution.py:139
  118.1 0.0 copy-done.4
  118.1 0.1 copy.34
  118.2 0.7 reshape_squeeze.3.lists_ref
  118.9 55.3 %all-to-all-done.1 = bf16[256,2,32,128]{3,1,0,2:T(2,128)(2,1)} async-done(((bf16[256,2,32,128]{3,1,0,2:T(2,128)(2,1)}), bf16[256,2,32,128]{3,1,0,2:T(2,128)(2,1)}, u32[]{:S(2)}, u32[]{:S(2)}) %all-to-all-start.1) | async-done | bytes 4194336 | tf_op jit(solution)/shard_map/all_to_all | solution.py:139
  174.2 2.7 %copy.45 = bf16[1024,8,2,128]{3,1,2,0:T(8,128)(2,1)S(1)} copy(bf16[1024,8,2,128]{3,2,1,0:T(2,128)(2,1)} %bitcast.21) | data formatting | bytes 8388608
  176.9 1.6 fusion.15
  178.5 3.0 %copy.38.kt_ref = bf16[128,8192]{1,0:T(8,128)(2,1)} copy(bf16[128,8192]{0,1:T(8,128)(2,1)S(1)} %get-tuple-element.10) | data formatting | bytes 4194304 | tf_op jit(solution)/shard_map/transpose | solution.py:142
  181.5 27.5 %shard_map.73 = bf16[32,128,128]{2,1,0:T(8,128)(2,1)} custom-call(s32[768]{0:T(1024)} %reshape_squeeze.3.lists_ref, s32[64]{0:T(128)} %bitcast.42, bf16[32,2,128,128]{3,2,1,0:T(8,128)(2,1)} %bitcast.33, bf16[128,8192]{1,0:T(8,128)(2,1)} %copy.38.kt_ref, bf16[8192,128]{1,0:T(8,128)(2,1)} %get-tuple-element.9.v_ref), custom_call_target="tpu_custom_call" | custom-call | tf_op jit(solution)/shard_map/pallas_call | solution.py:63
  209.0 5.8 %all-to-all-start.2 = ((bf16[32,128,128]{2,1,0:T(8,128)(2,1)}), bf16[32,128,128]{2,1,0:T(8,128)(2,1)S(1)}, u32[]{:S(2)}, u32[]{:S(2)}) async-start(bf16[32,128,128]{2,1,0:T(8,128)(2,1)} %shard_map.73), calls=%async_computation.2 | async-start | bytes 2097152 | tf_op jit(solution)/shard_map/all_to_all | solution.py:151
  214.8 27.5 %shard_map.74 = bf16[32,128,128]{2,1,0:T(8,128)(2,1)} custom-call(s32[768]{0:T(1024)} %reshape_squeeze.3.lists_ref, s32[64]{0:T(128)} %bitcast.43, bf16[32,2,128,128]{3,2,1,0:T(8,128)(2,1)} %bitcast.34, bf16[128,8192]{1,0:T(8,128)(2,1)} %copy.38.kt_ref, bf16[8192,128]{1,0:T(8,128)(2,1)} %get-tuple-element.9.v_ref), custom_call_target="tpu_custom_call" | custom-call | tf_op jit(solution)/shard_map/pallas_call | solution.py:63
  242.3 0.0 all-to-all-done.2
  242.3 8.3 %all-to-all-start.3 = ((bf16[32,128,128]{2,1,0:T(8,128)(2,1)}), bf16[32,128,128]{2,1,0:T(8,128)(2,1)S(1)}, u32[]{:S(2)}, u32[]{:S(2)}) async-start(bf16[32,128,128]{2,1,0:T(8,128)(2,1)} %shard_map.74), calls=%async_computation.3 | async-start | bytes 2097152 | tf_op jit(solution)/shard_map/all_to_all | solution.py:151
  250.6 0.7 copy.39
  251.3 14.2 %all-to-all-done.3 = bf16[32,128,128]{2,1,0:T(8,128)(2,1)S(1)} async-done(((bf16[32,128,128]{2,1,0:T(8,128)(2,1)}), bf16[32,128,128]{2,1,0:T(8,128)(2,1)S(1)}, u32[]{:S(2)}, u32[]{:S(2)}) %all-to-all-start.3) | async-done | bytes 1048608 | tf_op jit(solution)/shard_map/all_to_all | solution.py:151
  265.5 1.3 copy.41
  266.8 1.4 pad_maximum_fusion
  268.2 2.7 %copy.42 = bf16[2,128,4096]{2,1,0:T(8,128)(2,1)} copy(bf16[2,128,4096]{1,2,0:T(8,128)(2,1)S(1)} %pad_maximum_fusion) | data formatting | bytes 4194304 | tf_op jit(solution)/shard_map/stack | solution.py:155
  (3 shorter events, 0.0 us)
Async XLA Ops:
  0.0 3.2 %copy-start.2 = (bf16[2048,512]{1,0:T(8,128)(2,1)S(1)}, bf16[2048,512]{1,0:T(8,128)(2,1)}, u32[]{:S(2)}) copy-start(bf16[2048,512]{1,0:T(8,128)(2,1)} %param.11) | copy-start | bytes 6291460
  0.0 4.7 %copy-start.3 = (bf16[8192]{0:T(1024)(128)(2,1)S(1)}, bf16[8192]{0:T(1024)(128)(2,1)}, u32[]{:S(2)}) copy-start(bf16[8192]{0:T(1024)(128)(2,1)} %param.8) | copy-start | bytes 49156
  4.7 61.0 %collective-permute-start.1 = (bf16[2048,1024]{1,0:T(8,128)(2,1)}, bf16[2048,1024]{1,0:T(8,128)(2,1)}, u32[]{:S(2)}, u32[]{:S(2)}) collective-permute-start(bf16[2048,1024]{1,0:T(8,128)(2,1)} %constant_dynamic-update-slice_fusion), channel_id=1, source_target_pairs={{0,32},{32,0},{1,33},{33,1},{2,34},{34,2},{3,35},{35,3},{4,36},{36... | collective-permute-start | bytes 12582920 | tf_op jit(solution)/shard_map/ppermute | solution.py:122
  11.5 2.0 copy-start.1
  15.0 50.8 %collective-permute-start = (bf16[256,4096]{1,0:T(8,128)(2,1)}, bf16[256,4096]{1,0:T(8,128)(2,1)}, u32[]{:S(2)}, u32[]{:S(2)}) collective-permute-start(bf16[256,4096]{1,0:T(8,128)(2,1)} %constant_dynamic-slice_fusion), channel_id=1, source_target_pairs={{0,65},{1,64},{2,67},{3,66},{4,69},{5,68},{6,71},{7,70},{8,73},{9,... | collective-permute-start | bytes 6291464 | tf_op jit(solution)/shard_map/ppermute | solution.py:120
  25.3 36.1 %all-to-all-start = ((bf16[256,32,128]{2,0,1:T(8,128)(2,1)}), bf16[256,32,128]{2,0,1:T(8,128)(2,1)S(1)}, u32[]{:S(2)}, u32[]{:S(2)}) async-start(bf16[256,32,128]{2,0,1:T(8,128)(2,1)} %copy.36), calls=%async_computation | async-start | bytes 4194304 | tf_op jit(solution)/shard_map/all_to_all | solution.py:106
  61.4 12.0 %copy-start = (bf16[256,32,128]{2,0,1:T(8,128)(2,1)}, bf16[256,32,128]{2,0,1:T(8,128)(2,1)S(1)}, u32[]{:S(2)}) copy-start(bf16[256,32,128]{2,0,1:T(8,128)(2,1)S(1)} %all-to-all-done) | copy-start | bytes 6291460
  73.3 26.4 %collective-permute-start.2 = (f32[256,1024]{1,0:T(8,128)S(1)}, f32[256,1024]{1,0:T(8,128)}, u32[]{:S(2)}, u32[]{:S(2)}) collective-permute-start(f32[256,1024]{1,0:T(8,128)S(1)} %convolution_add_fusion), channel_id=1, source_target_pairs={{0,65},{1,64},{2,67},{3,66},{4,69},{5,68},{6,71},{7,70},{8,73},{9,... | collective-permute-start | bytes 3145736 | tf_op jit(solution)/shard_map/ppermute | solution.py:132
  110.3 7.8 %copy-start.4 = (s32[1,1,64,12]{2,1,3,0:T(1,128)S(1)}, s32[1,1,64,12]{2,1,3,0:T(1,128)}, u32[]{:S(2)}) copy-start(s32[1,1,64,12]{2,1,3,0:T(1,128)} %param.12) | copy-start | bytes 9220
  110.3 63.9 %all-to-all-start.1 = ((bf16[256,2,32,128]{3,1,0,2:T(2,128)(2,1)}), bf16[256,2,32,128]{3,1,0,2:T(2,128)(2,1)}, u32[]{:S(2)}, u32[]{:S(2)}) async-start(bf16[256,2,32,128]{3,1,0,2:T(2,128)(2,1)} %bitcast.35), calls=%async_computation.1 | async-start | bytes 8388608 | tf_op jit(solution)/shard_map/all_to_all | solution.py:139
  209.0 33.3 %all-to-all-start.2 = ((bf16[32,128,128]{2,1,0:T(8,128)(2,1)}), bf16[32,128,128]{2,1,0:T(8,128)(2,1)S(1)}, u32[]{:S(2)}, u32[]{:S(2)}) async-start(bf16[32,128,128]{2,1,0:T(8,128)(2,1)} %shard_map.73), calls=%async_computation.2 | async-start | bytes 2097152 | tf_op jit(solution)/shard_map/all_to_all | solution.py:151
  242.3 23.2 %all-to-all-start.3 = ((bf16[32,128,128]{2,1,0:T(8,128)(2,1)}), bf16[32,128,128]{2,1,0:T(8,128)(2,1)S(1)}, u32[]{:S(2)}, u32[]{:S(2)}) async-start(bf16[32,128,128]{2,1,0:T(8,128)(2,1)} %shard_map.74), calls=%async_computation.3 | async-start | bytes 2097152 | tf_op jit(solution)/shard_map/all_to_all | solution.py:151

commit v7 on v5

--- a/solution.py
+++ b/solution.py
@@ -38,20 +38,21 @@
         for scores in masked[1:]:
             peak = jnp.maximum(peak, scores)
         row_peak = jnp.max(peak, axis=1, keepdims=True)
-        denominator = jnp.zeros((BLK, 1), jnp.float32)
+        column_sums = jnp.zeros((BLK, BLK), jnp.float32)
         weighted = jnp.zeros((BLK, HD), jnp.float32)
         for slot in range(MAXB):
             start = pl.multiple_of(lists_ref[block * MAXB + slot] * BLK, BLK)
             value_tile = v_ref[pl.ds(start, BLK), :]
             exponent = jnp.exp(masked[slot] - row_peak)
-            denominator = denominator + jnp.sum(exponent, axis=1, keepdims=True)
+            column_sums = column_sums + exponent
             weighted = weighted + jnp.dot(
                 exponent.astype(jnp.bfloat16), value_tile, preferred_element_type=jnp.float32
             )
+        denominator = jnp.sum(column_sums, axis=1, keepdims=True)
         o_ref[pl.ds(first_row, BLK), :] = (weighted / denominator).astype(o_ref.dtype)
         return carry
 
-    lax.fori_loop(0, SUB_BLOCKS, one_block, 0)
+    lax.fori_loop(0, SUB_BLOCKS, one_block, 0, unroll=8)
 
 
 def attend(lists_flat, counts, head_queries, key_t, values):

time: 268 us -> 243 us (0.907)
  Pallas kernels: 51.2 us -> 26.2 us
    pallas_call x1, Pallas kernels: 51.2 us -> 26.2 us  [attend(): pl.pallas_call(attend_kernel, out_shape=jax.ShapeDtypeStruct((sequence_ro...]
where the time goes in v7:
time: 243 us; the launch traced here: 242 us
  waiting for transfers between devices  112 us (46%)
  blocking collectives  32.5 us (13%)
  local copies, waits for them, and re-layouts  27.1 us (11%)
  Pallas kernels  26.2 us (11%)
  starting transfers between devices  22.3 us (9%)
  matrix products  15.4 us (6%)
  other arithmetic  6.73 us (3%)
    all_to_all x1, waiting for transfers between devices, on_device(): lax.all_to_all(widened, CTX_AXES, split_axis=2, concat_axis=0, tiled=True)  55.5 us
    all_to_all x1, blocking collectives, on_device(): lax.all_to_all(attended_head, CTX_AXES, split_axis=0, concat_axis=1, tile...  32.5 us
    all_to_all x1, waiting for transfers between devices, on_device(): lax.all_to_all(queries[0], CTX_AXES, split_axis=1, concat_axis=0, tiled=T...  28.8 us
    pallas_call x1, Pallas kernels, attend(): pl.pallas_call(attend_kernel, out_shape=jax.ShapeDtypeStruct((sequence_ro...  26.2 us
    ppermute x1, waiting for transfers between devices, on_device(): from_partner = lax.ppermute(for_partner, ALL_AXES, partner_pairs)  19.6 us
    ppermute x1, waiting for transfers between devices, on_device(): partner_rows = lax.ppermute(far_features, ALL_AXES, partner_pairs)  7.89 us
    dot_general x2, matrix products, half_sum(): jnp.dot(other, sibling, preferred_element_type=jnp.float32)  7.81 us
    all_to_all x1, starting transfers between devices, on_device(): lax.all_to_all(widened, CTX_AXES, split_axis=2, concat_axis=0, tiled=True)  7.76 us
  transfers between devices with their start and end apart: 5, of which 4 were waited for; matrix products, arithmetic and copies ran while one was open for 6% of the time, Pallas kernels for 0%

profile of v7, /device:TPU:0, one launch (start us, length us, event | category | flops | bytes accessed | tf_op | source)
XLA Modules:
  0.0 242.0 jit_solution(16125490925232776829)
XLA Ops:
  0.0 0.0 copy-start.2
  0.0 0.0 copy-start.4
  0.0 3.2 %constant_dynamic-update-slice_fusion.1 = bf16[2048,1024]{1,0:T(8,128)(2,1)} fusion(bf16[2048,512]{1,0:T(8,128)(2,1)} %param.10), kind=kLoop, calls=%fused_computation.18 | loop fusion | bytes 4194304
  3.2 0.0 copy-done.2
  3.2 1.5 constant_dynamic-update-slice_fusion
  4.7 0.0 collective-permute-start.1
  4.7 0.0 copy-done.4
  4.7 3.1 %fusion = f32[256]{0:T(256)S(1)} fusion(bf16[1,256,8192]{2,1,0:T(8,128)(2,1)} %param.7), kind=kLoop, calls=%fused_computation.2 | loop fusion | flops 6291200 | bytes 4195328 | tf_op jit(solution)/shard_map/reduce_sum | solution.py:105
  7.9 3.6 %fusion.2 = bf16[256,8192]{1,0:T(8,128)(2,1)S(1)} fusion(bf16[1,256,8192]{2,1,0:T(8,128)(2,1)} %param.7, f32[8192]{0:T(1024)S(1)} %convert_element_type.25, f32[256]{0:T(256)S(1)} %add_rsqrt_fusion), kind=kLoop, calls=%fused_computation.4 | loop fusion | flops 8388608 | bytes 8422400 | tf_op jit(solution)/shard_map/convert_element_type | solution.py:106
  11.5 0.0 copy-start
  11.5 0.0 copy-start.3
  11.5 1.6 constant_dynamic-slice_fusion
  13.1 4.1 %collective-permute-start = (bf16[256,4096]{1,0:T(8,128)(2,1)}, bf16[256,4096]{1,0:T(8,128)(2,1)}, u32[]{:S(2)}, u32[]{:S(2)}) collective-permute-start(bf16[256,4096]{1,0:T(8,128)(2,1)} %constant_dynamic-slice_fusion), channel_id=1, source_target_pairs={{0,65},{1,64},{2,67},{3,66},{4,69},{5,68},{6,71},{7,70},{8,73},{9,... | collective-permute-start | bytes 6291464 | tf_op jit(solution)/shard_map/ppermute | solution.py:117
  17.2 0.0 copy-done.3
  17.2 0.5 copy.17
  17.7 0.0 copy-done
  17.7 2.1 copy.13
  19.8 7.3 %all-to-all-start = ((bf16[256,32,128]{2,0,1:T(8,128)(2,1)}), bf16[256,32,128]{2,0,1:T(8,128)(2,1)S(1)}, u32[]{:S(2)}, u32[]{:S(2)}) async-start(bf16[256,32,128]{2,0,1:T(8,128)(2,1)} %copy.13), calls=%async_computation | async-start | bytes 4194304 | tf_op jit(solution)/shard_map/all_to_all | solution.py:103
  27.2 28.8 %all-to-all-done = bf16[256,32,128]{2,0,1:T(8,128)(2,1)S(1)} async-done(((bf16[256,32,128]{2,0,1:T(8,128)(2,1)}), bf16[256,32,128]{2,0,1:T(8,128)(2,1)S(1)}, u32[]{:S(2)}, u32[]{:S(2)}) %all-to-all-start) | async-done | bytes 2097184 | tf_op jit(solution)/shard_map/all_to_all | solution.py:103
  55.9 0.0 copy-start.1
  55.9 7.9 %collective-permute-done = bf16[256,4096]{1,0:T(8,128)(2,1)} collective-permute-done((bf16[256,4096]{1,0:T(8,128)(2,1)}, bf16[256,4096]{1,0:T(8,128)(2,1)}, u32[]{:S(2)}, u32[]{:S(2)}) %collective-permute-start) | collective-permute-done | bytes 2097184 | tf_op jit(solution)/shard_map/ppermute | solution.py:117
  63.8 0.0 collective-permute-done.1
  63.8 3.8 %fusion.5 = f32[256,1024]{1,0:T(8,128)S(1)} fusion(bf16[2048,1024]{1,0:T(8,128)(2,1)} %collective-permute-done.1, bf16[256,4096]{1,0:T(8,128)(2,1)} %collective-permute-done, s32[]{:T(128)S(6)} %select_n.19), kind=kOutput, calls=%fused_computation.11 | convolution fusion | flops 1073741824 | bytes 6291460 | tf_op jit(solution)/shard_map/dot_general | solution.py:124
  67.6 3.8 %convolution_add_fusion = f32[256,1024]{1,0:T(8,128)S(1)} fusion(f32[256,1024]{1,0:T(8,128)S(1)} %fusion.5, bf16[2048,1024]{1,0:T(8,128)(2,1)} %constant_dynamic-update-slice_fusion, bf16[256,4096]{1,0:T(8,128)(2,1)} %collective-permute-done, s32[]{:T(128)S(6)} %select_n.18), kind=kOutput, calls=%fused_computation.7 | convolution fusion | flops 1074003968 | bytes 7340036 | tf_op jit(solution)/shard_map/dot_general | solution.py:124
  71.4 0.0 copy-done.1
  71.4 3.0 %collective-permute-start.2 = (f32[256,1024]{1,0:T(8,128)S(1)}, f32[256,1024]{1,0:T(8,128)}, u32[]{:S(2)}, u32[]{:S(2)}) collective-permute-start(f32[256,1024]{1,0:T(8,128)S(1)} %convolution_add_fusion), channel_id=1, source_target_pairs={{0,65},{1,64},{2,67},{3,66},{4,69},{5,68},{6,71},{7,70},{8,73},{9,... | collective-permute-start | bytes 3145736 | tf_op jit(solution)/shard_map/ppermute | solution.py:129
  74.4 3.8 %fusion.9 = f32[256,1024]{1,0:T(8,128)S(1)} fusion(bf16[2048,1024]{1,0:T(8,128)(2,1)} %constant_dynamic-update-slice_fusion, bf16[256,8192]{1,0:T(8,128)(2,1)} %copy-done, s32[]{:T(128)S(6)} %select_n.16), kind=kOutput, calls=%fused_computation.15 | convolution fusion | flops 1073741824 | bytes 6291460 | tf_op jit(solution)/shard_map/dot_general | solution.py:124
  78.2 19.6 %collective-permute-done.2 = f32[256,1024]{1,0:T(8,128)} collective-permute-done((f32[256,1024]{1,0:T(8,128)S(1)}, f32[256,1024]{1,0:T(8,128)}, u32[]{:S(2)}, u32[]{:S(2)}) %collective-permute-start.2) | collective-permute-done | bytes 1048608 | tf_op jit(solution)/shard_map/ppermute | solution.py:129
  97.8 4.1 %fusion.4 = bf16[256,1024]{1,0:T(8,128)(2,1)S(1)} fusion(f32[256,1024]{1,0:T(8,128)} %collective-permute-done.2, f32[256,1024]{1,0:T(8,128)S(1)} %fusion.9, bf16[2048,1024]{1,0:T(8,128)(2,1)} %collective-permute-done.1, bf16[256,8192]{1,0:T(8,128)(2,1)} %copy-done, s32[]{:T(128)S(6)} %select_n.17), kind=kOutput, calls=%fused_computation.10 | convolution fusion | flops 1074528256 | bytes 7864324 | tf_op jit(solution)/shard_map/dot_general | solution.py:124
  101.8 0.4 convert_element_type.28
  102.2 0.4 copy.14
  102.6 5.7 %broadcast_in_dim.4 = bf16[256,2,4,8,128]{4,1,0,3,2:T(2,128)(2,1)} broadcast(bf16[256,2,4,128]{3,1,0,2:T(2,128)(2,1)S(1)} %copy.14), dimensions={0,1,2,4} | broadcast | bytes 4718592 | tf_op jit(solution)/shard_map/broadcast_in_dim | solution.py:134
  108.4 0.0 copy-start.5
  108.4 7.8 %all-to-all-start.1 = ((bf16[256,2,32,128]{3,1,0,2:T(2,128)(2,1)}), bf16[256,2,32,128]{3,1,0,2:T(2,128)(2,1)}, u32[]{:S(2)}, u32[]{:S(2)}) async-start(bf16[256,2,32,128]{3,1,0,2:T(2,128)(2,1)} %bitcast.31), calls=%async_computation.1 | async-start | bytes 8388608 | tf_op jit(solution)/shard_map/all_to_all | solution.py:136
  116.1 0.0 copy-done.5
  116.1 0.1 copy.12
  116.2 0.7 reshape_squeeze.3.lists_ref
  116.9 55.5 %all-to-all-done.1 = bf16[256,2,32,128]{3,1,0,2:T(2,128)(2,1)} async-done(((bf16[256,2,32,128]{3,1,0,2:T(2,128)(2,1)}), bf16[256,2,32,128]{3,1,0,2:T(2,128)(2,1)}, u32[]{:S(2)}, u32[]{:S(2)}) %all-to-all-start.1) | async-done | bytes 4194336 | tf_op jit(solution)/shard_map/all_to_all | solution.py:136
  172.4 2.7 %copy.20 = bf16[1024,8,2,128]{3,1,2,0:T(8,128)(2,1)S(1)} copy(bf16[1024,8,2,128]{3,2,1,0:T(2,128)(2,1)} %bitcast.19) | data formatting | bytes 8388608
  175.2 1.6 fusion.15
  176.8 2.9 %copy.15.kt_ref = bf16[128,8192]{1,0:T(8,128)(2,1)} copy(bf16[128,8192]{0,1:T(8,128)(2,1)S(1)} %get-tuple-element.10) | data formatting | bytes 4194304 | tf_op jit(solution)/shard_map/transpose | solution.py:139
  179.7 26.2 %shard_map.73 = bf16[8192,128]{1,0:T(8,128)(2,1)} custom-call(s32[768]{0:T(1024)} %reshape_squeeze.3.lists_ref, s32[64]{0:T(128)} %bitcast.38, bf16[8192,128]{1,0:T(8,128)(2,1)} %bitcast.35, bf16[128,8192]{1,0:T(8,128)(2,1)} %copy.15.kt_ref, bf16[8192,128]{1,0:T(8,128)(2,1)} %get-tuple-element.9.v_ref), custom_call_target="tpu_custom_call" | custom-call | tf_op jit(solution)/shard_map/pallas_call | solution.py:62
  205.9 32.5 %all_to_all.50 = bf16[32,256,128]{2,1,0:T(8,128)(2,1)S(1)} all-to-all(bf16[32,256,128]{2,1,0:T(8,128)(2,1)} %bitcast.36), channel_id=1, replica_groups=mesh['zh'=2,'core'=2,'x'=4,'y'=4,'zl'=2] {'x','y','zl'}, dimensions={0} | all-to-all | bytes 4194304 | tf_op jit(solution)/shard_map/all_to_all | solution.py:144
  238.4 1.4 copy.16
  239.7 2.3 broadcast_in_dim.5
  (2 shorter events, 0.0 us)
Async XLA Ops:
  0.0 3.2 %copy-start.2 = (bf16[2048,512]{1,0:T(8,128)(2,1)S(1)}, bf16[2048,512]{1,0:T(8,128)(2,1)}, u32[]{:S(2)}) copy-start(bf16[2048,512]{1,0:T(8,128)(2,1)} %param.11) | copy-start | bytes 6291460
  0.0 4.7 %copy-start.4 = (bf16[8192]{0:T(1024)(128)(2,1)S(1)}, bf16[8192]{0:T(1024)(128)(2,1)}, u32[]{:S(2)}) copy-start(bf16[8192]{0:T(1024)(128)(2,1)} %param.8) | copy-start | bytes 49156
  4.7 59.1 %collective-permute-start.1 = (bf16[2048,1024]{1,0:T(8,128)(2,1)}, bf16[2048,1024]{1,0:T(8,128)(2,1)}, u32[]{:S(2)}, u32[]{:S(2)}) collective-permute-start(bf16[2048,1024]{1,0:T(8,128)(2,1)} %constant_dynamic-update-slice_fusion), channel_id=1, source_target_pairs={{0,32},{32,0},{1,33},{33,1},{2,34},{34,2},{3,35},{35,3},{4,36},{36... | collective-permute-start | bytes 12582920 | tf_op jit(solution)/shard_map/ppermute | solution.py:119
  11.5 6.2 %copy-start = (bf16[256,8192]{1,0:T(8,128)(2,1)}, bf16[256,8192]{1,0:T(8,128)(2,1)S(1)}, u32[]{:S(2)}) copy-start(bf16[256,8192]{1,0:T(8,128)(2,1)S(1)} %fusion.2) | copy-start | bytes 12582916
  11.5 5.7 %copy-start.3 = (bf16[1,256,4096]{2,1,0:T(8,128)(2,1)S(1)}, bf16[1,256,4096]{2,1,0:T(8,128)(2,1)}, u32[]{:S(2)}) copy-start(bf16[1,256,4096]{2,1,0:T(8,128)(2,1)} %param.9) | copy-start | bytes 6291460
  13.1 50.8 %collective-permute-start = (bf16[256,4096]{1,0:T(8,128)(2,1)}, bf16[256,4096]{1,0:T(8,128)(2,1)}, u32[]{:S(2)}, u32[]{:S(2)}) collective-permute-start(bf16[256,4096]{1,0:T(8,128)(2,1)} %constant_dynamic-slice_fusion), channel_id=1, source_target_pairs={{0,65},{1,64},{2,67},{3,66},{4,69},{5,68},{6,71},{7,70},{8,73},{9,... | collective-permute-start | bytes 6291464 | tf_op jit(solution)/shard_map/ppermute | solution.py:117
  19.8 36.1 %all-to-all-start = ((bf16[256,32,128]{2,0,1:T(8,128)(2,1)}), bf16[256,32,128]{2,0,1:T(8,128)(2,1)S(1)}, u32[]{:S(2)}, u32[]{:S(2)}) async-start(bf16[256,32,128]{2,0,1:T(8,128)(2,1)} %copy.13), calls=%async_computation | async-start | bytes 4194304 | tf_op jit(solution)/shard_map/all_to_all | solution.py:103
  55.9 15.5 %copy-start.1 = (bf16[256,32,128]{2,0,1:T(8,128)(2,1)}, bf16[256,32,128]{2,0,1:T(8,128)(2,1)S(1)}, u32[]{:S(2)}) copy-start(bf16[256,32,128]{2,0,1:T(8,128)(2,1)S(1)} %all-to-all-done) | copy-start | bytes 6291460
  71.4 26.4 %collective-permute-start.2 = (f32[256,1024]{1,0:T(8,128)S(1)}, f32[256,1024]{1,0:T(8,128)}, u32[]{:S(2)}, u32[]{:S(2)}) collective-permute-start(f32[256,1024]{1,0:T(8,128)S(1)} %convolution_add_fusion), channel_id=1, source_target_pairs={{0,65},{1,64},{2,67},{3,66},{4,69},{5,68},{6,71},{7,70},{8,73},{9,... | collective-permute-start | bytes 3145736 | tf_op jit(solution)/shard_map/ppermute | solution.py:129
  108.4 7.8 %copy-start.5 = (s32[1,1,64,12]{2,1,3,0:T(1,128)S(1)}, s32[1,1,64,12]{2,1,3,0:T(1,128)}, u32[]{:S(2)}) copy-start(s32[1,1,64,12]{2,1,3,0:T(1,128)} %param.12) | copy-start | bytes 9220
  108.4 64.1 %all-to-all-start.1 = ((bf16[256,2,32,128]{3,1,0,2:T(2,128)(2,1)}), bf16[256,2,32,128]{3,1,0,2:T(2,128)(2,1)}, u32[]{:S(2)}, u32[]{:S(2)}) async-start(bf16[256,2,32,128]{3,1,0,2:T(2,128)(2,1)} %bitcast.31), calls=%async_computation.1 | async-start | bytes 8388608 | tf_op jit(solution)/shard_map/all_to_all | solution.py:136

commit v8 on v7

--- a/solution.py
+++ b/solution.py
@@ -12,6 +12,7 @@
 
 
 SUB_BLOCKS = 8
+CHUNKS = 2
 
 
 def attend_kernel(lists_ref, counts_ref, q_ref, kt_ref, v_ref, o_ref):
@@ -113,9 +114,6 @@
     zh = lax.axis_index("zh")
     core = lax.axis_index("core")
     partner_pairs = cross_half_pairs(False)
-    far_features = lax.dynamic_slice_in_dim(normed, (1 - zh) * half_features, half_features, axis=1)
-    partner_rows = lax.ppermute(far_features, ALL_AXES, partner_pairs)
-    head_queries, partner_rows = lax.optimization_barrier((head_queries, partner_rows))
     sibling = lax.ppermute(local_weight, "core", [(0, 1), (1, 0)])
 
     def half_sum(rows, offset):
@@ -125,20 +123,29 @@
             other, sibling, preferred_element_type=jnp.float32
         )
 
-    for_partner = half_sum(partner_rows, 0)
-    from_partner = lax.ppermute(for_partner, ALL_AXES, partner_pairs)
-    summed = half_sum(normed, zh * half_features) + from_partner
-    paired = summed.reshape(local_rows, 2, KVH, 1, HD).astype(jnp.bfloat16)
     ctx_size = lax.axis_size(CTX_AXES)
     copies_per_head = ctx_size // KVH
-    widened = jnp.broadcast_to(paired, (local_rows, 2, KVH, copies_per_head, HD))
-    widened = widened.reshape(local_rows, 2, ctx_size, HD)
-    head_pair = lax.all_to_all(widened, CTX_AXES, split_axis=2, concat_axis=0, tiled=True)
+    chunk_rows = local_rows // CHUNKS
+    kv_chunks = []
+    for chunk in range(CHUNKS):
+        rows = normed[chunk * chunk_rows : (chunk + 1) * chunk_rows]
+        far_features = lax.dynamic_slice_in_dim(rows, (1 - zh) * half_features, half_features, axis=1)
+        partner_rows = lax.ppermute(far_features, ALL_AXES, partner_pairs)
+        if chunk == 0:
+            head_queries, partner_rows = lax.optimization_barrier((head_queries, partner_rows))
+        from_partner = lax.ppermute(half_sum(partner_rows, 0), ALL_AXES, partner_pairs)
+        summed = half_sum(rows, zh * half_features) + from_partner
+        paired = summed.reshape(chunk_rows, 2, KVH, 1, HD).astype(jnp.bfloat16)
+        widened = jnp.broadcast_to(paired, (chunk_rows, 2, KVH, copies_per_head, HD))
+        widened = widened.reshape(chunk_rows, 2, ctx_size, HD)
+        kv_chunks.append(lax.all_to_all(widened, CTX_AXES, split_axis=2, concat_axis=0, tiled=True))
+    head_pair = jnp.concatenate(kv_chunks, axis=0)
     sequence_rows = head_queries.shape[0]
     kv_rows = head_pair.reshape(sequence_rows, 2 * HD)
     key_t = kv_rows[:, :HD].T
     values = kv_rows[:, HD:]
-    lists_flat = block_lists[0, 0].reshape(-1)
+    lists = block_lists[0, 0]
+    lists_flat = ((lists % CHUNKS) * ctx_size + lists // CHUNKS).reshape(-1)
     counts = block_counts[0, 0]
     attended_head = attend(lists_flat, counts, head_queries, key_t, values)
     restored = lax.all_to_all(attended_head, CTX_AXES, split_axis=0, concat_axis=1, tiled=True)

time: 243 us -> 230 us (0.947)
  waiting for transfers between devices: 112 us -> 71.8 us
  starting transfers between devices: 22.3 us -> 33.3 us
  matrix products: 15.4 us -> 26.3 us
  local copies, waits for them, and re-layouts: 27.1 us -> 34.2 us
    all_to_all x1 -> x2, waiting for transfers between devices: 55.5 us -> 23.7 us  [on_device(): lax.all_to_all(widened, CTX_AXES, split_axis=2, concat_axis=0, tiled=True)]
    all_to_all x1, waiting for transfers between devices: 28.8 us -> 0.01 us  [on_device(): lax.all_to_all(queries[0], CTX_AXES, split_axis=1, concat_axis=0, tiled=T...]
    ppermute x1 -> x2, waiting for transfers between devices: 7.89 us -> 30.3 us  [on_device(): partner_rows = lax.ppermute(far_features, ALL_AXES, partner_pairs)]
    all_to_all x1 -> x2, starting transfers between devices: 7.76 us -> 14.2 us  [on_device(): lax.all_to_all(widened, CTX_AXES, split_axis=2, concat_axis=0, tiled=True)]
    dot_general x2 -> x4, matrix products: 7.54 us -> 13.3 us  [half_sum(): jnp.dot(own, local_weight, preferred_element_type=jnp.float32)]
    dot_general x2 -> x4, matrix products: 7.81 us -> 13.1 us  [half_sum(): jnp.dot(other, sibling, preferred_element_type=jnp.float32)]
    concatenate x0 -> x1, local copies, waits for them, and re-layouts: none -> 3.24 us  [on_device(): head_pair = jnp.concatenate(kv_chunks, axis=0)]
    ppermute x1 -> x2, starting transfers between devices: 3.03 us -> 5.88 us  [on_device(): lax.ppermute(half_sum(partner_rows, 0), ALL_AXES, partner_pairs)]
  transfers between devices with their start and end apart: 5 -> 8, of which waited for: 4 -> 5; matrix products, arithmetic and copies ran while one was open for 6% -> 16% of each run, Pallas kernels for 0% -> 0%
where the time goes in v8:
time: 230 us; the launch traced here: 229 us
  waiting for transfers between devices  71.8 us (31%)
  local copies, waits for them, and re-layouts  34.2 us (15%)
  starting transfers between devices  33.3 us (14%)
  blocking collectives  32.3 us (14%)
  matrix products  26.3 us (11%)
  Pallas kernels  26 us (11%)
  other arithmetic  5.06 us (2%)
    all_to_all x1, blocking collectives, on_device(): lax.all_to_all(attended_head, CTX_AXES, split_axis=0, concat_axis=1, tile...  32.3 us
    ppermute x2, waiting for transfers between devices, on_device(): partner_rows = lax.ppermute(far_features, ALL_AXES, partner_pairs)  30.3 us
    pallas_call x1, Pallas kernels, attend(): pl.pallas_call(attend_kernel, out_shape=jax.ShapeDtypeStruct((sequence_ro...  26 us
    all_to_all x2, waiting for transfers between devices, on_device(): lax.all_to_all(widened, CTX_AXES, split_axis=2, concat_axis=0, tiled=True)  23.7 us
    ppermute x2, waiting for transfers between devices, on_device(): lax.ppermute(half_sum(partner_rows, 0), ALL_AXES, partner_pairs)  17.8 us
    all_to_all x2, starting transfers between devices, on_device(): lax.all_to_all(widened, CTX_AXES, split_axis=2, concat_axis=0, tiled=True)  14.2 us
    dot_general x4, matrix products, half_sum(): jnp.dot(own, local_weight, preferred_element_type=jnp.float32)  13.3 us
    dot_general x4, matrix products, half_sum(): jnp.dot(other, sibling, preferred_element_type=jnp.float32)  13.1 us
  transfers between devices with their start and end apart: 8, of which 5 were waited for; matrix products, arithmetic and copies ran while one was open for 16% of the time, Pallas kernels for 0%

profile of v8, /device:TPU:0, one launch (start us, length us, event | category | flops | bytes accessed | tf_op | source)
XLA Modules:
  0.0 229.2 jit_solution(5349729580468141204)
XLA Ops:
  0.0 3.3 %constant_dynamic-update-slice_fusion.1 = bf16[2048,1024]{1,0:T(8,128)(2,1)} fusion(bf16[2048,512]{1,0:T(8,128)(2,1)} %param.10), kind=kLoop, calls=%fused_computation.29 | loop fusion | bytes 4194304
  3.3 1.5 constant_dynamic-update-slice_fusion
  4.8 0.5 copy.19
  5.3 0.0 copy-start.6
  5.3 2.1 copy.14
  7.4 8.8 %all-to-all-start = ((bf16[256,32,128]{2,0,1:T(8,128)(2,1)}), bf16[256,32,128]{2,0,1:T(8,128)(2,1)S(1)}, u32[]{:S(2)}, u32[]{:S(2)}) async-start(bf16[256,32,128]{2,0,1:T(8,128)(2,1)} %copy.14), calls=%async_computation | async-start | bytes 4194304 | tf_op jit(solution)/shard_map/all_to_all | solution.py:104
  16.3 3.3 %fusion = f32[256]{0:T(256)S(1)} fusion(bf16[1,256,8192]{2,1,0:T(8,128)(2,1)} %param.7), kind=kLoop, calls=%fused_computation.2 | loop fusion | flops 6291200 | bytes 4195328 | tf_op jit(solution)/shard_map/reduce_sum | solution.py:106
  19.5 0.2 copy-done
  19.7 1.2 fusion.2
  20.9 2.4 %fusion.34 = (bf16[128,8192]{1,0:T(8,128)(2,1)}, bf16[128,8192]{1,0:T(8,128)(2,1)}) fusion(bf16[256,8192]{1,0:T(8,128)(2,1)S(1)} %fusion.2), kind=kLoop, calls=%fused_computation.54 | loop fusion | bytes 8388608 | tf_op jit(solution)/shard_map/slice | solution.py:131
  23.3 1.3 constant_dynamic-slice_fusion.1
  24.6 4.0 %collective-permute-start = (bf16[128,4096]{1,0:T(8,128)(2,1)S(1)}, bf16[128,4096]{1,0:T(8,128)(2,1)}, u32[]{:S(2)}, u32[]{:S(2)}) collective-permute-start(bf16[128,4096]{1,0:T(8,128)(2,1)S(1)} %constant_dynamic-slice_fusion.1), channel_id=1, source_target_pairs={{0,65},{1,64},{2,67},{3,66},{4,69},{5,68},{6,71},{7,70},{8,73},{9,... | collective-permute-start | bytes 3145736 | tf_op jit(solution)/shard_map/ppermute | solution.py:133
  28.6 23.4 %collective-permute-done = bf16[128,4096]{1,0:T(8,128)(2,1)} collective-permute-done((bf16[128,4096]{1,0:T(8,128)(2,1)S(1)}, bf16[128,4096]{1,0:T(8,128)(2,1)}, u32[]{:S(2)}, u32[]{:S(2)}) %collective-permute-start) | collective-permute-done | bytes 1048608 | tf_op jit(solution)/shard_map/ppermute | solution.py:133
  52.0 3.8 %fusion.13 = f32[128,1024]{1,0:T(8,128)S(1)} fusion(bf16[2048,1024]{1,0:T(8,128)(2,1)} %collective-permute-done.1, bf16[128,4096]{1,0:T(8,128)(2,1)} %collective-permute-done, s32[]{:T(128)S(6)} %select_n.40), kind=kOutput, calls=%fused_computation.22 | convolution fusion | flops 536870912 | bytes 5242884 | tf_op jit(solution)/shard_map/dot_general | solution.py:122
  55.8 4.1 %convolution_add_fusion.2 = f32[128,1024]{1,0:T(8,128)} fusion(f32[128,1024]{1,0:T(8,128)S(1)} %fusion.13, bf16[2048,1024]{1,0:T(8,128)(2,1)} %constant_dynamic-update-slice_fusion, bf16[128,4096]{1,0:T(8,128)(2,1)} %collective-permute-done, s32[]{:T(128)S(6)} %select_n.39), kind=kOutput, calls=%fused_computation.10 | convolution fusion | flops 537001984 | bytes 5767172 | tf_op jit(solution)/shard_map/dot_general | solution.py:122
  59.9 2.9 %collective-permute-start.2 = (f32[128,1024]{1,0:T(8,128)}, f32[128,1024]{1,0:T(8,128)}, u32[]{:S(2)}, u32[]{:S(2)}) collective-permute-start(f32[128,1024]{1,0:T(8,128)} %convolution_add_fusion.2), channel_id=1, source_target_pairs={{0,65},{1,64},{2,67},{3,66},{4,69},{5,68},{6,71},{7,70},{8,73},{9,... | collective-permute-start | bytes 1572872 | tf_op jit(solution)/shard_map/ppermute | solution.py:136
  62.8 0.1 constant_dynamic-slice_fusion
  62.9 0.4 collective-permute-start.3
  63.3 3.1 %fusion.17 = f32[128,1024]{1,0:T(8,128)S(1)} fusion(bf16[2048,1024]{1,0:T(8,128)(2,1)} %constant_dynamic-update-slice_fusion, bf16[128,8192]{1,0:T(8,128)(2,1)} %get-tuple-element.12, s32[]{:T(128)S(6)} %select_n.37), kind=kOutput, calls=%fused_computation.26 | convolution fusion | flops 536870912 | bytes 5242884 | tf_op jit(solution)/shard_map/dot_general | solution.py:122
  66.3 9.9 %collective-permute-done.2 = f32[128,1024]{1,0:T(8,128)} collective-permute-done((f32[128,1024]{1,0:T(8,128)}, f32[128,1024]{1,0:T(8,128)}, u32[]{:S(2)}, u32[]{:S(2)}) %collective-permute-start.2) | collective-permute-done | bytes 524320 | tf_op jit(solution)/shard_map/ppermute | solution.py:136
  76.2 3.2 %fusion.6 = bf16[128,1024]{1,0:T(8,128)(2,1)S(1)} fusion(f32[128,1024]{1,0:T(8,128)} %collective-permute-done.2, f32[128,1024]{1,0:T(8,128)S(1)} %fusion.17, bf16[2048,1024]{1,0:T(8,128)(2,1)} %collective-permute-done.1, bf16[128,8192]{1,0:T(8,128)(2,1)} %get-tuple-element.12, s32[]{:T(128)S(6)} %select_n.38), kind=kOutput, calls=%fused_computation.15 | convolution fusion | flops 537264128 | bytes 6029316 | tf_op jit(solution)/shard_map/dot_general | solution.py:122
  79.4 0.2 convert_element_type.39
  79.6 0.2 copy.15
  79.8 3.2 %broadcast_in_dim.6 = bf16[128,2,4,8,128]{4,1,0,3,2:T(2,128)(2,1)} broadcast(bf16[128,2,4,128]{3,1,0,2:T(2,128)(2,1)S(1)} %copy.15), dimensions={0,1,2,4} | broadcast | bytes 2359296 | tf_op jit(solution)/shard_map/broadcast_in_dim | solution.py:139
  83.0 7.1 %all-to-all-start.1 = ((bf16[128,2,32,128]{3,1,0,2:T(2,128)(2,1)}), bf16[128,2,32,128]{3,1,0,2:T(2,128)(2,1)S(1)}, u32[]{:S(2)}, u32[]{:S(2)}) async-start(bf16[128,2,32,128]{3,1,0,2:T(2,128)(2,1)} %bitcast.44), calls=%async_computation.1 | async-start | bytes 4194304 | tf_op jit(solution)/shard_map/all_to_all | solution.py:141
  90.1 7.0 %collective-permute-done.3 = bf16[128,4096]{1,0:T(8,128)(2,1)} collective-permute-done((bf16[128,4096]{1,0:T(8,128)(2,1)S(1)}, bf16[128,4096]{1,0:T(8,128)(2,1)}, u32[]{:S(2)}, u32[]{:S(2)}) %collective-permute-start.3) | collective-permute-done | bytes 1048608 | tf_op jit(solution)/shard_map/ppermute | solution.py:133
  97.1 3.1 %fusion.7 = f32[128,1024]{1,0:T(8,128)S(1)} fusion(bf16[2048,1024]{1,0:T(8,128)(2,1)} %collective-permute-done.1, bf16[128,4096]{1,0:T(8,128)(2,1)} %collective-permute-done.3, s32[]{:T(128)S(6)} %select_n.40), kind=kOutput, calls=%fused_computation.16 | convolution fusion | flops 536870912 | bytes 5242884 | tf_op jit(solution)/shard_map/dot_general | solution.py:122
  100.1 3.2 %convolution_add_fusion = f32[128,1024]{1,0:T(8,128)S(1)} fusion(f32[128,1024]{1,0:T(8,128)S(1)} %fusion.7, bf16[2048,1024]{1,0:T(8,128)(2,1)} %constant_dynamic-update-slice_fusion, bf16[128,4096]{1,0:T(8,128)(2,1)} %collective-permute-done.3, s32[]{:T(128)S(6)} %select_n.39), kind=kOutput, calls=%fused_computation.8 | convolution fusion | flops 537001984 | bytes 5767172 | tf_op jit(solution)/shard_map/dot_general | solution.py:122
  103.4 2.9 %collective-permute-start.4 = (f32[128,1024]{1,0:T(8,128)S(1)}, f32[128,1024]{1,0:T(8,128)S(1)}, u32[]{:S(2)}, u32[]{:S(2)}) collective-permute-start(f32[128,1024]{1,0:T(8,128)S(1)} %convolution_add_fusion), channel_id=1, source_target_pairs={{0,65},{1,64},{2,67},{3,66},{4,69},{5,68},{6,71},{7,70},{8,73},{9,... | collective-permute-start | bytes 1572872 | tf_op jit(solution)/shard_map/ppermute | solution.py:136
  106.3 2.9 %fusion.11 = f32[128,1024]{1,0:T(8,128)S(1)} fusion(bf16[2048,1024]{1,0:T(8,128)(2,1)} %constant_dynamic-update-slice_fusion, bf16[128,8192]{1,0:T(8,128)(2,1)S(1)} %copy-done.3, s32[]{:T(128)S(6)} %select_n.37), kind=kOutput, calls=%fused_computation.20 | convolution fusion | flops 536870912 | bytes 5242884 | tf_op jit(solution)/shard_map/dot_general | solution.py:122
  109.2 8.0 %collective-permute-done.4 = f32[128,1024]{1,0:T(8,128)S(1)} collective-permute-done((f32[128,1024]{1,0:T(8,128)S(1)}, f32[128,1024]{1,0:T(8,128)S(1)}, u32[]{:S(2)}, u32[]{:S(2)}) %collective-permute-start.4) | collective-permute-done | bytes 524320 | tf_op jit(solution)/shard_map/ppermute | solution.py:136
  117.2 3.0 %fusion.5 = bf16[128,1024]{1,0:T(8,128)(2,1)S(1)} fusion(f32[128,1024]{1,0:T(8,128)S(1)} %collective-permute-done.4, f32[128,1024]{1,0:T(8,128)S(1)} %fusion.11, bf16[2048,1024]{1,0:T(8,128)(2,1)} %collective-permute-done.1, bf16[128,8192]{1,0:T(8,128)(2,1)S(1)} %copy-done.3, s32[]{:T(128)S(6)} %select_n.38), kind=kOutput, calls=%fused_computation.14 | convolution fusion | flops 537264128 | bytes 6029316 | tf_op jit(solution)/shard_map/dot_general | solution.py:122
  120.2 0.2 convert_element_type.41
  120.4 0.2 copy.16
  120.6 3.2 %broadcast_in_dim.7 = bf16[128,2,4,8,128]{4,1,0,3,2:T(2,128)(2,1)} broadcast(bf16[128,2,4,128]{3,1,0,2:T(2,128)(2,1)S(1)} %copy.16), dimensions={0,1,2,4} | broadcast | bytes 2359296 | tf_op jit(solution)/shard_map/broadcast_in_dim | solution.py:139
  123.8 7.2 %all-to-all-start.2 = ((bf16[128,2,32,128]{3,1,0,2:T(2,128)(2,1)}), bf16[128,2,32,128]{3,1,0,2:T(2,128)(2,1)}, u32[]{:S(2)}, u32[]{:S(2)}) async-start(bf16[128,2,32,128]{3,1,0,2:T(2,128)(2,1)} %bitcast.45), calls=%async_computation.2 | async-start | bytes 4194304 | tf_op jit(solution)/shard_map/all_to_all | solution.py:141
  131.0 0.1 copy.13
  131.1 0.1 squeeze.8
  131.2 0.6 fusion.20.lists_ref
  131.8 1.7 bitcast_dynamic-update-slice_fusion.1
  133.5 23.7 %all-to-all-done.2 = bf16[128,2,32,128]{3,1,0,2:T(2,128)(2,1)} async-done(((bf16[128,2,32,128]{3,1,0,2:T(2,128)(2,1)}), bf16[128,2,32,128]{3,1,0,2:T(2,128)(2,1)}, u32[]{:S(2)}, u32[]{:S(2)}) %all-to-all-start.2) | async-done | bytes 2097184 | tf_op jit(solution)/shard_map/all_to_all | solution.py:141
  157.2 3.2 %bitcast_dynamic-update-slice_fusion = bf16[8192,256]{1,0:T(8,128)(2,1)} fusion(bf16[8192,256]{1,0:T(8,128)(2,1)} %bitcast_dynamic-update-slice_fusion.1, bf16[512,8,2,128]{3,2,1,0:T(2,128)(2,1)} %bitcast.27), kind=kLoop, calls=%fused_computation.5 | loop fusion | bytes 4194304 | tf_op jit(solution)/shard_map/concatenate | solution.py:142
  160.4 3.9 %fusion.33 = (bf16[8192,128]{1,0:T(8,128)(2,1)}, bf16[128,8192]{0,1:T(8,128)(2,1)S(1)}) fusion(bf16[8192,256]{1,0:T(8,128)(2,1)} %bitcast_dynamic-update-slice_fusion), kind=kLoop, calls=%fused_computation.53 | loop fusion | bytes 8388608 | tf_op jit(solution)/shard_map/slice | solution.py:146
  164.3 3.0 %copy.17.kt_ref = bf16[128,8192]{1,0:T(8,128)(2,1)} copy(bf16[128,8192]{0,1:T(8,128)(2,1)S(1)} %get-tuple-element.10) | data formatting | bytes 4194304 | tf_op jit(solution)/shard_map/transpose | solution.py:145
  167.2 26.0 %shard_map.73 = bf16[8192,128]{1,0:T(8,128)(2,1)} custom-call(s32[768]{0:T(1024)} %fusion.20.lists_ref, s32[64]{0:T(128)} %bitcast.51, bf16[8192,128]{1,0:T(8,128)(2,1)} %bitcast.48, bf16[128,8192]{1,0:T(8,128)(2,1)} %copy.17.kt_ref, bf16[8192,128]{1,0:T(8,128)(2,1)} %get-tuple-element.9.v_ref), custom_call_target="tpu_custom_call" | custom-call | tf_op jit(solution)/shard_map/pallas_call | solution.py:63
  193.2 32.3 %all_to_all.65 = bf16[32,256,128]{2,1,0:T(8,128)(2,1)S(1)} all-to-all(bf16[32,256,128]{2,1,0:T(8,128)(2,1)} %bitcast.49), channel_id=1, replica_groups=mesh['zh'=2,'core'=2,'x'=4,'y'=4,'zl'=2] {'x','y','zl'}, dimensions={0} | all-to-all | bytes 4194304 | tf_op jit(solution)/shard_map/all_to_all | solution.py:151
  225.6 1.4 copy.18
  226.9 2.3 broadcast_in_dim.8
  (20 shorter events, 0.1 us)
Async XLA Ops:
  0.0 3.3 %copy-start.4 = (bf16[2048,512]{1,0:T(8,128)(2,1)S(1)}, bf16[2048,512]{1,0:T(8,128)(2,1)}, u32[]{:S(2)}) copy-start(bf16[2048,512]{1,0:T(8,128)(2,1)} %param.11) | copy-start | bytes 6291460
  0.0 4.8 %copy-start.5 = (bf16[1,256,4096]{2,1,0:T(8,128)(2,1)S(1)}, bf16[1,256,4096]{2,1,0:T(8,128)(2,1)}, u32[]{:S(2)}) copy-start(bf16[1,256,4096]{2,1,0:T(8,128)(2,1)} %param.9) | copy-start | bytes 6291460
  4.8 47.2 %collective-permute-start.1 = (bf16[2048,1024]{1,0:T(8,128)(2,1)}, bf16[2048,1024]{1,0:T(8,128)(2,1)}, u32[]{:S(2)}, u32[]{:S(2)}) collective-permute-start(bf16[2048,1024]{1,0:T(8,128)(2,1)} %constant_dynamic-update-slice_fusion), channel_id=1, source_target_pairs={{0,32},{32,0},{1,33},{33,1},{2,34},{34,2},{3,35},{35,3},{4,36},{36... | collective-permute-start | bytes 12582920 | tf_op jit(solution)/shard_map/ppermute | solution.py:117
  5.3 10.9 %copy-start.6 = (bf16[8192]{0:T(1024)(128)(2,1)S(1)}, bf16[8192]{0:T(1024)(128)(2,1)}, u32[]{:S(2)}) copy-start(bf16[8192]{0:T(1024)(128)(2,1)} %param.8) | copy-start | bytes 49156
  7.4 44.5 %all-to-all-start = ((bf16[256,32,128]{2,0,1:T(8,128)(2,1)}), bf16[256,32,128]{2,0,1:T(8,128)(2,1)S(1)}, u32[]{:S(2)}, u32[]{:S(2)}) async-start(bf16[256,32,128]{2,0,1:T(8,128)(2,1)} %copy.14), calls=%async_computation | async-start | bytes 4194304 | tf_op jit(solution)/shard_map/all_to_all | solution.py:104
  16.2 3.5 %copy-start = (bf16[1,256,8192]{2,1,0:T(8,128)(2,1)S(1)}, bf16[1,256,8192]{2,1,0:T(8,128)(2,1)}, u32[]{:S(2)}) copy-start(bf16[1,256,8192]{2,1,0:T(8,128)(2,1)} %param.7) | copy-start | bytes 12582916
  24.6 27.4 %collective-permute-start = (bf16[128,4096]{1,0:T(8,128)(2,1)S(1)}, bf16[128,4096]{1,0:T(8,128)(2,1)}, u32[]{:S(2)}, u32[]{:S(2)}) collective-permute-start(bf16[128,4096]{1,0:T(8,128)(2,1)S(1)} %constant_dynamic-slice_fusion.1), channel_id=1, source_target_pairs={{0,65},{1,64},{2,67},{3,66},{4,69},{5,68},{6,71},{7,70},{8,73},{9,... | collective-permute-start | bytes 3145736 | tf_op jit(solution)/shard_map/ppermute | solution.py:133
  52.0 7.9 %copy-start.1 = (bf16[256,32,128]{2,0,1:T(8,128)(2,1)}, bf16[256,32,128]{2,0,1:T(8,128)(2,1)S(1)}, u32[]{:S(2)}) copy-start(bf16[256,32,128]{2,0,1:T(8,128)(2,1)S(1)} %all-to-all-done) | copy-start | bytes 6291460
  55.8 7.0 %copy-start.2 = (bf16[128,8192]{1,0:T(8,128)(2,1)S(1)}, bf16[128,8192]{1,0:T(8,128)(2,1)}, u32[]{:S(2)}) copy-start(bf16[128,8192]{1,0:T(8,128)(2,1)} %get-tuple-element.11) | copy-start | bytes 6291460
  59.9 16.3 %collective-permute-start.2 = (f32[128,1024]{1,0:T(8,128)}, f32[128,1024]{1,0:T(8,128)}, u32[]{:S(2)}, u32[]{:S(2)}) collective-permute-start(f32[128,1024]{1,0:T(8,128)} %convolution_add_fusion.2), channel_id=1, source_target_pairs={{0,65},{1,64},{2,67},{3,66},{4,69},{5,68},{6,71},{7,70},{8,73},{9,... | collective-permute-start | bytes 1572872 | tf_op jit(solution)/shard_map/ppermute | solution.py:136
  62.9 34.2 %collective-permute-start.3 = (bf16[128,4096]{1,0:T(8,128)(2,1)S(1)}, bf16[128,4096]{1,0:T(8,128)(2,1)}, u32[]{:S(2)}, u32[]{:S(2)}) collective-permute-start(bf16[128,4096]{1,0:T(8,128)(2,1)S(1)} %constant_dynamic-slice_fusion), channel_id=1, source_target_pairs={{0,65},{1,64},{2,67},{3,66},{4,69},{5,68},{6,71},{7,70},{8,73},{9,... | collective-permute-start | bytes 3145736 | tf_op jit(solution)/shard_map/ppermute | solution.py:133
  83.0 37.6 %all-to-all-start.1 = ((bf16[128,2,32,128]{3,1,0,2:T(2,128)(2,1)}), bf16[128,2,32,128]{3,1,0,2:T(2,128)(2,1)S(1)}, u32[]{:S(2)}, u32[]{:S(2)}) async-start(bf16[128,2,32,128]{3,1,0,2:T(2,128)(2,1)} %bitcast.44), calls=%async_computation.1 | async-start | bytes 4194304 | tf_op jit(solution)/shard_map/all_to_all | solution.py:141
  100.1 6.2 %copy-start.3 = (bf16[128,8192]{1,0:T(8,128)(2,1)S(1)}, bf16[128,8192]{1,0:T(8,128)(2,1)}, u32[]{:S(2)}) copy-start(bf16[128,8192]{1,0:T(8,128)(2,1)} %get-tuple-element.11) | copy-start | bytes 6291460
  103.4 13.8 %collective-permute-start.4 = (f32[128,1024]{1,0:T(8,128)S(1)}, f32[128,1024]{1,0:T(8,128)S(1)}, u32[]{:S(2)}, u32[]{:S(2)}) collective-permute-start(f32[128,1024]{1,0:T(8,128)S(1)} %convolution_add_fusion), channel_id=1, source_target_pairs={{0,65},{1,64},{2,67},{3,66},{4,69},{5,68},{6,71},{7,70},{8,73},{9,... | collective-permute-start | bytes 1572872 | tf_op jit(solution)/shard_map/ppermute | solution.py:136
  120.2 10.8 %copy-start.7 = (s32[1,1,64,12]{2,1,3,0:T(1,128)S(1)}, s32[1,1,64,12]{2,1,3,0:T(1,128)}, u32[]{:S(2)}) copy-start(s32[1,1,64,12]{2,1,3,0:T(1,128)} %param.12) | copy-start | bytes 9220
  123.8 33.3 %all-to-all-start.2 = ((bf16[128,2,32,128]{3,1,0,2:T(2,128)(2,1)}), bf16[128,2,32,128]{3,1,0,2:T(2,128)(2,1)}, u32[]{:S(2)}, u32[]{:S(2)}) async-start(bf16[128,2,32,128]{3,1,0,2:T(2,128)(2,1)} %bitcast.45), calls=%async_computation.2 | async-start | bytes 4194304 | tf_op jit(solution)/shard_map/all_to_all | solution.py:141

commit v9 on v8

--- a/solution.py
+++ b/solution.py
@@ -56,7 +56,7 @@
     lax.fori_loop(0, SUB_BLOCKS, one_block, 0, unroll=8)
 
 
-def attend(lists_flat, counts, head_queries, key_t, values):
+def attend(lists_flat, counts, head_queries, key_t, kv_rows):
     sequence_rows = head_queries.shape[0]
     block_total = sequence_rows // BLK
     step_rows = SUB_BLOCKS * BLK
@@ -69,12 +69,12 @@
             in_specs=[
                 pl.BlockSpec((step_rows, HD), lambda i, lists, counts: (i, 0)),
                 pl.BlockSpec((HD, sequence_rows), lambda i, lists, counts: (0, 0)),
-                pl.BlockSpec((sequence_rows, HD), lambda i, lists, counts: (0, 0)),
+                pl.BlockSpec((sequence_rows, HD), lambda i, lists, counts: (0, 1)),
             ],
             out_specs=pl.BlockSpec((step_rows, HD), lambda i, lists, counts: (i, 0)),
         ),
         compiler_params=pltpu.CompilerParams(dimension_semantics=("arbitrary",)),
-    )(lists_flat, counts, head_queries, key_t, values)
+    )(lists_flat, counts, head_queries, key_t, kv_rows)
 
 
 ALL_AXES = ("zh", "core", "x", "y", "zl")
@@ -133,8 +133,9 @@
         partner_rows = lax.ppermute(far_features, ALL_AXES, partner_pairs)
         if chunk == 0:
             head_queries, partner_rows = lax.optimization_barrier((head_queries, partner_rows))
-        from_partner = lax.ppermute(half_sum(partner_rows, 0), ALL_AXES, partner_pairs)
-        summed = half_sum(rows, zh * half_features) + from_partner
+        for_partner = half_sum(partner_rows, 0).astype(jnp.bfloat16)
+        from_partner = lax.ppermute(for_partner, ALL_AXES, partner_pairs)
+        summed = half_sum(rows, zh * half_features) + from_partner.astype(jnp.float32)
         paired = summed.reshape(chunk_rows, 2, KVH, 1, HD).astype(jnp.bfloat16)
         widened = jnp.broadcast_to(paired, (chunk_rows, 2, KVH, copies_per_head, HD))
         widened = widened.reshape(chunk_rows, 2, ctx_size, HD)
@@ -143,11 +144,10 @@
     sequence_rows = head_queries.shape[0]
     kv_rows = head_pair.reshape(sequence_rows, 2 * HD)
     key_t = kv_rows[:, :HD].T
-    values = kv_rows[:, HD:]
     lists = block_lists[0, 0]
     lists_flat = ((lists % CHUNKS) * ctx_size + lists // CHUNKS).reshape(-1)
     counts = block_counts[0, 0]
-    attended_head = attend(lists_flat, counts, head_queries, key_t, values)
+    attended_head = attend(lists_flat, counts, head_queries, key_t, kv_rows)
     restored = lax.all_to_all(attended_head, CTX_AXES, split_axis=0, concat_axis=1, tiled=True)
     return restored[None]
 

time: 230 us -> 229 us (level)
    all_to_all x2, waiting for transfers between devices: 23.7 us -> 34.7 us  [on_device(): lax.all_to_all(widened, CTX_AXES, split_axis=2, concat_axis=0, tiled=True)]
    ppermute x2, waiting for transfers between devices: 30.3 us -> 22.9 us  [on_device(): partner_rows = lax.ppermute(far_features, ALL_AXES, partner_pairs)]
    slice x1 -> x0, local copies, waits for them, and re-layouts: 3.86 us -> none  [on_device(): values = kv_rows[:, HD:]]
    all_to_all x2, starting transfers between devices: 14.2 us -> 11.8 us  [on_device(): lax.all_to_all(widened, CTX_AXES, split_axis=2, concat_axis=0, tiled=True)]
    transpose x1 -> x2, local copies, waits for them, and re-layouts: 2.97 us -> 4.72 us  [on_device(): key_t = kv_rows[:, :HD].T]
    unnamed x20 -> x18, local copies, waits for them, and re-layouts: 5.7 us -> 5.7 us
  transfers between devices with their start and end apart: 8 -> 8, of which waited for: 5 -> 5; matrix products, arithmetic and copies ran while one was open for 16% -> 20% of each run, Pallas kernels for 0% -> 0%
where the time goes in v9:
time: 229 us; the launch traced here: 228 us
  waiting for transfers between devices  73.7 us (32%)
  local copies, waits for them, and re-layouts  34.3 us (15%)
  starting transfers between devices  32.4 us (14%)
  blocking collectives  31.1 us (14%)
  Pallas kernels  26.3 us (11%)
  matrix products  25.2 us (11%)
  other arithmetic  5.05 us (2%)
    all_to_all x2, waiting for transfers between devices, on_device(): lax.all_to_all(widened, CTX_AXES, split_axis=2, concat_axis=0, tiled=True)  34.7 us
    all_to_all x1, blocking collectives, on_device(): lax.all_to_all(attended_head, CTX_AXES, split_axis=0, concat_axis=1, tile...  31.1 us
    pallas_call x1, Pallas kernels, attend(): pl.pallas_call(attend_kernel, out_shape=jax.ShapeDtypeStruct((sequence_ro...  26.3 us
    ppermute x2, waiting for transfers between devices, on_device(): partner_rows = lax.ppermute(far_features, ALL_AXES, partner_pairs)  22.9 us
    ppermute x2, waiting for transfers between devices, on_device(): from_partner = lax.ppermute(for_partner, ALL_AXES, partner_pairs)  16.1 us
    dot_general x4, matrix products, half_sum(): jnp.dot(other, sibling, preferred_element_type=jnp.float32)  13.1 us
    dot_general x4, matrix products, half_sum(): jnp.dot(own, local_weight, preferred_element_type=jnp.float32)  12.2 us
    all_to_all x2, starting transfers between devices, on_device(): lax.all_to_all(widened, CTX_AXES, split_axis=2, concat_axis=0, tiled=True)  11.8 us
  transfers between devices with their start and end apart: 8, of which 5 were waited for; matrix products, arithmetic and copies ran while one was open for 20% of the time, Pallas kernels for 0%

profile of v9, /device:TPU:0, one launch (start us, length us, event | category | flops | bytes accessed | tf_op | source)
XLA Modules:
  0.0 228.4 jit_solution(6544967728026928480)
XLA Ops:
  0.0 3.3 %constant_dynamic-update-slice_fusion.1 = bf16[2048,1024]{1,0:T(8,128)(2,1)} fusion(bf16[2048,512]{1,0:T(8,128)(2,1)} %param.10), kind=kLoop, calls=%fused_computation.31 | loop fusion | bytes 4194304
  3.3 1.6 constant_dynamic-update-slice_fusion
  4.8 0.5 copy.19
  5.3 0.0 copy-start.5
  5.3 2.1 copy.14
  7.5 8.8 %all-to-all-start = ((bf16[256,32,128]{2,0,1:T(8,128)(2,1)}), bf16[256,32,128]{2,0,1:T(8,128)(2,1)S(1)}, u32[]{:S(2)}, u32[]{:S(2)}) async-start(bf16[256,32,128]{2,0,1:T(8,128)(2,1)} %copy.14), calls=%async_computation | async-start | bytes 4194304 | tf_op jit(solution)/shard_map/all_to_all | solution.py:104
  16.3 3.3 %fusion = f32[256]{0:T(256)S(1)} fusion(bf16[1,256,8192]{2,1,0:T(8,128)(2,1)} %param.7), kind=kLoop, calls=%fused_computation.2 | loop fusion | flops 6291200 | bytes 4195328 | tf_op jit(solution)/shard_map/reduce_sum | solution.py:106
  19.6 0.2 copy-done
  19.7 1.2 fusion.2
  20.9 2.4 %fusion.35 = (bf16[128,8192]{1,0:T(8,128)(2,1)}, bf16[128,8192]{1,0:T(8,128)(2,1)}) fusion(bf16[256,8192]{1,0:T(8,128)(2,1)S(1)} %fusion.2), kind=kLoop, calls=%fused_computation.55 | loop fusion | bytes 8388608 | tf_op jit(solution)/shard_map/slice | solution.py:131
  23.3 2.3 constant_dynamic-slice_fusion.1
  25.6 3.9 %collective-permute-start = (bf16[128,4096]{1,0:T(8,128)(2,1)}, bf16[128,4096]{1,0:T(8,128)(2,1)}, u32[]{:S(2)}, u32[]{:S(2)}) collective-permute-start(bf16[128,4096]{1,0:T(8,128)(2,1)} %constant_dynamic-slice_fusion.1), channel_id=1, source_target_pairs={{0,65},{1,64},{2,67},{3,66},{4,69},{5,68},{6,71},{7,70},{8,73},{9,... | collective-permute-start | bytes 3145736 | tf_op jit(solution)/shard_map/ppermute | solution.py:133
  29.5 1.3 constant_dynamic-slice_fusion
  30.8 0.1 collective-permute-start.3
  30.9 22.9 %collective-permute-done = bf16[128,4096]{1,0:T(8,128)(2,1)} collective-permute-done((bf16[128,4096]{1,0:T(8,128)(2,1)}, bf16[128,4096]{1,0:T(8,128)(2,1)}, u32[]{:S(2)}, u32[]{:S(2)}) %collective-permute-start) | collective-permute-done | bytes 1048608 | tf_op jit(solution)/shard_map/ppermute | solution.py:133
  53.8 3.8 %fusion.15 = f32[128,1024]{1,0:T(8,128)S(1)} fusion(bf16[2048,1024]{1,0:T(8,128)(2,1)} %collective-permute-done.1, bf16[128,4096]{1,0:T(8,128)(2,1)} %collective-permute-done, s32[]{:T(128)S(6)} %select_n.40), kind=kOutput, calls=%fused_computation.24 | convolution fusion | flops 536870912 | bytes 5242884 | tf_op jit(solution)/shard_map/dot_general | solution.py:122
  57.7 3.1 %fusion.7 = bf16[128,1024]{1,0:T(8,128)(2,1)S(1)} fusion(f32[128,1024]{1,0:T(8,128)S(1)} %fusion.15, bf16[2048,1024]{1,0:T(8,128)(2,1)} %constant_dynamic-update-slice_fusion, bf16[128,4096]{1,0:T(8,128)(2,1)} %collective-permute-done, s32[]{:T(128)S(6)} %select_n.39), kind=kOutput, calls=%fused_computation.16 | convolution fusion | flops 537133056 | bytes 5505028 | tf_op jit(solution)/shard_map/dot_general | solution.py:122
  60.8 3.3 %collective-permute-start.2 = (bf16[128,1024]{1,0:T(8,128)(2,1)S(1)}, bf16[128,1024]{1,0:T(8,128)(2,1)}, u32[]{:S(2)}, u32[]{:S(2)}) collective-permute-start(bf16[128,1024]{1,0:T(8,128)(2,1)S(1)} %fusion.7), channel_id=1, source_target_pairs={{0,65},{1,64},{2,67},{3,66},{4,69},{5,68},{6,71},{7,70},{8,73},{9,... | collective-permute-start | bytes 786440 | tf_op jit(solution)/shard_map/ppermute | solution.py:137
  64.1 3.1 %fusion.19 = f32[128,1024]{1,0:T(8,128)S(1)} fusion(bf16[2048,1024]{1,0:T(8,128)(2,1)} %constant_dynamic-update-slice_fusion, bf16[128,8192]{1,0:T(8,128)(2,1)} %get-tuple-element.10, s32[]{:T(128)S(6)} %select_n.37), kind=kOutput, calls=%fused_computation.28 | convolution fusion | flops 536870912 | bytes 5242884 | tf_op jit(solution)/shard_map/dot_general | solution.py:122
  67.2 14.0 %collective-permute-done.2 = bf16[128,1024]{1,0:T(8,128)(2,1)} collective-permute-done((bf16[128,1024]{1,0:T(8,128)(2,1)S(1)}, bf16[128,1024]{1,0:T(8,128)(2,1)}, u32[]{:S(2)}, u32[]{:S(2)}) %collective-permute-start.2) | collective-permute-done | bytes 262176 | tf_op jit(solution)/shard_map/ppermute | solution.py:137
  81.2 3.1 %fusion.6 = bf16[128,1024]{1,0:T(8,128)(2,1)S(1)} fusion(f32[128,1024]{1,0:T(8,128)S(1)} %fusion.19, bf16[2048,1024]{1,0:T(8,128)(2,1)} %collective-permute-done.1, bf16[128,1024]{1,0:T(8,128)(2,1)} %collective-permute-done.2, bf16[128,8192]{1,0:T(8,128)(2,1)} %get-tuple-element.10, s32[]{:T(128)S(6)} %select_n.38), kind=kOutput, calls=%fused_computation.15 | convolution fusion | flops 537395200 | bytes 5767172 | tf_op jit(solution)/shard_map/dot_general | solution.py:122
  84.3 0.2 convert_element_type.53
  84.5 0.2 copy.15
  84.7 3.2 %broadcast_in_dim.6 = bf16[128,2,4,8,128]{4,1,0,3,2:T(2,128)(2,1)} broadcast(bf16[128,2,4,128]{3,1,0,2:T(2,128)(2,1)S(1)} %copy.15), dimensions={0,1,2,4} | broadcast | bytes 2359296 | tf_op jit(solution)/shard_map/broadcast_in_dim | solution.py:140
  87.9 7.1 %all-to-all-start.1 = ((bf16[128,2,32,128]{3,1,0,2:T(2,128)(2,1)}), bf16[128,2,32,128]{3,1,0,2:T(2,128)(2,1)S(1)}, u32[]{:S(2)}, u32[]{:S(2)}) async-start(bf16[128,2,32,128]{3,1,0,2:T(2,128)(2,1)} %bitcast.46), calls=%async_computation.1 | async-start | bytes 4194304 | tf_op jit(solution)/shard_map/all_to_all | solution.py:142
  95.0 3.2 %fusion.9 = f32[128,1024]{1,0:T(8,128)S(1)} fusion(bf16[2048,1024]{1,0:T(8,128)(2,1)} %collective-permute-done.1, bf16[128,4096]{1,0:T(8,128)(2,1)} %collective-permute-done.3, s32[]{:T(128)S(6)} %select_n.40), kind=kOutput, calls=%fused_computation.18 | convolution fusion | flops 536870912 | bytes 5242884 | tf_op jit(solution)/shard_map/dot_general | solution.py:122
  98.2 3.1 %fusion.8 = bf16[128,1024]{1,0:T(8,128)(2,1)S(1)} fusion(f32[128,1024]{1,0:T(8,128)S(1)} %fusion.9, bf16[2048,1024]{1,0:T(8,128)(2,1)} %constant_dynamic-update-slice_fusion, bf16[128,4096]{1,0:T(8,128)(2,1)} %collective-permute-done.3, s32[]{:T(128)S(6)} %select_n.39), kind=kOutput, calls=%fused_computation.17 | convolution fusion | flops 537133056 | bytes 5505028 | tf_op jit(solution)/shard_map/dot_general | solution.py:122
  101.3 4.4 %collective-permute-start.4 = (bf16[128,1024]{1,0:T(8,128)(2,1)S(1)}, bf16[128,1024]{1,0:T(8,128)(2,1)S(1)}, u32[]{:S(2)}, u32[]{:S(2)}) collective-permute-start(bf16[128,1024]{1,0:T(8,128)(2,1)S(1)} %fusion.8), channel_id=1, source_target_pairs={{0,65},{1,64},{2,67},{3,66},{4,69},{5,68},{6,71},{7,70},{8,73},{9,... | collective-permute-start | bytes 786440 | tf_op jit(solution)/shard_map/ppermute | solution.py:137
  105.8 2.9 %fusion.13 = f32[128,1024]{1,0:T(8,128)S(1)} fusion(bf16[2048,1024]{1,0:T(8,128)(2,1)} %constant_dynamic-update-slice_fusion, bf16[128,8192]{1,0:T(8,128)(2,1)S(1)} %copy-done.2, s32[]{:T(128)S(6)} %select_n.37), kind=kOutput, calls=%fused_computation.22 | convolution fusion | flops 536870912 | bytes 5242884 | tf_op jit(solution)/shard_map/dot_general | solution.py:122
  108.7 2.1 collective-permute-done.4
  110.7 2.9 %fusion.5 = bf16[128,1024]{1,0:T(8,128)(2,1)S(1)} fusion(f32[128,1024]{1,0:T(8,128)S(1)} %fusion.13, bf16[2048,1024]{1,0:T(8,128)(2,1)} %collective-permute-done.1, bf16[128,1024]{1,0:T(8,128)(2,1)S(1)} %collective-permute-done.4, bf16[128,8192]{1,0:T(8,128)(2,1)S(1)} %copy-done.2, s32[]{:T(128)S(6)} %select_n.38), kind=kOutput, calls=%fused_computation.14 | convolution fusion | flops 537395200 | bytes 5767172 | tf_op jit(solution)/shard_map/dot_general | solution.py:122
  113.7 0.2 convert_element_type.57
  113.9 0.2 copy.16
  114.1 8.8 %all-to-all-done.1 = bf16[128,2,32,128]{3,1,0,2:T(2,128)(2,1)S(1)} async-done(((bf16[128,2,32,128]{3,1,0,2:T(2,128)(2,1)}), bf16[128,2,32,128]{3,1,0,2:T(2,128)(2,1)S(1)}, u32[]{:S(2)}, u32[]{:S(2)}) %all-to-all-start.1) | async-done | bytes 2097184 | tf_op jit(solution)/shard_map/all_to_all | solution.py:142
  122.9 3.2 %broadcast_in_dim.7 = bf16[128,2,4,8,128]{4,1,0,3,2:T(2,128)(2,1)} broadcast(bf16[128,2,4,128]{3,1,0,2:T(2,128)(2,1)S(1)} %copy.16), dimensions={0,1,2,4} | broadcast | bytes 2359296 | tf_op jit(solution)/shard_map/broadcast_in_dim | solution.py:140
  126.1 4.8 %all-to-all-start.2 = ((bf16[128,2,32,128]{3,1,0,2:T(2,128)(2,1)}), bf16[128,2,32,128]{3,1,0,2:T(2,128)(2,1)}, u32[]{:S(2)}, u32[]{:S(2)}) async-start(bf16[128,2,32,128]{3,1,0,2:T(2,128)(2,1)} %bitcast.47), calls=%async_computation.2 | async-start | bytes 4194304 | tf_op jit(solution)/shard_map/all_to_all | solution.py:142
  130.9 0.1 copy.13
  131.0 0.1 squeeze.8
  131.1 0.6 fusion.22.lists_ref
  131.7 1.7 bitcast_dynamic-update-slice_fusion.1
  133.4 25.9 %all-to-all-done.2 = bf16[128,2,32,128]{3,1,0,2:T(2,128)(2,1)} async-done(((bf16[128,2,32,128]{3,1,0,2:T(2,128)(2,1)}), bf16[128,2,32,128]{3,1,0,2:T(2,128)(2,1)}, u32[]{:S(2)}, u32[]{:S(2)}) %all-to-all-start.2) | async-done | bytes 2097184 | tf_op jit(solution)/shard_map/all_to_all | solution.py:142
  159.3 3.2 %bitcast_dynamic-update-slice_fusion.v_ref = bf16[8192,256]{1,0:T(8,128)(2,1)} fusion(bf16[8192,256]{1,0:T(8,128)(2,1)} %bitcast_dynamic-update-slice_fusion.1, bf16[512,8,2,128]{3,2,1,0:T(2,128)(2,1)} %bitcast.27), kind=kLoop, calls=%fused_computation.5 | loop fusion | bytes 4194304 | tf_op jit(solution)/shard_map/concatenate | solution.py:143
  162.5 1.7 slice_bitcast_fusion
  164.3 3.0 %copy.17.kt_ref = bf16[128,8192]{1,0:T(8,128)(2,1)} copy(bf16[128,8192]{0,1:T(8,128)(2,1)S(1)} %slice_bitcast_fusion) | data formatting | bytes 4194304 | tf_op jit(solution)/shard_map/transpose | solution.py:146
  167.3 26.3 %shard_map.73 = bf16[8192,128]{1,0:T(8,128)(2,1)} custom-call(s32[768]{0:T(1024)} %fusion.22.lists_ref, s32[64]{0:T(128)} %bitcast.51, bf16[8192,128]{1,0:T(8,128)(2,1)} %bitcast.43, bf16[128,8192]{1,0:T(8,128)(2,1)} %copy.17.kt_ref, bf16[8192,256]{1,0:T(8,128)(2,1)} %bitcast_dynamic-update-slice_fusion.v_ref), custom_call_target="tpu_custom_call" | custom-call | tf_op jit(solution)/shard_map/pallas_call | solution.py:63
  193.6 31.1 %all_to_all.65 = bf16[32,256,128]{2,1,0:T(8,128)(2,1)S(1)} all-to-all(bf16[32,256,128]{2,1,0:T(8,128)(2,1)} %bitcast.44), channel_id=1, replica_groups=mesh['zh'=2,'core'=2,'x'=4,'y'=4,'zl'=2] {'x','y','zl'}, dimensions={0} | all-to-all | bytes 4194304 | tf_op jit(solution)/shard_map/all_to_all | solution.py:151
  224.7 1.4 copy.18
  226.1 2.3 %broadcast_in_dim.8 = bf16[1,256,4096]{2,1,0:T(8,128)(2,1)} reshape(bf16[256,32,128]{2,1,0:T(8,128)(2,1)S(1)} %copy.18) | data formatting | bytes 4194304 | tf_op jit(solution)/shard_map/broadcast_in_dim | solution.py:152
  (18 shorter events, 0.1 us)
Async XLA Ops:
  0.0 3.3 %copy-start.3 = (bf16[2048,512]{1,0:T(8,128)(2,1)S(1)}, bf16[2048,512]{1,0:T(8,128)(2,1)}, u32[]{:S(2)}) copy-start(bf16[2048,512]{1,0:T(8,128)(2,1)} %param.11) | copy-start | bytes 6291460
  0.0 4.8 %copy-start.4 = (bf16[1,256,4096]{2,1,0:T(8,128)(2,1)S(1)}, bf16[1,256,4096]{2,1,0:T(8,128)(2,1)}, u32[]{:S(2)}) copy-start(bf16[1,256,4096]{2,1,0:T(8,128)(2,1)} %param.9) | copy-start | bytes 6291460
  4.8 49.0 %collective-permute-start.1 = (bf16[2048,1024]{1,0:T(8,128)(2,1)}, bf16[2048,1024]{1,0:T(8,128)(2,1)}, u32[]{:S(2)}, u32[]{:S(2)}) collective-permute-start(bf16[2048,1024]{1,0:T(8,128)(2,1)} %constant_dynamic-update-slice_fusion), channel_id=1, source_target_pairs={{0,32},{32,0},{1,33},{33,1},{2,34},{34,2},{3,35},{35,3},{4,36},{36... | collective-permute-start | bytes 12582920 | tf_op jit(solution)/shard_map/ppermute | solution.py:117
  5.3 10.9 %copy-start.5 = (bf16[8192]{0:T(1024)(128)(2,1)S(1)}, bf16[8192]{0:T(1024)(128)(2,1)}, u32[]{:S(2)}) copy-start(bf16[8192]{0:T(1024)(128)(2,1)} %param.8) | copy-start | bytes 49156
  7.5 46.4 %all-to-all-start = ((bf16[256,32,128]{2,0,1:T(8,128)(2,1)}), bf16[256,32,128]{2,0,1:T(8,128)(2,1)S(1)}, u32[]{:S(2)}, u32[]{:S(2)}) async-start(bf16[256,32,128]{2,0,1:T(8,128)(2,1)} %copy.14), calls=%async_computation | async-start | bytes 4194304 | tf_op jit(solution)/shard_map/all_to_all | solution.py:104
  16.3 3.5 %copy-start = (bf16[1,256,8192]{2,1,0:T(8,128)(2,1)S(1)}, bf16[1,256,8192]{2,1,0:T(8,128)(2,1)}, u32[]{:S(2)}) copy-start(bf16[1,256,8192]{2,1,0:T(8,128)(2,1)} %param.7) | copy-start | bytes 12582916
  25.6 28.2 %collective-permute-start = (bf16[128,4096]{1,0:T(8,128)(2,1)}, bf16[128,4096]{1,0:T(8,128)(2,1)}, u32[]{:S(2)}, u32[]{:S(2)}) collective-permute-start(bf16[128,4096]{1,0:T(8,128)(2,1)} %constant_dynamic-slice_fusion.1), channel_id=1, source_target_pairs={{0,65},{1,64},{2,67},{3,66},{4,69},{5,68},{6,71},{7,70},{8,73},{9,... | collective-permute-start | bytes 3145736 | tf_op jit(solution)/shard_map/ppermute | solution.py:133
  30.8 64.2 %collective-permute-start.3 = (bf16[128,4096]{1,0:T(8,128)(2,1)S(1)}, bf16[128,4096]{1,0:T(8,128)(2,1)}, u32[]{:S(2)}, u32[]{:S(2)}) collective-permute-start(bf16[128,4096]{1,0:T(8,128)(2,1)S(1)} %constant_dynamic-slice_fusion), channel_id=1, source_target_pairs={{0,65},{1,64},{2,67},{3,66},{4,69},{5,68},{6,71},{7,70},{8,73},{9,... | collective-permute-start | bytes 3145736 | tf_op jit(solution)/shard_map/ppermute | solution.py:133
  53.8 6.9 %copy-start.1 = (bf16[256,32,128]{2,0,1:T(8,128)(2,1)}, bf16[256,32,128]{2,0,1:T(8,128)(2,1)S(1)}, u32[]{:S(2)}) copy-start(bf16[256,32,128]{2,0,1:T(8,128)(2,1)S(1)} %all-to-all-done) | copy-start | bytes 6291460
  60.8 20.4 %collective-permute-start.2 = (bf16[128,1024]{1,0:T(8,128)(2,1)S(1)}, bf16[128,1024]{1,0:T(8,128)(2,1)}, u32[]{:S(2)}, u32[]{:S(2)}) collective-permute-start(bf16[128,1024]{1,0:T(8,128)(2,1)S(1)} %fusion.7), channel_id=1, source_target_pairs={{0,65},{1,64},{2,67},{3,66},{4,69},{5,68},{6,71},{7,70},{8,73},{9,... | collective-permute-start | bytes 786440 | tf_op jit(solution)/shard_map/ppermute | solution.py:137
  87.9 35.0 %all-to-all-start.1 = ((bf16[128,2,32,128]{3,1,0,2:T(2,128)(2,1)}), bf16[128,2,32,128]{3,1,0,2:T(2,128)(2,1)S(1)}, u32[]{:S(2)}, u32[]{:S(2)}) async-start(bf16[128,2,32,128]{3,1,0,2:T(2,128)(2,1)} %bitcast.46), calls=%async_computation.1 | async-start | bytes 4194304 | tf_op jit(solution)/shard_map/all_to_all | solution.py:142
  95.0 10.8 %copy-start.2 = (bf16[128,8192]{1,0:T(8,128)(2,1)S(1)}, bf16[128,8192]{1,0:T(8,128)(2,1)}, u32[]{:S(2)}) copy-start(bf16[128,8192]{1,0:T(8,128)(2,1)} %get-tuple-element.9) | copy-start | bytes 6291460
  101.3 9.4 %collective-permute-start.4 = (bf16[128,1024]{1,0:T(8,128)(2,1)S(1)}, bf16[128,1024]{1,0:T(8,128)(2,1)S(1)}, u32[]{:S(2)}, u32[]{:S(2)}) collective-permute-start(bf16[128,1024]{1,0:T(8,128)(2,1)S(1)} %fusion.8), channel_id=1, source_target_pairs={{0,65},{1,64},{2,67},{3,66},{4,69},{5,68},{6,71},{7,70},{8,73},{9,... | collective-permute-start | bytes 786440 | tf_op jit(solution)/shard_map/ppermute | solution.py:137
  113.7 17.2 %copy-start.6 = (s32[1,1,64,12]{2,1,3,0:T(1,128)S(1)}, s32[1,1,64,12]{2,1,3,0:T(1,128)}, u32[]{:S(2)}) copy-start(s32[1,1,64,12]{2,1,3,0:T(1,128)} %param.12) | copy-start | bytes 9220
  126.1 33.2 %all-to-all-start.2 = ((bf16[128,2,32,128]{3,1,0,2:T(2,128)(2,1)}), bf16[128,2,32,128]{3,1,0,2:T(2,128)(2,1)}, u32[]{:S(2)}, u32[]{:S(2)}) async-start(bf16[128,2,32,128]{3,1,0,2:T(2,128)(2,1)} %bitcast.47), calls=%async_computation.2 | async-start | bytes 4194304 | tf_op jit(solution)/shard_map/all_to_all | solution.py:142

commit v10 on v9

--- a/solution.py
+++ b/solution.py
@@ -127,15 +127,15 @@
     copies_per_head = ctx_size // KVH
     chunk_rows = local_rows // CHUNKS
     kv_chunks = []
+    own_half = half_sum(normed, zh * half_features)
     for chunk in range(CHUNKS):
         rows = normed[chunk * chunk_rows : (chunk + 1) * chunk_rows]
         far_features = lax.dynamic_slice_in_dim(rows, (1 - zh) * half_features, half_features, axis=1)
         partner_rows = lax.ppermute(far_features, ALL_AXES, partner_pairs)
         if chunk == 0:
             head_queries, partner_rows = lax.optimization_barrier((head_queries, partner_rows))
-        for_partner = half_sum(partner_rows, 0).astype(jnp.bfloat16)
-        from_partner = lax.ppermute(for_partner, ALL_AXES, partner_pairs)
-        summed = half_sum(rows, zh * half_features) + from_partner.astype(jnp.float32)
+        from_partner = lax.ppermute(half_sum(partner_rows, 0), ALL_AXES, partner_pairs)
+        summed = own_half[chunk * chunk_rows : (chunk + 1) * chunk_rows] + from_partner
         paired = summed.reshape(chunk_rows, 2, KVH, 1, HD).astype(jnp.bfloat16)
         widened = jnp.broadcast_to(paired, (chunk_rows, 2, KVH, copies_per_head, HD))
         widened = widened.reshape(chunk_rows, 2, ctx_size, HD)

time: 229 us -> 255 us (1.11)
  waiting for transfers between devices: 73.7 us -> 103 us
  local copies, waits for them, and re-layouts: 34.3 us -> 39.1 us
  starting transfers between devices: 32.4 us -> 27.9 us
    all_to_all x2, waiting for transfers between devices: 34.7 us -> 51.8 us  [on_device(): lax.all_to_all(widened, CTX_AXES, split_axis=2, concat_axis=0, tiled=True)]
    ppermute x2, waiting for transfers between devices: 22.9 us -> 37.5 us  [on_device(): partner_rows = lax.ppermute(far_features, ALL_AXES, partner_pairs)]
    ppermute x2, starting transfers between devices: 7.76 us -> 3.32 us  [on_device(): lax.ppermute(half_sum(partner_rows, 0), ALL_AXES, partner_pairs)]
    unnamed x18 -> x14, local copies, waits for them, and re-layouts: 5.7 us -> 9.04 us
    dot_general x4 -> x3, matrix products: 13.1 us -> 10.9 us  [half_sum(): jnp.dot(other, sibling, preferred_element_type=jnp.float32)]
    dot_general x4 -> x3, matrix products: 12.2 us -> 11.8 us  [half_sum(): jnp.dot(own, local_weight, preferred_element_type=jnp.float32)]
  transfers between devices with their start and end apart: 8 -> 8, of which waited for: 5 -> 6; matrix products, arithmetic and copies ran while one was open for 20% -> 13% of each run, Pallas kernels for 0% -> 0%
where the time goes in v10:
time: 255 us; the launch traced here: 254 us
  waiting for transfers between devices  103 us (40%)
  local copies, waits for them, and re-layouts  39.1 us (15%)
  blocking collectives  32.1 us (13%)
  starting transfers between devices  27.9 us (11%)
  Pallas kernels  26.1 us (10%)
  matrix products  22.7 us (9%)
  other arithmetic  2.89 us (1%)
    all_to_all x2, waiting for transfers between devices, on_device(): lax.all_to_all(widened, CTX_AXES, split_axis=2, concat_axis=0, tiled=True)  51.8 us
    ppermute x2, waiting for transfers between devices, on_device(): partner_rows = lax.ppermute(far_features, ALL_AXES, partner_pairs)  37.5 us
    all_to_all x1, blocking collectives, on_device(): lax.all_to_all(attended_head, CTX_AXES, split_axis=0, concat_axis=1, tile...  32.1 us
    pallas_call x1, Pallas kernels, attend(): pl.pallas_call(attend_kernel, out_shape=jax.ShapeDtypeStruct((sequence_ro...  26.1 us
    ppermute x2, waiting for transfers between devices, on_device(): lax.ppermute(half_sum(partner_rows, 0), ALL_AXES, partner_pairs)  14.1 us
    all_to_all x2, starting transfers between devices, on_device(): lax.all_to_all(widened, CTX_AXES, split_axis=2, concat_axis=0, tiled=True)  11.8 us
    dot_general x3, matrix products, half_sum(): jnp.dot(own, local_weight, preferred_element_type=jnp.float32)  11.8 us
    dot_general x3, matrix products, half_sum(): jnp.dot(other, sibling, preferred_element_type=jnp.float32)  10.9 us
  transfers between devices with their start and end apart: 8, of which 6 were waited for; matrix products, arithmetic and copies ran while one was open for 13% of the time, Pallas kernels for 0%

profile of v10, /device:TPU:0, one launch (start us, length us, event | category | flops | bytes accessed | tf_op | source)
XLA Modules:
  0.0 254.4 jit_solution(4268714117332491259)
XLA Ops:
  0.0 2.1 copy.19
  2.1 2.1 copy.14
  4.2 8.8 %all-to-all-start = ((bf16[256,32,128]{2,0,1:T(8,128)(2,1)}), bf16[256,32,128]{2,0,1:T(8,128)(2,1)S(1)}, u32[]{:S(2)}, u32[]{:S(2)}) async-start(bf16[256,32,128]{2,0,1:T(8,128)(2,1)} %copy.14), calls=%async_computation | async-start | bytes 4194304 | tf_op jit(solution)/shard_map/all_to_all | solution.py:104
  13.0 0.0 copy-start
  13.0 3.2 %constant_dynamic-update-slice_fusion.1 = bf16[2048,1024]{1,0:T(8,128)(2,1)} fusion(bf16[2048,512]{1,0:T(8,128)(2,1)} %param.10), kind=kLoop, calls=%fused_computation.25 | loop fusion | bytes 4194304
  16.2 3.1 %constant_dynamic-update-slice_fusion = bf16[2048,1024]{1,0:T(8,128)(2,1)} fusion(bf16[2048,1024]{1,0:T(8,128)(2,1)} %constant_dynamic-update-slice_fusion.1, bf16[2048,512]{1,0:T(8,128)(2,1)} %param.11), kind=kLoop, calls=%fused_computation.24 | loop fusion | bytes 4194304 | tf_op jit(solution)/shard_map/concatenate | solution.py:111
  19.3 0.9 fusion
  20.3 1.2 fusion.2
  21.5 2.0 copy-done.1
  23.4 2.4 fusion.26
  25.8 2.3 constant_dynamic-slice_fusion.1
  28.1 3.9 %collective-permute-start = (bf16[128,4096]{1,0:T(8,128)(2,1)}, bf16[128,4096]{1,0:T(8,128)(2,1)}, u32[]{:S(2)}, u32[]{:S(2)}) collective-permute-start(bf16[128,4096]{1,0:T(8,128)(2,1)} %constant_dynamic-slice_fusion.1), channel_id=1, source_target_pairs={{0,65},{1,64},{2,67},{3,66},{4,69},{5,68},{6,71},{7,70},{8,73},{9,... | collective-permute-start | bytes 3145736 | tf_op jit(solution)/shard_map/ppermute | solution.py:134
  32.0 1.3 constant_dynamic-slice_fusion
  33.3 0.1 collective-permute-start.3
  33.4 22.9 %collective-permute-done = bf16[128,4096]{1,0:T(8,128)(2,1)} collective-permute-done((bf16[128,4096]{1,0:T(8,128)(2,1)}, bf16[128,4096]{1,0:T(8,128)(2,1)}, u32[]{:S(2)}, u32[]{:S(2)}) %collective-permute-start) | collective-permute-done | bytes 1048608 | tf_op jit(solution)/shard_map/ppermute | solution.py:134
  56.3 3.8 %fusion.11 = f32[128,1024]{1,0:T(8,128)S(1)} fusion(bf16[2048,1024]{1,0:T(8,128)(2,1)} %collective-permute-done.1, bf16[128,4096]{1,0:T(8,128)(2,1)} %collective-permute-done, s32[]{:T(128)S(6)} %select_n.38), kind=kOutput, calls=%fused_computation.21 | convolution fusion | flops 536870912 | bytes 5242884 | tf_op jit(solution)/shard_map/dot_general | solution.py:122
  60.2 3.9 %convolution_add_fusion.2 = f32[128,1024]{1,0:T(8,128)} fusion(f32[128,1024]{1,0:T(8,128)S(1)} %fusion.11, bf16[2048,1024]{1,0:T(8,128)(2,1)} %constant_dynamic-update-slice_fusion, bf16[128,4096]{1,0:T(8,128)(2,1)} %collective-permute-done, s32[]{:T(128)S(6)} %select_n.37), kind=kOutput, calls=%fused_computation.10 | convolution fusion | flops 537001984 | bytes 5767172 | tf_op jit(solution)/shard_map/dot_general | solution.py:122
  64.1 14.5 %collective-permute-done.3 = bf16[128,4096]{1,0:T(8,128)(2,1)} collective-permute-done((bf16[128,4096]{1,0:T(8,128)(2,1)S(1)}, bf16[128,4096]{1,0:T(8,128)(2,1)}, u32[]{:S(2)}, u32[]{:S(2)}) %collective-permute-start.3) | collective-permute-done | bytes 1048608 | tf_op jit(solution)/shard_map/ppermute | solution.py:134
  78.6 3.1 %fusion.8 = f32[128,1024]{1,0:T(8,128)S(1)} fusion(bf16[2048,1024]{1,0:T(8,128)(2,1)} %collective-permute-done.1, bf16[128,4096]{1,0:T(8,128)(2,1)} %collective-permute-done.3, s32[]{:T(128)S(6)} %select_n.38), kind=kOutput, calls=%fused_computation.18 | convolution fusion | flops 536870912 | bytes 5242884 | tf_op jit(solution)/shard_map/dot_general | solution.py:122
  81.7 3.1 %convolution_add_fusion.1 = f32[128,1024]{1,0:T(8,128)S(1)} fusion(f32[128,1024]{1,0:T(8,128)S(1)} %fusion.8, bf16[2048,1024]{1,0:T(8,128)(2,1)} %constant_dynamic-update-slice_fusion, bf16[128,4096]{1,0:T(8,128)(2,1)} %collective-permute-done.3, s32[]{:T(128)S(6)} %select_n.37), kind=kOutput, calls=%fused_computation.9 | convolution fusion | flops 537001984 | bytes 5767172 | tf_op jit(solution)/shard_map/dot_general | solution.py:122
  84.8 3.0 %collective-permute-start.4 = (f32[128,1024]{1,0:T(8,128)S(1)}, f32[128,1024]{1,0:T(8,128)S(1)}, u32[]{:S(2)}, u32[]{:S(2)}) collective-permute-start(f32[128,1024]{1,0:T(8,128)S(1)} %convolution_add_fusion.1), channel_id=1, source_target_pairs={{0,65},{1,64},{2,67},{3,66},{4,69},{5,68},{6,71},{7,70},{8,73},{9,... | collective-permute-start | bytes 1572872 | tf_op jit(solution)/shard_map/ppermute | solution.py:137
  87.8 0.3 collective-permute-start.2
  88.1 4.8 %fusion.4 = f32[256,1024]{1,0:T(8,128)} fusion(bf16[2048,1024]{1,0:T(8,128)(2,1)} %constant_dynamic-update-slice_fusion, bf16[256,8192]{1,0:T(8,128)(2,1)} %copy-done.1, s32[]{:T(128)S(6)} %select_n.35), kind=kOutput, calls=%fused_computation.12 | convolution fusion | flops 1073741824 | bytes 6291460 | tf_op jit(solution)/shard_map/dot_general | solution.py:122
  92.9 4.0 %convolution_add_fusion = f32[256,1024]{1,0:T(8,128)S(1)} fusion(f32[256,1024]{1,0:T(8,128)} %fusion.4, bf16[2048,1024]{1,0:T(8,128)(2,1)} %collective-permute-done.1, bf16[256,8192]{1,0:T(8,128)(2,1)} %copy-done.1, s32[]{:T(128)S(6)} %select_n.36), kind=kOutput, calls=%fused_computation.8 | convolution fusion | flops 1074003968 | bytes 7340036 | tf_op jit(solution)/shard_map/dot_general | solution.py:122
  97.0 3.9 %collective-permute-done.4 = f32[128,1024]{1,0:T(8,128)S(1)} collective-permute-done((f32[128,1024]{1,0:T(8,128)S(1)}, f32[128,1024]{1,0:T(8,128)S(1)}, u32[]{:S(2)}, u32[]{:S(2)}) %collective-permute-start.4) | collective-permute-done | bytes 524320 | tf_op jit(solution)/shard_map/ppermute | solution.py:137
  100.9 10.2 %collective-permute-done.2 = f32[128,1024]{1,0:T(8,128)S(1)} collective-permute-done((f32[128,1024]{1,0:T(8,128)}, f32[128,1024]{1,0:T(8,128)S(1)}, u32[]{:S(2)}, u32[]{:S(2)}) %collective-permute-start.2) | collective-permute-done | bytes 524320 | tf_op jit(solution)/shard_map/ppermute | solution.py:137
  111.1 0.2 fusion.6
  111.3 0.2 convert_element_type.39
  111.4 0.2 copy.15
  111.6 3.2 %broadcast_in_dim.6 = bf16[128,2,4,8,128]{4,1,0,3,2:T(2,128)(2,1)} broadcast(bf16[128,2,4,128]{3,1,0,2:T(2,128)(2,1)S(1)} %copy.15), dimensions={0,1,2,4} | broadcast | bytes 2359296 | tf_op jit(solution)/shard_map/broadcast_in_dim | solution.py:140
  114.9 7.1 %all-to-all-start.1 = ((bf16[128,2,32,128]{3,1,0,2:T(2,128)(2,1)}), bf16[128,2,32,128]{3,1,0,2:T(2,128)(2,1)S(1)}, u32[]{:S(2)}, u32[]{:S(2)}) async-start(bf16[128,2,32,128]{3,1,0,2:T(2,128)(2,1)} %bitcast.45), calls=%async_computation.1 | async-start | bytes 4194304 | tf_op jit(solution)/shard_map/all_to_all | solution.py:142
  122.0 0.2 convert_element_type.41
  122.1 0.2 copy.16
  122.3 28.1 %all-to-all-done.1 = bf16[128,2,32,128]{3,1,0,2:T(2,128)(2,1)S(1)} async-done(((bf16[128,2,32,128]{3,1,0,2:T(2,128)(2,1)}), bf16[128,2,32,128]{3,1,0,2:T(2,128)(2,1)S(1)}, u32[]{:S(2)}, u32[]{:S(2)}) %all-to-all-start.1) | async-done | bytes 2097184 | tf_op jit(solution)/shard_map/all_to_all | solution.py:142
  150.4 3.2 %broadcast_in_dim.7 = bf16[128,2,4,8,128]{4,1,0,3,2:T(2,128)(2,1)} broadcast(bf16[128,2,4,128]{3,1,0,2:T(2,128)(2,1)S(1)} %copy.16), dimensions={0,1,2,4} | broadcast | bytes 2359296 | tf_op jit(solution)/shard_map/broadcast_in_dim | solution.py:140
  153.6 4.8 %all-to-all-start.2 = ((bf16[128,2,32,128]{3,1,0,2:T(2,128)(2,1)}), bf16[128,2,32,128]{3,1,0,2:T(2,128)(2,1)}, u32[]{:S(2)}, u32[]{:S(2)}) async-start(bf16[128,2,32,128]{3,1,0,2:T(2,128)(2,1)} %bitcast.44), calls=%async_computation.2 | async-start | bytes 4194304 | tf_op jit(solution)/shard_map/all_to_all | solution.py:142
  158.4 0.1 copy.13
  158.5 0.1 squeeze.8
  158.6 0.6 fusion.15.lists_ref
  159.2 1.7 bitcast_dynamic-update-slice_fusion.1
  160.9 23.7 %all-to-all-done.2 = bf16[128,2,32,128]{3,1,0,2:T(2,128)(2,1)} async-done(((bf16[128,2,32,128]{3,1,0,2:T(2,128)(2,1)}), bf16[128,2,32,128]{3,1,0,2:T(2,128)(2,1)}, u32[]{:S(2)}, u32[]{:S(2)}) %all-to-all-start.2) | async-done | bytes 2097184 | tf_op jit(solution)/shard_map/all_to_all | solution.py:142
  184.6 3.2 %bitcast_dynamic-update-slice_fusion.v_ref = bf16[8192,256]{1,0:T(8,128)(2,1)} fusion(bf16[8192,256]{1,0:T(8,128)(2,1)} %bitcast_dynamic-update-slice_fusion.1, bf16[512,8,2,128]{3,2,1,0:T(2,128)(2,1)} %bitcast.27), kind=kLoop, calls=%fused_computation.5 | loop fusion | bytes 4194304 | tf_op jit(solution)/shard_map/concatenate | solution.py:143
  187.8 1.7 slice_bitcast_fusion
  189.6 3.0 %copy.17.kt_ref = bf16[128,8192]{1,0:T(8,128)(2,1)} copy(bf16[128,8192]{0,1:T(8,128)(2,1)S(1)} %slice_bitcast_fusion) | data formatting | bytes 4194304 | tf_op jit(solution)/shard_map/transpose | solution.py:146
  192.5 26.1 %shard_map.73 = bf16[8192,128]{1,0:T(8,128)(2,1)} custom-call(s32[768]{0:T(1024)} %fusion.15.lists_ref, s32[64]{0:T(128)} %bitcast.49, bf16[8192,128]{1,0:T(8,128)(2,1)} %bitcast.41, bf16[128,8192]{1,0:T(8,128)(2,1)} %copy.17.kt_ref, bf16[8192,256]{1,0:T(8,128)(2,1)} %bitcast_dynamic-update-slice_fusion.v_ref), custom_call_target="tpu_custom_call" | custom-call | tf_op jit(solution)/shard_map/pallas_call | solution.py:63
  218.6 32.1 %all_to_all.65 = bf16[32,256,128]{2,1,0:T(8,128)(2,1)S(1)} all-to-all(bf16[32,256,128]{2,1,0:T(8,128)(2,1)} %bitcast.42), channel_id=1, replica_groups=mesh['zh'=2,'core'=2,'x'=4,'y'=4,'zl'=2] {'x','y','zl'}, dimensions={0} | all-to-all | bytes 4194304 | tf_op jit(solution)/shard_map/all_to_all | solution.py:151
  250.7 1.4 copy.18
  252.1 2.3 broadcast_in_dim.8
  (13 shorter events, 0.0 us)
Async XLA Ops:
  4.2 52.1 %all-to-all-start = ((bf16[256,32,128]{2,0,1:T(8,128)(2,1)}), bf16[256,32,128]{2,0,1:T(8,128)(2,1)S(1)}, u32[]{:S(2)}, u32[]{:S(2)}) async-start(bf16[256,32,128]{2,0,1:T(8,128)(2,1)} %copy.14), calls=%async_computation | async-start | bytes 4194304 | tf_op jit(solution)/shard_map/all_to_all | solution.py:104
  13.0 6.3 %copy-start = (bf16[1,256,8192]{2,1,0:T(8,128)(2,1)S(1)}, bf16[1,256,8192]{2,1,0:T(8,128)(2,1)}, u32[]{:S(2)}) copy-start(bf16[1,256,8192]{2,1,0:T(8,128)(2,1)} %param.7) | copy-start | bytes 12582916
  16.2 4.0 %copy-start.3 = (bf16[8192]{0:T(1024)(128)(2,1)S(1)}, bf16[8192]{0:T(1024)(128)(2,1)}, u32[]{:S(2)}) copy-start(bf16[8192]{0:T(1024)(128)(2,1)} %param.8) | copy-start | bytes 49156
  19.3 37.0 %collective-permute-start.1 = (bf16[2048,1024]{1,0:T(8,128)(2,1)}, bf16[2048,1024]{1,0:T(8,128)(2,1)}, u32[]{:S(2)}, u32[]{:S(2)}) collective-permute-start(bf16[2048,1024]{1,0:T(8,128)(2,1)} %constant_dynamic-update-slice_fusion), channel_id=1, source_target_pairs={{0,32},{32,0},{1,33},{33,1},{2,34},{34,2},{3,35},{35,3},{4,36},{36... | collective-permute-start | bytes 12582920 | tf_op jit(solution)/shard_map/ppermute | solution.py:117
  21.5 2.0 copy-start.1
  28.1 28.2 %collective-permute-start = (bf16[128,4096]{1,0:T(8,128)(2,1)}, bf16[128,4096]{1,0:T(8,128)(2,1)}, u32[]{:S(2)}, u32[]{:S(2)}) collective-permute-start(bf16[128,4096]{1,0:T(8,128)(2,1)} %constant_dynamic-slice_fusion.1), channel_id=1, source_target_pairs={{0,65},{1,64},{2,67},{3,66},{4,69},{5,68},{6,71},{7,70},{8,73},{9,... | collective-permute-start | bytes 3145736 | tf_op jit(solution)/shard_map/ppermute | solution.py:134
  33.3 45.3 %collective-permute-start.3 = (bf16[128,4096]{1,0:T(8,128)(2,1)S(1)}, bf16[128,4096]{1,0:T(8,128)(2,1)}, u32[]{:S(2)}, u32[]{:S(2)}) collective-permute-start(bf16[128,4096]{1,0:T(8,128)(2,1)S(1)} %constant_dynamic-slice_fusion), channel_id=1, source_target_pairs={{0,65},{1,64},{2,67},{3,66},{4,69},{5,68},{6,71},{7,70},{8,73},{9,... | collective-permute-start | bytes 3145736 | tf_op jit(solution)/shard_map/ppermute | solution.py:134
  56.3 7.7 %copy-start.2 = (bf16[256,32,128]{2,0,1:T(8,128)(2,1)}, bf16[256,32,128]{2,0,1:T(8,128)(2,1)S(1)}, u32[]{:S(2)}) copy-start(bf16[256,32,128]{2,0,1:T(8,128)(2,1)S(1)} %all-to-all-done) | copy-start | bytes 6291460
  84.8 16.1 %collective-permute-start.4 = (f32[128,1024]{1,0:T(8,128)S(1)}, f32[128,1024]{1,0:T(8,128)S(1)}, u32[]{:S(2)}, u32[]{:S(2)}) collective-permute-start(f32[128,1024]{1,0:T(8,128)S(1)} %convolution_add_fusion.1), channel_id=1, source_target_pairs={{0,65},{1,64},{2,67},{3,66},{4,69},{5,68},{6,71},{7,70},{8,73},{9,... | collective-permute-start | bytes 1572872 | tf_op jit(solution)/shard_map/ppermute | solution.py:137
  87.8 23.2 %collective-permute-start.2 = (f32[128,1024]{1,0:T(8,128)}, f32[128,1024]{1,0:T(8,128)S(1)}, u32[]{:S(2)}, u32[]{:S(2)}) collective-permute-start(f32[128,1024]{1,0:T(8,128)} %convolution_add_fusion.2), channel_id=1, source_target_pairs={{0,65},{1,64},{2,67},{3,66},{4,69},{5,68},{6,71},{7,70},{8,73},{9,... | collective-permute-start | bytes 1572872 | tf_op jit(solution)/shard_map/ppermute | solution.py:137
  114.9 35.5 %all-to-all-start.1 = ((bf16[128,2,32,128]{3,1,0,2:T(2,128)(2,1)}), bf16[128,2,32,128]{3,1,0,2:T(2,128)(2,1)S(1)}, u32[]{:S(2)}, u32[]{:S(2)}) async-start(bf16[128,2,32,128]{3,1,0,2:T(2,128)(2,1)} %bitcast.45), calls=%async_computation.1 | async-start | bytes 4194304 | tf_op jit(solution)/shard_map/all_to_all | solution.py:142
  121.9 36.5 %copy-start.4 = (s32[1,1,64,12]{2,1,3,0:T(1,128)S(1)}, s32[1,1,64,12]{2,1,3,0:T(1,128)}, u32[]{:S(2)}) copy-start(s32[1,1,64,12]{2,1,3,0:T(1,128)} %param.12) | copy-start | bytes 9220
  153.6 31.0 %all-to-all-start.2 = ((bf16[128,2,32,128]{3,1,0,2:T(2,128)(2,1)}), bf16[128,2,32,128]{3,1,0,2:T(2,128)(2,1)}, u32[]{:S(2)}, u32[]{:S(2)}) async-start(bf16[128,2,32,128]{3,1,0,2:T(2,128)(2,1)} %bitcast.44), calls=%async_computation.2 | async-start | bytes 4194304 | tf_op jit(solution)/shard_map/all_to_all | solution.py:142

commit v11 on v10

--- a/solution.py
+++ b/solution.py
@@ -127,7 +127,6 @@
     copies_per_head = ctx_size // KVH
     chunk_rows = local_rows // CHUNKS
     kv_chunks = []
-    own_half = half_sum(normed, zh * half_features)
     for chunk in range(CHUNKS):
         rows = normed[chunk * chunk_rows : (chunk + 1) * chunk_rows]
         far_features = lax.dynamic_slice_in_dim(rows, (1 - zh) * half_features, half_features, axis=1)
@@ -135,7 +134,7 @@
         if chunk == 0:
             head_queries, partner_rows = lax.optimization_barrier((head_queries, partner_rows))
         from_partner = lax.ppermute(half_sum(partner_rows, 0), ALL_AXES, partner_pairs)
-        summed = own_half[chunk * chunk_rows : (chunk + 1) * chunk_rows] + from_partner
+        summed = half_sum(rows, zh * half_features) + from_partner
         paired = summed.reshape(chunk_rows, 2, KVH, 1, HD).astype(jnp.bfloat16)
         widened = jnp.broadcast_to(paired, (chunk_rows, 2, KVH, copies_per_head, HD))
         widened = widened.reshape(chunk_rows, 2, ctx_size, HD)

time: 255 us -> 228 us (0.89)
  waiting for transfers between devices: 103 us -> 71.8 us
  local copies, waits for them, and re-layouts: 39.1 us -> 32 us
  starting transfers between devices: 27.9 us -> 33.3 us
  matrix products: 22.7 us -> 26.3 us
    all_to_all x2, waiting for transfers between devices: 51.8 us -> 23.7 us  [on_device(): lax.all_to_all(widened, CTX_AXES, split_axis=2, concat_axis=0, tiled=True)]
    ppermute x2, waiting for transfers between devices: 37.5 us -> 30.3 us  [on_device(): partner_rows = lax.ppermute(far_features, ALL_AXES, partner_pairs)]
    ppermute x2, waiting for transfers between devices: 14.1 us -> 17.8 us  [on_device(): lax.ppermute(half_sum(partner_rows, 0), ALL_AXES, partner_pairs)]
    unnamed x14 -> x20, local copies, waits for them, and re-layouts: 9.04 us -> 5.71 us
    ppermute x2, starting transfers between devices: 3.32 us -> 5.88 us  [on_device(): lax.ppermute(half_sum(partner_rows, 0), ALL_AXES, partner_pairs)]
    dot_general x3 -> x4, matrix products: 10.9 us -> 13.1 us  [half_sum(): jnp.dot(other, sibling, preferred_element_type=jnp.float32)]
    dot_general x3 -> x4, matrix products: 11.8 us -> 13.2 us  [half_sum(): jnp.dot(own, local_weight, preferred_element_type=jnp.float32)]
  transfers between devices with their start and end apart: 8 -> 8, of which waited for: 6 -> 5; matrix products, arithmetic and copies ran while one was open for 13% -> 16% of each run, Pallas kernels for 0% -> 0%
where the time goes in v11:
time: 228 us; the launch traced here: 227 us
  waiting for transfers between devices  71.8 us (31%)
  starting transfers between devices  33.3 us (15%)
  blocking collectives  32.1 us (14%)
  local copies, waits for them, and re-layouts  32 us (14%)
  matrix products  26.3 us (12%)
  Pallas kernels  26.1 us (11%)
  other arithmetic  5.06 us (2%)
    all_to_all x1, blocking collectives, on_device(): lax.all_to_all(attended_head, CTX_AXES, split_axis=0, concat_axis=1, tile...  32.1 us
    ppermute x2, waiting for transfers between devices, on_device(): partner_rows = lax.ppermute(far_features, ALL_AXES, partner_pairs)  30.3 us
    pallas_call x1, Pallas kernels, attend(): pl.pallas_call(attend_kernel, out_shape=jax.ShapeDtypeStruct((sequence_ro...  26.1 us
    all_to_all x2, waiting for transfers between devices, on_device(): lax.all_to_all(widened, CTX_AXES, split_axis=2, concat_axis=0, tiled=True)  23.7 us
    ppermute x2, waiting for transfers between devices, on_device(): lax.ppermute(half_sum(partner_rows, 0), ALL_AXES, partner_pairs)  17.8 us
    all_to_all x2, starting transfers between devices, on_device(): lax.all_to_all(widened, CTX_AXES, split_axis=2, concat_axis=0, tiled=True)  14.3 us
    dot_general x4, matrix products, half_sum(): jnp.dot(own, local_weight, preferred_element_type=jnp.float32)  13.2 us
    dot_general x4, matrix products, half_sum(): jnp.dot(other, sibling, preferred_element_type=jnp.float32)  13.1 us
  transfers between devices with their start and end apart: 8, of which 5 were waited for; matrix products, arithmetic and copies ran while one was open for 16% of the time, Pallas kernels for 0%

profile of v11, /device:TPU:0, one launch (start us, length us, event | category | flops | bytes accessed | tf_op | source)
XLA Modules:
  0.0 227.0 jit_solution(9446734562996036916)
XLA Ops:
  0.0 3.3 %constant_dynamic-update-slice_fusion.1 = bf16[2048,1024]{1,0:T(8,128)(2,1)} fusion(bf16[2048,512]{1,0:T(8,128)(2,1)} %param.10), kind=kLoop, calls=%fused_computation.29 | loop fusion | bytes 4194304
  3.3 1.5 constant_dynamic-update-slice_fusion
  4.8 0.5 copy.19
  5.3 0.0 copy-start.6
  5.3 2.1 copy.14
  7.5 8.8 %all-to-all-start = ((bf16[256,32,128]{2,0,1:T(8,128)(2,1)}), bf16[256,32,128]{2,0,1:T(8,128)(2,1)S(1)}, u32[]{:S(2)}, u32[]{:S(2)}) async-start(bf16[256,32,128]{2,0,1:T(8,128)(2,1)} %copy.14), calls=%async_computation | async-start | bytes 4194304 | tf_op jit(solution)/shard_map/all_to_all | solution.py:104
  16.3 3.3 %fusion = f32[256]{0:T(256)S(1)} fusion(bf16[1,256,8192]{2,1,0:T(8,128)(2,1)} %param.7), kind=kLoop, calls=%fused_computation.2 | loop fusion | flops 6291200 | bytes 4195328 | tf_op jit(solution)/shard_map/reduce_sum | solution.py:106
  19.5 0.2 copy-done
  19.7 1.2 fusion.2
  20.9 2.4 %fusion.33 = (bf16[128,8192]{1,0:T(8,128)(2,1)}, bf16[128,8192]{1,0:T(8,128)(2,1)}) fusion(bf16[256,8192]{1,0:T(8,128)(2,1)S(1)} %fusion.2), kind=kLoop, calls=%fused_computation.53 | loop fusion | bytes 8388608 | tf_op jit(solution)/shard_map/slice | solution.py:131
  23.3 1.3 constant_dynamic-slice_fusion.1
  24.6 4.0 %collective-permute-start = (bf16[128,4096]{1,0:T(8,128)(2,1)S(1)}, bf16[128,4096]{1,0:T(8,128)(2,1)}, u32[]{:S(2)}, u32[]{:S(2)}) collective-permute-start(bf16[128,4096]{1,0:T(8,128)(2,1)S(1)} %constant_dynamic-slice_fusion.1), channel_id=1, source_target_pairs={{0,65},{1,64},{2,67},{3,66},{4,69},{5,68},{6,71},{7,70},{8,73},{9,... | collective-permute-start | bytes 3145736 | tf_op jit(solution)/shard_map/ppermute | solution.py:133
  28.6 23.4 %collective-permute-done = bf16[128,4096]{1,0:T(8,128)(2,1)} collective-permute-done((bf16[128,4096]{1,0:T(8,128)(2,1)S(1)}, bf16[128,4096]{1,0:T(8,128)(2,1)}, u32[]{:S(2)}, u32[]{:S(2)}) %collective-permute-start) | collective-permute-done | bytes 1048608 | tf_op jit(solution)/shard_map/ppermute | solution.py:133
  52.0 3.8 %fusion.13 = f32[128,1024]{1,0:T(8,128)S(1)} fusion(bf16[2048,1024]{1,0:T(8,128)(2,1)} %collective-permute-done.1, bf16[128,4096]{1,0:T(8,128)(2,1)} %collective-permute-done, s32[]{:T(128)S(6)} %select_n.40), kind=kOutput, calls=%fused_computation.22 | convolution fusion | flops 536870912 | bytes 5242884 | tf_op jit(solution)/shard_map/dot_general | solution.py:122
  55.8 4.1 %convolution_add_fusion.2 = f32[128,1024]{1,0:T(8,128)} fusion(f32[128,1024]{1,0:T(8,128)S(1)} %fusion.13, bf16[2048,1024]{1,0:T(8,128)(2,1)} %constant_dynamic-update-slice_fusion, bf16[128,4096]{1,0:T(8,128)(2,1)} %collective-permute-done, s32[]{:T(128)S(6)} %select_n.39), kind=kOutput, calls=%fused_computation.10 | convolution fusion | flops 537001984 | bytes 5767172 | tf_op jit(solution)/shard_map/dot_general | solution.py:122
  59.9 2.9 %collective-permute-start.2 = (f32[128,1024]{1,0:T(8,128)}, f32[128,1024]{1,0:T(8,128)}, u32[]{:S(2)}, u32[]{:S(2)}) collective-permute-start(f32[128,1024]{1,0:T(8,128)} %convolution_add_fusion.2), channel_id=1, source_target_pairs={{0,65},{1,64},{2,67},{3,66},{4,69},{5,68},{6,71},{7,70},{8,73},{9,... | collective-permute-start | bytes 1572872 | tf_op jit(solution)/shard_map/ppermute | solution.py:136
  62.8 0.1 constant_dynamic-slice_fusion
  62.9 0.4 collective-permute-start.3
  63.3 3.1 %fusion.17 = f32[128,1024]{1,0:T(8,128)S(1)} fusion(bf16[2048,1024]{1,0:T(8,128)(2,1)} %constant_dynamic-update-slice_fusion, bf16[128,8192]{1,0:T(8,128)(2,1)} %get-tuple-element.10, s32[]{:T(128)S(6)} %select_n.37), kind=kOutput, calls=%fused_computation.26 | convolution fusion | flops 536870912 | bytes 5242884 | tf_op jit(solution)/shard_map/dot_general | solution.py:122
  66.3 9.9 %collective-permute-done.2 = f32[128,1024]{1,0:T(8,128)} collective-permute-done((f32[128,1024]{1,0:T(8,128)}, f32[128,1024]{1,0:T(8,128)}, u32[]{:S(2)}, u32[]{:S(2)}) %collective-permute-start.2) | collective-permute-done | bytes 524320 | tf_op jit(solution)/shard_map/ppermute | solution.py:136
  76.2 3.2 %fusion.6 = bf16[128,1024]{1,0:T(8,128)(2,1)S(1)} fusion(f32[128,1024]{1,0:T(8,128)} %collective-permute-done.2, f32[128,1024]{1,0:T(8,128)S(1)} %fusion.17, bf16[2048,1024]{1,0:T(8,128)(2,1)} %collective-permute-done.1, bf16[128,8192]{1,0:T(8,128)(2,1)} %get-tuple-element.10, s32[]{:T(128)S(6)} %select_n.38), kind=kOutput, calls=%fused_computation.15 | convolution fusion | flops 537264128 | bytes 6029316 | tf_op jit(solution)/shard_map/dot_general | solution.py:122
  79.4 0.2 convert_element_type.39
  79.6 0.2 copy.15
  79.8 3.2 %broadcast_in_dim.6 = bf16[128,2,4,8,128]{4,1,0,3,2:T(2,128)(2,1)} broadcast(bf16[128,2,4,128]{3,1,0,2:T(2,128)(2,1)S(1)} %copy.15), dimensions={0,1,2,4} | broadcast | bytes 2359296 | tf_op jit(solution)/shard_map/broadcast_in_dim | solution.py:139
  83.0 7.1 %all-to-all-start.1 = ((bf16[128,2,32,128]{3,1,0,2:T(2,128)(2,1)}), bf16[128,2,32,128]{3,1,0,2:T(2,128)(2,1)S(1)}, u32[]{:S(2)}, u32[]{:S(2)}) async-start(bf16[128,2,32,128]{3,1,0,2:T(2,128)(2,1)} %bitcast.46), calls=%async_computation.1 | async-start | bytes 4194304 | tf_op jit(solution)/shard_map/all_to_all | solution.py:141
  90.1 7.0 %collective-permute-done.3 = bf16[128,4096]{1,0:T(8,128)(2,1)} collective-permute-done((bf16[128,4096]{1,0:T(8,128)(2,1)S(1)}, bf16[128,4096]{1,0:T(8,128)(2,1)}, u32[]{:S(2)}, u32[]{:S(2)}) %collective-permute-start.3) | collective-permute-done | bytes 1048608 | tf_op jit(solution)/shard_map/ppermute | solution.py:133
  97.1 3.1 %fusion.7 = f32[128,1024]{1,0:T(8,128)S(1)} fusion(bf16[2048,1024]{1,0:T(8,128)(2,1)} %collective-permute-done.1, bf16[128,4096]{1,0:T(8,128)(2,1)} %collective-permute-done.3, s32[]{:T(128)S(6)} %select_n.40), kind=kOutput, calls=%fused_computation.16 | convolution fusion | flops 536870912 | bytes 5242884 | tf_op jit(solution)/shard_map/dot_general | solution.py:122
  100.1 3.2 %convolution_add_fusion = f32[128,1024]{1,0:T(8,128)S(1)} fusion(f32[128,1024]{1,0:T(8,128)S(1)} %fusion.7, bf16[2048,1024]{1,0:T(8,128)(2,1)} %constant_dynamic-update-slice_fusion, bf16[128,4096]{1,0:T(8,128)(2,1)} %collective-permute-done.3, s32[]{:T(128)S(6)} %select_n.39), kind=kOutput, calls=%fused_computation.8 | convolution fusion | flops 537001984 | bytes 5767172 | tf_op jit(solution)/shard_map/dot_general | solution.py:122
  103.4 2.9 %collective-permute-start.4 = (f32[128,1024]{1,0:T(8,128)S(1)}, f32[128,1024]{1,0:T(8,128)S(1)}, u32[]{:S(2)}, u32[]{:S(2)}) collective-permute-start(f32[128,1024]{1,0:T(8,128)S(1)} %convolution_add_fusion), channel_id=1, source_target_pairs={{0,65},{1,64},{2,67},{3,66},{4,69},{5,68},{6,71},{7,70},{8,73},{9,... | collective-permute-start | bytes 1572872 | tf_op jit(solution)/shard_map/ppermute | solution.py:136
  106.3 2.9 %fusion.11 = f32[128,1024]{1,0:T(8,128)S(1)} fusion(bf16[2048,1024]{1,0:T(8,128)(2,1)} %constant_dynamic-update-slice_fusion, bf16[128,8192]{1,0:T(8,128)(2,1)S(1)} %copy-done.3, s32[]{:T(128)S(6)} %select_n.37), kind=kOutput, calls=%fused_computation.20 | convolution fusion | flops 536870912 | bytes 5242884 | tf_op jit(solution)/shard_map/dot_general | solution.py:122
  109.2 8.0 %collective-permute-done.4 = f32[128,1024]{1,0:T(8,128)S(1)} collective-permute-done((f32[128,1024]{1,0:T(8,128)S(1)}, f32[128,1024]{1,0:T(8,128)S(1)}, u32[]{:S(2)}, u32[]{:S(2)}) %collective-permute-start.4) | collective-permute-done | bytes 524320 | tf_op jit(solution)/shard_map/ppermute | solution.py:136
  117.2 3.0 %fusion.5 = bf16[128,1024]{1,0:T(8,128)(2,1)S(1)} fusion(f32[128,1024]{1,0:T(8,128)S(1)} %collective-permute-done.4, f32[128,1024]{1,0:T(8,128)S(1)} %fusion.11, bf16[2048,1024]{1,0:T(8,128)(2,1)} %collective-permute-done.1, bf16[128,8192]{1,0:T(8,128)(2,1)S(1)} %copy-done.3, s32[]{:T(128)S(6)} %select_n.38), kind=kOutput, calls=%fused_computation.14 | convolution fusion | flops 537264128 | bytes 6029316 | tf_op jit(solution)/shard_map/dot_general | solution.py:122
  120.2 0.2 convert_element_type.41
  120.4 0.2 copy.16
  120.6 3.2 %broadcast_in_dim.7 = bf16[128,2,4,8,128]{4,1,0,3,2:T(2,128)(2,1)} broadcast(bf16[128,2,4,128]{3,1,0,2:T(2,128)(2,1)S(1)} %copy.16), dimensions={0,1,2,4} | broadcast | bytes 2359296 | tf_op jit(solution)/shard_map/broadcast_in_dim | solution.py:139
  123.8 7.2 %all-to-all-start.2 = ((bf16[128,2,32,128]{3,1,0,2:T(2,128)(2,1)}), bf16[128,2,32,128]{3,1,0,2:T(2,128)(2,1)}, u32[]{:S(2)}, u32[]{:S(2)}) async-start(bf16[128,2,32,128]{3,1,0,2:T(2,128)(2,1)} %bitcast.47), calls=%async_computation.2 | async-start | bytes 4194304 | tf_op jit(solution)/shard_map/all_to_all | solution.py:141
  131.0 0.1 copy.13
  131.1 0.1 squeeze.8
  131.2 0.6 fusion.20.lists_ref
  131.8 1.7 bitcast_dynamic-update-slice_fusion.1
  133.5 23.7 %all-to-all-done.2 = bf16[128,2,32,128]{3,1,0,2:T(2,128)(2,1)} async-done(((bf16[128,2,32,128]{3,1,0,2:T(2,128)(2,1)}), bf16[128,2,32,128]{3,1,0,2:T(2,128)(2,1)}, u32[]{:S(2)}, u32[]{:S(2)}) %all-to-all-start.2) | async-done | bytes 2097184 | tf_op jit(solution)/shard_map/all_to_all | solution.py:141
  157.2 3.2 %bitcast_dynamic-update-slice_fusion.v_ref = bf16[8192,256]{1,0:T(8,128)(2,1)} fusion(bf16[8192,256]{1,0:T(8,128)(2,1)} %bitcast_dynamic-update-slice_fusion.1, bf16[512,8,2,128]{3,2,1,0:T(2,128)(2,1)} %bitcast.27), kind=kLoop, calls=%fused_computation.5 | loop fusion | bytes 4194304 | tf_op jit(solution)/shard_map/concatenate | solution.py:142
  160.5 1.7 slice_bitcast_fusion
  162.2 2.9 %copy.17.kt_ref = bf16[128,8192]{1,0:T(8,128)(2,1)} copy(bf16[128,8192]{0,1:T(8,128)(2,1)S(1)} %slice_bitcast_fusion) | data formatting | bytes 4194304 | tf_op jit(solution)/shard_map/transpose | solution.py:145
  165.1 26.1 %shard_map.73 = bf16[8192,128]{1,0:T(8,128)(2,1)} custom-call(s32[768]{0:T(1024)} %fusion.20.lists_ref, s32[64]{0:T(128)} %bitcast.51, bf16[8192,128]{1,0:T(8,128)(2,1)} %bitcast.43, bf16[128,8192]{1,0:T(8,128)(2,1)} %copy.17.kt_ref, bf16[8192,256]{1,0:T(8,128)(2,1)} %bitcast_dynamic-update-slice_fusion.v_ref), custom_call_target="tpu_custom_call" | custom-call | tf_op jit(solution)/shard_map/pallas_call | solution.py:63
  191.2 32.1 %all_to_all.65 = bf16[32,256,128]{2,1,0:T(8,128)(2,1)S(1)} all-to-all(bf16[32,256,128]{2,1,0:T(8,128)(2,1)} %bitcast.44), channel_id=1, replica_groups=mesh['zh'=2,'core'=2,'x'=4,'y'=4,'zl'=2] {'x','y','zl'}, dimensions={0} | all-to-all | bytes 4194304 | tf_op jit(solution)/shard_map/all_to_all | solution.py:150
  223.4 1.4 copy.18
  224.7 2.3 %broadcast_in_dim.8 = bf16[1,256,4096]{2,1,0:T(8,128)(2,1)} reshape(bf16[256,32,128]{2,1,0:T(8,128)(2,1)S(1)} %copy.18) | data formatting | bytes 4194304 | tf_op jit(solution)/shard_map/broadcast_in_dim | solution.py:151
  (20 shorter events, 0.1 us)
Async XLA Ops:
  0.0 3.3 %copy-start.4 = (bf16[2048,512]{1,0:T(8,128)(2,1)S(1)}, bf16[2048,512]{1,0:T(8,128)(2,1)}, u32[]{:S(2)}) copy-start(bf16[2048,512]{1,0:T(8,128)(2,1)} %param.11) | copy-start | bytes 6291460
  0.0 4.8 %copy-start.5 = (bf16[1,256,4096]{2,1,0:T(8,128)(2,1)S(1)}, bf16[1,256,4096]{2,1,0:T(8,128)(2,1)}, u32[]{:S(2)}) copy-start(bf16[1,256,4096]{2,1,0:T(8,128)(2,1)} %param.9) | copy-start | bytes 6291460
  4.8 47.2 %collective-permute-start.1 = (bf16[2048,1024]{1,0:T(8,128)(2,1)}, bf16[2048,1024]{1,0:T(8,128)(2,1)}, u32[]{:S(2)}, u32[]{:S(2)}) collective-permute-start(bf16[2048,1024]{1,0:T(8,128)(2,1)} %constant_dynamic-update-slice_fusion), channel_id=1, source_target_pairs={{0,32},{32,0},{1,33},{33,1},{2,34},{34,2},{3,35},{35,3},{4,36},{36... | collective-permute-start | bytes 12582920 | tf_op jit(solution)/shard_map/ppermute | solution.py:117
  5.3 10.9 %copy-start.6 = (bf16[8192]{0:T(1024)(128)(2,1)S(1)}, bf16[8192]{0:T(1024)(128)(2,1)}, u32[]{:S(2)}) copy-start(bf16[8192]{0:T(1024)(128)(2,1)} %param.8) | copy-start | bytes 49156
  7.5 44.5 %all-to-all-start = ((bf16[256,32,128]{2,0,1:T(8,128)(2,1)}), bf16[256,32,128]{2,0,1:T(8,128)(2,1)S(1)}, u32[]{:S(2)}, u32[]{:S(2)}) async-start(bf16[256,32,128]{2,0,1:T(8,128)(2,1)} %copy.14), calls=%async_computation | async-start | bytes 4194304 | tf_op jit(solution)/shard_map/all_to_all | solution.py:104
  16.3 3.5 %copy-start = (bf16[1,256,8192]{2,1,0:T(8,128)(2,1)S(1)}, bf16[1,256,8192]{2,1,0:T(8,128)(2,1)}, u32[]{:S(2)}) copy-start(bf16[1,256,8192]{2,1,0:T(8,128)(2,1)} %param.7) | copy-start | bytes 12582916
  24.6 27.4 %collective-permute-start = (bf16[128,4096]{1,0:T(8,128)(2,1)S(1)}, bf16[128,4096]{1,0:T(8,128)(2,1)}, u32[]{:S(2)}, u32[]{:S(2)}) collective-permute-start(bf16[128,4096]{1,0:T(8,128)(2,1)S(1)} %constant_dynamic-slice_fusion.1), channel_id=1, source_target_pairs={{0,65},{1,64},{2,67},{3,66},{4,69},{5,68},{6,71},{7,70},{8,73},{9,... | collective-permute-start | bytes 3145736 | tf_op jit(solution)/shard_map/ppermute | solution.py:133
  52.0 7.9 %copy-start.1 = (bf16[256,32,128]{2,0,1:T(8,128)(2,1)}, bf16[256,32,128]{2,0,1:T(8,128)(2,1)S(1)}, u32[]{:S(2)}) copy-start(bf16[256,32,128]{2,0,1:T(8,128)(2,1)S(1)} %all-to-all-done) | copy-start | bytes 6291460
  55.8 7.0 %copy-start.2 = (bf16[128,8192]{1,0:T(8,128)(2,1)S(1)}, bf16[128,8192]{1,0:T(8,128)(2,1)}, u32[]{:S(2)}) copy-start(bf16[128,8192]{1,0:T(8,128)(2,1)} %get-tuple-element.9) | copy-start | bytes 6291460
  59.9 16.3 %collective-permute-start.2 = (f32[128,1024]{1,0:T(8,128)}, f32[128,1024]{1,0:T(8,128)}, u32[]{:S(2)}, u32[]{:S(2)}) collective-permute-start(f32[128,1024]{1,0:T(8,128)} %convolution_add_fusion.2), channel_id=1, source_target_pairs={{0,65},{1,64},{2,67},{3,66},{4,69},{5,68},{6,71},{7,70},{8,73},{9,... | collective-permute-start | bytes 1572872 | tf_op jit(solution)/shard_map/ppermute | solution.py:136
  62.9 34.2 %collective-permute-start.3 = (bf16[128,4096]{1,0:T(8,128)(2,1)S(1)}, bf16[128,4096]{1,0:T(8,128)(2,1)}, u32[]{:S(2)}, u32[]{:S(2)}) collective-permute-start(bf16[128,4096]{1,0:T(8,128)(2,1)S(1)} %constant_dynamic-slice_fusion), channel_id=1, source_target_pairs={{0,65},{1,64},{2,67},{3,66},{4,69},{5,68},{6,71},{7,70},{8,73},{9,... | collective-permute-start | bytes 3145736 | tf_op jit(solution)/shard_map/ppermute | solution.py:133
  83.0 37.5 %all-to-all-start.1 = ((bf16[128,2,32,128]{3,1,0,2:T(2,128)(2,1)}), bf16[128,2,32,128]{3,1,0,2:T(2,128)(2,1)S(1)}, u32[]{:S(2)}, u32[]{:S(2)}) async-start(bf16[128,2,32,128]{3,1,0,2:T(2,128)(2,1)} %bitcast.46), calls=%async_computation.1 | async-start | bytes 4194304 | tf_op jit(solution)/shard_map/all_to_all | solution.py:141
  100.1 6.2 %copy-start.3 = (bf16[128,8192]{1,0:T(8,128)(2,1)S(1)}, bf16[128,8192]{1,0:T(8,128)(2,1)}, u32[]{:S(2)}) copy-start(bf16[128,8192]{1,0:T(8,128)(2,1)} %get-tuple-element.9) | copy-start | bytes 6291460
  103.4 13.8 %collective-permute-start.4 = (f32[128,1024]{1,0:T(8,128)S(1)}, f32[128,1024]{1,0:T(8,128)S(1)}, u32[]{:S(2)}, u32[]{:S(2)}) collective-permute-start(f32[128,1024]{1,0:T(8,128)S(1)} %convolution_add_fusion), channel_id=1, source_target_pairs={{0,65},{1,64},{2,67},{3,66},{4,69},{5,68},{6,71},{7,70},{8,73},{9,... | collective-permute-start | bytes 1572872 | tf_op jit(solution)/shard_map/ppermute | solution.py:136
  120.2 10.9 %copy-start.7 = (s32[1,1,64,12]{2,1,3,0:T(1,128)S(1)}, s32[1,1,64,12]{2,1,3,0:T(1,128)}, u32[]{:S(2)}) copy-start(s32[1,1,64,12]{2,1,3,0:T(1,128)} %param.12) | copy-start | bytes 9220
  123.8 33.4 %all-to-all-start.2 = ((bf16[128,2,32,128]{3,1,0,2:T(2,128)(2,1)}), bf16[128,2,32,128]{3,1,0,2:T(2,128)(2,1)}, u32[]{:S(2)}, u32[]{:S(2)}) async-start(bf16[128,2,32,128]{3,1,0,2:T(2,128)(2,1)} %bitcast.47), calls=%async_computation.2 | async-start | bytes 4194304 | tf_op jit(solution)/shard_map/all_to_all | solution.py:141

commit v12 on v11

--- a/solution.py
+++ b/solution.py
@@ -101,7 +101,6 @@
 
 
 def on_device(hidden, norm_gain, queries, key_weight, value_weight, block_lists, block_counts):
-    head_queries = lax.all_to_all(queries[0], CTX_AXES, split_axis=1, concat_axis=0, tiled=True)
     upcast = hidden[0].astype(jnp.float32)
     mean_square = jnp.mean(upcast * upcast, axis=-1, keepdims=True)
     normed = (upcast * lax.rsqrt(mean_square + 1e-05) * norm_gain.astype(jnp.float32)).astype(
@@ -132,12 +131,15 @@
         far_features = lax.dynamic_slice_in_dim(rows, (1 - zh) * half_features, half_features, axis=1)
         partner_rows = lax.ppermute(far_features, ALL_AXES, partner_pairs)
         if chunk == 0:
-            head_queries, partner_rows = lax.optimization_barrier((head_queries, partner_rows))
+            local_queries, partner_rows = lax.optimization_barrier((queries[0], partner_rows))
+            head_queries = lax.all_to_all(local_queries, CTX_AXES, split_axis=1, concat_axis=0, tiled=True)
         from_partner = lax.ppermute(half_sum(partner_rows, 0), ALL_AXES, partner_pairs)
         summed = half_sum(rows, zh * half_features) + from_partner
         paired = summed.reshape(chunk_rows, 2, KVH, 1, HD).astype(jnp.bfloat16)
         widened = jnp.broadcast_to(paired, (chunk_rows, 2, KVH, copies_per_head, HD))
         widened = widened.reshape(chunk_rows, 2, ctx_size, HD)
+        if chunk == 0:
+            head_queries, widened = lax.optimization_barrier((head_queries, widened))
         kv_chunks.append(lax.all_to_all(widened, CTX_AXES, split_axis=2, concat_axis=0, tiled=True))
     head_pair = jnp.concatenate(kv_chunks, axis=0)
     sequence_rows = head_queries.shape[0]

time: 228 us -> 233 us (1.022)
  local copies, waits for them, and re-layouts: 32 us -> 41.7 us
  waiting for transfers between devices: 71.8 us -> 68.6 us
    transpose x2, local copies, waits for them, and re-layouts: 4.66 us -> 7.1 us  [on_device(): key_t = kv_rows[:, :HD].T]
    reduce_sum x1, other arithmetic: 3.25 us -> 0.92 us  [on_device(): mean_square = jnp.mean(upcast * upcast, axis=-1, keepdims=True)]
    unnamed x20 -> x19, local copies, waits for them, and re-layouts: 5.71 us -> 7.98 us
  transfers between devices with their start and end apart: 8 -> 8, of which waited for: 5 -> 5; matrix products, arithmetic and copies ran while one was open for 16% -> 19% of each run, Pallas kernels for 0% -> 0%
where the time goes in v12:
time: 233 us; the launch traced here: 232 us
  waiting for transfers between devices  68.6 us (29%)
  local copies, waits for them, and re-layouts  41.7 us (18%)
  starting transfers between devices  33.5 us (14%)
  blocking collectives  32.3 us (14%)
  Pallas kernels  26.1 us (11%)
  matrix products  25.3 us (11%)
  other arithmetic  4.7 us (2%)
    all_to_all x1, blocking collectives, on_device(): lax.all_to_all(attended_head, CTX_AXES, split_axis=0, concat_axis=1, tile...  32.3 us
    ppermute x2, waiting for transfers between devices, on_device(): partner_rows = lax.ppermute(far_features, ALL_AXES, partner_pairs)  29 us
    pallas_call x1, Pallas kernels, attend(): pl.pallas_call(attend_kernel, out_shape=jax.ShapeDtypeStruct((sequence_ro...  26.1 us
    all_to_all x2, waiting for transfers between devices, on_device(): lax.all_to_all(widened, CTX_AXES, split_axis=2, concat_axis=0, tiled=True)  22.1 us
    ppermute x2, waiting for transfers between devices, on_device(): lax.ppermute(half_sum(partner_rows, 0), ALL_AXES, partner_pairs)  17.5 us
    all_to_all x2, starting transfers between devices, on_device(): lax.all_to_all(widened, CTX_AXES, split_axis=2, concat_axis=0, tiled=True)  14.4 us
    dot_general x4, matrix products, half_sum(): jnp.dot(own, local_weight, preferred_element_type=jnp.float32)  13.1 us
    dot_general x4, matrix products, half_sum(): jnp.dot(other, sibling, preferred_element_type=jnp.float32)  12.2 us
  transfers between devices with their start and end apart: 8, of which 5 were waited for; matrix products, arithmetic and copies ran while one was open for 19% of the time, Pallas kernels for 0%

profile of v12, /device:TPU:0, one launch (start us, length us, event | category | flops | bytes accessed | tf_op | source)
XLA Modules:
  0.0 232.3 jit_solution(7283715462161526676)
XLA Ops:
  0.0 3.3 %constant_dynamic-update-slice_fusion.1 = bf16[2048,1024]{1,0:T(8,128)(2,1)} fusion(bf16[2048,512]{1,0:T(8,128)(2,1)} %param.10), kind=kLoop, calls=%fused_computation.30 | loop fusion | bytes 4194304
  3.3 1.6 constant_dynamic-update-slice_fusion
  4.8 0.0 collective-permute-start.1
  4.8 0.9 fusion
  5.8 3.2 %fusion.2 = bf16[256,8192]{1,0:T(8,128)(2,1)} fusion(bf16[1,256,8192]{2,1,0:T(8,128)(2,1)S(1)} %copy-done.1, f32[8192]{0:T(1024)S(1)} %convert_element_type.36, f32[256]{0:T(256)S(1)} %add_rsqrt_fusion), kind=kLoop, calls=%fused_computation.4 | loop fusion | flops 8388608 | bytes 8422400 | tf_op jit(solution)/shard_map/convert_element_type | solution.py:106
  8.9 4.0 %fusion.33 = (bf16[128,8192]{1,0:T(8,128)(2,1)}, bf16[128,8192]{1,0:T(8,128)(2,1)S(1)}) fusion(bf16[256,8192]{1,0:T(8,128)(2,1)} %fusion.2), kind=kLoop, calls=%fused_computation.54 | loop fusion | bytes 8388608 | tf_op jit(solution)/shard_map/slice | solution.py:130
  12.9 1.3 copy-done.4
  14.3 0.1 constant_dynamic-slice_fusion.1
  14.3 4.2 %collective-permute-start = (bf16[128,4096]{1,0:T(8,128)(2,1)S(1)}, bf16[128,4096]{1,0:T(8,128)(2,1)S(1)}, u32[]{:S(2)}, u32[]{:S(2)}) collective-permute-start(bf16[128,4096]{1,0:T(8,128)(2,1)S(1)} %constant_dynamic-slice_fusion.1), channel_id=1, source_target_pairs={{0,65},{1,64},{2,67},{3,66},{4,69},{5,68},{6,71},{7,70},{8,73},{9,... | collective-permute-start | bytes 3145736 | tf_op jit(solution)/shard_map/ppermute | solution.py:132
  18.6 23.8 %collective-permute-done = bf16[128,4096]{1,0:T(8,128)(2,1)S(1)} collective-permute-done((bf16[128,4096]{1,0:T(8,128)(2,1)S(1)}, bf16[128,4096]{1,0:T(8,128)(2,1)S(1)}, u32[]{:S(2)}, u32[]{:S(2)}) %collective-permute-start) | collective-permute-done | bytes 1048608 | tf_op jit(solution)/shard_map/ppermute | solution.py:132
  42.4 1.9 copy_bitcast_fusion
  44.3 7.5 %all-to-all-start = ((bf16[256,32,128]{2,0,1:T(8,128)(2,1)}), bf16[256,32,128]{2,0,1:T(8,128)(2,1)}, u32[]{:S(2)}, u32[]{:S(2)}) async-start(bf16[256,32,128]{2,0,1:T(8,128)(2,1)} %copy_bitcast_fusion), calls=%async_computation | async-start | bytes 4194304 | tf_op jit(solution)/shard_map/all_to_all | solution.py:135
  51.8 2.9 %fusion.13 = f32[128,1024]{1,0:T(8,128)S(1)} fusion(bf16[2048,1024]{1,0:T(8,128)(2,1)} %collective-permute-done.1, bf16[128,4096]{1,0:T(8,128)(2,1)S(1)} %collective-permute-done, s32[]{:T(128)S(6)} %select_n.40), kind=kOutput, calls=%fused_computation.23 | convolution fusion | flops 536870912 | bytes 5242884 | tf_op jit(solution)/shard_map/dot_general | solution.py:121
  54.7 3.9 %convolution_add_fusion.2 = f32[128,1024]{1,0:T(8,128)} fusion(f32[128,1024]{1,0:T(8,128)S(1)} %fusion.13, bf16[2048,1024]{1,0:T(8,128)(2,1)} %constant_dynamic-update-slice_fusion, bf16[128,4096]{1,0:T(8,128)(2,1)S(1)} %collective-permute-done, s32[]{:T(128)S(6)} %select_n.39), kind=kOutput, calls=%fused_computation.11 | convolution fusion | flops 537001984 | bytes 5767172 | tf_op jit(solution)/shard_map/dot_general | solution.py:121
  58.6 4.1 %collective-permute-start.2 = (f32[128,1024]{1,0:T(8,128)}, f32[128,1024]{1,0:T(8,128)}, u32[]{:S(2)}, u32[]{:S(2)}) collective-permute-start(f32[128,1024]{1,0:T(8,128)} %convolution_add_fusion.2), channel_id=1, source_target_pairs={{0,65},{1,64},{2,67},{3,66},{4,69},{5,68},{6,71},{7,70},{8,73},{9,... | collective-permute-start | bytes 1572872 | tf_op jit(solution)/shard_map/ppermute | solution.py:136
  62.7 0.1 constant_dynamic-slice_fusion
  62.8 0.1 collective-permute-start.3
  62.9 3.1 %fusion.17 = f32[128,1024]{1,0:T(8,128)S(1)} fusion(bf16[2048,1024]{1,0:T(8,128)(2,1)} %constant_dynamic-update-slice_fusion, bf16[128,8192]{1,0:T(8,128)(2,1)} %copy-done.4, s32[]{:T(128)S(6)} %select_n.37), kind=kOutput, calls=%fused_computation.27 | convolution fusion | flops 536870912 | bytes 5242884 | tf_op jit(solution)/shard_map/dot_general | solution.py:121
  66.0 9.8 %collective-permute-done.2 = f32[128,1024]{1,0:T(8,128)} collective-permute-done((f32[128,1024]{1,0:T(8,128)}, f32[128,1024]{1,0:T(8,128)}, u32[]{:S(2)}, u32[]{:S(2)}) %collective-permute-start.2) | collective-permute-done | bytes 524320 | tf_op jit(solution)/shard_map/ppermute | solution.py:136
  75.8 3.2 %fusion.6 = bf16[128,1024]{1,0:T(8,128)(2,1)S(1)} fusion(f32[128,1024]{1,0:T(8,128)} %collective-permute-done.2, f32[128,1024]{1,0:T(8,128)S(1)} %fusion.17, bf16[2048,1024]{1,0:T(8,128)(2,1)} %collective-permute-done.1, bf16[128,8192]{1,0:T(8,128)(2,1)} %copy-done.4, s32[]{:T(128)S(6)} %select_n.38), kind=kOutput, calls=%fused_computation.16 | convolution fusion | flops 537264128 | bytes 6029316 | tf_op jit(solution)/shard_map/dot_general | solution.py:121
  79.0 0.9 convert_element_type.39
  79.9 1.2 copy.15
  81.1 3.2 %broadcast_in_dim.6 = bf16[128,2,4,8,128]{4,1,0,3,2:T(2,128)(2,1)} broadcast(bf16[128,2,4,128]{3,1,0,2:T(2,128)(2,1)S(1)} %copy.15), dimensions={0,1,2,4} | broadcast | bytes 2359296 | tf_op jit(solution)/shard_map/broadcast_in_dim | solution.py:139
  84.3 7.2 %all-to-all-start.1 = ((bf16[128,2,32,128]{3,1,0,2:T(2,128)(2,1)}), bf16[128,2,32,128]{3,1,0,2:T(2,128)(2,1)}, u32[]{:S(2)}, u32[]{:S(2)}) async-start(bf16[128,2,32,128]{3,1,0,2:T(2,128)(2,1)} %bitcast.48), calls=%async_computation.1 | async-start | bytes 4194304 | tf_op jit(solution)/shard_map/all_to_all | solution.py:143
  91.5 5.2 %collective-permute-done.3 = bf16[128,4096]{1,0:T(8,128)(2,1)} collective-permute-done((bf16[128,4096]{1,0:T(8,128)(2,1)S(1)}, bf16[128,4096]{1,0:T(8,128)(2,1)}, u32[]{:S(2)}, u32[]{:S(2)}) %collective-permute-start.3) | collective-permute-done | bytes 1048608 | tf_op jit(solution)/shard_map/ppermute | solution.py:132
  96.7 3.1 %fusion.7 = f32[128,1024]{1,0:T(8,128)S(1)} fusion(bf16[2048,1024]{1,0:T(8,128)(2,1)} %collective-permute-done.1, bf16[128,4096]{1,0:T(8,128)(2,1)} %collective-permute-done.3, s32[]{:T(128)S(6)} %select_n.40), kind=kOutput, calls=%fused_computation.17 | convolution fusion | flops 536870912 | bytes 5242884 | tf_op jit(solution)/shard_map/dot_general | solution.py:121
  99.8 3.2 %convolution_add_fusion = f32[128,1024]{1,0:T(8,128)S(1)} fusion(f32[128,1024]{1,0:T(8,128)S(1)} %fusion.7, bf16[2048,1024]{1,0:T(8,128)(2,1)} %constant_dynamic-update-slice_fusion, bf16[128,4096]{1,0:T(8,128)(2,1)} %collective-permute-done.3, s32[]{:T(128)S(6)} %select_n.39), kind=kOutput, calls=%fused_computation.9 | convolution fusion | flops 537001984 | bytes 5767172 | tf_op jit(solution)/shard_map/dot_general | solution.py:121
  103.0 3.2 %collective-permute-start.4 = (f32[128,1024]{1,0:T(8,128)S(1)}, f32[128,1024]{1,0:T(8,128)S(1)}, u32[]{:S(2)}, u32[]{:S(2)}) collective-permute-start(f32[128,1024]{1,0:T(8,128)S(1)} %convolution_add_fusion), channel_id=1, source_target_pairs={{0,65},{1,64},{2,67},{3,66},{4,69},{5,68},{6,71},{7,70},{8,73},{9,... | collective-permute-start | bytes 1572872 | tf_op jit(solution)/shard_map/ppermute | solution.py:136
  106.2 2.9 %fusion.11 = f32[128,1024]{1,0:T(8,128)S(1)} fusion(bf16[2048,1024]{1,0:T(8,128)(2,1)} %constant_dynamic-update-slice_fusion, bf16[128,8192]{1,0:T(8,128)(2,1)S(1)} %copy-done.3, s32[]{:T(128)S(6)} %select_n.37), kind=kOutput, calls=%fused_computation.21 | convolution fusion | flops 536870912 | bytes 5242884 | tf_op jit(solution)/shard_map/dot_general | solution.py:121
  109.1 7.7 %collective-permute-done.4 = f32[128,1024]{1,0:T(8,128)S(1)} collective-permute-done((f32[128,1024]{1,0:T(8,128)S(1)}, f32[128,1024]{1,0:T(8,128)S(1)}, u32[]{:S(2)}, u32[]{:S(2)}) %collective-permute-start.4) | collective-permute-done | bytes 524320 | tf_op jit(solution)/shard_map/ppermute | solution.py:136
  116.8 3.0 %fusion.5 = bf16[128,1024]{1,0:T(8,128)(2,1)S(1)} fusion(f32[128,1024]{1,0:T(8,128)S(1)} %collective-permute-done.4, f32[128,1024]{1,0:T(8,128)S(1)} %fusion.11, bf16[2048,1024]{1,0:T(8,128)(2,1)} %collective-permute-done.1, bf16[128,8192]{1,0:T(8,128)(2,1)S(1)} %copy-done.3, s32[]{:T(128)S(6)} %select_n.38), kind=kOutput, calls=%fused_computation.15 | convolution fusion | flops 537264128 | bytes 6029316 | tf_op jit(solution)/shard_map/dot_general | solution.py:121
  119.8 0.0 copy-start.7
  119.8 0.2 convert_element_type.41
  120.0 0.2 copy.16
  120.2 3.2 %broadcast_in_dim.7 = bf16[128,2,4,8,128]{4,1,0,3,2:T(2,128)(2,1)} broadcast(bf16[128,2,4,128]{3,1,0,2:T(2,128)(2,1)S(1)} %copy.16), dimensions={0,1,2,4} | broadcast | bytes 2359296 | tf_op jit(solution)/shard_map/broadcast_in_dim | solution.py:139
  123.4 7.2 %all-to-all-start.2 = ((bf16[128,2,32,128]{3,1,0,2:T(2,128)(2,1)}), bf16[128,2,32,128]{3,1,0,2:T(2,128)(2,1)}, u32[]{:S(2)}, u32[]{:S(2)}) async-start(bf16[128,2,32,128]{3,1,0,2:T(2,128)(2,1)} %bitcast.49), calls=%async_computation.2 | async-start | bytes 4194304 | tf_op jit(solution)/shard_map/all_to_all | solution.py:143
  130.6 0.1 copy.13
  130.7 0.1 squeeze.10
  130.8 0.6 fusion.20.lists_ref
  131.4 3.3 %bitcast_dynamic-update-slice_fusion.1 = bf16[8192,256]{1,0:T(8,128)(2,1)} fusion(bf16[512,8,2,128]{3,2,1,0:T(2,128)(2,1)} %bitcast.23), kind=kLoop, calls=%fused_computation.6 | loop fusion | bytes 4194304
  134.7 22.1 %all-to-all-done.2 = bf16[128,2,32,128]{3,1,0,2:T(2,128)(2,1)} async-done(((bf16[128,2,32,128]{3,1,0,2:T(2,128)(2,1)}), bf16[128,2,32,128]{3,1,0,2:T(2,128)(2,1)}, u32[]{:S(2)}, u32[]{:S(2)}) %all-to-all-start.2) | async-done | bytes 2097184 | tf_op jit(solution)/shard_map/all_to_all | solution.py:143
  156.8 3.2 %bitcast_dynamic-update-slice_fusion.v_ref = bf16[8192,256]{1,0:T(8,128)(2,1)} fusion(bf16[8192,256]{1,0:T(8,128)(2,1)} %bitcast_dynamic-update-slice_fusion.1, bf16[512,8,2,128]{3,2,1,0:T(2,128)(2,1)} %bitcast.27), kind=kLoop, calls=%fused_computation.5 | loop fusion | bytes 4194304 | tf_op jit(solution)/shard_map/concatenate | solution.py:144
  160.0 3.0 %slice_bitcast_fusion = bf16[128,8192]{0,1:T(8,128)(2,1)} fusion(bf16[8192,256]{1,0:T(8,128)(2,1)} %bitcast_dynamic-update-slice_fusion.v_ref), kind=kLoop, calls=%fused_computation.8 | loop fusion | bytes 4194304 | tf_op jit(solution)/shard_map/transpose | solution.py:147
  163.1 4.1 %copy.17.kt_ref = bf16[128,8192]{1,0:T(8,128)(2,1)} copy(bf16[128,8192]{0,1:T(8,128)(2,1)} %slice_bitcast_fusion) | data formatting | bytes 4194304 | tf_op jit(solution)/shard_map/transpose | solution.py:147
  167.1 26.1 %shard_map.73 = bf16[8192,128]{1,0:T(8,128)(2,1)} custom-call(s32[768]{0:T(1024)} %fusion.20.lists_ref, s32[64]{0:T(128)} %bitcast.51, bf16[8192,128]{1,0:T(8,128)(2,1)} %bitcast.5.q_ref, bf16[128,8192]{1,0:T(8,128)(2,1)} %copy.17.kt_ref, bf16[8192,256]{1,0:T(8,128)(2,1)} %bitcast_dynamic-update-slice_fusion.v_ref), custom_call_target="tpu_custom_call" | custom-call | tf_op jit(solution)/shard_map/pallas_call | solution.py:63
  193.2 32.3 %all_to_all.65 = bf16[32,256,128]{2,1,0:T(8,128)(2,1)S(1)} all-to-all(bf16[32,256,128]{2,1,0:T(8,128)(2,1)} %bitcast.47), channel_id=1, replica_groups=mesh['zh'=2,'core'=2,'x'=4,'y'=4,'zl'=2] {'x','y','zl'}, dimensions={0} | all-to-all | bytes 4194304 | tf_op jit(solution)/shard_map/all_to_all | solution.py:152
  225.5 2.7 %copy.18 = bf16[256,32,128]{2,1,0:T(8,128)(2,1)} copy(bf16[256,32,128]{2,0,1:T(8,128)(2,1)S(1)} %bitcast.50) | data formatting | bytes 4194304 | tf_op jit(solution)/shard_map/all_to_all | solution.py:152
  228.2 4.2 %broadcast_in_dim.8 = bf16[1,256,4096]{2,1,0:T(8,128)(2,1)} reshape(bf16[256,32,128]{2,1,0:T(8,128)(2,1)} %copy.18) | data formatting | bytes 4194304 | tf_op jit(solution)/shard_map/broadcast_in_dim | solution.py:153
  (19 shorter events, 0.0 us)
Async XLA Ops:
  0.0 42.4 %copy-start = (bf16[1,256,4096]{2,1,0:T(8,128)(2,1)S(1)}, bf16[1,256,4096]{2,1,0:T(8,128)(2,1)}, u32[]{:S(2)}) copy-start(bf16[1,256,4096]{2,1,0:T(8,128)(2,1)} %param.9) | copy-start | bytes 6291460
  0.0 3.3 %copy-start.5 = (bf16[2048,512]{1,0:T(8,128)(2,1)S(1)}, bf16[2048,512]{1,0:T(8,128)(2,1)}, u32[]{:S(2)}) copy-start(bf16[2048,512]{1,0:T(8,128)(2,1)} %param.11) | copy-start | bytes 6291460
  0.0 4.8 %copy-start.6 = (bf16[8192]{0:T(1024)(128)(2,1)S(1)}, bf16[8192]{0:T(1024)(128)(2,1)}, u32[]{:S(2)}) copy-start(bf16[8192]{0:T(1024)(128)(2,1)} %param.8) | copy-start | bytes 49156
  0.0 4.8 %copy-start.1 = (bf16[1,256,8192]{2,1,0:T(8,128)(2,1)S(1)}, bf16[1,256,8192]{2,1,0:T(8,128)(2,1)}, u32[]{:S(2)}) copy-start(bf16[1,256,8192]{2,1,0:T(8,128)(2,1)} %param.7) | copy-start | bytes 12582916
  4.8 47.0 %collective-permute-start.1 = (bf16[2048,1024]{1,0:T(8,128)(2,1)}, bf16[2048,1024]{1,0:T(8,128)(2,1)}, u32[]{:S(2)}, u32[]{:S(2)}) collective-permute-start(bf16[2048,1024]{1,0:T(8,128)(2,1)} %constant_dynamic-update-slice_fusion), channel_id=1, source_target_pairs={{0,32},{32,0},{1,33},{33,1},{2,34},{34,2},{3,35},{35,3},{4,36},{36... | collective-permute-start | bytes 12582920 | tf_op jit(solution)/shard_map/ppermute | solution.py:116
  12.9 1.3 copy-start.4
  14.3 28.1 %collective-permute-start = (bf16[128,4096]{1,0:T(8,128)(2,1)S(1)}, bf16[128,4096]{1,0:T(8,128)(2,1)S(1)}, u32[]{:S(2)}, u32[]{:S(2)}) collective-permute-start(bf16[128,4096]{1,0:T(8,128)(2,1)S(1)} %constant_dynamic-slice_fusion.1), channel_id=1, source_target_pairs={{0,65},{1,64},{2,67},{3,66},{4,69},{5,68},{6,71},{7,70},{8,73},{9,... | collective-permute-start | bytes 3145736 | tf_op jit(solution)/shard_map/ppermute | solution.py:132
  44.3 36.8 %all-to-all-start = ((bf16[256,32,128]{2,0,1:T(8,128)(2,1)}), bf16[256,32,128]{2,0,1:T(8,128)(2,1)}, u32[]{:S(2)}, u32[]{:S(2)}) async-start(bf16[256,32,128]{2,0,1:T(8,128)(2,1)} %copy_bitcast_fusion), calls=%async_computation | async-start | bytes 4194304 | tf_op jit(solution)/shard_map/all_to_all | solution.py:135
  54.7 8.0 %copy-start.2 = (bf16[128,8192]{1,0:T(8,128)(2,1)S(1)}, bf16[128,8192]{1,0:T(8,128)(2,1)}, u32[]{:S(2)}) copy-start(bf16[128,8192]{1,0:T(8,128)(2,1)} %get-tuple-element.13) | copy-start | bytes 6291460
  58.6 17.2 %collective-permute-start.2 = (f32[128,1024]{1,0:T(8,128)}, f32[128,1024]{1,0:T(8,128)}, u32[]{:S(2)}, u32[]{:S(2)}) collective-permute-start(f32[128,1024]{1,0:T(8,128)} %convolution_add_fusion.2), channel_id=1, source_target_pairs={{0,65},{1,64},{2,67},{3,66},{4,69},{5,68},{6,71},{7,70},{8,73},{9,... | collective-permute-start | bytes 1572872 | tf_op jit(solution)/shard_map/ppermute | solution.py:136
  62.8 33.9 %collective-permute-start.3 = (bf16[128,4096]{1,0:T(8,128)(2,1)S(1)}, bf16[128,4096]{1,0:T(8,128)(2,1)}, u32[]{:S(2)}, u32[]{:S(2)}) collective-permute-start(bf16[128,4096]{1,0:T(8,128)(2,1)S(1)} %constant_dynamic-slice_fusion), channel_id=1, source_target_pairs={{0,65},{1,64},{2,67},{3,66},{4,69},{5,68},{6,71},{7,70},{8,73},{9,... | collective-permute-start | bytes 3145736 | tf_op jit(solution)/shard_map/ppermute | solution.py:132
  84.3 35.9 %all-to-all-start.1 = ((bf16[128,2,32,128]{3,1,0,2:T(2,128)(2,1)}), bf16[128,2,32,128]{3,1,0,2:T(2,128)(2,1)}, u32[]{:S(2)}, u32[]{:S(2)}) async-start(bf16[128,2,32,128]{3,1,0,2:T(2,128)(2,1)} %bitcast.48), calls=%async_computation.1 | async-start | bytes 4194304 | tf_op jit(solution)/shard_map/all_to_all | solution.py:143
  99.7 6.5 %copy-start.3 = (bf16[128,8192]{1,0:T(8,128)(2,1)S(1)}, bf16[128,8192]{1,0:T(8,128)(2,1)}, u32[]{:S(2)}) copy-start(bf16[128,8192]{1,0:T(8,128)(2,1)} %get-tuple-element.13) | copy-start | bytes 6291460
  103.0 13.8 %collective-permute-start.4 = (f32[128,1024]{1,0:T(8,128)S(1)}, f32[128,1024]{1,0:T(8,128)S(1)}, u32[]{:S(2)}, u32[]{:S(2)}) collective-permute-start(f32[128,1024]{1,0:T(8,128)S(1)} %convolution_add_fusion), channel_id=1, source_target_pairs={{0,65},{1,64},{2,67},{3,66},{4,69},{5,68},{6,71},{7,70},{8,73},{9,... | collective-permute-start | bytes 1572872 | tf_op jit(solution)/shard_map/ppermute | solution.py:136
  119.8 10.8 %copy-start.7 = (s32[1,1,64,12]{2,1,3,0:T(1,128)S(1)}, s32[1,1,64,12]{2,1,3,0:T(1,128)}, u32[]{:S(2)}) copy-start(s32[1,1,64,12]{2,1,3,0:T(1,128)} %param.12) | copy-start | bytes 9220
  123.4 33.4 %all-to-all-start.2 = ((bf16[128,2,32,128]{3,1,0,2:T(2,128)(2,1)}), bf16[128,2,32,128]{3,1,0,2:T(2,128)(2,1)}, u32[]{:S(2)}, u32[]{:S(2)}) async-start(bf16[128,2,32,128]{3,1,0,2:T(2,128)(2,1)} %bitcast.49), calls=%async_computation.2 | async-start | bytes 4194304 | tf_op jit(solution)/shard_map/all_to_all | solution.py:143

commit v13 on v11

--- a/solution.py
+++ b/solution.py
@@ -69,7 +69,7 @@
             in_specs=[
                 pl.BlockSpec((step_rows, HD), lambda i, lists, counts: (i, 0)),
                 pl.BlockSpec((HD, sequence_rows), lambda i, lists, counts: (0, 0)),
-                pl.BlockSpec((sequence_rows, HD), lambda i, lists, counts: (0, 1)),
+                pl.BlockSpec((sequence_rows, HD), lambda i, lists, counts: (0, 0)),
             ],
             out_specs=pl.BlockSpec((step_rows, HD), lambda i, lists, counts: (i, 0)),
         ),
@@ -138,11 +138,15 @@
         paired = summed.reshape(chunk_rows, 2, KVH, 1, HD).astype(jnp.bfloat16)
         widened = jnp.broadcast_to(paired, (chunk_rows, 2, KVH, copies_per_head, HD))
         widened = widened.reshape(chunk_rows, 2, ctx_size, HD)
-        kv_chunks.append(lax.all_to_all(widened, CTX_AXES, split_axis=2, concat_axis=0, tiled=True))
-    head_pair = jnp.concatenate(kv_chunks, axis=0)
+        arrived = lax.all_to_all(widened, CTX_AXES, split_axis=2, concat_axis=0, tiled=True)
+        kv_chunks.append(arrived.reshape(ctx_size * chunk_rows, 2 * HD))
+    if CHUNKS > 1:
+        early_key_t, early_values = lax.optimization_barrier(
+            (kv_chunks[0][:, :HD].T, kv_chunks[0][:, HD:])
+        )
     sequence_rows = head_queries.shape[0]
-    kv_rows = head_pair.reshape(sequence_rows, 2 * HD)
-    key_t = kv_rows[:, :HD].T
+    key_t = jnp.concatenate([early_key_t] + [part[:, :HD].T for part in kv_chunks[1:]], axis=1)
+    kv_rows = jnp.concatenate([early_values] + [part[:, HD:] for part in kv_chunks[1:]], axis=0)
     lists = block_lists[0, 0]
     lists_flat = ((lists % CHUNKS) * ctx_size + lists // CHUNKS).reshape(-1)
     counts = block_counts[0, 0]

time: 228 us -> 231 us (1.013)
  waiting for transfers between devices: 71.8 us -> 74.3 us
    transpose x2 -> x0, local copies, waits for them, and re-layouts: 4.66 us -> none  [on_device(): key_t = kv_rows[:, :HD].T]
    concatenate x0 -> x2, other arithmetic: none -> 2.82 us  [the longest x1 2.68 us: on_device(): jnp.concatenate([early_values] + [part[:, HD:] for part in kv_chunks[1:]]...]
    reduce_sum x1, other arithmetic: 3.25 us -> 0.92 us  [on_device(): mean_square = jnp.mean(upcast * upcast, axis=-1, keepdims=True)]
    unnamed x20 -> x19, local copies, waits for them, and re-layouts: 5.71 us -> 7.68 us
where the time goes in v13:
time: 231 us
  waiting for transfers between devices  74.3 us (32%)
  starting transfers between devices  33.3 us (14%)
  local copies, waits for them, and re-layouts  32.9 us (14%)
  blocking collectives  31.9 us (14%)
  matrix products  26.3 us (11%)
  Pallas kernels  26.1 us (11%)
  other arithmetic  5.53 us (2%)
    all_to_all x1, blocking collectives, on_device(): lax.all_to_all(attended_head, CTX_AXES, split_axis=0, concat_axis=1, tile...  31.9 us
    ppermute x2, waiting for transfers between devices, on_device(): partner_rows = lax.ppermute(far_features, ALL_AXES, partner_pairs)  31.4 us
    pallas_call x1, Pallas kernels, attend(): pl.pallas_call(attend_kernel, out_shape=jax.ShapeDtypeStruct((sequence_ro...  26.1 us
    all_to_all x2, waiting for transfers between devices, on_device(): lax.all_to_all(widened, CTX_AXES, split_axis=2, concat_axis=0, tiled=True)  24.5 us
    ppermute x2, waiting for transfers between devices, on_device(): lax.ppermute(half_sum(partner_rows, 0), ALL_AXES, partner_pairs)  18.4 us
    all_to_all x2, starting transfers between devices, on_device(): lax.all_to_all(widened, CTX_AXES, split_axis=2, concat_axis=0, tiled=True)  14.3 us
    dot_general x4, matrix products, half_sum(): jnp.dot(own, local_weight, preferred_element_type=jnp.float32)  13.3 us
    dot_general x4, matrix products, half_sum(): jnp.dot(other, sibling, preferred_element_type=jnp.float32)  13.1 us
  transfers between devices with their start and end apart: 8, of which 5 were waited for; matrix products, arithmetic and copies ran while one was open for 16% of the time, Pallas kernels for 0%

profile of v13, /device:TPU:0, one launch (start us, length us, event | category | flops | bytes accessed | tf_op | source)
XLA Modules:
  0.0 230.6 jit_solution(7264811671772679430)
XLA Ops:
  0.0 2.1 copy.19
  2.1 2.1 copy.14
  4.2 8.8 %all-to-all-start = ((bf16[256,32,128]{2,0,1:T(8,128)(2,1)}), bf16[256,32,128]{2,0,1:T(8,128)(2,1)S(1)}, u32[]{:S(2)}, u32[]{:S(2)}) async-start(bf16[256,32,128]{2,0,1:T(8,128)(2,1)} %copy.14), calls=%async_computation | async-start | bytes 4194304 | tf_op jit(solution)/shard_map/all_to_all | solution.py:104
  13.0 3.3 %constant_dynamic-update-slice_fusion.1 = bf16[2048,1024]{1,0:T(8,128)(2,1)} fusion(bf16[2048,512]{1,0:T(8,128)(2,1)} %param.10), kind=kLoop, calls=%fused_computation.32 | loop fusion | bytes 4194304
  16.3 3.1 %constant_dynamic-update-slice_fusion = bf16[2048,1024]{1,0:T(8,128)(2,1)} fusion(bf16[2048,1024]{1,0:T(8,128)(2,1)} %constant_dynamic-update-slice_fusion.1, bf16[2048,512]{1,0:T(8,128)(2,1)} %param.11), kind=kLoop, calls=%fused_computation.31 | loop fusion | bytes 4194304 | tf_op jit(solution)/shard_map/concatenate | solution.py:111
  19.4 0.9 fusion
  20.4 1.2 fusion.2
  21.6 2.4 %fusion.33 = (bf16[128,8192]{1,0:T(8,128)(2,1)}, bf16[128,8192]{1,0:T(8,128)(2,1)}) fusion(bf16[256,8192]{1,0:T(8,128)(2,1)S(1)} %fusion.2), kind=kLoop, calls=%fused_computation.56 | loop fusion | bytes 8388608 | tf_op jit(solution)/shard_map/slice | solution.py:131
  24.0 1.3 constant_dynamic-slice_fusion.1
  25.3 4.0 %collective-permute-start = (bf16[128,4096]{1,0:T(8,128)(2,1)S(1)}, bf16[128,4096]{1,0:T(8,128)(2,1)}, u32[]{:S(2)}, u32[]{:S(2)}) collective-permute-start(bf16[128,4096]{1,0:T(8,128)(2,1)S(1)} %constant_dynamic-slice_fusion.1), channel_id=1, source_target_pairs={{0,65},{1,64},{2,67},{3,66},{4,69},{5,68},{6,71},{7,70},{8,73},{9,... | collective-permute-start | bytes 3145736 | tf_op jit(solution)/shard_map/ppermute | solution.py:133
  29.3 23.9 %collective-permute-done = bf16[128,4096]{1,0:T(8,128)(2,1)} collective-permute-done((bf16[128,4096]{1,0:T(8,128)(2,1)S(1)}, bf16[128,4096]{1,0:T(8,128)(2,1)}, u32[]{:S(2)}, u32[]{:S(2)}) %collective-permute-start) | collective-permute-done | bytes 1048608 | tf_op jit(solution)/shard_map/ppermute | solution.py:133
  53.2 3.8 %fusion.13 = f32[128,1024]{1,0:T(8,128)S(1)} fusion(bf16[2048,1024]{1,0:T(8,128)(2,1)} %collective-permute-done.1, bf16[128,4096]{1,0:T(8,128)(2,1)} %collective-permute-done, s32[]{:T(128)S(6)} %select_n.40), kind=kOutput, calls=%fused_computation.25 | convolution fusion | flops 536870912 | bytes 5242884 | tf_op jit(solution)/shard_map/dot_general | solution.py:122
  57.0 4.1 %convolution_add_fusion.2 = f32[128,1024]{1,0:T(8,128)} fusion(f32[128,1024]{1,0:T(8,128)S(1)} %fusion.13, bf16[2048,1024]{1,0:T(8,128)(2,1)} %constant_dynamic-update-slice_fusion, bf16[128,4096]{1,0:T(8,128)(2,1)} %collective-permute-done, s32[]{:T(128)S(6)} %select_n.39), kind=kOutput, calls=%fused_computation.11 | convolution fusion | flops 537001984 | bytes 5767172 | tf_op jit(solution)/shard_map/dot_general | solution.py:122
  61.1 2.9 %collective-permute-start.2 = (f32[128,1024]{1,0:T(8,128)}, f32[128,1024]{1,0:T(8,128)}, u32[]{:S(2)}, u32[]{:S(2)}) collective-permute-start(f32[128,1024]{1,0:T(8,128)} %convolution_add_fusion.2), channel_id=1, source_target_pairs={{0,65},{1,64},{2,67},{3,66},{4,69},{5,68},{6,71},{7,70},{8,73},{9,... | collective-permute-start | bytes 1572872 | tf_op jit(solution)/shard_map/ppermute | solution.py:136
  64.1 0.4 collective-permute-start.3
  64.5 3.1 %fusion.17 = f32[128,1024]{1,0:T(8,128)S(1)} fusion(bf16[2048,1024]{1,0:T(8,128)(2,1)} %constant_dynamic-update-slice_fusion, bf16[128,8192]{1,0:T(8,128)(2,1)} %get-tuple-element.14, s32[]{:T(128)S(6)} %select_n.37), kind=kOutput, calls=%fused_computation.29 | convolution fusion | flops 536870912 | bytes 5242884 | tf_op jit(solution)/shard_map/dot_general | solution.py:122
  67.6 9.9 %collective-permute-done.2 = f32[128,1024]{1,0:T(8,128)} collective-permute-done((f32[128,1024]{1,0:T(8,128)}, f32[128,1024]{1,0:T(8,128)}, u32[]{:S(2)}, u32[]{:S(2)}) %collective-permute-start.2) | collective-permute-done | bytes 524320 | tf_op jit(solution)/shard_map/ppermute | solution.py:136
  77.4 3.2 %fusion.6 = bf16[128,1024]{1,0:T(8,128)(2,1)S(1)} fusion(f32[128,1024]{1,0:T(8,128)} %collective-permute-done.2, f32[128,1024]{1,0:T(8,128)S(1)} %fusion.17, bf16[2048,1024]{1,0:T(8,128)(2,1)} %collective-permute-done.1, bf16[128,8192]{1,0:T(8,128)(2,1)} %get-tuple-element.14, s32[]{:T(128)S(6)} %select_n.38), kind=kOutput, calls=%fused_computation.16 | convolution fusion | flops 537264128 | bytes 6029316 | tf_op jit(solution)/shard_map/dot_general | solution.py:122
  80.7 0.2 convert_element_type.39
  80.8 0.2 copy.15
  81.0 3.2 %broadcast_in_dim.6 = bf16[128,2,4,8,128]{4,1,0,3,2:T(2,128)(2,1)} broadcast(bf16[128,2,4,128]{3,1,0,2:T(2,128)(2,1)S(1)} %copy.15), dimensions={0,1,2,4} | broadcast | bytes 2359296 | tf_op jit(solution)/shard_map/broadcast_in_dim | solution.py:139
  84.3 7.1 %all-to-all-start.1 = ((bf16[128,2,32,128]{3,1,0,2:T(2,128)(2,1)}), bf16[128,2,32,128]{3,1,0,2:T(2,128)(2,1)S(1)}, u32[]{:S(2)}, u32[]{:S(2)}) async-start(bf16[128,2,32,128]{3,1,0,2:T(2,128)(2,1)} %bitcast.48), calls=%async_computation.1 | async-start | bytes 4194304 | tf_op jit(solution)/shard_map/all_to_all | solution.py:141
  91.3 7.5 %collective-permute-done.3 = bf16[128,4096]{1,0:T(8,128)(2,1)} collective-permute-done((bf16[128,4096]{1,0:T(8,128)(2,1)S(1)}, bf16[128,4096]{1,0:T(8,128)(2,1)}, u32[]{:S(2)}, u32[]{:S(2)}) %collective-permute-start.3) | collective-permute-done | bytes 1048608 | tf_op jit(solution)/shard_map/ppermute | solution.py:133
  98.8 3.1 %fusion.7 = f32[128,1024]{1,0:T(8,128)S(1)} fusion(bf16[2048,1024]{1,0:T(8,128)(2,1)} %collective-permute-done.1, bf16[128,4096]{1,0:T(8,128)(2,1)} %collective-permute-done.3, s32[]{:T(128)S(6)} %select_n.40), kind=kOutput, calls=%fused_computation.19 | convolution fusion | flops 536870912 | bytes 5242884 | tf_op jit(solution)/shard_map/dot_general | solution.py:122
  101.9 3.2 %convolution_add_fusion = f32[128,1024]{1,0:T(8,128)S(1)} fusion(f32[128,1024]{1,0:T(8,128)S(1)} %fusion.7, bf16[2048,1024]{1,0:T(8,128)(2,1)} %constant_dynamic-update-slice_fusion, bf16[128,4096]{1,0:T(8,128)(2,1)} %collective-permute-done.3, s32[]{:T(128)S(6)} %select_n.39), kind=kOutput, calls=%fused_computation.9 | convolution fusion | flops 537001984 | bytes 5767172 | tf_op jit(solution)/shard_map/dot_general | solution.py:122
  105.2 2.9 %collective-permute-start.4 = (f32[128,1024]{1,0:T(8,128)S(1)}, f32[128,1024]{1,0:T(8,128)S(1)}, u32[]{:S(2)}, u32[]{:S(2)}) collective-permute-start(f32[128,1024]{1,0:T(8,128)S(1)} %convolution_add_fusion), channel_id=1, source_target_pairs={{0,65},{1,64},{2,67},{3,66},{4,69},{5,68},{6,71},{7,70},{8,73},{9,... | collective-permute-start | bytes 1572872 | tf_op jit(solution)/shard_map/ppermute | solution.py:136
  108.1 2.9 %fusion.11 = f32[128,1024]{1,0:T(8,128)S(1)} fusion(bf16[2048,1024]{1,0:T(8,128)(2,1)} %constant_dynamic-update-slice_fusion, bf16[128,8192]{1,0:T(8,128)(2,1)S(1)} %copy-done.3, s32[]{:T(128)S(6)} %select_n.37), kind=kOutput, calls=%fused_computation.23 | convolution fusion | flops 536870912 | bytes 5242884 | tf_op jit(solution)/shard_map/dot_general | solution.py:122
  111.0 8.5 %collective-permute-done.4 = f32[128,1024]{1,0:T(8,128)S(1)} collective-permute-done((f32[128,1024]{1,0:T(8,128)S(1)}, f32[128,1024]{1,0:T(8,128)S(1)}, u32[]{:S(2)}, u32[]{:S(2)}) %collective-permute-start.4) | collective-permute-done | bytes 524320 | tf_op jit(solution)/shard_map/ppermute | solution.py:136
  119.5 3.0 %fusion.5 = bf16[128,1024]{1,0:T(8,128)(2,1)S(1)} fusion(f32[128,1024]{1,0:T(8,128)S(1)} %collective-permute-done.4, f32[128,1024]{1,0:T(8,128)S(1)} %fusion.11, bf16[2048,1024]{1,0:T(8,128)(2,1)} %collective-permute-done.1, bf16[128,8192]{1,0:T(8,128)(2,1)S(1)} %copy-done.3, s32[]{:T(128)S(6)} %select_n.38), kind=kOutput, calls=%fused_computation.15 | convolution fusion | flops 537264128 | bytes 6029316 | tf_op jit(solution)/shard_map/dot_general | solution.py:122
  122.5 0.2 convert_element_type.41
  122.7 0.2 copy.16
  122.9 3.2 %broadcast_in_dim.7 = bf16[128,2,4,8,128]{4,1,0,3,2:T(2,128)(2,1)} broadcast(bf16[128,2,4,128]{3,1,0,2:T(2,128)(2,1)S(1)} %copy.16), dimensions={0,1,2,4} | broadcast | bytes 2359296 | tf_op jit(solution)/shard_map/broadcast_in_dim | solution.py:139
  126.1 7.2 %all-to-all-start.2 = ((bf16[128,2,32,128]{3,1,0,2:T(2,128)(2,1)}), bf16[128,2,32,128]{3,1,0,2:T(2,128)(2,1)}, u32[]{:S(2)}, u32[]{:S(2)}) async-start(bf16[128,2,32,128]{3,1,0,2:T(2,128)(2,1)} %bitcast.49), calls=%async_computation.2 | async-start | bytes 4194304 | tf_op jit(solution)/shard_map/all_to_all | solution.py:141
  133.3 0.1 copy.13
  133.4 0.1 squeeze.8
  133.5 0.6 fusion.20.lists_ref
  134.1 0.3 copy.25
  134.4 1.2 fusion.35
  135.6 24.5 %all-to-all-done.2 = bf16[128,2,32,128]{3,1,0,2:T(2,128)(2,1)} async-done(((bf16[128,2,32,128]{3,1,0,2:T(2,128)(2,1)}), bf16[128,2,32,128]{3,1,0,2:T(2,128)(2,1)}, u32[]{:S(2)}, u32[]{:S(2)}) %all-to-all-start.2) | async-done | bytes 2097184 | tf_op jit(solution)/shard_map/all_to_all | solution.py:141
  160.1 2.0 copy.24
  162.0 1.1 fusion.34
  163.1 0.1 pad_maximum_fusion
  163.3 3.0 %copy.17.kt_ref = bf16[128,8192]{1,0:T(8,128)(2,1)} copy(bf16[128,8192]{0,1:T(8,128)(2,1)S(1)} %pad_maximum_fusion) | data formatting | bytes 4194304 | tf_op jit(solution)/shard_map/concatenate | solution.py:148
  166.3 2.7 %pad_maximum_fusion.1.v_ref = bf16[8192,128]{1,0:T(8,128)(2,1)} fusion(bf16[4096,128]{1,0:T(8,128)(2,1)} %get-tuple-element.15, bf16[4096,128]{1,0:T(8,128)(2,1)S(1)} %get-tuple-element.12), kind=kLoop, calls=%fused_computation.8 | loop fusion | flops 4194304 | bytes 4194304 | tf_op jit(solution)/shard_map/concatenate | solution.py:149
  168.9 26.1 %shard_map.73 = bf16[8192,128]{1,0:T(8,128)(2,1)} custom-call(s32[768]{0:T(1024)} %fusion.20.lists_ref, s32[64]{0:T(128)} %bitcast.57, bf16[8192,128]{1,0:T(8,128)(2,1)} %bitcast.54, bf16[128,8192]{1,0:T(8,128)(2,1)} %copy.17.kt_ref, bf16[8192,128]{1,0:T(8,128)(2,1)} %pad_maximum_fusion.1.v_ref), custom_call_target="tpu_custom_call" | custom-call | tf_op jit(solution)/shard_map/pallas_call | solution.py:63
  195.0 31.9 %all_to_all.65 = bf16[32,256,128]{2,1,0:T(8,128)(2,1)S(1)} all-to-all(bf16[32,256,128]{2,1,0:T(8,128)(2,1)} %bitcast.55), channel_id=1, replica_groups=mesh['zh'=2,'core'=2,'x'=4,'y'=4,'zl'=2] {'x','y','zl'}, dimensions={0} | all-to-all | bytes 4194304 | tf_op jit(solution)/shard_map/all_to_all | solution.py:154
  227.0 1.4 copy.18
  228.3 2.3 broadcast_in_dim.8
  (21 shorter events, 0.1 us)
Async XLA Ops:
  4.2 49.0 %all-to-all-start = ((bf16[256,32,128]{2,0,1:T(8,128)(2,1)}), bf16[256,32,128]{2,0,1:T(8,128)(2,1)S(1)}, u32[]{:S(2)}, u32[]{:S(2)}) async-start(bf16[256,32,128]{2,0,1:T(8,128)(2,1)} %copy.14), calls=%async_computation | async-start | bytes 4194304 | tf_op jit(solution)/shard_map/all_to_all | solution.py:104
  13.0 6.4 %copy-start.5 = (bf16[8192]{0:T(1024)(128)(2,1)S(1)}, bf16[8192]{0:T(1024)(128)(2,1)}, u32[]{:S(2)}) copy-start(bf16[8192]{0:T(1024)(128)(2,1)} %param.8) | copy-start | bytes 49156
  13.0 6.4 %copy-start = (bf16[1,256,8192]{2,1,0:T(8,128)(2,1)S(1)}, bf16[1,256,8192]{2,1,0:T(8,128)(2,1)}, u32[]{:S(2)}) copy-start(bf16[1,256,8192]{2,1,0:T(8,128)(2,1)} %param.7) | copy-start | bytes 12582916
  19.4 33.8 %collective-permute-start.1 = (bf16[2048,1024]{1,0:T(8,128)(2,1)}, bf16[2048,1024]{1,0:T(8,128)(2,1)}, u32[]{:S(2)}, u32[]{:S(2)}) collective-permute-start(bf16[2048,1024]{1,0:T(8,128)(2,1)} %constant_dynamic-update-slice_fusion), channel_id=1, source_target_pairs={{0,32},{32,0},{1,33},{33,1},{2,34},{34,2},{3,35},{35,3},{4,36},{36... | collective-permute-start | bytes 12582920 | tf_op jit(solution)/shard_map/ppermute | solution.py:117
  25.3 27.9 %collective-permute-start = (bf16[128,4096]{1,0:T(8,128)(2,1)S(1)}, bf16[128,4096]{1,0:T(8,128)(2,1)}, u32[]{:S(2)}, u32[]{:S(2)}) collective-permute-start(bf16[128,4096]{1,0:T(8,128)(2,1)S(1)} %constant_dynamic-slice_fusion.1), channel_id=1, source_target_pairs={{0,65},{1,64},{2,67},{3,66},{4,69},{5,68},{6,71},{7,70},{8,73},{9,... | collective-permute-start | bytes 3145736 | tf_op jit(solution)/shard_map/ppermute | solution.py:133
  53.2 7.9 %copy-start.1 = (bf16[256,32,128]{2,0,1:T(8,128)(2,1)}, bf16[256,32,128]{2,0,1:T(8,128)(2,1)S(1)}, u32[]{:S(2)}) copy-start(bf16[256,32,128]{2,0,1:T(8,128)(2,1)S(1)} %all-to-all-done) | copy-start | bytes 6291460
  57.0 7.0 %copy-start.2 = (bf16[128,8192]{1,0:T(8,128)(2,1)S(1)}, bf16[128,8192]{1,0:T(8,128)(2,1)}, u32[]{:S(2)}) copy-start(bf16[128,8192]{1,0:T(8,128)(2,1)} %get-tuple-element.13) | copy-start | bytes 6291460
  61.1 16.3 %collective-permute-start.2 = (f32[128,1024]{1,0:T(8,128)}, f32[128,1024]{1,0:T(8,128)}, u32[]{:S(2)}, u32[]{:S(2)}) collective-permute-start(f32[128,1024]{1,0:T(8,128)} %convolution_add_fusion.2), channel_id=1, source_target_pairs={{0,65},{1,64},{2,67},{3,66},{4,69},{5,68},{6,71},{7,70},{8,73},{9,... | collective-permute-start | bytes 1572872 | tf_op jit(solution)/shard_map/ppermute | solution.py:136
  64.1 34.7 %collective-permute-start.3 = (bf16[128,4096]{1,0:T(8,128)(2,1)S(1)}, bf16[128,4096]{1,0:T(8,128)(2,1)}, u32[]{:S(2)}, u32[]{:S(2)}) collective-permute-start(bf16[128,4096]{1,0:T(8,128)(2,1)S(1)} %constant_dynamic-slice_fusion), channel_id=1, source_target_pairs={{0,65},{1,64},{2,67},{3,66},{4,69},{5,68},{6,71},{7,70},{8,73},{9,... | collective-permute-start | bytes 3145736 | tf_op jit(solution)/shard_map/ppermute | solution.py:133
  84.3 38.6 %all-to-all-start.1 = ((bf16[128,2,32,128]{3,1,0,2:T(2,128)(2,1)}), bf16[128,2,32,128]{3,1,0,2:T(2,128)(2,1)S(1)}, u32[]{:S(2)}, u32[]{:S(2)}) async-start(bf16[128,2,32,128]{3,1,0,2:T(2,128)(2,1)} %bitcast.48), calls=%async_computation.1 | async-start | bytes 4194304 | tf_op jit(solution)/shard_map/all_to_all | solution.py:141
  101.9 6.2 %copy-start.3 = (bf16[128,8192]{1,0:T(8,128)(2,1)S(1)}, bf16[128,8192]{1,0:T(8,128)(2,1)}, u32[]{:S(2)}) copy-start(bf16[128,8192]{1,0:T(8,128)(2,1)} %get-tuple-element.13) | copy-start | bytes 6291460
  105.2 14.4 %collective-permute-start.4 = (f32[128,1024]{1,0:T(8,128)S(1)}, f32[128,1024]{1,0:T(8,128)S(1)}, u32[]{:S(2)}, u32[]{:S(2)}) collective-permute-start(f32[128,1024]{1,0:T(8,128)S(1)} %convolution_add_fusion), channel_id=1, source_target_pairs={{0,65},{1,64},{2,67},{3,66},{4,69},{5,68},{6,71},{7,70},{8,73},{9,... | collective-permute-start | bytes 1572872 | tf_op jit(solution)/shard_map/ppermute | solution.py:136
  122.5 10.8 %copy-start.6 = (s32[1,1,64,12]{2,1,3,0:T(1,128)S(1)}, s32[1,1,64,12]{2,1,3,0:T(1,128)}, u32[]{:S(2)}) copy-start(s32[1,1,64,12]{2,1,3,0:T(1,128)} %param.12) | copy-start | bytes 9220
  126.1 33.9 %all-to-all-start.2 = ((bf16[128,2,32,128]{3,1,0,2:T(2,128)(2,1)}), bf16[128,2,32,128]{3,1,0,2:T(2,128)(2,1)}, u32[]{:S(2)}, u32[]{:S(2)}) async-start(bf16[128,2,32,128]{3,1,0,2:T(2,128)(2,1)} %bitcast.49), calls=%async_computation.2 | async-start | bytes 4194304 | tf_op jit(solution)/shard_map/all_to_all | solution.py:141
  160.1 3.1 %copy-start.4 = (bf16[128,4096]{0,1:T(8,128)(2,1)S(1)}, bf16[128,4096]{0,1:T(8,128)(2,1)}, u32[]{:S(2)}) copy-start(bf16[128,4096]{0,1:T(8,128)(2,1)} %get-tuple-element.11) | copy-start | bytes 3145732

commit v14 on v11

--- a/solution.py
+++ b/solution.py
@@ -108,8 +108,8 @@
         jnp.bfloat16
     )
     local_rows, features = normed.shape
-    local_weight = jnp.concatenate([key_weight, value_weight], axis=1)
-    weight_rows = local_weight.shape[0]
+    local_weight = (key_weight, value_weight)
+    weight_rows = key_weight.shape[0]
     half_features = 2 * weight_rows
     zh = lax.axis_index("zh")
     core = lax.axis_index("core")
@@ -119,8 +119,13 @@
     def half_sum(rows, offset):
         own = lax.dynamic_slice_in_dim(rows, offset + core * weight_rows, weight_rows, axis=1)
         other = lax.dynamic_slice_in_dim(rows, offset + (1 - core) * weight_rows, weight_rows, axis=1)
-        return jnp.dot(own, local_weight, preferred_element_type=jnp.float32) + jnp.dot(
-            other, sibling, preferred_element_type=jnp.float32
+        return jnp.concatenate(
+            [
+                jnp.dot(own, mine, preferred_element_type=jnp.float32)
+                + jnp.dot(other, theirs, preferred_element_type=jnp.float32)
+                for mine, theirs in zip(local_weight, sibling)
+            ],
+            axis=1,
         )
 
     ctx_size = lax.axis_size(CTX_AXES)

time: 228 us -> 243 us (1.066)
  waiting for transfers between devices: 71.8 us -> 81.8 us
  local copies, waits for them, and re-layouts: 32 us -> 38.2 us
    all_to_all x2, waiting for transfers between devices: 23.7 us -> 31.3 us  [on_device(): lax.all_to_all(widened, CTX_AXES, split_axis=2, concat_axis=0, tiled=True)]
    ppermute x2, waiting for transfers between devices: 30.3 us -> 37.5 us  [on_device(): partner_rows = lax.ppermute(far_features, ALL_AXES, partner_pairs)]
    ppermute x2, waiting for transfers between devices: 17.8 us -> 13 us  [on_device(): lax.ppermute(half_sum(partner_rows, 0), ALL_AXES, partner_pairs)]
    dynamic_slice x2, local copies, waits for them, and re-layouts: 1.36 us -> 4.76 us  [on_device(): lax.dynamic_slice_in_dim(rows, (1 - zh) * half_features, half_features, a...]
    all_to_all x2, starting transfers between devices: 14.3 us -> 11.5 us  [on_device(): lax.all_to_all(widened, CTX_AXES, split_axis=2, concat_axis=0, tiled=True)]
    unnamed x20 -> x29, local copies, waits for them, and re-layouts: 5.71 us -> 6.77 us
    dot_general x8 -> x16, matrix products: 26.3 us -> 27.1 us  [the longest x8 16.8 us: half_sum(): jnp.dot(other, theirs, preferred_element_type=jnp.float32)]
  transfers between devices with their start and end apart: 8 -> 9, of which waited for: 5 -> 5; matrix products, arithmetic and copies ran while one was open for 16% -> 22% of each run, Pallas kernels for 0% -> 0%
where the time goes in v14:
time: 243 us; the launch traced here: 241 us
  waiting for transfers between devices  81.8 us (34%)
  local copies, waits for them, and re-layouts  38.2 us (16%)
  blocking collectives  31.6 us (13%)
  starting transfers between devices  31.2 us (13%)
  matrix products  27.1 us (11%)
  Pallas kernels  26 us (11%)
  other arithmetic  5.24 us (2%)
    ppermute x2, waiting for transfers between devices, on_device(): partner_rows = lax.ppermute(far_features, ALL_AXES, partner_pairs)  37.5 us
    all_to_all x1, blocking collectives, on_device(): lax.all_to_all(attended_head, CTX_AXES, split_axis=0, concat_axis=1, tile...  31.6 us
    all_to_all x2, waiting for transfers between devices, on_device(): lax.all_to_all(widened, CTX_AXES, split_axis=2, concat_axis=0, tiled=True)  31.3 us
    pallas_call x1, Pallas kernels, attend(): pl.pallas_call(attend_kernel, out_shape=jax.ShapeDtypeStruct((sequence_ro...  26 us
    dot_general x8, matrix products, half_sum(): jnp.dot(other, theirs, preferred_element_type=jnp.float32)  16.8 us
    ppermute x2, waiting for transfers between devices, on_device(): lax.ppermute(half_sum(partner_rows, 0), ALL_AXES, partner_pairs)  13 us
    all_to_all x2, starting transfers between devices, on_device(): lax.all_to_all(widened, CTX_AXES, split_axis=2, concat_axis=0, tiled=True)  11.5 us
    dot_general x8, matrix products, half_sum(): jnp.dot(own, mine, preferred_element_type=jnp.float32)  10.3 us
  transfers between devices with their start and end apart: 9, of which 5 were waited for; matrix products, arithmetic and copies ran while one was open for 22% of the time, Pallas kernels for 0%

profile of v14, /device:TPU:0, one launch (start us, length us, event | category | flops | bytes accessed | tf_op | source)
XLA Modules:
  0.0 241.4 jit_solution(16334764157214385509)
XLA Ops:
  0.0 2.1 copy.19
  2.1 2.1 copy.14
  4.2 9.0 %all-to-all-start = ((bf16[256,32,128]{2,0,1:T(8,128)(2,1)}), bf16[256,32,128]{2,0,1:T(8,128)(2,1)}, u32[]{:S(2)}, u32[]{:S(2)}) async-start(bf16[256,32,128]{2,0,1:T(8,128)(2,1)} %copy.14), calls=%async_computation | async-start | bytes 4194304 | tf_op jit(solution)/shard_map/all_to_all | solution.py:104
  13.3 3.3 %fusion = f32[256]{0:T(256)S(1)} fusion(bf16[1,256,8192]{2,1,0:T(8,128)(2,1)} %param.7), kind=kLoop, calls=%fused_computation.2 | loop fusion | flops 6291200 | bytes 4195328 | tf_op jit(solution)/shard_map/reduce_sum | solution.py:106
  16.7 1.2 fusion.2
  17.9 2.5 %fusion.51 = (bf16[128,8192]{1,0:T(8,128)(2,1)}, bf16[128,8192]{1,0:T(8,128)(2,1)}) fusion(bf16[256,8192]{1,0:T(8,128)(2,1)S(1)} %fusion.2), kind=kLoop, calls=%fused_computation.77 | loop fusion | bytes 8388608 | tf_op jit(solution)/shard_map/slice | solution.py:136
  20.4 2.4 %constant_dynamic-slice_fusion = bf16[128,4096]{1,0:T(8,128)(2,1)} fusion(bf16[128,8192]{1,0:T(8,128)(2,1)} %get-tuple-element.9, s32[]{:T(128)S(6)} %select_n.36), kind=kLoop, calls=%fused_computation.68 | loop fusion | bytes 2097156 | tf_op jit(solution)/shard_map/dynamic_slice | solution.py:137
  22.9 3.8 %collective-permute-start.4 = (bf16[128,4096]{1,0:T(8,128)(2,1)}, bf16[128,4096]{1,0:T(8,128)(2,1)S(1)}, u32[]{:S(2)}, u32[]{:S(2)}) collective-permute-start(bf16[128,4096]{1,0:T(8,128)(2,1)} %constant_dynamic-slice_fusion), channel_id=1, source_target_pairs={{0,65},{1,64},{2,67},{3,66},{4,69},{5,68},{6,71},{7,70},{8,73},{9,... | collective-permute-start | bytes 3145736 | tf_op jit(solution)/shard_map/ppermute | solution.py:138
  26.7 2.3 constant_dynamic-slice_fusion.1
  29.1 2.3 fusion.13
  31.4 2.3 fusion.15
  33.7 1.1 fusion.25
  34.9 0.5 fusion.27
  35.3 37.5 %collective-permute-done = bf16[128,4096]{1,0:T(8,128)(2,1)} collective-permute-done((bf16[128,4096]{1,0:T(8,128)(2,1)}, bf16[128,4096]{1,0:T(8,128)(2,1)}, u32[]{:S(2)}, u32[]{:S(2)}) %collective-permute-start) | collective-permute-done | bytes 1048608 | tf_op jit(solution)/shard_map/ppermute | solution.py:138
  72.8 2.4 fusion.19
  75.2 1.5 convolution_add_fusion.5
  76.7 2.2 fusion.17
  78.9 1.6 convolution_add_fusion.4
  80.6 3.0 %collective-permute-start.3 = (f32[128,1024]{1,0:T(8,128)S(1)}, f32[128,1024]{1,0:T(8,128)S(1)}, u32[]{:S(2)}, u32[]{:S(2)}) collective-permute-start(f32[128,1024]{1,0:T(8,128)S(1)} %pad_maximum_fusion), channel_id=1, source_target_pairs={{0,65},{1,64},{2,67},{3,66},{4,69},{5,68},{6,71},{7,70},{8,73},{9,... | collective-permute-start | bytes 1572872 | tf_op jit(solution)/shard_map/ppermute | solution.py:141
  83.7 2.0 convolution_add_fusion.6
  85.7 2.0 convolution_add_fusion.7
  87.8 7.4 %collective-permute-done.3 = f32[128,1024]{1,0:T(8,128)S(1)} collective-permute-done((f32[128,1024]{1,0:T(8,128)S(1)}, f32[128,1024]{1,0:T(8,128)S(1)}, u32[]{:S(2)}, u32[]{:S(2)}) %collective-permute-start.3) | collective-permute-done | bytes 524320 | tf_op jit(solution)/shard_map/ppermute | solution.py:141
  95.2 0.9 convert_element_type.39
  96.0 1.2 copy.15
  97.2 3.2 %broadcast_in_dim.6 = bf16[128,2,4,8,128]{4,1,0,3,2:T(2,128)(2,1)} broadcast(bf16[128,2,4,128]{3,1,0,2:T(2,128)(2,1)S(1)} %copy.15), dimensions={0,1,2,4} | broadcast | bytes 2359296 | tf_op jit(solution)/shard_map/broadcast_in_dim | solution.py:144
  100.4 7.4 %all-to-all-start.1 = ((bf16[128,2,32,128]{3,1,0,2:T(2,128)(2,1)}), bf16[128,2,32,128]{3,1,0,2:T(2,128)(2,1)}, u32[]{:S(2)}, u32[]{:S(2)}) async-start(bf16[128,2,32,128]{3,1,0,2:T(2,128)(2,1)} %bitcast.52), calls=%async_computation.1 | async-start | bytes 4194304 | tf_op jit(solution)/shard_map/all_to_all | solution.py:146
  107.8 2.0 fusion.5
  109.9 2.0 fusion.7
  111.9 0.4 convolution_add_fusion
  112.4 1.1 copy-done.3
  113.5 0.4 convolution_add_fusion.1
  114.0 3.7 %collective-permute-start.5 = (f32[128,1024]{1,0:T(8,128)S(1)}, f32[128,1024]{1,0:T(8,128)S(1)}, u32[]{:S(2)}, u32[]{:S(2)}) collective-permute-start(f32[128,1024]{1,0:T(8,128)S(1)} %pad_maximum_fusion.1), channel_id=1, source_target_pairs={{0,65},{1,64},{2,67},{3,66},{4,69},{5,68},{6,71},{7,70},{8,73},{9,... | collective-permute-start | bytes 1572872 | tf_op jit(solution)/shard_map/ppermute | solution.py:141
  117.7 2.0 convolution_add_fusion.2
  119.8 2.0 convolution_add_fusion.3
  121.8 5.7 %collective-permute-done.5 = f32[128,1024]{1,0:T(8,128)S(1)} collective-permute-done((f32[128,1024]{1,0:T(8,128)S(1)}, f32[128,1024]{1,0:T(8,128)S(1)}, u32[]{:S(2)}, u32[]{:S(2)}) %collective-permute-start.5) | collective-permute-done | bytes 524320 | tf_op jit(solution)/shard_map/ppermute | solution.py:141
  127.9 7.5 %all-to-all-done.1 = bf16[128,2,32,128]{3,1,0,2:T(2,128)(2,1)} async-done(((bf16[128,2,32,128]{3,1,0,2:T(2,128)(2,1)}), bf16[128,2,32,128]{3,1,0,2:T(2,128)(2,1)}, u32[]{:S(2)}, u32[]{:S(2)}) %all-to-all-start.1) | async-done | bytes 2097184 | tf_op jit(solution)/shard_map/all_to_all | solution.py:146
  135.5 3.2 %broadcast_in_dim.7 = bf16[128,2,4,8,128]{4,1,0,3,2:T(2,128)(2,1)} broadcast(bf16[128,2,4,128]{3,1,0,2:T(2,128)(2,1)S(1)} %copy.16), dimensions={0,1,2,4} | broadcast | bytes 2359296 | tf_op jit(solution)/shard_map/broadcast_in_dim | solution.py:144
  138.7 4.1 %all-to-all-start.2 = ((bf16[128,2,32,128]{3,1,0,2:T(2,128)(2,1)}), bf16[128,2,32,128]{3,1,0,2:T(2,128)(2,1)S(1)}, u32[]{:S(2)}, u32[]{:S(2)}) async-start(bf16[128,2,32,128]{3,1,0,2:T(2,128)(2,1)} %bitcast.54), calls=%async_computation.2 | async-start | bytes 4194304 | tf_op jit(solution)/shard_map/all_to_all | solution.py:146
  143.0 0.6 fusion.30.lists_ref
  143.6 3.2 %bitcast_dynamic-update-slice_fusion.1 = bf16[8192,256]{1,0:T(8,128)(2,1)} fusion(bf16[512,8,2,128]{3,2,1,0:T(2,128)(2,1)} %bitcast.23), kind=kLoop, calls=%fused_computation.6 | loop fusion | bytes 4194304
  146.9 23.8 %all-to-all-done.2 = bf16[128,2,32,128]{3,1,0,2:T(2,128)(2,1)S(1)} async-done(((bf16[128,2,32,128]{3,1,0,2:T(2,128)(2,1)}), bf16[128,2,32,128]{3,1,0,2:T(2,128)(2,1)S(1)}, u32[]{:S(2)}, u32[]{:S(2)}) %all-to-all-start.2) | async-done | bytes 2097184 | tf_op jit(solution)/shard_map/all_to_all | solution.py:146
  170.7 1.6 bitcast_dynamic-update-slice_fusion.v_ref
  172.3 1.7 slice_bitcast_fusion
  174.0 2.9 %copy.17.kt_ref = bf16[128,8192]{1,0:T(8,128)(2,1)} copy(bf16[128,8192]{0,1:T(8,128)(2,1)S(1)} %slice_bitcast_fusion) | data formatting | bytes 4194304 | tf_op jit(solution)/shard_map/transpose | solution.py:150
  176.9 26.0 %shard_map.73 = bf16[8192,128]{1,0:T(8,128)(2,1)} custom-call(s32[768]{0:T(1024)} %fusion.30.lists_ref, s32[64]{0:T(128)} %bitcast.58, bf16[8192,128]{1,0:T(8,128)(2,1)} %bitcast.2.q_ref, bf16[128,8192]{1,0:T(8,128)(2,1)} %copy.17.kt_ref, bf16[8192,256]{1,0:T(8,128)(2,1)} %bitcast_dynamic-update-slice_fusion.v_ref), custom_call_target="tpu_custom_call" | custom-call | tf_op jit(solution)/shard_map/pallas_call | solution.py:63
  202.9 31.6 %all_to_all.65 = bf16[32,256,128]{2,1,0:T(8,128)(2,1)S(1)} all-to-all(bf16[32,256,128]{2,1,0:T(8,128)(2,1)} %bitcast.51), channel_id=1, replica_groups=mesh['zh'=2,'core'=2,'x'=4,'y'=4,'zl'=2] {'x','y','zl'}, dimensions={0} | all-to-all | bytes 4194304 | tf_op jit(solution)/shard_map/all_to_all | solution.py:155
  234.6 2.7 %copy.18 = bf16[256,32,128]{2,1,0:T(8,128)(2,1)} copy(bf16[256,32,128]{2,0,1:T(8,128)(2,1)S(1)} %bitcast.55) | data formatting | bytes 4194304 | tf_op jit(solution)/shard_map/all_to_all | solution.py:155
  237.3 4.2 %broadcast_in_dim.8 = bf16[1,256,4096]{2,1,0:T(8,128)(2,1)} reshape(bf16[256,32,128]{2,1,0:T(8,128)(2,1)} %copy.18) | data formatting | bytes 4194304 | tf_op jit(solution)/shard_map/broadcast_in_dim | solution.py:156
  (42 shorter events, 1.0 us)
Async XLA Ops:
  0.0 72.8 %collective-permute-start.1 = (bf16[2048,512]{1,0:T(8,128)(2,1)}, bf16[2048,512]{1,0:T(8,128)(2,1)}, u32[]{:S(2)}, u32[]{:S(2)}) collective-permute-start(bf16[2048,512]{1,0:T(8,128)(2,1)} %param.10), channel_id=1, source_target_pairs={{0,32},{32,0},{1,33},{33,1},{2,34},{34,2},{3,35},{35,3},{4,36},{36... | collective-permute-start | bytes 6291464 | tf_op jit(solution)/shard_map/ppermute | solution.py:117
  4.2 9.1 %copy-start.11 = (bf16[8192]{0:T(1024)(128)(2,1)S(1)}, bf16[8192]{0:T(1024)(128)(2,1)}, u32[]{:S(2)}) copy-start(bf16[8192]{0:T(1024)(128)(2,1)} %param.8) | copy-start | bytes 49156
  4.2 68.6 %all-to-all-start = ((bf16[256,32,128]{2,0,1:T(8,128)(2,1)}), bf16[256,32,128]{2,0,1:T(8,128)(2,1)}, u32[]{:S(2)}, u32[]{:S(2)}) async-start(bf16[256,32,128]{2,0,1:T(8,128)(2,1)} %copy.14), calls=%async_computation | async-start | bytes 4194304 | tf_op jit(solution)/shard_map/all_to_all | solution.py:104
  13.3 3.5 %copy-start.4 = (bf16[1,256,8192]{2,1,0:T(8,128)(2,1)S(1)}, bf16[1,256,8192]{2,1,0:T(8,128)(2,1)}, u32[]{:S(2)}) copy-start(bf16[1,256,8192]{2,1,0:T(8,128)(2,1)} %param.7) | copy-start | bytes 12582916
  20.4 6.3 %copy-start = (bf16[2048,512]{1,0:T(8,128)(2,1)S(1)}, bf16[2048,512]{1,0:T(8,128)(2,1)}, u32[]{:S(2)}) copy-start(bf16[2048,512]{1,0:T(8,128)(2,1)} %param.11) | copy-start | bytes 6291460
  22.9 84.9 %collective-permute-start.4 = (bf16[128,4096]{1,0:T(8,128)(2,1)}, bf16[128,4096]{1,0:T(8,128)(2,1)S(1)}, u32[]{:S(2)}, u32[]{:S(2)}) collective-permute-start(bf16[128,4096]{1,0:T(8,128)(2,1)} %constant_dynamic-slice_fusion), channel_id=1, source_target_pairs={{0,65},{1,64},{2,67},{3,66},{4,69},{5,68},{6,71},{7,70},{8,73},{9,... | collective-permute-start | bytes 3145736 | tf_op jit(solution)/shard_map/ppermute | solution.py:138
  26.7 49.9 %collective-permute-start.2 = (bf16[2048,512]{1,0:T(8,128)(2,1)S(1)}, bf16[2048,512]{1,0:T(8,128)(2,1)}, u32[]{:S(2)}, u32[]{:S(2)}) collective-permute-start(bf16[2048,512]{1,0:T(8,128)(2,1)S(1)} %copy-done), channel_id=1, source_target_pairs={{0,32},{32,0},{1,33},{33,1},{2,34},{34,2},{3,35},{35,3},{4,36},{36... | collective-permute-start | bytes 6291464 | tf_op jit(solution)/shard_map/ppermute | solution.py:117
  29.0 43.7 %collective-permute-start = (bf16[128,4096]{1,0:T(8,128)(2,1)}, bf16[128,4096]{1,0:T(8,128)(2,1)}, u32[]{:S(2)}, u32[]{:S(2)}) collective-permute-start(bf16[128,4096]{1,0:T(8,128)(2,1)} %constant_dynamic-slice_fusion.1), channel_id=1, source_target_pairs={{0,65},{1,64},{2,67},{3,66},{4,69},{5,68},{6,71},{7,70},{8,73},{9,... | collective-permute-start | bytes 3145736 | tf_op jit(solution)/shard_map/ppermute | solution.py:138
  29.1 2.3 copy-start.1
  31.4 2.4 copy-start.6
  72.8 2.4 copy-start.2
  78.9 4.7 %copy-start.7 = (bf16[128,8192]{1,0:T(8,128)(2,1)S(1)}, bf16[128,8192]{1,0:T(8,128)(2,1)}, u32[]{:S(2)}) copy-start(bf16[128,8192]{1,0:T(8,128)(2,1)} %get-tuple-element.10) | copy-start | bytes 6291460
  78.9 4.7 %copy-start.10 = (f32[128,512]{1,0:T(8,128)S(1)}, f32[128,512]{1,0:T(8,128)}, u32[]{:S(2)}) copy-start(f32[128,512]{1,0:T(8,128)} %fusion.25) | copy-start | bytes 786436
  80.6 14.5 %collective-permute-start.3 = (f32[128,1024]{1,0:T(8,128)S(1)}, f32[128,1024]{1,0:T(8,128)S(1)}, u32[]{:S(2)}, u32[]{:S(2)}) collective-permute-start(f32[128,1024]{1,0:T(8,128)S(1)} %pad_maximum_fusion), channel_id=1, source_target_pairs={{0,65},{1,64},{2,67},{3,66},{4,69},{5,68},{6,71},{7,70},{8,73},{9,... | collective-permute-start | bytes 1572872 | tf_op jit(solution)/shard_map/ppermute | solution.py:141
  100.4 35.0 %all-to-all-start.1 = ((bf16[128,2,32,128]{3,1,0,2:T(2,128)(2,1)}), bf16[128,2,32,128]{3,1,0,2:T(2,128)(2,1)}, u32[]{:S(2)}, u32[]{:S(2)}) async-start(bf16[128,2,32,128]{3,1,0,2:T(2,128)(2,1)} %bitcast.52), calls=%async_computation.1 | async-start | bytes 4194304 | tf_op jit(solution)/shard_map/all_to_all | solution.py:146
  111.9 1.6 copy-start.3
  113.5 4.2 %copy-start.5 = (bf16[128,8192]{1,0:T(8,128)(2,1)S(1)}, bf16[128,8192]{1,0:T(8,128)(2,1)}, u32[]{:S(2)}) copy-start(bf16[128,8192]{1,0:T(8,128)(2,1)} %get-tuple-element.9) | copy-start | bytes 6291460
  113.5 4.2 %copy-start.9 = (f32[128,512]{1,0:T(8,128)S(1)}, f32[128,512]{1,0:T(8,128)}, u32[]{:S(2)}) copy-start(f32[128,512]{1,0:T(8,128)} %fusion.13) | copy-start | bytes 786436
  113.9 5.8 %copy-start.8 = (f32[128,512]{1,0:T(8,128)S(1)}, f32[128,512]{1,0:T(8,128)}, u32[]{:S(2)}) copy-start(f32[128,512]{1,0:T(8,128)} %fusion.15) | copy-start | bytes 786436
  114.0 13.5 %collective-permute-start.5 = (f32[128,1024]{1,0:T(8,128)S(1)}, f32[128,1024]{1,0:T(8,128)S(1)}, u32[]{:S(2)}, u32[]{:S(2)}) collective-permute-start(f32[128,1024]{1,0:T(8,128)S(1)} %pad_maximum_fusion.1), channel_id=1, source_target_pairs={{0,65},{1,64},{2,67},{3,66},{4,69},{5,68},{6,71},{7,70},{8,73},{9,... | collective-permute-start | bytes 1572872 | tf_op jit(solution)/shard_map/ppermute | solution.py:141
  138.7 4.2 %copy-start.12 = (s32[1,1,64,12]{2,1,3,0:T(1,128)S(1)}, s32[1,1,64,12]{2,1,3,0:T(1,128)}, u32[]{:S(2)}) copy-start(s32[1,1,64,12]{2,1,3,0:T(1,128)} %param.12) | copy-start | bytes 9220
  138.7 32.0 %all-to-all-start.2 = ((bf16[128,2,32,128]{3,1,0,2:T(2,128)(2,1)}), bf16[128,2,32,128]{3,1,0,2:T(2,128)(2,1)S(1)}, u32[]{:S(2)}, u32[]{:S(2)}) async-start(bf16[128,2,32,128]{3,1,0,2:T(2,128)(2,1)} %bitcast.54), calls=%async_computation.2 | async-start | bytes 4194304 | tf_op jit(solution)/shard_map/all_to_all | solution.py:146

commit v15 on v12

--- a/solution.py
+++ b/solution.py
@@ -130,10 +130,11 @@
         rows = normed[chunk * chunk_rows : (chunk + 1) * chunk_rows]
         far_features = lax.dynamic_slice_in_dim(rows, (1 - zh) * half_features, half_features, axis=1)
         partner_rows = lax.ppermute(far_features, ALL_AXES, partner_pairs)
+        for_partner = half_sum(partner_rows, 0)
         if chunk == 0:
-            local_queries, partner_rows = lax.optimization_barrier((queries[0], partner_rows))
+            local_queries, for_partner = lax.optimization_barrier((queries[0], for_partner))
             head_queries = lax.all_to_all(local_queries, CTX_AXES, split_axis=1, concat_axis=0, tiled=True)
-        from_partner = lax.ppermute(half_sum(partner_rows, 0), ALL_AXES, partner_pairs)
+        from_partner = lax.ppermute(for_partner, ALL_AXES, partner_pairs)
         summed = half_sum(rows, zh * half_features) + from_partner
         paired = summed.reshape(chunk_rows, 2, KVH, 1, HD).astype(jnp.bfloat16)
         widened = jnp.broadcast_to(paired, (chunk_rows, 2, KVH, copies_per_head, HD))

time: 233 us -> 235 us (level)
  waiting for transfers between devices: 68.6 us -> 74.8 us
  starting transfers between devices: 33.5 us -> 28.9 us
    all_to_all x1, waiting for transfers between devices: 0.01 us -> 5.87 us  [on_device(): lax.all_to_all(local_queries, CTX_AXES, split_axis=1, concat_axis=0, tile...]
    all_to_all x2, waiting for transfers between devices: 22.1 us -> 27.1 us  [on_device(): lax.all_to_all(widened, CTX_AXES, split_axis=2, concat_axis=0, tiled=True)]
    all_to_all x2, starting transfers between devices: 14.4 us -> 9.69 us  [on_device(): lax.all_to_all(widened, CTX_AXES, split_axis=2, concat_axis=0, tiled=True)]
    ppermute x2, waiting for transfers between devices: 29 us -> 25.5 us  [on_device(): partner_rows = lax.ppermute(far_features, ALL_AXES, partner_pairs)]
    unnamed x19 -> x17, local copies, waits for them, and re-layouts: 7.98 us -> 7.97 us
  transfers between devices with their start and end apart: 8 -> 8, of which waited for: 5 -> 7; matrix products, arithmetic and copies ran while one was open for 19% -> 16% of each run, Pallas kernels for 0% -> 0%
where the time goes in v15:
time: 235 us; the launch traced here: 234 us
  waiting for transfers between devices  74.8 us (32%)
  local copies, waits for them, and re-layouts  43 us (18%)
  blocking collectives  31.5 us (13%)
  starting transfers between devices  28.9 us (12%)
  Pallas kernels  26.1 us (11%)
  matrix products  25.5 us (11%)
  other arithmetic  4.7 us (2%)
    all_to_all x1, blocking collectives, on_device(): lax.all_to_all(attended_head, CTX_AXES, split_axis=0, concat_axis=1, tile...  31.5 us
    all_to_all x2, waiting for transfers between devices, on_device(): lax.all_to_all(widened, CTX_AXES, split_axis=2, concat_axis=0, tiled=True)  27.1 us
    pallas_call x1, Pallas kernels, attend(): pl.pallas_call(attend_kernel, out_shape=jax.ShapeDtypeStruct((sequence_ro...  26.1 us
    ppermute x2, waiting for transfers between devices, on_device(): partner_rows = lax.ppermute(far_features, ALL_AXES, partner_pairs)  25.5 us
    ppermute x2, waiting for transfers between devices, on_device(): from_partner = lax.ppermute(for_partner, ALL_AXES, partner_pairs)  16.3 us
    dot_general x4, matrix products, half_sum(): jnp.dot(own, local_weight, preferred_element_type=jnp.float32)  13.1 us
    dot_general x4, matrix products, half_sum(): jnp.dot(other, sibling, preferred_element_type=jnp.float32)  12.3 us
    all_to_all x2, starting transfers between devices, on_device(): lax.all_to_all(widened, CTX_AXES, split_axis=2, concat_axis=0, tiled=True)  9.69 us
  transfers between devices with their start and end apart: 8, of which 7 were waited for; matrix products, arithmetic and copies ran while one was open for 16% of the time, Pallas kernels for 0%

profile of v15, /device:TPU:0, one launch (start us, length us, event | category | flops | bytes accessed | tf_op | source)
XLA Modules:
  0.0 234.5 jit_solution(13170189597219165708)
XLA Ops:
  0.0 3.3 %constant_dynamic-update-slice_fusion.1 = bf16[2048,1024]{1,0:T(8,128)(2,1)} fusion(bf16[2048,512]{1,0:T(8,128)(2,1)} %param.10), kind=kLoop, calls=%fused_computation.30 | loop fusion | bytes 4194304
  3.3 1.6 constant_dynamic-update-slice_fusion
  4.9 0.9 fusion
  5.8 3.2 %fusion.2 = bf16[256,8192]{1,0:T(8,128)(2,1)} fusion(bf16[1,256,8192]{2,1,0:T(8,128)(2,1)S(1)} %copy-done.1, f32[8192]{0:T(1024)S(1)} %convert_element_type.36, f32[256]{0:T(256)S(1)} %add_rsqrt_fusion), kind=kLoop, calls=%fused_computation.4 | loop fusion | flops 8388608 | bytes 8422400 | tf_op jit(solution)/shard_map/convert_element_type | solution.py:106
  9.0 4.0 %fusion.33 = (bf16[128,8192]{1,0:T(8,128)(2,1)}, bf16[128,8192]{1,0:T(8,128)(2,1)S(1)}) fusion(bf16[256,8192]{1,0:T(8,128)(2,1)} %fusion.2), kind=kLoop, calls=%fused_computation.54 | loop fusion | bytes 8388608 | tf_op jit(solution)/shard_map/slice | solution.py:130
  13.0 1.3 copy-done.3
  14.3 0.1 constant_dynamic-slice_fusion.1
  14.4 4.2 %collective-permute-start = (bf16[128,4096]{1,0:T(8,128)(2,1)S(1)}, bf16[128,4096]{1,0:T(8,128)(2,1)}, u32[]{:S(2)}, u32[]{:S(2)}) collective-permute-start(bf16[128,4096]{1,0:T(8,128)(2,1)S(1)} %constant_dynamic-slice_fusion.1), channel_id=1, source_target_pairs={{0,65},{1,64},{2,67},{3,66},{4,69},{5,68},{6,71},{7,70},{8,73},{9,... | collective-permute-start | bytes 3145736 | tf_op jit(solution)/shard_map/ppermute | solution.py:132
  18.6 23.9 %collective-permute-done = bf16[128,4096]{1,0:T(8,128)(2,1)} collective-permute-done((bf16[128,4096]{1,0:T(8,128)(2,1)S(1)}, bf16[128,4096]{1,0:T(8,128)(2,1)}, u32[]{:S(2)}, u32[]{:S(2)}) %collective-permute-start) | collective-permute-done | bytes 1048608 | tf_op jit(solution)/shard_map/ppermute | solution.py:132
  42.5 3.1 %fusion.16 = f32[128,1024]{1,0:T(8,128)S(1)} fusion(bf16[2048,1024]{1,0:T(8,128)(2,1)} %collective-permute-done.1, bf16[128,4096]{1,0:T(8,128)(2,1)} %collective-permute-done, s32[]{:T(128)S(6)} %select_n.38), kind=kOutput, calls=%fused_computation.26 | convolution fusion | flops 536870912 | bytes 5242884 | tf_op jit(solution)/shard_map/dot_general | solution.py:121
  45.6 3.9 %convolution_add_fusion.3 = f32[128,1024]{1,0:T(8,128)} fusion(f32[128,1024]{1,0:T(8,128)S(1)} %fusion.16, bf16[2048,1024]{1,0:T(8,128)(2,1)} %constant_dynamic-update-slice_fusion, bf16[128,4096]{1,0:T(8,128)(2,1)} %collective-permute-done, s32[]{:T(128)S(6)} %select_n.37), kind=kOutput, calls=%fused_computation.12 | convolution fusion | flops 537001984 | bytes 5767172 | tf_op jit(solution)/shard_map/dot_general | solution.py:121
  49.5 1.9 copy_bitcast_fusion
  51.4 7.4 %all-to-all-start = ((bf16[256,32,128]{2,0,1:T(8,128)(2,1)}), bf16[256,32,128]{2,0,1:T(8,128)(2,1)}, u32[]{:S(2)}, u32[]{:S(2)}) async-start(bf16[256,32,128]{2,0,1:T(8,128)(2,1)} %copy_bitcast_fusion), calls=%async_computation | async-start | bytes 4194304 | tf_op jit(solution)/shard_map/all_to_all | solution.py:136
  58.9 4.2 %collective-permute-start.2 = (f32[128,1024]{1,0:T(8,128)}, f32[128,1024]{1,0:T(8,128)}, u32[]{:S(2)}, u32[]{:S(2)}) collective-permute-start(f32[128,1024]{1,0:T(8,128)} %convolution_add_fusion.3), channel_id=1, source_target_pairs={{0,65},{1,64},{2,67},{3,66},{4,69},{5,68},{6,71},{7,70},{8,73},{9,... | collective-permute-start | bytes 1572872 | tf_op jit(solution)/shard_map/ppermute | solution.py:137
  63.1 1.3 constant_dynamic-slice_fusion
  64.4 0.1 collective-permute-start.3
  64.5 3.1 %fusion.14 = f32[128,1024]{1,0:T(8,128)S(1)} fusion(bf16[2048,1024]{1,0:T(8,128)(2,1)} %constant_dynamic-update-slice_fusion, bf16[128,8192]{1,0:T(8,128)(2,1)} %copy-done.3, s32[]{:T(128)S(6)} %select_n.39), kind=kOutput, calls=%fused_computation.24 | convolution fusion | flops 536870912 | bytes 5242884 | tf_op jit(solution)/shard_map/dot_general | solution.py:121
  67.6 8.6 %collective-permute-done.2 = f32[128,1024]{1,0:T(8,128)} collective-permute-done((f32[128,1024]{1,0:T(8,128)}, f32[128,1024]{1,0:T(8,128)}, u32[]{:S(2)}, u32[]{:S(2)}) %collective-permute-start.2) | collective-permute-done | bytes 524320 | tf_op jit(solution)/shard_map/ppermute | solution.py:137
  76.2 3.2 %fusion.6 = bf16[128,1024]{1,0:T(8,128)(2,1)S(1)} fusion(f32[128,1024]{1,0:T(8,128)} %collective-permute-done.2, f32[128,1024]{1,0:T(8,128)S(1)} %fusion.14, bf16[2048,1024]{1,0:T(8,128)(2,1)} %collective-permute-done.1, bf16[128,8192]{1,0:T(8,128)(2,1)} %copy-done.3, s32[]{:T(128)S(6)} %select_n.40), kind=kOutput, calls=%fused_computation.16 | convolution fusion | flops 537264128 | bytes 6029316 | tf_op jit(solution)/shard_map/dot_general | solution.py:121
  79.4 0.9 convert_element_type.39
  80.3 1.2 copy.15
  81.5 5.9 %all-to-all-done = bf16[256,32,128]{2,0,1:T(8,128)(2,1)} async-done(((bf16[256,32,128]{2,0,1:T(8,128)(2,1)}), bf16[256,32,128]{2,0,1:T(8,128)(2,1)}, u32[]{:S(2)}, u32[]{:S(2)}) %all-to-all-start) | async-done | bytes 2097184 | tf_op jit(solution)/shard_map/all_to_all | solution.py:136
  87.3 3.2 %broadcast_in_dim.6 = bf16[128,2,4,8,128]{4,1,0,3,2:T(2,128)(2,1)} broadcast(bf16[128,2,4,128]{3,1,0,2:T(2,128)(2,1)S(1)} %copy.15), dimensions={0,1,2,4} | broadcast | bytes 2359296 | tf_op jit(solution)/shard_map/broadcast_in_dim | solution.py:140
  90.5 4.9 %all-to-all-start.1 = ((bf16[128,2,32,128]{3,1,0,2:T(2,128)(2,1)}), bf16[128,2,32,128]{3,1,0,2:T(2,128)(2,1)}, u32[]{:S(2)}, u32[]{:S(2)}) async-start(bf16[128,2,32,128]{3,1,0,2:T(2,128)(2,1)} %bitcast.48), calls=%async_computation.1 | async-start | bytes 4194304 | tf_op jit(solution)/shard_map/all_to_all | solution.py:144
  95.5 1.6 collective-permute-done.3
  97.0 3.1 %fusion.7 = f32[128,1024]{1,0:T(8,128)S(1)} fusion(bf16[2048,1024]{1,0:T(8,128)(2,1)} %collective-permute-done.1, bf16[128,4096]{1,0:T(8,128)(2,1)} %collective-permute-done.3, s32[]{:T(128)S(6)} %select_n.38), kind=kOutput, calls=%fused_computation.17 | convolution fusion | flops 536870912 | bytes 5242884 | tf_op jit(solution)/shard_map/dot_general | solution.py:121
  100.1 3.2 %convolution_add_fusion = f32[128,1024]{1,0:T(8,128)S(1)} fusion(f32[128,1024]{1,0:T(8,128)S(1)} %fusion.7, bf16[2048,1024]{1,0:T(8,128)(2,1)} %constant_dynamic-update-slice_fusion, bf16[128,4096]{1,0:T(8,128)(2,1)} %collective-permute-done.3, s32[]{:T(128)S(6)} %select_n.37), kind=kOutput, calls=%fused_computation.9 | convolution fusion | flops 537001984 | bytes 5767172 | tf_op jit(solution)/shard_map/dot_general | solution.py:121
  103.4 3.2 %collective-permute-start.4 = (f32[128,1024]{1,0:T(8,128)S(1)}, f32[128,1024]{1,0:T(8,128)S(1)}, u32[]{:S(2)}, u32[]{:S(2)}) collective-permute-start(f32[128,1024]{1,0:T(8,128)S(1)} %convolution_add_fusion), channel_id=1, source_target_pairs={{0,65},{1,64},{2,67},{3,66},{4,69},{5,68},{6,71},{7,70},{8,73},{9,... | collective-permute-start | bytes 1572872 | tf_op jit(solution)/shard_map/ppermute | solution.py:137
  106.6 2.9 %fusion.11 = f32[128,1024]{1,0:T(8,128)S(1)} fusion(bf16[2048,1024]{1,0:T(8,128)(2,1)} %constant_dynamic-update-slice_fusion, bf16[128,8192]{1,0:T(8,128)(2,1)S(1)} %copy-done.2, s32[]{:T(128)S(6)} %select_n.39), kind=kOutput, calls=%fused_computation.21 | convolution fusion | flops 536870912 | bytes 5242884 | tf_op jit(solution)/shard_map/dot_general | solution.py:121
  109.5 7.7 %collective-permute-done.4 = f32[128,1024]{1,0:T(8,128)S(1)} collective-permute-done((f32[128,1024]{1,0:T(8,128)S(1)}, f32[128,1024]{1,0:T(8,128)S(1)}, u32[]{:S(2)}, u32[]{:S(2)}) %collective-permute-start.4) | collective-permute-done | bytes 524320 | tf_op jit(solution)/shard_map/ppermute | solution.py:137
  117.2 3.0 %fusion.5 = bf16[128,1024]{1,0:T(8,128)(2,1)S(1)} fusion(f32[128,1024]{1,0:T(8,128)S(1)} %collective-permute-done.4, f32[128,1024]{1,0:T(8,128)S(1)} %fusion.11, bf16[2048,1024]{1,0:T(8,128)(2,1)} %collective-permute-done.1, bf16[128,8192]{1,0:T(8,128)(2,1)S(1)} %copy-done.2, s32[]{:T(128)S(6)} %select_n.40), kind=kOutput, calls=%fused_computation.15 | convolution fusion | flops 537264128 | bytes 6029316 | tf_op jit(solution)/shard_map/dot_general | solution.py:121
  120.2 0.2 convert_element_type.41
  120.3 0.2 copy.16
  120.5 3.2 %all-to-all-done.1 = bf16[128,2,32,128]{3,1,0,2:T(2,128)(2,1)} async-done(((bf16[128,2,32,128]{3,1,0,2:T(2,128)(2,1)}), bf16[128,2,32,128]{3,1,0,2:T(2,128)(2,1)}, u32[]{:S(2)}, u32[]{:S(2)}) %all-to-all-start.1) | async-done | bytes 2097184 | tf_op jit(solution)/shard_map/all_to_all | solution.py:144
  123.7 3.2 %broadcast_in_dim.7 = bf16[128,2,4,8,128]{4,1,0,3,2:T(2,128)(2,1)} broadcast(bf16[128,2,4,128]{3,1,0,2:T(2,128)(2,1)S(1)} %copy.16), dimensions={0,1,2,4} | broadcast | bytes 2359296 | tf_op jit(solution)/shard_map/broadcast_in_dim | solution.py:140
  127.0 4.8 %all-to-all-start.2 = ((bf16[128,2,32,128]{3,1,0,2:T(2,128)(2,1)}), bf16[128,2,32,128]{3,1,0,2:T(2,128)(2,1)}, u32[]{:S(2)}, u32[]{:S(2)}) async-start(bf16[128,2,32,128]{3,1,0,2:T(2,128)(2,1)} %bitcast.49), calls=%async_computation.2 | async-start | bytes 4194304 | tf_op jit(solution)/shard_map/all_to_all | solution.py:144
  131.7 0.1 copy.13
  131.8 0.1 squeeze.10
  131.9 0.6 fusion.20.lists_ref
  132.5 3.3 %bitcast_dynamic-update-slice_fusion.1 = bf16[8192,256]{1,0:T(8,128)(2,1)} fusion(bf16[512,8,2,128]{3,2,1,0:T(2,128)(2,1)} %bitcast.23), kind=kLoop, calls=%fused_computation.6 | loop fusion | bytes 4194304
  135.8 23.9 %all-to-all-done.2 = bf16[128,2,32,128]{3,1,0,2:T(2,128)(2,1)} async-done(((bf16[128,2,32,128]{3,1,0,2:T(2,128)(2,1)}), bf16[128,2,32,128]{3,1,0,2:T(2,128)(2,1)}, u32[]{:S(2)}, u32[]{:S(2)}) %all-to-all-start.2) | async-done | bytes 2097184 | tf_op jit(solution)/shard_map/all_to_all | solution.py:144
  159.7 3.2 %bitcast_dynamic-update-slice_fusion.v_ref = bf16[8192,256]{1,0:T(8,128)(2,1)} fusion(bf16[8192,256]{1,0:T(8,128)(2,1)} %bitcast_dynamic-update-slice_fusion.1, bf16[512,8,2,128]{3,2,1,0:T(2,128)(2,1)} %bitcast.27), kind=kLoop, calls=%fused_computation.5 | loop fusion | bytes 4194304 | tf_op jit(solution)/shard_map/concatenate | solution.py:145
  163.0 3.0 %slice_bitcast_fusion = bf16[128,8192]{0,1:T(8,128)(2,1)} fusion(bf16[8192,256]{1,0:T(8,128)(2,1)} %bitcast_dynamic-update-slice_fusion.v_ref), kind=kLoop, calls=%fused_computation.8 | loop fusion | bytes 4194304 | tf_op jit(solution)/shard_map/transpose | solution.py:148
  166.0 4.1 %copy.17.kt_ref = bf16[128,8192]{1,0:T(8,128)(2,1)} copy(bf16[128,8192]{0,1:T(8,128)(2,1)} %slice_bitcast_fusion) | data formatting | bytes 4194304 | tf_op jit(solution)/shard_map/transpose | solution.py:148
  170.1 26.1 %shard_map.73 = bf16[8192,128]{1,0:T(8,128)(2,1)} custom-call(s32[768]{0:T(1024)} %fusion.20.lists_ref, s32[64]{0:T(128)} %bitcast.51, bf16[8192,128]{1,0:T(8,128)(2,1)} %bitcast.5.q_ref, bf16[128,8192]{1,0:T(8,128)(2,1)} %copy.17.kt_ref, bf16[8192,256]{1,0:T(8,128)(2,1)} %bitcast_dynamic-update-slice_fusion.v_ref), custom_call_target="tpu_custom_call" | custom-call | tf_op jit(solution)/shard_map/pallas_call | solution.py:63
  196.2 31.5 %all_to_all.65 = bf16[32,256,128]{2,1,0:T(8,128)(2,1)S(1)} all-to-all(bf16[32,256,128]{2,1,0:T(8,128)(2,1)} %bitcast.47), channel_id=1, replica_groups=mesh['zh'=2,'core'=2,'x'=4,'y'=4,'zl'=2] {'x','y','zl'}, dimensions={0} | all-to-all | bytes 4194304 | tf_op jit(solution)/shard_map/all_to_all | solution.py:153
  227.7 2.7 %copy.18 = bf16[256,32,128]{2,1,0:T(8,128)(2,1)} copy(bf16[256,32,128]{2,0,1:T(8,128)(2,1)S(1)} %bitcast.50) | data formatting | bytes 4194304 | tf_op jit(solution)/shard_map/all_to_all | solution.py:153
  230.3 4.2 %broadcast_in_dim.8 = bf16[1,256,4096]{2,1,0:T(8,128)(2,1)} reshape(bf16[256,32,128]{2,1,0:T(8,128)(2,1)} %copy.18) | data formatting | bytes 4194304 | tf_op jit(solution)/shard_map/broadcast_in_dim | solution.py:154
  (17 shorter events, 0.0 us)
Async XLA Ops:
  0.0 49.5 %copy-start = (bf16[1,256,4096]{2,1,0:T(8,128)(2,1)S(1)}, bf16[1,256,4096]{2,1,0:T(8,128)(2,1)}, u32[]{:S(2)}) copy-start(bf16[1,256,4096]{2,1,0:T(8,128)(2,1)} %param.9) | copy-start | bytes 6291460
  0.0 3.3 %copy-start.4 = (bf16[2048,512]{1,0:T(8,128)(2,1)S(1)}, bf16[2048,512]{1,0:T(8,128)(2,1)}, u32[]{:S(2)}) copy-start(bf16[2048,512]{1,0:T(8,128)(2,1)} %param.11) | copy-start | bytes 6291460
  0.0 4.8 %copy-start.5 = (bf16[8192]{0:T(1024)(128)(2,1)S(1)}, bf16[8192]{0:T(1024)(128)(2,1)}, u32[]{:S(2)}) copy-start(bf16[8192]{0:T(1024)(128)(2,1)} %param.8) | copy-start | bytes 49156
  0.0 4.8 %copy-start.1 = (bf16[1,256,8192]{2,1,0:T(8,128)(2,1)S(1)}, bf16[1,256,8192]{2,1,0:T(8,128)(2,1)}, u32[]{:S(2)}) copy-start(bf16[1,256,8192]{2,1,0:T(8,128)(2,1)} %param.7) | copy-start | bytes 12582916
  4.8 37.7 %collective-permute-start.1 = (bf16[2048,1024]{1,0:T(8,128)(2,1)}, bf16[2048,1024]{1,0:T(8,128)(2,1)}, u32[]{:S(2)}, u32[]{:S(2)}) collective-permute-start(bf16[2048,1024]{1,0:T(8,128)(2,1)} %constant_dynamic-update-slice_fusion), channel_id=1, source_target_pairs={{0,32},{32,0},{1,33},{33,1},{2,34},{34,2},{3,35},{35,3},{4,36},{36... | collective-permute-start | bytes 12582920 | tf_op jit(solution)/shard_map/ppermute | solution.py:116
  13.0 1.3 copy-start.3
  14.4 28.2 %collective-permute-start = (bf16[128,4096]{1,0:T(8,128)(2,1)S(1)}, bf16[128,4096]{1,0:T(8,128)(2,1)}, u32[]{:S(2)}, u32[]{:S(2)}) collective-permute-start(bf16[128,4096]{1,0:T(8,128)(2,1)S(1)} %constant_dynamic-slice_fusion.1), channel_id=1, source_target_pairs={{0,65},{1,64},{2,67},{3,66},{4,69},{5,68},{6,71},{7,70},{8,73},{9,... | collective-permute-start | bytes 3145736 | tf_op jit(solution)/shard_map/ppermute | solution.py:132
  51.4 35.9 %all-to-all-start = ((bf16[256,32,128]{2,0,1:T(8,128)(2,1)}), bf16[256,32,128]{2,0,1:T(8,128)(2,1)}, u32[]{:S(2)}, u32[]{:S(2)}) async-start(bf16[256,32,128]{2,0,1:T(8,128)(2,1)} %copy_bitcast_fusion), calls=%async_computation | async-start | bytes 4194304 | tf_op jit(solution)/shard_map/all_to_all | solution.py:136
  58.9 17.3 %collective-permute-start.2 = (f32[128,1024]{1,0:T(8,128)}, f32[128,1024]{1,0:T(8,128)}, u32[]{:S(2)}, u32[]{:S(2)}) collective-permute-start(f32[128,1024]{1,0:T(8,128)} %convolution_add_fusion.3), channel_id=1, source_target_pairs={{0,65},{1,64},{2,67},{3,66},{4,69},{5,68},{6,71},{7,70},{8,73},{9,... | collective-permute-start | bytes 1572872 | tf_op jit(solution)/shard_map/ppermute | solution.py:137
  64.4 32.7 %collective-permute-start.3 = (bf16[128,4096]{1,0:T(8,128)(2,1)S(1)}, bf16[128,4096]{1,0:T(8,128)(2,1)}, u32[]{:S(2)}, u32[]{:S(2)}) collective-permute-start(bf16[128,4096]{1,0:T(8,128)(2,1)S(1)} %constant_dynamic-slice_fusion), channel_id=1, source_target_pairs={{0,65},{1,64},{2,67},{3,66},{4,69},{5,68},{6,71},{7,70},{8,73},{9,... | collective-permute-start | bytes 3145736 | tf_op jit(solution)/shard_map/ppermute | solution.py:132
  90.5 33.2 %all-to-all-start.1 = ((bf16[128,2,32,128]{3,1,0,2:T(2,128)(2,1)}), bf16[128,2,32,128]{3,1,0,2:T(2,128)(2,1)}, u32[]{:S(2)}, u32[]{:S(2)}) async-start(bf16[128,2,32,128]{3,1,0,2:T(2,128)(2,1)} %bitcast.48), calls=%async_computation.1 | async-start | bytes 4194304 | tf_op jit(solution)/shard_map/all_to_all | solution.py:144
  100.1 6.5 %copy-start.2 = (bf16[128,8192]{1,0:T(8,128)(2,1)S(1)}, bf16[128,8192]{1,0:T(8,128)(2,1)}, u32[]{:S(2)}) copy-start(bf16[128,8192]{1,0:T(8,128)(2,1)} %get-tuple-element.13) | copy-start | bytes 6291460
  103.4 13.8 %collective-permute-start.4 = (f32[128,1024]{1,0:T(8,128)S(1)}, f32[128,1024]{1,0:T(8,128)S(1)}, u32[]{:S(2)}, u32[]{:S(2)}) collective-permute-start(f32[128,1024]{1,0:T(8,128)S(1)} %convolution_add_fusion), channel_id=1, source_target_pairs={{0,65},{1,64},{2,67},{3,66},{4,69},{5,68},{6,71},{7,70},{8,73},{9,... | collective-permute-start | bytes 1572872 | tf_op jit(solution)/shard_map/ppermute | solution.py:137
  120.1 11.6 %copy-start.6 = (s32[1,1,64,12]{2,1,3,0:T(1,128)S(1)}, s32[1,1,64,12]{2,1,3,0:T(1,128)}, u32[]{:S(2)}) copy-start(s32[1,1,64,12]{2,1,3,0:T(1,128)} %param.12) | copy-start | bytes 9220
  127.0 32.8 %all-to-all-start.2 = ((bf16[128,2,32,128]{3,1,0,2:T(2,128)(2,1)}), bf16[128,2,32,128]{3,1,0,2:T(2,128)(2,1)}, u32[]{:S(2)}, u32[]{:S(2)}) async-start(bf16[128,2,32,128]{3,1,0,2:T(2,128)(2,1)} %bitcast.49), calls=%async_computation.2 | async-start | bytes 4194304 | tf_op jit(solution)/shard_map/all_to_all | solution.py:144

commit v16 on v11

--- a/solution.py
+++ b/solution.py
@@ -11,7 +11,7 @@
 MAXB = 12
 
 
-SUB_BLOCKS = 8
+SUB_BLOCKS = 16
 CHUNKS = 2
 
 
@@ -53,7 +53,7 @@
         o_ref[pl.ds(first_row, BLK), :] = (weighted / denominator).astype(o_ref.dtype)
         return carry
 
-    lax.fori_loop(0, SUB_BLOCKS, one_block, 0, unroll=8)
+    lax.fori_loop(0, SUB_BLOCKS, one_block, 0, unroll=16)
 
 
 def attend(lists_flat, counts, head_queries, key_t, kv_rows):

time: 228 us -> 225 us (0.987)
  Pallas kernels: 26.1 us -> 23.8 us
    pallas_call x1, Pallas kernels: 26.1 us -> 23.8 us  [attend(): pl.pallas_call(attend_kernel, out_shape=jax.ShapeDtypeStruct((sequence_ro...]
where the time goes in v16:
time: 225 us
  waiting for transfers between devices  71.8 us (32%)
  starting transfers between devices  33.3 us (15%)
  blocking collectives  32.3 us (14%)
  local copies, waits for them, and re-layouts  32 us (14%)
  matrix products  26.3 us (12%)
  Pallas kernels  23.8 us (11%)
  other arithmetic  5.06 us (2%)
    all_to_all x1, blocking collectives, on_device(): lax.all_to_all(attended_head, CTX_AXES, split_axis=0, concat_axis=1, tile...  32.3 us
    ppermute x2, waiting for transfers between devices, on_device(): partner_rows = lax.ppermute(far_features, ALL_AXES, partner_pairs)  30.3 us
    pallas_call x1, Pallas kernels, attend(): pl.pallas_call(attend_kernel, out_shape=jax.ShapeDtypeStruct((sequence_ro...  23.8 us
    all_to_all x2, waiting for transfers between devices, on_device(): lax.all_to_all(widened, CTX_AXES, split_axis=2, concat_axis=0, tiled=True)  23.7 us
    ppermute x2, waiting for transfers between devices, on_device(): lax.ppermute(half_sum(partner_rows, 0), ALL_AXES, partner_pairs)  17.8 us
    all_to_all x2, starting transfers between devices, on_device(): lax.all_to_all(widened, CTX_AXES, split_axis=2, concat_axis=0, tiled=True)  14.3 us
    dot_general x4, matrix products, half_sum(): jnp.dot(own, local_weight, preferred_element_type=jnp.float32)  13.2 us
    dot_general x4, matrix products, half_sum(): jnp.dot(other, sibling, preferred_element_type=jnp.float32)  13.1 us
  transfers between devices with their start and end apart: 8, of which 5 were waited for; matrix products, arithmetic and copies ran while one was open for 16% of the time, Pallas kernels for 0%

profile of v16, /device:TPU:0, one launch (start us, length us, event | category | flops | bytes accessed | tf_op | source)
XLA Modules:
  0.0 224.8 jit_solution(12349970006063178403)
XLA Ops:
  0.0 3.3 %constant_dynamic-update-slice_fusion.1 = bf16[2048,1024]{1,0:T(8,128)(2,1)} fusion(bf16[2048,512]{1,0:T(8,128)(2,1)} %param.10), kind=kLoop, calls=%fused_computation.29 | loop fusion | bytes 4194304
  3.3 1.5 constant_dynamic-update-slice_fusion
  4.8 0.5 copy.19
  5.3 2.1 copy.14
  7.5 8.8 %all-to-all-start = ((bf16[256,32,128]{2,0,1:T(8,128)(2,1)}), bf16[256,32,128]{2,0,1:T(8,128)(2,1)S(1)}, u32[]{:S(2)}, u32[]{:S(2)}) async-start(bf16[256,32,128]{2,0,1:T(8,128)(2,1)} %copy.14), calls=%async_computation | async-start | bytes 4194304 | tf_op jit(solution)/shard_map/all_to_all | solution.py:104
  16.3 0.0 copy-start
  16.3 3.3 %fusion = f32[256]{0:T(256)S(1)} fusion(bf16[1,256,8192]{2,1,0:T(8,128)(2,1)} %param.7), kind=kLoop, calls=%fused_computation.2 | loop fusion | flops 6291200 | bytes 4195328 | tf_op jit(solution)/shard_map/reduce_sum | solution.py:106
  19.5 0.2 copy-done
  19.7 1.2 fusion.2
  20.9 2.4 %fusion.33 = (bf16[128,8192]{1,0:T(8,128)(2,1)}, bf16[128,8192]{1,0:T(8,128)(2,1)}) fusion(bf16[256,8192]{1,0:T(8,128)(2,1)S(1)} %fusion.2), kind=kLoop, calls=%fused_computation.53 | loop fusion | bytes 8388608 | tf_op jit(solution)/shard_map/slice | solution.py:131
  23.3 1.3 constant_dynamic-slice_fusion.1
  24.6 4.0 %collective-permute-start = (bf16[128,4096]{1,0:T(8,128)(2,1)S(1)}, bf16[128,4096]{1,0:T(8,128)(2,1)}, u32[]{:S(2)}, u32[]{:S(2)}) collective-permute-start(bf16[128,4096]{1,0:T(8,128)(2,1)S(1)} %constant_dynamic-slice_fusion.1), channel_id=1, source_target_pairs={{0,65},{1,64},{2,67},{3,66},{4,69},{5,68},{6,71},{7,70},{8,73},{9,... | collective-permute-start | bytes 3145736 | tf_op jit(solution)/shard_map/ppermute | solution.py:133
  28.6 23.4 %collective-permute-done = bf16[128,4096]{1,0:T(8,128)(2,1)} collective-permute-done((bf16[128,4096]{1,0:T(8,128)(2,1)S(1)}, bf16[128,4096]{1,0:T(8,128)(2,1)}, u32[]{:S(2)}, u32[]{:S(2)}) %collective-permute-start) | collective-permute-done | bytes 1048608 | tf_op jit(solution)/shard_map/ppermute | solution.py:133
  52.0 3.8 %fusion.13 = f32[128,1024]{1,0:T(8,128)S(1)} fusion(bf16[2048,1024]{1,0:T(8,128)(2,1)} %collective-permute-done.1, bf16[128,4096]{1,0:T(8,128)(2,1)} %collective-permute-done, s32[]{:T(128)S(6)} %select_n.40), kind=kOutput, calls=%fused_computation.22 | convolution fusion | flops 536870912 | bytes 5242884 | tf_op jit(solution)/shard_map/dot_general | solution.py:122
  55.8 4.1 %convolution_add_fusion.2 = f32[128,1024]{1,0:T(8,128)} fusion(f32[128,1024]{1,0:T(8,128)S(1)} %fusion.13, bf16[2048,1024]{1,0:T(8,128)(2,1)} %constant_dynamic-update-slice_fusion, bf16[128,4096]{1,0:T(8,128)(2,1)} %collective-permute-done, s32[]{:T(128)S(6)} %select_n.39), kind=kOutput, calls=%fused_computation.10 | convolution fusion | flops 537001984 | bytes 5767172 | tf_op jit(solution)/shard_map/dot_general | solution.py:122
  59.9 2.9 %collective-permute-start.2 = (f32[128,1024]{1,0:T(8,128)}, f32[128,1024]{1,0:T(8,128)}, u32[]{:S(2)}, u32[]{:S(2)}) collective-permute-start(f32[128,1024]{1,0:T(8,128)} %convolution_add_fusion.2), channel_id=1, source_target_pairs={{0,65},{1,64},{2,67},{3,66},{4,69},{5,68},{6,71},{7,70},{8,73},{9,... | collective-permute-start | bytes 1572872 | tf_op jit(solution)/shard_map/ppermute | solution.py:136
  62.8 0.1 constant_dynamic-slice_fusion
  62.9 0.4 collective-permute-start.3
  63.3 3.1 %fusion.17 = f32[128,1024]{1,0:T(8,128)S(1)} fusion(bf16[2048,1024]{1,0:T(8,128)(2,1)} %constant_dynamic-update-slice_fusion, bf16[128,8192]{1,0:T(8,128)(2,1)} %get-tuple-element.10, s32[]{:T(128)S(6)} %select_n.37), kind=kOutput, calls=%fused_computation.26 | convolution fusion | flops 536870912 | bytes 5242884 | tf_op jit(solution)/shard_map/dot_general | solution.py:122
  66.3 9.9 %collective-permute-done.2 = f32[128,1024]{1,0:T(8,128)} collective-permute-done((f32[128,1024]{1,0:T(8,128)}, f32[128,1024]{1,0:T(8,128)}, u32[]{:S(2)}, u32[]{:S(2)}) %collective-permute-start.2) | collective-permute-done | bytes 524320 | tf_op jit(solution)/shard_map/ppermute | solution.py:136
  76.2 3.2 %fusion.6 = bf16[128,1024]{1,0:T(8,128)(2,1)S(1)} fusion(f32[128,1024]{1,0:T(8,128)} %collective-permute-done.2, f32[128,1024]{1,0:T(8,128)S(1)} %fusion.17, bf16[2048,1024]{1,0:T(8,128)(2,1)} %collective-permute-done.1, bf16[128,8192]{1,0:T(8,128)(2,1)} %get-tuple-element.10, s32[]{:T(128)S(6)} %select_n.38), kind=kOutput, calls=%fused_computation.15 | convolution fusion | flops 537264128 | bytes 6029316 | tf_op jit(solution)/shard_map/dot_general | solution.py:122
  79.4 0.2 convert_element_type.39
  79.6 0.2 copy.15
  79.8 3.2 %broadcast_in_dim.6 = bf16[128,2,4,8,128]{4,1,0,3,2:T(2,128)(2,1)} broadcast(bf16[128,2,4,128]{3,1,0,2:T(2,128)(2,1)S(1)} %copy.15), dimensions={0,1,2,4} | broadcast | bytes 2359296 | tf_op jit(solution)/shard_map/broadcast_in_dim | solution.py:139
  83.0 7.1 %all-to-all-start.1 = ((bf16[128,2,32,128]{3,1,0,2:T(2,128)(2,1)}), bf16[128,2,32,128]{3,1,0,2:T(2,128)(2,1)S(1)}, u32[]{:S(2)}, u32[]{:S(2)}) async-start(bf16[128,2,32,128]{3,1,0,2:T(2,128)(2,1)} %bitcast.46), calls=%async_computation.1 | async-start | bytes 4194304 | tf_op jit(solution)/shard_map/all_to_all | solution.py:141
  90.1 7.0 %collective-permute-done.3 = bf16[128,4096]{1,0:T(8,128)(2,1)} collective-permute-done((bf16[128,4096]{1,0:T(8,128)(2,1)S(1)}, bf16[128,4096]{1,0:T(8,128)(2,1)}, u32[]{:S(2)}, u32[]{:S(2)}) %collective-permute-start.3) | collective-permute-done | bytes 1048608 | tf_op jit(solution)/shard_map/ppermute | solution.py:133
  97.1 3.1 %fusion.7 = f32[128,1024]{1,0:T(8,128)S(1)} fusion(bf16[2048,1024]{1,0:T(8,128)(2,1)} %collective-permute-done.1, bf16[128,4096]{1,0:T(8,128)(2,1)} %collective-permute-done.3, s32[]{:T(128)S(6)} %select_n.40), kind=kOutput, calls=%fused_computation.16 | convolution fusion | flops 536870912 | bytes 5242884 | tf_op jit(solution)/shard_map/dot_general | solution.py:122
  100.1 3.2 %convolution_add_fusion = f32[128,1024]{1,0:T(8,128)S(1)} fusion(f32[128,1024]{1,0:T(8,128)S(1)} %fusion.7, bf16[2048,1024]{1,0:T(8,128)(2,1)} %constant_dynamic-update-slice_fusion, bf16[128,4096]{1,0:T(8,128)(2,1)} %collective-permute-done.3, s32[]{:T(128)S(6)} %select_n.39), kind=kOutput, calls=%fused_computation.8 | convolution fusion | flops 537001984 | bytes 5767172 | tf_op jit(solution)/shard_map/dot_general | solution.py:122
  103.4 2.9 %collective-permute-start.4 = (f32[128,1024]{1,0:T(8,128)S(1)}, f32[128,1024]{1,0:T(8,128)S(1)}, u32[]{:S(2)}, u32[]{:S(2)}) collective-permute-start(f32[128,1024]{1,0:T(8,128)S(1)} %convolution_add_fusion), channel_id=1, source_target_pairs={{0,65},{1,64},{2,67},{3,66},{4,69},{5,68},{6,71},{7,70},{8,73},{9,... | collective-permute-start | bytes 1572872 | tf_op jit(solution)/shard_map/ppermute | solution.py:136
  106.3 2.9 %fusion.11 = f32[128,1024]{1,0:T(8,128)S(1)} fusion(bf16[2048,1024]{1,0:T(8,128)(2,1)} %constant_dynamic-update-slice_fusion, bf16[128,8192]{1,0:T(8,128)(2,1)S(1)} %copy-done.3, s32[]{:T(128)S(6)} %select_n.37), kind=kOutput, calls=%fused_computation.20 | convolution fusion | flops 536870912 | bytes 5242884 | tf_op jit(solution)/shard_map/dot_general | solution.py:122
  109.2 8.0 %collective-permute-done.4 = f32[128,1024]{1,0:T(8,128)S(1)} collective-permute-done((f32[128,1024]{1,0:T(8,128)S(1)}, f32[128,1024]{1,0:T(8,128)S(1)}, u32[]{:S(2)}, u32[]{:S(2)}) %collective-permute-start.4) | collective-permute-done | bytes 524320 | tf_op jit(solution)/shard_map/ppermute | solution.py:136
  117.2 3.0 %fusion.5 = bf16[128,1024]{1,0:T(8,128)(2,1)S(1)} fusion(f32[128,1024]{1,0:T(8,128)S(1)} %collective-permute-done.4, f32[128,1024]{1,0:T(8,128)S(1)} %fusion.11, bf16[2048,1024]{1,0:T(8,128)(2,1)} %collective-permute-done.1, bf16[128,8192]{1,0:T(8,128)(2,1)S(1)} %copy-done.3, s32[]{:T(128)S(6)} %select_n.38), kind=kOutput, calls=%fused_computation.14 | convolution fusion | flops 537264128 | bytes 6029316 | tf_op jit(solution)/shard_map/dot_general | solution.py:122
  120.2 0.2 convert_element_type.41
  120.4 0.2 copy.16
  120.6 3.2 %broadcast_in_dim.7 = bf16[128,2,4,8,128]{4,1,0,3,2:T(2,128)(2,1)} broadcast(bf16[128,2,4,128]{3,1,0,2:T(2,128)(2,1)S(1)} %copy.16), dimensions={0,1,2,4} | broadcast | bytes 2359296 | tf_op jit(solution)/shard_map/broadcast_in_dim | solution.py:139
  123.8 7.2 %all-to-all-start.2 = ((bf16[128,2,32,128]{3,1,0,2:T(2,128)(2,1)}), bf16[128,2,32,128]{3,1,0,2:T(2,128)(2,1)}, u32[]{:S(2)}, u32[]{:S(2)}) async-start(bf16[128,2,32,128]{3,1,0,2:T(2,128)(2,1)} %bitcast.47), calls=%async_computation.2 | async-start | bytes 4194304 | tf_op jit(solution)/shard_map/all_to_all | solution.py:141
  131.0 0.1 copy.13
  131.1 0.1 squeeze.8
  131.2 0.6 fusion.20.lists_ref
  131.8 1.7 bitcast_dynamic-update-slice_fusion.1
  133.5 23.7 %all-to-all-done.2 = bf16[128,2,32,128]{3,1,0,2:T(2,128)(2,1)} async-done(((bf16[128,2,32,128]{3,1,0,2:T(2,128)(2,1)}), bf16[128,2,32,128]{3,1,0,2:T(2,128)(2,1)}, u32[]{:S(2)}, u32[]{:S(2)}) %all-to-all-start.2) | async-done | bytes 2097184 | tf_op jit(solution)/shard_map/all_to_all | solution.py:141
  157.2 3.2 %bitcast_dynamic-update-slice_fusion.v_ref = bf16[8192,256]{1,0:T(8,128)(2,1)} fusion(bf16[8192,256]{1,0:T(8,128)(2,1)} %bitcast_dynamic-update-slice_fusion.1, bf16[512,8,2,128]{3,2,1,0:T(2,128)(2,1)} %bitcast.27), kind=kLoop, calls=%fused_computation.5 | loop fusion | bytes 4194304 | tf_op jit(solution)/shard_map/concatenate | solution.py:142
  160.5 1.7 slice_bitcast_fusion
  162.2 2.9 %copy.17.kt_ref = bf16[128,8192]{1,0:T(8,128)(2,1)} copy(bf16[128,8192]{0,1:T(8,128)(2,1)S(1)} %slice_bitcast_fusion) | data formatting | bytes 4194304 | tf_op jit(solution)/shard_map/transpose | solution.py:145
  165.1 23.8 %shard_map.73 = bf16[8192,128]{1,0:T(8,128)(2,1)} custom-call(s32[768]{0:T(1024)} %fusion.20.lists_ref, s32[64]{0:T(128)} %bitcast.51, bf16[8192,128]{1,0:T(8,128)(2,1)} %bitcast.43, bf16[128,8192]{1,0:T(8,128)(2,1)} %copy.17.kt_ref, bf16[8192,256]{1,0:T(8,128)(2,1)} %bitcast_dynamic-update-slice_fusion.v_ref), custom_call_target="tpu_custom_call" | custom-call | tf_op jit(solution)/shard_map/pallas_call | solution.py:63
  188.9 32.3 %all_to_all.65 = bf16[32,256,128]{2,1,0:T(8,128)(2,1)S(1)} all-to-all(bf16[32,256,128]{2,1,0:T(8,128)(2,1)} %bitcast.44), channel_id=1, replica_groups=mesh['zh'=2,'core'=2,'x'=4,'y'=4,'zl'=2] {'x','y','zl'}, dimensions={0} | all-to-all | bytes 4194304 | tf_op jit(solution)/shard_map/all_to_all | solution.py:150
  221.2 1.4 copy.18
  222.5 2.3 %broadcast_in_dim.8 = bf16[1,256,4096]{2,1,0:T(8,128)(2,1)} reshape(bf16[256,32,128]{2,1,0:T(8,128)(2,1)S(1)} %copy.18) | data formatting | bytes 4194304 | tf_op jit(solution)/shard_map/broadcast_in_dim | solution.py:151
  (20 shorter events, 0.1 us)
Async XLA Ops:
  0.0 3.3 %copy-start.4 = (bf16[2048,512]{1,0:T(8,128)(2,1)S(1)}, bf16[2048,512]{1,0:T(8,128)(2,1)}, u32[]{:S(2)}) copy-start(bf16[2048,512]{1,0:T(8,128)(2,1)} %param.11) | copy-start | bytes 6291460
  0.0 4.8 %copy-start.5 = (bf16[1,256,4096]{2,1,0:T(8,128)(2,1)S(1)}, bf16[1,256,4096]{2,1,0:T(8,128)(2,1)}, u32[]{:S(2)}) copy-start(bf16[1,256,4096]{2,1,0:T(8,128)(2,1)} %param.9) | copy-start | bytes 6291460
  4.8 47.2 %collective-permute-start.1 = (bf16[2048,1024]{1,0:T(8,128)(2,1)}, bf16[2048,1024]{1,0:T(8,128)(2,1)}, u32[]{:S(2)}, u32[]{:S(2)}) collective-permute-start(bf16[2048,1024]{1,0:T(8,128)(2,1)} %constant_dynamic-update-slice_fusion), channel_id=1, source_target_pairs={{0,32},{32,0},{1,33},{33,1},{2,34},{34,2},{3,35},{35,3},{4,36},{36... | collective-permute-start | bytes 12582920 | tf_op jit(solution)/shard_map/ppermute | solution.py:117
  5.3 10.9 %copy-start.6 = (bf16[8192]{0:T(1024)(128)(2,1)S(1)}, bf16[8192]{0:T(1024)(128)(2,1)}, u32[]{:S(2)}) copy-start(bf16[8192]{0:T(1024)(128)(2,1)} %param.8) | copy-start | bytes 49156
  7.5 44.5 %all-to-all-start = ((bf16[256,32,128]{2,0,1:T(8,128)(2,1)}), bf16[256,32,128]{2,0,1:T(8,128)(2,1)S(1)}, u32[]{:S(2)}, u32[]{:S(2)}) async-start(bf16[256,32,128]{2,0,1:T(8,128)(2,1)} %copy.14), calls=%async_computation | async-start | bytes 4194304 | tf_op jit(solution)/shard_map/all_to_all | solution.py:104
  16.3 3.5 %copy-start = (bf16[1,256,8192]{2,1,0:T(8,128)(2,1)S(1)}, bf16[1,256,8192]{2,1,0:T(8,128)(2,1)}, u32[]{:S(2)}) copy-start(bf16[1,256,8192]{2,1,0:T(8,128)(2,1)} %param.7) | copy-start | bytes 12582916
  24.6 27.4 %collective-permute-start = (bf16[128,4096]{1,0:T(8,128)(2,1)S(1)}, bf16[128,4096]{1,0:T(8,128)(2,1)}, u32[]{:S(2)}, u32[]{:S(2)}) collective-permute-start(bf16[128,4096]{1,0:T(8,128)(2,1)S(1)} %constant_dynamic-slice_fusion.1), channel_id=1, source_target_pairs={{0,65},{1,64},{2,67},{3,66},{4,69},{5,68},{6,71},{7,70},{8,73},{9,... | collective-permute-start | bytes 3145736 | tf_op jit(solution)/shard_map/ppermute | solution.py:133
  52.0 7.9 %copy-start.1 = (bf16[256,32,128]{2,0,1:T(8,128)(2,1)}, bf16[256,32,128]{2,0,1:T(8,128)(2,1)S(1)}, u32[]{:S(2)}) copy-start(bf16[256,32,128]{2,0,1:T(8,128)(2,1)S(1)} %all-to-all-done) | copy-start | bytes 6291460
  55.8 7.0 %copy-start.2 = (bf16[128,8192]{1,0:T(8,128)(2,1)S(1)}, bf16[128,8192]{1,0:T(8,128)(2,1)}, u32[]{:S(2)}) copy-start(bf16[128,8192]{1,0:T(8,128)(2,1)} %get-tuple-element.9) | copy-start | bytes 6291460
  59.9 16.3 %collective-permute-start.2 = (f32[128,1024]{1,0:T(8,128)}, f32[128,1024]{1,0:T(8,128)}, u32[]{:S(2)}, u32[]{:S(2)}) collective-permute-start(f32[128,1024]{1,0:T(8,128)} %convolution_add_fusion.2), channel_id=1, source_target_pairs={{0,65},{1,64},{2,67},{3,66},{4,69},{5,68},{6,71},{7,70},{8,73},{9,... | collective-permute-start | bytes 1572872 | tf_op jit(solution)/shard_map/ppermute | solution.py:136
  62.9 34.2 %collective-permute-start.3 = (bf16[128,4096]{1,0:T(8,128)(2,1)S(1)}, bf16[128,4096]{1,0:T(8,128)(2,1)}, u32[]{:S(2)}, u32[]{:S(2)}) collective-permute-start(bf16[128,4096]{1,0:T(8,128)(2,1)S(1)} %constant_dynamic-slice_fusion), channel_id=1, source_target_pairs={{0,65},{1,64},{2,67},{3,66},{4,69},{5,68},{6,71},{7,70},{8,73},{9,... | collective-permute-start | bytes 3145736 | tf_op jit(solution)/shard_map/ppermute | solution.py:133
  83.0 37.5 %all-to-all-start.1 = ((bf16[128,2,32,128]{3,1,0,2:T(2,128)(2,1)}), bf16[128,2,32,128]{3,1,0,2:T(2,128)(2,1)S(1)}, u32[]{:S(2)}, u32[]{:S(2)}) async-start(bf16[128,2,32,128]{3,1,0,2:T(2,128)(2,1)} %bitcast.46), calls=%async_computation.1 | async-start | bytes 4194304 | tf_op jit(solution)/shard_map/all_to_all | solution.py:141
  100.1 6.2 %copy-start.3 = (bf16[128,8192]{1,0:T(8,128)(2,1)S(1)}, bf16[128,8192]{1,0:T(8,128)(2,1)}, u32[]{:S(2)}) copy-start(bf16[128,8192]{1,0:T(8,128)(2,1)} %get-tuple-element.9) | copy-start | bytes 6291460
  103.4 13.8 %collective-permute-start.4 = (f32[128,1024]{1,0:T(8,128)S(1)}, f32[128,1024]{1,0:T(8,128)S(1)}, u32[]{:S(2)}, u32[]{:S(2)}) collective-permute-start(f32[128,1024]{1,0:T(8,128)S(1)} %convolution_add_fusion), channel_id=1, source_target_pairs={{0,65},{1,64},{2,67},{3,66},{4,69},{5,68},{6,71},{7,70},{8,73},{9,... | collective-permute-start | bytes 1572872 | tf_op jit(solution)/shard_map/ppermute | solution.py:136
  120.2 10.9 %copy-start.7 = (s32[1,1,64,12]{2,1,3,0:T(1,128)S(1)}, s32[1,1,64,12]{2,1,3,0:T(1,128)}, u32[]{:S(2)}) copy-start(s32[1,1,64,12]{2,1,3,0:T(1,128)} %param.12) | copy-start | bytes 9220
  123.8 33.4 %all-to-all-start.2 = ((bf16[128,2,32,128]{3,1,0,2:T(2,128)(2,1)}), bf16[128,2,32,128]{3,1,0,2:T(2,128)(2,1)}, u32[]{:S(2)}, u32[]{:S(2)}) async-start(bf16[128,2,32,128]{3,1,0,2:T(2,128)(2,1)} %bitcast.47), calls=%async_computation.2 | async-start | bytes 4194304 | tf_op jit(solution)/shard_map/all_to_all | solution.py:141
